TPU v7x, 512 devices: a whole 4x4x16 slice. The times are simulated.
512 devices in a mesh: section: 2 (over core), expert: 32 (over z_lo, x), tensor: 8 (over y, z_hi).
Axes of the slice: x: 4, y: 4, z: 16 (z_hi: 2, z_lo: 8; z = z_hi * 8 + z_lo), core: 2. Of those that a mesh axis runs over, the one named last changes fastest.
Arguments:
- sent: bfloat16 [2, 4096, 4096], P('section', ('expert', 'tensor')), may hold values from -20 to 20
- norm_gain: float32 [2, 4096], P('section'), may hold values from 0.1 to 1.9
- router: bfloat16 [2, 4096, 32], P('section'), may hold values from -0.09375 to 0.09375
- w_in: bfloat16 [2, 32, 4096, 2048], P('section', 'expert', None, 'tensor'), may hold values from -0.09375 to 0.09375
- w_out: bfloat16 [2, 32, 2048, 4096], P('section', 'expert', 'tensor'), may hold values from -0.125 to 0.125
- expert_ids: int32 [2, 4096, 2], P('section', ('expert', 'tensor')), may hold values from 0 to 31, as said below
Outputs:
- handed: bfloat16 [2, 4096, 4096], P('section', ('expert', 'tensor'))
Inputs may be any that keep to these rules, and one draw needn't show every extreme that they name: `expert_ids`: each token names two different experts of the 32.
All inputs are finite; a program needn't handle non-finite values.
Results may differ from a plain program's by a relative error of at most 0.0054.
Values may be sent and summed in bfloat16 or wider, within the bound.
No kernel may reach another device: no remote copies, remote signals or barrier semaphores. Data moves between devices by JAX's collectives and lax.ppermute only.
A program may use at most 64 MiB of HBM per device.

v0:
```python
import jax
import jax.numpy as jnp
from jax import lax
from jax.sharding import PartitionSpec as P


def passed_along(value, axis, steps):
    count = lax.axis_size(axis)
    pairs = [(source, (source + steps) % count) for source in range(count)]
    return lax.ppermute(value, axis, pairs)


def normalize(inputs, gain_row):
    widened = inputs.astype(jnp.float32)
    mean_sq = jnp.mean(widened * widened, axis=-1, keepdims=True)
    return (widened * lax.rsqrt(mean_sq + 1e-05) * gain_row).astype(jnp.bfloat16)


def route(normed, router_mat, expert_pick, tok_block, capacity):
    logits = jnp.dot(normed, router_mat, preferred_element_type=jnp.float32)
    experts = router_mat.shape[1]
    labels = jnp.arange(experts, dtype=jnp.int32)
    pair_hot = (expert_pick[:, :, None] == labels[None, None, :]).astype(jnp.float32)
    picked = jnp.sum(pair_hot * logits[:, None, :], axis=-1)
    squashed = jax.nn.sigmoid(picked)
    gate_vals = squashed / jnp.sum(squashed, axis=-1, keepdims=True)
    blocks = expert_pick.shape[0] // tok_block
    pair_order = jnp.transpose(expert_pick.reshape(blocks, tok_block, 2), (0, 2, 1)).reshape(
        blocks, 2 * tok_block
    )
    one_hot = (pair_order[:, :, None] == labels[None, None, :]).astype(jnp.int32)
    before = jnp.cumsum(one_hot, axis=1) - one_hot
    pair_ranks = jnp.sum(before * one_hot, axis=-1)
    pair_ranks = jnp.transpose(pair_ranks.reshape(blocks, 2, tok_block), (0, 2, 1)).reshape(-1, 2)
    is_kept = pair_ranks < capacity
    return (gate_vals, pair_ranks, is_kept)


def on_device(sent, norm_gain, router, w_in, w_out, expert_ids):
    arrived = passed_along(sent, "section", 1)[0]
    tok_count = arrived.shape[0]
    model_width = arrived.shape[1]
    experts = router.shape[2]
    top_count = expert_ids.shape[2]
    n_tensor = lax.axis_size("tensor")
    capacity = max(2, (5 * top_count * tok_count + 4 * experts - 1) // (4 * experts))
    slot_count = experts * capacity
    normed = normalize(arrived, norm_gain[0])
    expert_pick = expert_ids[0]
    gate_vals, pair_ranks, is_kept = route(normed, router[0], expert_pick, tok_count, capacity)
    slot_ids = expert_pick * capacity + pair_ranks
    slot_labels = jnp.arange(slot_count, dtype=jnp.int32)
    slot_hot = ((slot_ids[:, :, None] == slot_labels[None, None, :]) & is_kept[:, :, None]).astype(
        jnp.float32
    )
    placement = jnp.transpose(jnp.sum(slot_hot, axis=1)).astype(jnp.bfloat16)
    combine_mat = jnp.sum(slot_hot * gate_vals[:, :, None], axis=1)
    send_rows = jnp.dot(placement, normed, preferred_element_type=jnp.float32).astype(jnp.bfloat16)
    w_first = w_in[0, 0]
    w_second = w_out[0, 0]
    grouped = lax.all_gather(send_rows[None], "tensor", axis=0, tiled=True)
    slot_grid = grouped.reshape(n_tensor, experts, capacity, model_width)
    received = lax.all_to_all(slot_grid, "expert", split_axis=1, concat_axis=1, tiled=True)
    hidden = jax.nn.gelu(
        jnp.dot(received.reshape(-1, model_width), w_first, preferred_element_type=jnp.float32)
    ).astype(jnp.bfloat16)
    summed = lax.psum_scatter(
        jnp.dot(hidden, w_second, preferred_element_type=jnp.float32).astype(jnp.bfloat16),
        "tensor",
        scatter_dimension=0,
        tiled=True,
    )
    returned = lax.all_to_all(summed, "expert", split_axis=0, concat_axis=0, tiled=True)
    combined = arrived.astype(jnp.float32) + jnp.dot(
        combine_mat, returned.astype(jnp.float32), precision=lax.Precision.HIGHEST
    )
    return passed_along(combined.astype(jnp.bfloat16)[None], "section", 1)


def solution(mesh):
    return jax.shard_map(
        on_device,
        mesh=mesh,
        in_specs=(
            P("section", ("expert", "tensor"), None),
            P("section", None),
            P("section", None, None),
            P("section", "expert", None, "tensor"),
            P("section", "expert", "tensor", None),
            P("section", ("expert", "tensor"), None),
        ),
        out_specs=P("section", ("expert", "tensor"), None),
        check_vma=False,
    )
```

profile of v0, /device:TPU:1, one launch (start us, length us, event | category | flops | bytes accessed | tf_op | source)
XLA Modules:
  0.0 680.8 jit_solution(18257232397446213814)
XLA Ops:
  6.5 8.9 %collective-permute-start = (bf16[1,16,4096]{2,1,0:T(8,128)(2,1)}, bf16[1,16,4096]{2,1,0:T(8,128)(2,1)S(1)}, u32[]{:S(2)}, u32[]{:S(2)}) collective-permute-start(bf16[1,16,4096]{2,1,0:T(8,128)(2,1)} %param.6), channel_id=1, source_target_pairs={{0,256},{256,0},{1,257},{257,1},{2,258},{258,2},{3,259},{259,3},{4... | collective-permute-start | bytes 393224 | tf_op jit(solution)/shard_map/ppermute | solution.py:10
  15.4 0.8 eq.53
  16.3 0.2 select_reduce_fusion.2
  16.6 0.7 bitcast_add_fusion
  17.3 0.1 fusion.21
  17.4 1.2 fusion.26
  18.7 0.9 select_reduce_fusion.1
  19.5 0.1 convert_reduce_fusion
  19.6 1.9 convolution_convert_fusion.1
  21.6 177.2 %all-gather.3.cloned.1.call-done = bf16[512,4096]{1,0:T(8,128)(2,1)} async-done(((bf16[64,4096]{1,0:T(8,128)(2,1)}), bf16[512,4096]{1,0:T(8,128)(2,1)}) %all-gather.3.cloned.1.call-update) | async-done | bytes 4194320 | tf_op jit(solution)/shard_map/all_gather | solution.py:61
  198.8 7.6 %reshape.172 = bf16[8,32,2,4096]{3,2,1,0:T(2,128)(2,1)} reshape(bf16[512,4096]{1,0:T(8,128)(2,1)} %all-gather.3.cloned.1.call-done) | data formatting | bytes 8388608 | tf_op jit(solution)/shard_map/reshape | solution.py:62
  206.4 6.3 copy.19
  212.7 190.5 %all_to_all.17 = bf16[8,32,2,4096]{3,2,0,1:T(2,128)(2,1)} all-to-all(bf16[8,32,2,4096]{3,2,0,1:T(2,128)(2,1)S(1)} %copy.19), channel_id=1, replica_groups=mesh['section'=2,'expert'=32,'tensor'=8] {'expert'}, dimensions={1} | all-to-all | bytes 8388608 | tf_op jit(solution)/shard_map/all_to_all | solution.py:63
  403.2 9.9 %copy.20 = bf16[8,32,2,4096]{3,2,1,0:T(2,128)(2,1)} copy(bf16[8,32,2,4096]{3,2,0,1:T(2,128)(2,1)} %all_to_all.17) | data formatting | bytes 8388608 | tf_op jit(solution)/shard_map/all_to_all | solution.py:63
  413.1 7.2 %reshape.173 = bf16[512,4096]{1,0:T(8,128)(2,1)} reshape(bf16[8,32,2,4096]{3,2,1,0:T(2,128)(2,1)} %copy.20) | data formatting | bytes 8388608 | tf_op jit(solution)/shard_map/reshape | solution.py:65
  420.3 9.3 %convolution_convert_fusion = bf16[512,4096]{1,0:T(8,128)(2,1)} fusion(bf16[1,1,256,4096]{3,2,1,0:T(8,128)(2,1)S(1)} %copy-done, bf16[512,4096]{1,0:T(8,128)(2,1)} %reshape.173, bf16[1,1,4096,256]{3,2,1,0:T(8,128)(2,1)} %param.9), kind=kOutput, calls=%fused_computation | convolution fusion | flops 2150760448 | bytes 12582912 | tf_op jit(solution)/shard_map/dot_general | solution.py:68
  429.6 203.4 %reduce-scatter.2.cloned.1.call-done = bf16[64,4096]{1,0:T(8,128)(2,1)} async-done(((bf16[512,4096]{1,0:T(8,128)(2,1)}), bf16[64,4096]{1,0:T(8,128)(2,1)}) %reduce-scatter.2.cloned.1.call-update) | async-done | bytes 524304 | tf_op jit(solution)/shard_map/reduce_scatter | solution.py:67
  633.1 1.4 all_to_all.12
  634.5 31.6 %all_to_all.18 = bf16[32,2,4096]{2,1,0:T(2,128)(2,1)S(1)} all-to-all(bf16[32,2,4096]{2,1,0:T(2,128)(2,1)S(1)} %all_to_all.12), channel_id=1, replica_groups=mesh['section'=2,'expert'=32,'tensor'=8] {'expert'}, dimensions={0} | all-to-all | bytes 1048576 | tf_op jit(solution)/shard_map/all_to_all | solution.py:73
  666.0 0.2 all_to_all.14
  666.2 0.3 fusion.1
  666.6 5.8 collective-permute-start.1
  672.4 1.0 collective-permute-done.1
  673.3 0.7 copy.22
  (14 shorter events, 0.3 us)
Async XLA Ops:
  6.5 413.8 %copy-start = (bf16[1,1,256,4096]{3,2,1,0:T(8,128)(2,1)S(1)}, bf16[1,1,256,4096]{3,2,1,0:T(8,128)(2,1)}, u32[]{:S(2)}) copy-start(bf16[1,1,256,4096]{3,2,1,0:T(8,128)(2,1)} %param.10) | copy-start | bytes 6291460
  6.5 192.2 %all-gather.3.cloned.1.call-start = ((), (), s32[]{:S(2)}) async-start(), calls=%async_computation.4 | async-start | bytes 4718592 | tf_op jit(solution)/shard_map/all_gather | solution.py:61
  6.5 10.7 %collective-permute-start = (bf16[1,16,4096]{2,1,0:T(8,128)(2,1)}, bf16[1,16,4096]{2,1,0:T(8,128)(2,1)S(1)}, u32[]{:S(2)}, u32[]{:S(2)}) collective-permute-start(bf16[1,16,4096]{2,1,0:T(8,128)(2,1)} %param.6), channel_id=1, source_target_pairs={{0,256},{256,0},{1,257},{257,1},{2,258},{258,2},{3,259},{259,3},{4... | collective-permute-start | bytes 393224 | tf_op jit(solution)/shard_map/ppermute | solution.py:10
  21.5 611.6 %reduce-scatter.2.cloned.1.call-start = ((), (), s32[]{:S(2)}) async-start(), calls=%async_computation.3 | async-start | bytes 4718592 | tf_op jit(solution)/shard_map/reduce_scatter | solution.py:67
  666.6 6.8 collective-permute-start.1
Sparse Core Ops, SparseCore 0:
  21.6 177.0 all-gather.2
  429.8 203.2 reduce-scatter.1
where the time goes:
time: 682 us; the launch traced here: 681 us
  waiting for transfers between devices  382 us (56%)
  blocking collectives  222 us (33%)
  local copies, waits for them, and re-layouts  34.1 us (5%)
  starting transfers between devices  14.7 us (2%)
  between operations  13.5 us (2%)
  matrix products  12.7 us (2%)
    reduce_scatter x1, waiting for transfers between devices, on_device(): lax.psum_scatter(jnp.dot(hidden, w_second, preferred_element_type=jnp.flo...  203 us
    all_to_all x1, blocking collectives, on_device(): lax.all_to_all(slot_grid, 'expert', split_axis=1, concat_axis=1, tiled=True)  190 us
    all_gather x1, waiting for transfers between devices, on_device(): grouped = lax.all_gather(send_rows[None], 'tensor', axis=0, tiled=True)  177 us
    all_to_all x1, blocking collectives, on_device(): lax.all_to_all(summed, 'expert', split_axis=0, concat_axis=0, tiled=True)  31.6 us
    ppermute x2, starting transfers between devices, passed_along(): return lax.ppermute(value, axis, pairs)  14.7 us
    reshape x2, local copies, waits for them, and re-layouts, on_device(): slot_grid = grouped.reshape(n_tensor, experts, capacity, model_width)  13.9 us
  transfers between devices with their start and end apart: 4, of which 3 were waited for; matrix products, arithmetic and copies ran while one was open for 0% of the time, Pallas kernels for 0%

commit v1 on v0

v1 whole, which is shorter than its diff:
```python
import jax
import jax.numpy as jnp
from jax import lax
from jax.sharding import Mesh
from jax.sharding import PartitionSpec as P


def passed_along(value, axis, steps):
    count = lax.axis_size(axis)
    pairs = [(source, (source + steps) % count) for source in range(count)]
    return lax.ppermute(value, axis, pairs)


def normalize(inputs, gain_row):
    widened = inputs.astype(jnp.float32)
    mean_sq = jnp.mean(widened * widened, axis=-1, keepdims=True)
    return (widened * lax.rsqrt(mean_sq + 1e-05) * gain_row).astype(jnp.bfloat16)


def route(normed, router_mat, expert_pick, tok_block, capacity):
    logits = jnp.dot(normed, router_mat, preferred_element_type=jnp.float32)
    experts = router_mat.shape[1]
    labels = jnp.arange(experts, dtype=jnp.int32)
    pair_hot = (expert_pick[:, :, None] == labels[None, None, :]).astype(jnp.float32)
    picked = jnp.sum(pair_hot * logits[:, None, :], axis=-1)
    squashed = jax.nn.sigmoid(picked)
    gate_vals = squashed / jnp.sum(squashed, axis=-1, keepdims=True)
    blocks = expert_pick.shape[0] // tok_block
    pair_order = jnp.transpose(expert_pick.reshape(blocks, tok_block, 2), (0, 2, 1)).reshape(
        blocks, 2 * tok_block
    )
    one_hot = (pair_order[:, :, None] == labels[None, None, :]).astype(jnp.int32)
    before = jnp.cumsum(one_hot, axis=1) - one_hot
    pair_ranks = jnp.sum(before * one_hot, axis=-1)
    pair_ranks = jnp.transpose(pair_ranks.reshape(blocks, 2, tok_block), (0, 2, 1)).reshape(-1, 2)
    is_kept = pair_ranks < capacity
    return (gate_vals, pair_ranks, is_kept)


def on_device(sent, norm_gain, router, w_in, w_out, expert_ids):
    arrived = passed_along(sent, "section", 1)[0]
    tok_count = arrived.shape[0]
    model_width = arrived.shape[1]
    experts = router.shape[2]
    top_count = expert_ids.shape[2]
    n_y = lax.axis_size("y")
    capacity = max(2, (5 * top_count * tok_count + 4 * experts - 1) // (4 * experts))
    normed = normalize(arrived, norm_gain[0])
    own_pick = expert_ids[0]
    partner_rows = passed_along(normed, "zh", 1)
    partner_pick = passed_along(own_pick, "zh", 1)
    rows_both = jnp.concatenate([normed, partner_rows], axis=0)
    pick_both = jnp.concatenate([own_pick, partner_pick], axis=0)
    gate_vals, pair_ranks, is_kept = route(rows_both, router[0], pick_both, tok_count, capacity)
    n_tok = 2 * tok_count
    block_of = (jnp.arange(n_tok, dtype=jnp.int32) // tok_count)[:, None]
    per_expert = 2 * capacity
    slot_ids = pick_both * per_expert + block_of * capacity + pair_ranks
    slot_count = experts * per_expert
    slot_labels = jnp.arange(slot_count, dtype=jnp.int32)
    slot_hot = ((slot_ids[:, :, None] == slot_labels[None, None, :]) & is_kept[:, :, None]).astype(
        jnp.float32
    )
    placement = jnp.transpose(jnp.sum(slot_hot, axis=1)).astype(jnp.bfloat16)
    combine_mat = jnp.sum(slot_hot * gate_vals[:, :, None], axis=1)
    send_rows = jnp.dot(placement, rows_both, preferred_element_type=jnp.float32).astype(jnp.bfloat16)
    slot_grid = send_rows.reshape(experts, per_expert, model_width)
    received = lax.all_to_all(slot_grid, "expert", split_axis=0, concat_axis=0, tiled=True)
    gathered = lax.all_gather(received[None], "y", axis=0, tiled=True)
    rows_in = gathered.reshape(-1, model_width)
    hidden = jax.nn.gelu(
        jnp.dot(rows_in, w_in[0, 0], preferred_element_type=jnp.float32)
    ).astype(jnp.bfloat16)
    partial = jnp.dot(hidden, w_out[0, 0], preferred_element_type=jnp.float32).astype(jnp.bfloat16)
    summed = lax.psum_scatter(
        partial.reshape(n_y, -1, model_width), "y", scatter_dimension=0, tiled=True
    )
    back = lax.all_to_all(
        summed.reshape(experts, per_expert, model_width), "expert", split_axis=0, concat_axis=0, tiled=True
    )
    half_sum = jnp.dot(
        combine_mat,
        back.reshape(slot_count, model_width).astype(jnp.float32),
        precision=lax.Precision.HIGHEST,
    )
    from_partner = passed_along(half_sum[tok_count:].astype(jnp.bfloat16), "zh", 1)
    combined = arrived.astype(jnp.float32) + half_sum[:tok_count] + from_partner.astype(jnp.float32)
    return passed_along(combined.astype(jnp.bfloat16)[None], "section", 1)


def solution(mesh):
    sizes = dict(mesh.shape)
    n_tensor = sizes["tensor"]
    fine = Mesh(
        mesh.devices.reshape(sizes["section"], sizes["expert"], n_tensor // 2, 2),
        ("section", "expert", "y", "zh"),
    )
    tokens = ("expert", "y", "zh")
    hidden_units = ("y", "zh")
    return jax.shard_map(
        on_device,
        mesh=fine,
        in_specs=(
            P("section", tokens, None),
            P("section", None),
            P("section", None, None),
            P("section", "expert", None, hidden_units),
            P("section", "expert", hidden_units, None),
            P("section", tokens, None),
        ),
        out_specs=P("section", tokens, None),
        check_vma=False,
    )
```

time: 682 us -> 339 us (0.50)
  waiting for transfers between devices: 382 us -> 132 us
  blocking collectives: 222 us -> 127 us
  starting transfers between devices: 14.7 us -> 37.7 us
  local copies, waits for them, and re-layouts: 34.1 us -> 11.9 us
    reduce_scatter x1, waiting for transfers between devices: 203 us -> 55.2 us  [on_device(): lax.psum_scatter(partial.reshape(n_y, -1, model_width), 'y', scatter_dime...]
    all_gather x1, waiting for transfers between devices: 177 us -> 56.1 us  [on_device(): gathered = lax.all_gather(received[None], 'y', axis=0, tiled=True)]
    all_to_all x2, blocking collectives: 222 us -> 127 us  [the longest x1 65.2 us: on_device(): lax.all_to_all(slot_grid, 'expert', split_axis=0, concat_axis=0, tiled=True)]
    ppermute x2 -> x5, starting transfers between devices: 14.7 us -> 37.6 us  [passed_along(): return lax.ppermute(value, axis, pairs)]
    ppermute x2 -> x5, waiting for transfers between devices: 0.97 us -> 20.4 us  [passed_along(): return lax.ppermute(value, axis, pairs)]
    all_to_all x3 -> x0, local copies, waits for them, and re-layouts: 11.5 us -> none  [the longest x1 9.9 us: on_device(): lax.all_to_all(slot_grid, 'expert', split_axis=1, concat_axis=1, tiled=True)]
    reshape x3 -> x6, local copies, waits for them, and re-layouts: 21.1 us -> 11.1 us  [the longest x1 6.91 us: on_device(): rows_in = gathered.reshape(-1, model_width)]
  transfers between devices with their start and end apart: 4 -> 7, of which waited for: 3 -> 5; matrix products, arithmetic and copies ran while one was open for 0% -> 1% of each run, Pallas kernels for 0% -> 0%
where the time goes in v1:
time: 339 us; the launch traced here: 337 us
  waiting for transfers between devices  132 us (39%)
  blocking collectives  127 us (37%)
  starting transfers between devices  37.7 us (11%)
  between operations  13.5 us (4%)
  local copies, waits for them, and re-layouts  11.9 us (4%)
  matrix products  11.4 us (3%)
    all_to_all x1, blocking collectives, on_device(): lax.all_to_all(slot_grid, 'expert', split_axis=0, concat_axis=0, tiled=True)  65.2 us
    all_to_all x1, blocking collectives, on_device(): lax.all_to_all(summed.reshape(experts, per_expert, model_width), 'expert'...  62.2 us
    all_gather x1, waiting for transfers between devices, on_device(): gathered = lax.all_gather(received[None], 'y', axis=0, tiled=True)  56.1 us
    reduce_scatter x1, waiting for transfers between devices, on_device(): lax.psum_scatter(partial.reshape(n_y, -1, model_width), 'y', scatter_dime...  55.2 us
    ppermute x5, starting transfers between devices, passed_along(): return lax.ppermute(value, axis, pairs)  37.6 us
    ppermute x5, waiting for transfers between devices, passed_along(): return lax.ppermute(value, axis, pairs)  20.4 us
    dot_general x1, matrix products, on_device(): jnp.dot(hidden, w_out[0, 0], preferred_element_type=jnp.float32)  9.31 us
    reshape x1, local copies, waits for them, and re-layouts, on_device(): rows_in = gathered.reshape(-1, model_width)  6.91 us
  transfers between devices with their start and end apart: 7, of which 5 were waited for; matrix products, arithmetic and copies ran while one was open for 1% of the time, Pallas kernels for 0%

profile of v1, /device:TPU:1, one launch (start us, length us, event | category | flops | bytes accessed | tf_op | source)
XLA Modules:
  0.0 336.9 jit_solution(3203111217646648346)
XLA Ops:
  6.5 16.4 %collective-permute-start.1 = (s32[16,2]{0,1:T(2,128)}, s32[16,2]{0,1:T(2,128)S(1)}, u32[]{:S(2)}, u32[]{:S(2)}) collective-permute-start(s32[16,2]{0,1:T(2,128)} %bitcast.39), channel_id=1, source_target_pairs={{0,1},{1,0},{2,3},{3,2},{4,5},{5,4},{6,7},{7,6},{8,9},{9,8},{10,11... | collective-permute-start | bytes 392 | tf_op jit(solution)/shard_map/ppermute | solution.py:11
  22.9 2.9 collective-permute-start
  25.8 0.8 pad_add_fusion
  27.2 0.8 add_add_fusion
  28.2 0.8 fusion.19
  29.0 10.3 %collective-permute-start.2 = (bf16[16,4096]{1,0:T(8,128)(2,1)S(1)}, bf16[16,4096]{1,0:T(8,128)(2,1)S(1)}, u32[]{:S(2)}, u32[]{:S(2)}) collective-permute-start(bf16[16,4096]{1,0:T(8,128)(2,1)S(1)} %fusion.19), channel_id=1, source_target_pairs={{0,1},{1,0},{2,3},{3,2},{4,5},{5,4},{6,7},{7,6},{8,9},{9,8},{10,11... | collective-permute-start | bytes 393224 | tf_op jit(solution)/shard_map/ppermute | solution.py:11
  39.4 5.5 %collective-permute-done.2 = bf16[16,4096]{1,0:T(8,128)(2,1)S(1)} collective-permute-done((bf16[16,4096]{1,0:T(8,128)(2,1)S(1)}, bf16[16,4096]{1,0:T(8,128)(2,1)S(1)}, u32[]{:S(2)}, u32[]{:S(2)}) %collective-permute-start.2) | collective-permute-done | bytes 131104 | tf_op jit(solution)/shard_map/ppermute | solution.py:11
  44.9 1.1 fusion.22
  46.3 0.5 convolution_convert_fusion.1
  46.8 1.2 reshape.118
  48.0 65.2 %all_to_all.10 = bf16[32,4,4096]{2,1,0:T(4,128)(2,1)} all-to-all(bf16[32,4,4096]{2,1,0:T(4,128)(2,1)} %reshape.118), channel_id=1, replica_groups=mesh['section'=2,'expert'=32,'y'=4,'zh'=2] {'expert'}, dimensions={0} | all-to-all | bytes 2097152 | tf_op jit(solution)/shard_map/all_to_all | solution.py:68
  113.3 56.1 %all-gather.3.cloned.1.call-done = bf16[128,4,4096]{2,1,0:T(4,128)(2,1)} async-done(((bf16[32,4,4096]{2,1,0:T(4,128)(2,1)}), bf16[128,4,4096]{2,1,0:T(4,128)(2,1)}) %all-gather.3.cloned.1.call-update) | async-done | bytes 4194320 | tf_op jit(solution)/shard_map/all_gather | solution.py:69
  169.4 6.9 %reshape.119 = bf16[512,4096]{1,0:T(8,128)(2,1)} reshape(bf16[128,4,4096]{2,1,0:T(4,128)(2,1)} %all-gather.3.cloned.1.call-done) | data formatting | bytes 8388608 | tf_op jit(solution)/shard_map/reshape | solution.py:70
  176.3 9.3 %convolution_convert_fusion = bf16[512,4096]{1,0:T(8,128)(2,1)} fusion(bf16[1,1,256,4096]{3,2,1,0:T(8,128)(2,1)S(1)} %copy-done, bf16[512,4096]{1,0:T(8,128)(2,1)} %reshape.119, bf16[1,1,4096,256]{3,2,1,0:T(8,128)(2,1)} %param.9), kind=kOutput, calls=%fused_computation | convolution fusion | flops 2150760448 | bytes 12582912 | tf_op jit(solution)/shard_map/dot_general | solution.py:74
  185.7 55.2 %reduce-scatter.2.cloned.1.call-done = bf16[1,128,4096]{2,1,0:T(8,128)(2,1)} async-done(((bf16[4,128,4096]{2,1,0:T(8,128)(2,1)}), bf16[1,128,4096]{2,1,0:T(8,128)(2,1)}) %reduce-scatter.2.cloned.1.call-update) | async-done | bytes 1048592 | tf_op jit(solution)/shard_map/reduce_scatter | solution.py:75
  240.9 1.5 reshape.121
  242.3 62.2 %all_to_all.11 = bf16[32,4,4096]{2,1,0:T(4,128)(2,1)} all-to-all(bf16[32,4,4096]{2,1,0:T(4,128)(2,1)S(1)} %reshape.121), channel_id=1, replica_groups=mesh['section'=2,'expert'=32,'y'=4,'zh'=2] {'expert'}, dimensions={0} | all-to-all | bytes 2097152 | tf_op jit(solution)/shard_map/all_to_all | solution.py:78
  304.5 1.3 reshape.122
  305.9 0.5 fusion.39
  306.4 5.0 %collective-permute-start.3 = (bf16[16,4096]{1,0:T(8,128)(2,1)S(1)}, bf16[16,4096]{1,0:T(8,128)(2,1)S(1)}, u32[]{:S(2)}, u32[]{:S(2)}) collective-permute-start(bf16[16,4096]{1,0:T(8,128)(2,1)S(1)} %slice.15), channel_id=1, source_target_pairs={{0,1},{1,0},{2,3},{3,2},{4,5},{5,4},{6,7},{7,6},{8,9},{9,8},{10,11... | collective-permute-start | bytes 393224 | tf_op jit(solution)/shard_map/ppermute | solution.py:11
  311.5 13.9 %collective-permute-done.3 = bf16[16,4096]{1,0:T(8,128)(2,1)S(1)} collective-permute-done((bf16[16,4096]{1,0:T(8,128)(2,1)S(1)}, bf16[16,4096]{1,0:T(8,128)(2,1)S(1)}, u32[]{:S(2)}, u32[]{:S(2)}) %collective-permute-start.3) | collective-permute-done | bytes 131104 | tf_op jit(solution)/shard_map/ppermute | solution.py:11
  325.5 3.0 collective-permute-start.4
  328.5 1.0 collective-permute-done.4
  329.4 0.7 copy.20
  (27 shorter events, 1.3 us)
Async XLA Ops:
  6.5 169.8 %copy-start = (bf16[1,1,256,4096]{3,2,1,0:T(8,128)(2,1)S(1)}, bf16[1,1,256,4096]{3,2,1,0:T(8,128)(2,1)}, u32[]{:S(2)}) copy-start(bf16[1,1,256,4096]{3,2,1,0:T(8,128)(2,1)} %param.10) | copy-start | bytes 6291460
  6.5 162.9 %all-gather.3.cloned.1.call-start = ((), (), s32[]{:S(2)}) async-start(), calls=%async_computation.4 | async-start | bytes 5242880 | tf_op jit(solution)/shard_map/all_gather | solution.py:69
  6.5 19.3 %collective-permute-start.1 = (s32[16,2]{0,1:T(2,128)}, s32[16,2]{0,1:T(2,128)S(1)}, u32[]{:S(2)}, u32[]{:S(2)}) collective-permute-start(s32[16,2]{0,1:T(2,128)} %bitcast.39), channel_id=1, source_target_pairs={{0,1},{1,0},{2,3},{3,2},{4,5},{5,4},{6,7},{7,6},{8,9},{9,8},{10,11... | collective-permute-start | bytes 392 | tf_op jit(solution)/shard_map/ppermute | solution.py:11
  22.9 5.1 %collective-permute-start = (bf16[1,16,4096]{2,1,0:T(8,128)(2,1)}, bf16[1,16,4096]{2,1,0:T(8,128)(2,1)S(1)}, u32[]{:S(2)}, u32[]{:S(2)}) collective-permute-start(bf16[1,16,4096]{2,1,0:T(8,128)(2,1)} %param.6), channel_id=1, source_target_pairs={{0,256},{256,0},{1,257},{257,1},{2,258},{258,2},{3,259},{259,3},{4... | collective-permute-start | bytes 393224 | tf_op jit(solution)/shard_map/ppermute | solution.py:11
  29.0 15.9 %collective-permute-start.2 = (bf16[16,4096]{1,0:T(8,128)(2,1)S(1)}, bf16[16,4096]{1,0:T(8,128)(2,1)S(1)}, u32[]{:S(2)}, u32[]{:S(2)}) collective-permute-start(bf16[16,4096]{1,0:T(8,128)(2,1)S(1)} %fusion.19), channel_id=1, source_target_pairs={{0,1},{1,0},{2,3},{3,2},{4,5},{5,4},{6,7},{7,6},{8,9},{9,8},{10,11... | collective-permute-start | bytes 393224 | tf_op jit(solution)/shard_map/ppermute | solution.py:11
  113.3 127.6 %reduce-scatter.2.cloned.1.call-start = ((), (), s32[]{:S(2)}) async-start(), calls=%async_computation.3 | async-start | bytes 5242880 | tf_op jit(solution)/shard_map/reduce_scatter | solution.py:75
  306.4 19.0 %collective-permute-start.3 = (bf16[16,4096]{1,0:T(8,128)(2,1)S(1)}, bf16[16,4096]{1,0:T(8,128)(2,1)S(1)}, u32[]{:S(2)}, u32[]{:S(2)}) collective-permute-start(bf16[16,4096]{1,0:T(8,128)(2,1)S(1)} %slice.15), channel_id=1, source_target_pairs={{0,1},{1,0},{2,3},{3,2},{4,5},{5,4},{6,7},{7,6},{8,9},{9,8},{10,11... | collective-permute-start | bytes 393224 | tf_op jit(solution)/shard_map/ppermute | solution.py:11
  325.5 4.0 %collective-permute-start.4 = (bf16[1,16,4096]{2,1,0:T(8,128)(2,1)S(1)}, bf16[1,16,4096]{2,1,0:T(8,128)(2,1)S(1)}, u32[]{:S(2)}, u32[]{:S(2)}) collective-permute-start(bf16[1,16,4096]{2,1,0:T(8,128)(2,1)S(1)} %fusion.28), channel_id=1, source_target_pairs={{0,256},{256,0},{1,257},{257,1},{2,258},{258,2},{3,259},{259,3},{4... | collective-permute-start | bytes 393224 | tf_op jit(solution)/shard_map/ppermute | solution.py:11
Sparse Core Ops, SparseCore 0:
  113.4 55.9 all-gather.2
  185.8 55.0 reduce-scatter.1

commit v2 on v1

--- a/solution.py
+++ b/solution.py
@@ -37,54 +37,63 @@
     return (gate_vals, pair_ranks, is_kept)
 
 
-def on_device(sent, norm_gain, router, w_in, w_out, expert_ids):
-    arrived = passed_along(sent, "section", 1)[0]
-    tok_count = arrived.shape[0]
-    model_width = arrived.shape[1]
-    experts = router.shape[2]
-    top_count = expert_ids.shape[2]
-    n_y = lax.axis_size("y")
-    capacity = max(2, (5 * top_count * tok_count + 4 * experts - 1) // (4 * experts))
-    normed = normalize(arrived, norm_gain[0])
-    own_pick = expert_ids[0]
-    partner_rows = passed_along(normed, "zh", 1)
-    partner_pick = passed_along(own_pick, "zh", 1)
-    rows_both = jnp.concatenate([normed, partner_rows], axis=0)
-    pick_both = jnp.concatenate([own_pick, partner_pick], axis=0)
-    gate_vals, pair_ranks, is_kept = route(rows_both, router[0], pick_both, tok_count, capacity)
-    n_tok = 2 * tok_count
-    block_of = (jnp.arange(n_tok, dtype=jnp.int32) // tok_count)[:, None]
-    per_expert = 2 * capacity
-    slot_ids = pick_both * per_expert + block_of * capacity + pair_ranks
-    slot_count = experts * per_expert
+def dispatch(rows, pick, router_mat, capacity):
+    tok_count, model_width = rows.shape
+    experts = router_mat.shape[1]
+    gate_vals, pair_ranks, is_kept = route(rows, router_mat, pick, tok_count, capacity)
+    slot_ids = pick * capacity + pair_ranks
+    slot_count = experts * capacity
     slot_labels = jnp.arange(slot_count, dtype=jnp.int32)
     slot_hot = ((slot_ids[:, :, None] == slot_labels[None, None, :]) & is_kept[:, :, None]).astype(
         jnp.float32
     )
     placement = jnp.transpose(jnp.sum(slot_hot, axis=1)).astype(jnp.bfloat16)
     combine_mat = jnp.sum(slot_hot * gate_vals[:, :, None], axis=1)
-    send_rows = jnp.dot(placement, rows_both, preferred_element_type=jnp.float32).astype(jnp.bfloat16)
-    slot_grid = send_rows.reshape(experts, per_expert, model_width)
+    send_rows = jnp.dot(placement, rows, preferred_element_type=jnp.float32).astype(jnp.bfloat16)
+    return send_rows.reshape(experts, capacity, model_width), combine_mat
+
+
+def expert_pass(slot_grid, combine_mat, w_first, w_second):
+    experts, capacity, model_width = slot_grid.shape
+    n_y = lax.axis_size("y")
     received = lax.all_to_all(slot_grid, "expert", split_axis=0, concat_axis=0, tiled=True)
     gathered = lax.all_gather(received[None], "y", axis=0, tiled=True)
     rows_in = gathered.reshape(-1, model_width)
     hidden = jax.nn.gelu(
-        jnp.dot(rows_in, w_in[0, 0], preferred_element_type=jnp.float32)
+        jnp.dot(rows_in, w_first, preferred_element_type=jnp.float32)
     ).astype(jnp.bfloat16)
-    partial = jnp.dot(hidden, w_out[0, 0], preferred_element_type=jnp.float32).astype(jnp.bfloat16)
+    partial = jnp.dot(hidden, w_second, preferred_element_type=jnp.float32).astype(jnp.bfloat16)
     summed = lax.psum_scatter(
         partial.reshape(n_y, -1, model_width), "y", scatter_dimension=0, tiled=True
     )
     back = lax.all_to_all(
-        summed.reshape(experts, per_expert, model_width), "expert", split_axis=0, concat_axis=0, tiled=True
+        summed.reshape(experts, capacity, model_width), "expert", split_axis=0, concat_axis=0, tiled=True
     )
-    half_sum = jnp.dot(
+    return jnp.dot(
         combine_mat,
-        back.reshape(slot_count, model_width).astype(jnp.float32),
+        back.reshape(experts * capacity, model_width).astype(jnp.float32),
         precision=lax.Precision.HIGHEST,
     )
-    from_partner = passed_along(half_sum[tok_count:].astype(jnp.bfloat16), "zh", 1)
-    combined = arrived.astype(jnp.float32) + half_sum[:tok_count] + from_partner.astype(jnp.float32)
+
+
+def on_device(sent, norm_gain, router, w_in, w_out, expert_ids):
+    arrived = passed_along(sent, "section", 1)[0]
+    tok_count = arrived.shape[0]
+    experts = router.shape[2]
+    top_count = expert_ids.shape[2]
+    capacity = max(2, (5 * top_count * tok_count + 4 * experts - 1) // (4 * experts))
+    normed = normalize(arrived, norm_gain[0])
+    own_pick = expert_ids[0]
+    partner_rows = passed_along(normed, "zh", 1)
+    partner_pick = passed_along(own_pick, "zh", 1)
+    w_first = w_in[0, 0]
+    w_second = w_out[0, 0]
+    own_slots, own_combine = dispatch(normed, own_pick, router[0], capacity)
+    own_half = expert_pass(own_slots, own_combine, w_first, w_second)
+    partner_slots, partner_combine = dispatch(partner_rows, partner_pick, router[0], capacity)
+    partner_half = expert_pass(partner_slots, partner_combine, w_first, w_second)
+    from_partner = passed_along(partner_half.astype(jnp.bfloat16), "zh", 1)
+    combined = arrived.astype(jnp.float32) + own_half + from_partner.astype(jnp.float32)
     return passed_along(combined.astype(jnp.bfloat16)[None], "section", 1)
 
 

time: 339 us -> 317 us (0.935)
  blocking collectives: 127 us -> 36.4 us
  starting transfers between devices: 37.7 us -> 82.3 us
  waiting for transfers between devices: 132 us -> 145 us
  local copies, waits for them, and re-layouts: 11.9 us -> 17.8 us
  matrix products: 11.4 us -> 17.2 us
    all_to_all x2 -> x1, blocking collectives: 127 us -> 36.4 us  [expert_pass(): lax.all_to_all(slot_grid, 'expert', split_axis=0, concat_axis=0, tiled=True)]
    all_to_all x0 -> x3, waiting for transfers between devices: none -> 51.4 us  [the longest x2 27.8 us: expert_pass(): lax.all_to_all(summed.reshape(experts, capacity, model_width), 'expert',...]
    all_to_all x0 -> x3, starting transfers between devices: none -> 40.8 us  [the longest x2 25.2 us: expert_pass(): lax.all_to_all(summed.reshape(experts, capacity, model_width), 'expert',...]
    all_gather x1 -> x2, waiting for transfers between devices: 56.1 us -> 30.8 us  [expert_pass(): gathered = lax.all_gather(received[None], 'y', axis=0, tiled=True)]
    ppermute x5, waiting for transfers between devices: 20.4 us -> 7.65 us  [passed_along(): return lax.ppermute(value, axis, pairs)]
    dot_general x3 -> x6, matrix products: 10.3 us -> 15.1 us  [the longest x2 11.9 us: expert_pass(): jnp.dot(hidden, w_second, preferred_element_type=jnp.float32)]
    reshape x6 -> x8, local copies, waits for them, and re-layouts: 11.1 us -> 15.3 us  [the longest x2 8.23 us: expert_pass(): rows_in = gathered.reshape(-1, model_width)]
    ppermute x5, starting transfers between devices: 37.6 us -> 41.3 us  [passed_along(): return lax.ppermute(value, axis, pairs)]
  transfers between devices with their start and end apart: 7 -> 12, of which waited for: 5 -> 9; matrix products, arithmetic and copies ran while one was open for 1% -> 10% of each run, Pallas kernels for 0% -> 0%
where the time goes in v2:
time: 317 us; the launch traced here: 316 us
  waiting for transfers between devices  145 us (46%)
  starting transfers between devices  82.3 us (26%)
  blocking collectives  36.4 us (11%)
  local copies, waits for them, and re-layouts  17.8 us (6%)
  matrix products  17.2 us (5%)
  between operations  13.3 us (4%)
  other arithmetic  4.19 us (1%)
    reduce_scatter x2, waiting for transfers between devices, expert_pass(): lax.psum_scatter(partial.reshape(n_y, -1, model_width), 'y', scatter_dime...  55.4 us
    ppermute x5, starting transfers between devices, passed_along(): return lax.ppermute(value, axis, pairs)  41.3 us
    all_to_all x1, blocking collectives, expert_pass(): lax.all_to_all(slot_grid, 'expert', split_axis=0, concat_axis=0, tiled=True)  36.4 us
    all_gather x2, waiting for transfers between devices, expert_pass(): gathered = lax.all_gather(received[None], 'y', axis=0, tiled=True)  30.8 us
    all_to_all x2, waiting for transfers between devices, expert_pass(): lax.all_to_all(summed.reshape(experts, capacity, model_width), 'expert',...  27.8 us
    all_to_all x2, starting transfers between devices, expert_pass(): lax.all_to_all(summed.reshape(experts, capacity, model_width), 'expert',...  25.2 us
    all_to_all x1, waiting for transfers between devices, expert_pass(): lax.all_to_all(slot_grid, 'expert', split_axis=0, concat_axis=0, tiled=True)  23.7 us
    all_to_all x1, starting transfers between devices, expert_pass(): lax.all_to_all(slot_grid, 'expert', split_axis=0, concat_axis=0, tiled=True)  15.7 us
  transfers between devices with their start and end apart: 12, of which 9 were waited for; matrix products, arithmetic and copies ran while one was open for 10% of the time, Pallas kernels for 0%

profile of v2, /device:TPU:1, one launch (start us, length us, event | category | flops | bytes accessed | tf_op | source)
XLA Modules:
  0.0 316.5 jit_solution(13920588506394158781)
XLA Ops:
  6.5 16.4 %collective-permute-start.1 = (s32[16,2]{0,1:T(2,128)}, s32[16,2]{0,1:T(2,128)S(1)}, u32[]{:S(2)}, u32[]{:S(2)}) collective-permute-start(s32[16,2]{0,1:T(2,128)} %bitcast.80), channel_id=1, source_target_pairs={{0,1},{1,0},{2,3},{3,2},{4,5},{5,4},{6,7},{7,6},{8,9},{9,8},{10,11... | collective-permute-start | bytes 392 | tf_op jit(solution)/shard_map/ppermute | solution.py:11
  22.9 2.9 collective-permute-start
  28.0 9.7 %collective-permute-start.2 = (bf16[16,4096]{1,0:T(8,128)(2,1)S(1)}, bf16[16,4096]{1,0:T(8,128)(2,1)S(1)}, u32[]{:S(2)}, u32[]{:S(2)}) collective-permute-start(bf16[16,4096]{1,0:T(8,128)(2,1)S(1)} %fusion.13), channel_id=1, source_target_pairs={{0,1},{1,0},{2,3},{3,2},{4,5},{5,4},{6,7},{7,6},{8,9},{9,8},{10,11... | collective-permute-start | bytes 393224 | tf_op jit(solution)/shard_map/ppermute | solution.py:11
  37.7 6.0 %collective-permute-done.2 = bf16[16,4096]{1,0:T(8,128)(2,1)S(1)} collective-permute-done((bf16[16,4096]{1,0:T(8,128)(2,1)S(1)}, bf16[16,4096]{1,0:T(8,128)(2,1)S(1)}, u32[]{:S(2)}, u32[]{:S(2)}) %collective-permute-start.2) | collective-permute-done | bytes 131104 | tf_op jit(solution)/shard_map/ppermute | solution.py:11
  46.1 1.1 reshape.334
  47.2 15.7 %all-to-all-start.2 = ((bf16[32,2,4096]{2,1,0:T(2,128)(2,1)}), bf16[32,2,4096]{2,1,0:T(2,128)(2,1)S(1)}, u32[]{:S(2)}, u32[]{:S(2)}) async-start(bf16[32,2,4096]{2,1,0:T(2,128)(2,1)} %reshape.334), calls=%async_computation.3 | async-start | bytes 1048576 | tf_op jit(solution)/shard_map/all_to_all | solution.py:59
  64.8 23.7 %all-to-all-done.2 = bf16[32,2,4096]{2,1,0:T(2,128)(2,1)S(1)} async-done(((bf16[32,2,4096]{2,1,0:T(2,128)(2,1)}), bf16[32,2,4096]{2,1,0:T(2,128)(2,1)S(1)}, u32[]{:S(2)}, u32[]{:S(2)}) %all-to-all-start.2) | async-done | bytes 524320 | tf_op jit(solution)/shard_map/all_to_all | solution.py:59
  91.3 1.2 convolution_convert_fusion.3
  92.8 36.4 %all_to_all.20 = bf16[32,2,4096]{2,1,0:T(2,128)(2,1)} all-to-all(bf16[32,2,4096]{2,1,0:T(2,128)(2,1)S(1)} %reshape.326), channel_id=1, replica_groups=mesh['section'=2,'expert'=32,'y'=4,'zh'=2] {'expert'}, dimensions={0} | all-to-all | bytes 1048576 | tf_op jit(solution)/shard_map/all_to_all | solution.py:59
  129.5 4.1 %reshape.335 = bf16[256,4096]{1,0:T(8,128)(2,1)} reshape(bf16[128,2,4096]{2,1,0:T(2,128)(2,1)} %all-gather.7.cloned.1.call-done) | data formatting | bytes 4194304 | tf_op jit(solution)/shard_map/reshape | solution.py:61
  133.6 5.9 %convolution_convert_fusion = bf16[256,4096]{1,0:T(8,128)(2,1)} fusion(bf16[1,1,256,4096]{3,2,1,0:T(8,128)(2,1)S(1)} %copy-done, bf16[256,4096]{1,0:T(8,128)(2,1)} %reshape.335, bf16[1,1,4096,256]{3,2,1,0:T(8,128)(2,1)} %param.9), kind=kOutput, calls=%fused_computation | convolution fusion | flops 1075380224 | bytes 8388608 | tf_op jit(solution)/shard_map/dot_general | solution.py:65
  139.6 30.6 %all-gather.5.cloned.1.call-done = bf16[128,2,4096]{2,1,0:T(2,128)(2,1)} async-done(((bf16[32,2,4096]{2,1,0:T(2,128)(2,1)}), bf16[128,2,4096]{2,1,0:T(2,128)(2,1)}) %all-gather.5.cloned.1.call-update) | async-done | bytes 2097168 | tf_op jit(solution)/shard_map/all_gather | solution.py:60
  170.2 4.1 %reshape.327 = bf16[256,4096]{1,0:T(8,128)(2,1)} reshape(bf16[128,2,4096]{2,1,0:T(2,128)(2,1)} %all-gather.5.cloned.1.call-done) | data formatting | bytes 4194304 | tf_op jit(solution)/shard_map/reshape | solution.py:61
  174.3 6.0 %convolution_convert_fusion.1 = bf16[256,4096]{1,0:T(8,128)(2,1)} fusion(bf16[1,1,256,4096]{3,2,1,0:T(8,128)(2,1)S(1)} %copy-done, bf16[256,4096]{1,0:T(8,128)(2,1)} %reshape.327, bf16[1,1,4096,256]{3,2,1,0:T(8,128)(2,1)} %param.9), kind=kOutput, calls=%fused_computation.1 | convolution fusion | flops 1075380224 | bytes 8388608 | tf_op jit(solution)/shard_map/dot_general | solution.py:65
  180.3 30.3 %reduce-scatter.5.cloned.1.call-done = bf16[1,64,4096]{2,1,0:T(8,128)(2,1)} async-done(((bf16[4,64,4096]{2,1,0:T(8,128)(2,1)}), bf16[1,64,4096]{2,1,0:T(8,128)(2,1)}) %reduce-scatter.5.cloned.1.call-update) | async-done | bytes 524304 | tf_op jit(solution)/shard_map/reduce_scatter | solution.py:66
  210.7 2.2 reshape.337
  212.9 12.6 %all-to-all-start.3 = ((bf16[32,2,4096]{2,1,0:T(2,128)(2,1)}), bf16[32,2,4096]{2,1,0:T(2,128)(2,1)S(1)}, u32[]{:S(2)}, u32[]{:S(2)}) async-start(bf16[32,2,4096]{2,1,0:T(2,128)(2,1)} %reshape.337), calls=%async_computation.5 | async-start | bytes 1048576 | tf_op jit(solution)/shard_map/all_to_all | solution.py:69
  225.5 25.1 %reduce-scatter.3.cloned.1.call-done = bf16[1,64,4096]{2,1,0:T(8,128)(2,1)} async-done(((bf16[4,64,4096]{2,1,0:T(8,128)(2,1)}), bf16[1,64,4096]{2,1,0:T(8,128)(2,1)}) %reduce-scatter.3.cloned.1.call-update) | async-done | bytes 524304 | tf_op jit(solution)/shard_map/reduce_scatter | solution.py:66
  250.6 2.2 reshape.329
  252.8 12.5 %all-to-all-start.1 = ((bf16[32,2,4096]{2,1,0:T(2,128)(2,1)}), bf16[32,2,4096]{2,1,0:T(2,128)(2,1)S(1)}, u32[]{:S(2)}, u32[]{:S(2)}) async-start(bf16[32,2,4096]{2,1,0:T(2,128)(2,1)} %reshape.329), calls=%async_computation.2 | async-start | bytes 1048576 | tf_op jit(solution)/shard_map/all_to_all | solution.py:69
  266.3 1.4 convolution_convert_fusion.4
  267.6 5.0 %collective-permute-start.3 = (bf16[16,4096]{1,0:T(8,128)(2,1)S(1)}, bf16[16,4096]{1,0:T(8,128)(2,1)S(1)}, u32[]{:S(2)}, u32[]{:S(2)}) collective-permute-start(bf16[16,4096]{1,0:T(8,128)(2,1)S(1)} %convolution_convert_fusion.4), channel_id=1, source_target_pairs={{0,1},{1,0},{2,3},{3,2},{4,5},{5,4},{6,7},{7,6},{8,9},{9,8},{10,11... | collective-permute-start | bytes 393224 | tf_op jit(solution)/shard_map/ppermute | solution.py:11
  272.7 27.8 %all-to-all-done.1 = bf16[32,2,4096]{2,1,0:T(2,128)(2,1)S(1)} async-done(((bf16[32,2,4096]{2,1,0:T(2,128)(2,1)}), bf16[32,2,4096]{2,1,0:T(2,128)(2,1)S(1)}, u32[]{:S(2)}, u32[]{:S(2)}) %all-to-all-start.1) | async-done | bytes 524320 | tf_op jit(solution)/shard_map/all_to_all | solution.py:69
  301.0 7.3 %collective-permute-start.4 = (bf16[1,16,4096]{2,1,0:T(8,128)(2,1)S(1)}, bf16[1,16,4096]{2,1,0:T(8,128)(2,1)S(1)}, u32[]{:S(2)}, u32[]{:S(2)}) collective-permute-start(bf16[1,16,4096]{2,1,0:T(8,128)(2,1)S(1)} %fusion.2), channel_id=1, source_target_pairs={{0,256},{256,0},{1,257},{257,1},{2,258},{258,2},{3,259},{259,3},{4... | collective-permute-start | bytes 393224 | tf_op jit(solution)/shard_map/ppermute | solution.py:11
  (61 shorter events, 13.0 us)
Async XLA Ops:
  6.5 127.1 %copy-start = (bf16[1,1,256,4096]{3,2,1,0:T(8,128)(2,1)S(1)}, bf16[1,1,256,4096]{3,2,1,0:T(8,128)(2,1)}, u32[]{:S(2)}) copy-start(bf16[1,1,256,4096]{3,2,1,0:T(8,128)(2,1)} %param.10) | copy-start | bytes 6291460
  6.5 19.3 %collective-permute-start.1 = (s32[16,2]{0,1:T(2,128)}, s32[16,2]{0,1:T(2,128)S(1)}, u32[]{:S(2)}, u32[]{:S(2)}) collective-permute-start(s32[16,2]{0,1:T(2,128)} %bitcast.80), channel_id=1, source_target_pairs={{0,1},{1,0},{2,3},{3,2},{4,5},{5,4},{6,7},{7,6},{8,9},{9,8},{10,11... | collective-permute-start | bytes 392 | tf_op jit(solution)/shard_map/ppermute | solution.py:11
  22.9 4.0 %collective-permute-start = (bf16[1,16,4096]{2,1,0:T(8,128)(2,1)}, bf16[1,16,4096]{2,1,0:T(8,128)(2,1)S(1)}, u32[]{:S(2)}, u32[]{:S(2)}) collective-permute-start(bf16[1,16,4096]{2,1,0:T(8,128)(2,1)} %param.6), channel_id=1, source_target_pairs={{0,256},{256,0},{1,257},{257,1},{2,258},{258,2},{3,259},{259,3},{4... | collective-permute-start | bytes 393224 | tf_op jit(solution)/shard_map/ppermute | solution.py:11
  26.3 63.0 %copy-start.2 = (bf16[1,4096,32]{1,2,0:T(8,128)(2,1)S(1)}, bf16[1,4096,32]{1,2,0:T(8,128)(2,1)}, u32[]{:S(2)}) copy-start(bf16[1,4096,32]{1,2,0:T(8,128)(2,1)} %param.8) | copy-start | bytes 786436
  26.3 63.0 %copy-start.4 = (f32[1,4096]{1,0:T(1,128)S(1)}, f32[1,4096]{1,0:T(1,128)}, u32[]{:S(2)}) copy-start(f32[1,4096]{1,0:T(1,128)} %param.7) | copy-start | bytes 49156
  27.1 16.6 %copy-start.6 = (f32[16]{0:T(128)}, f32[16]{0:T(128)S(1)}, u32[]{:S(2)}) copy-start(f32[16]{0:T(128)S(1)} %add_rsqrt_fusion) | copy-start | bytes 196
  28.0 19.2 %copy-start.3 = (bf16[16,4096]{1,0:T(8,128)(2,1)}, bf16[16,4096]{1,0:T(8,128)(2,1)S(1)}, u32[]{:S(2)}) copy-start(bf16[16,4096]{1,0:T(8,128)(2,1)S(1)} %fusion.13) | copy-start | bytes 393220
  28.0 15.7 %collective-permute-start.2 = (bf16[16,4096]{1,0:T(8,128)(2,1)S(1)}, bf16[16,4096]{1,0:T(8,128)(2,1)S(1)}, u32[]{:S(2)}, u32[]{:S(2)}) collective-permute-start(bf16[16,4096]{1,0:T(8,128)(2,1)S(1)} %fusion.13), channel_id=1, source_target_pairs={{0,1},{1,0},{2,3},{3,2},{4,5},{5,4},{6,7},{7,6},{8,9},{9,8},{10,11... | collective-permute-start | bytes 393224 | tf_op jit(solution)/shard_map/ppermute | solution.py:11
  47.2 41.3 %all-to-all-start.2 = ((bf16[32,2,4096]{2,1,0:T(2,128)(2,1)}), bf16[32,2,4096]{2,1,0:T(2,128)(2,1)S(1)}, u32[]{:S(2)}, u32[]{:S(2)}) async-start(bf16[32,2,4096]{2,1,0:T(2,128)(2,1)} %reshape.334), calls=%async_computation.3 | async-start | bytes 1048576 | tf_op jit(solution)/shard_map/all_to_all | solution.py:59
  62.9 66.6 %all-gather.7.cloned.1.call-start = ((), (), s32[]{:S(2)}) async-start(), calls=%async_computation.9 | async-start | bytes 2621440 | tf_op jit(solution)/shard_map/all_gather | solution.py:60
  88.4 0.8 copy-start.1
  89.3 80.9 %all-gather.5.cloned.1.call-start = ((), (), s32[]{:S(2)}) async-start(), calls=%async_computation.8 | async-start | bytes 2621440 | tf_op jit(solution)/shard_map/all_gather | solution.py:60
  129.3 81.4 %reduce-scatter.5.cloned.1.call-start = ((), (), s32[]{:S(2)}) async-start(), calls=%async_computation.7 | async-start | bytes 2621440 | tf_op jit(solution)/shard_map/reduce_scatter | solution.py:66
  139.6 111.0 %reduce-scatter.3.cloned.1.call-start = ((), (), s32[]{:S(2)}) async-start(), calls=%async_computation.6 | async-start | bytes 2621440 | tf_op jit(solution)/shard_map/reduce_scatter | solution.py:66
  212.9 53.4 %copy-start.5 = (f32[16,64]{1,0:T(8,128)S(1)}, f32[16,64]{1,0:T(8,128)}, u32[]{:S(2)}) copy-start(f32[16,64]{1,0:T(8,128)} %get-tuple-element.6) | copy-start | bytes 12292
  212.9 39.9 %all-to-all-start.3 = ((bf16[32,2,4096]{2,1,0:T(2,128)(2,1)}), bf16[32,2,4096]{2,1,0:T(2,128)(2,1)S(1)}, u32[]{:S(2)}, u32[]{:S(2)}) async-start(bf16[32,2,4096]{2,1,0:T(2,128)(2,1)} %reshape.337), calls=%async_computation.5 | async-start | bytes 1048576 | tf_op jit(solution)/shard_map/all_to_all | solution.py:69
  252.8 47.7 %all-to-all-start.1 = ((bf16[32,2,4096]{2,1,0:T(2,128)(2,1)}), bf16[32,2,4096]{2,1,0:T(2,128)(2,1)S(1)}, u32[]{:S(2)}, u32[]{:S(2)}) async-start(bf16[32,2,4096]{2,1,0:T(2,128)(2,1)} %reshape.329), calls=%async_computation.2 | async-start | bytes 1048576 | tf_op jit(solution)/shard_map/all_to_all | solution.py:69
  267.6 33.0 %collective-permute-start.3 = (bf16[16,4096]{1,0:T(8,128)(2,1)S(1)}, bf16[16,4096]{1,0:T(8,128)(2,1)S(1)}, u32[]{:S(2)}, u32[]{:S(2)}) collective-permute-start(bf16[16,4096]{1,0:T(8,128)(2,1)S(1)} %convolution_convert_fusion.4), channel_id=1, source_target_pairs={{0,1},{1,0},{2,3},{3,2},{4,5},{5,4},{6,7},{7,6},{8,9},{9,8},{10,11... | collective-permute-start | bytes 393224 | tf_op jit(solution)/shard_map/ppermute | solution.py:11
  301.0 8.3 %collective-permute-start.4 = (bf16[1,16,4096]{2,1,0:T(8,128)(2,1)S(1)}, bf16[1,16,4096]{2,1,0:T(8,128)(2,1)S(1)}, u32[]{:S(2)}, u32[]{:S(2)}) collective-permute-start(bf16[1,16,4096]{2,1,0:T(8,128)(2,1)S(1)} %fusion.2), channel_id=1, source_target_pairs={{0,256},{256,0},{1,257},{257,1},{2,258},{258,2},{3,259},{259,3},{4... | collective-permute-start | bytes 393224 | tf_op jit(solution)/shard_map/ppermute | solution.py:11
Sparse Core Ops, SparseCore 0:
  89.4 40.0 all-gather.6
  131.6 38.5 all-gather.4
  173.0 37.5 reduce-scatter.4
  213.4 37.1 reduce-scatter.2

commit v3 on v2

--- a/solution.py
+++ b/solution.py
@@ -57,17 +57,19 @@
     experts, capacity, model_width = slot_grid.shape
     n_y = lax.axis_size("y")
     received = lax.all_to_all(slot_grid, "expert", split_axis=0, concat_axis=0, tiled=True)
-    gathered = lax.all_gather(received[None], "y", axis=0, tiled=True)
-    rows_in = gathered.reshape(-1, model_width)
+    shifted = [received] + [passed_along(received, "y", k) for k in range(1, n_y)]
+    rows_in = jnp.concatenate(shifted, axis=0).reshape(-1, model_width)
     hidden = jax.nn.gelu(
         jnp.dot(rows_in, w_first, preferred_element_type=jnp.float32)
     ).astype(jnp.bfloat16)
     partial = jnp.dot(hidden, w_second, preferred_element_type=jnp.float32).astype(jnp.bfloat16)
-    summed = lax.psum_scatter(
-        partial.reshape(n_y, -1, model_width), "y", scatter_dimension=0, tiled=True
-    )
+    partial = partial.reshape(n_y, experts * capacity, model_width)
+    summed = partial[0].astype(jnp.float32)
+    for k in range(1, n_y):
+        summed = summed + passed_along(partial[k], "y", n_y - k).astype(jnp.float32)
     back = lax.all_to_all(
-        summed.reshape(experts, capacity, model_width), "expert", split_axis=0, concat_axis=0, tiled=True
+        summed.astype(jnp.bfloat16).reshape(experts, capacity, model_width),
+        "expert", split_axis=0, concat_axis=0, tiled=True,
     )
     return jnp.dot(
         combine_mat,

time: 317 us -> 283 us (0.89)
  starting transfers between devices: 82.3 us -> 132 us
  waiting for transfers between devices: 145 us -> 95.3 us
  blocking collectives: 36.4 us -> 0 us
  other arithmetic: 4.19 us -> 18 us
  between operations: 13.3 us -> 0.37 us
    reduce_scatter x2 -> x0, waiting for transfers between devices: 55.4 us -> none  [expert_pass(): lax.psum_scatter(partial.reshape(n_y, -1, model_width), 'y', scatter_dime...]
    ppermute x5 -> x17, starting transfers between devices: 41.3 us -> 84 us  [passed_along(): return lax.ppermute(value, axis, pairs)]
    all_to_all x1 -> x0, blocking collectives: 36.4 us -> none  [expert_pass(): lax.all_to_all(slot_grid, 'expert', split_axis=0, concat_axis=0, tiled=True)]
    all_gather x2 -> x0, waiting for transfers between devices: 30.8 us -> none  [expert_pass(): gathered = lax.all_gather(received[None], 'y', axis=0, tiled=True)]
    ppermute x5 -> x17, waiting for transfers between devices: 7.65 us -> 34.9 us  [passed_along(): return lax.ppermute(value, axis, pairs)]
    all_to_all x1 -> x2, waiting for transfers between devices: 23.7 us -> 36 us  [expert_pass(): lax.all_to_all(slot_grid, 'expert', split_axis=0, concat_axis=0, tiled=True)]
    concatenate x0 -> x2, other arithmetic: none -> 10.9 us  [expert_pass(): rows_in = jnp.concatenate(shifted, axis=0).reshape(-1, model_width)]
    all_to_all x1 -> x2, starting transfers between devices: 15.7 us -> 25.4 us  [expert_pass(): lax.all_to_all(slot_grid, 'expert', split_axis=0, concat_axis=0, tiled=True)]
  transfers between devices with their start and end apart: 12 -> 21, of which waited for: 9 -> 10; matrix products, arithmetic and copies ran while one was open for 10% -> 16% of each run, Pallas kernels for 0% -> 0%
where the time goes in v3:
time: 283 us; the launch traced here: 282 us
  starting transfers between devices  132 us (47%)
  waiting for transfers between devices  95.3 us (34%)
  local copies, waits for them, and re-layouts  20.1 us (7%)
  other arithmetic  18 us (6%)
  matrix products  16.1 us (6%)
    ppermute x17, starting transfers between devices, passed_along(): return lax.ppermute(value, axis, pairs)  84 us
    all_to_all x2, waiting for transfers between devices, expert_pass(): lax.all_to_all(slot_grid, 'expert', split_axis=0, concat_axis=0, tiled=True)  36 us
    ppermute x17, waiting for transfers between devices, passed_along(): return lax.ppermute(value, axis, pairs)  34.9 us
    all_to_all x2, starting transfers between devices, expert_pass(): lax.all_to_all(slot_grid, 'expert', split_axis=0, concat_axis=0, tiled=True)  25.4 us
    all_to_all x2, waiting for transfers between devices, expert_pass(): lax.all_to_all(summed.astype(jnp.bfloat16).reshape(experts, capacity, mod...  24.3 us
    all_to_all x2, starting transfers between devices, expert_pass(): lax.all_to_all(summed.astype(jnp.bfloat16).reshape(experts, capacity, mod...  22.5 us
    dot_general x2, matrix products, expert_pass(): jnp.dot(hidden, w_second, preferred_element_type=jnp.float32)  11.9 us
    concatenate x2, other arithmetic, expert_pass(): rows_in = jnp.concatenate(shifted, axis=0).reshape(-1, model_width)  10.9 us
  transfers between devices with their start and end apart: 21, of which 10 were waited for; matrix products, arithmetic and copies ran while one was open for 16% of the time, Pallas kernels for 0%

profile of v3, /device:TPU:1, one launch (start us, length us, event | category | flops | bytes accessed | tf_op | source)
XLA Modules:
  0.0 281.8 jit_solution(8041863561794262027)
XLA Ops:
  0.0 16.4 %collective-permute-start.7 = (s32[16,2]{0,1:T(2,128)}, s32[16,2]{0,1:T(2,128)S(1)}, u32[]{:S(2)}, u32[]{:S(2)}) collective-permute-start(s32[16,2]{0,1:T(2,128)} %bitcast.76), channel_id=1, source_target_pairs={{0,1},{1,0},{2,3},{3,2},{4,5},{5,4},{6,7},{7,6},{8,9},{9,8},{10,11... | collective-permute-start | bytes 392 | tf_op jit(solution)/shard_map/ppermute | solution.py:11
  21.5 9.7 %collective-permute-start.8 = (bf16[16,4096]{1,0:T(8,128)(2,1)S(1)}, bf16[16,4096]{1,0:T(8,128)(2,1)S(1)}, u32[]{:S(2)}, u32[]{:S(2)}) collective-permute-start(bf16[16,4096]{1,0:T(8,128)(2,1)S(1)} %fusion.13), channel_id=1, source_target_pairs={{0,1},{1,0},{2,3},{3,2},{4,5},{5,4},{6,7},{7,6},{8,9},{9,8},{10,11... | collective-permute-start | bytes 393224 | tf_op jit(solution)/shard_map/ppermute | solution.py:11
  31.2 6.0 %collective-permute-done.8 = bf16[16,4096]{1,0:T(8,128)(2,1)S(1)} collective-permute-done((bf16[16,4096]{1,0:T(8,128)(2,1)S(1)}, bf16[16,4096]{1,0:T(8,128)(2,1)S(1)}, u32[]{:S(2)}, u32[]{:S(2)}) %collective-permute-start.8) | collective-permute-done | bytes 131104 | tf_op jit(solution)/shard_map/ppermute | solution.py:11
  40.7 15.7 %all-to-all-start.2 = ((bf16[32,2,4096]{2,1,0:T(2,128)(2,1)}), bf16[32,2,4096]{2,1,0:T(2,128)(2,1)S(1)}, u32[]{:S(2)}, u32[]{:S(2)}) async-start(bf16[32,2,4096]{2,1,0:T(2,128)(2,1)} %reshape.345), calls=%async_computation.2 | async-start | bytes 1048576 | tf_op jit(solution)/shard_map/all_to_all | solution.py:59
  62.5 19.4 %all-to-all-done.2 = bf16[32,2,4096]{2,1,0:T(2,128)(2,1)S(1)} async-done(((bf16[32,2,4096]{2,1,0:T(2,128)(2,1)}), bf16[32,2,4096]{2,1,0:T(2,128)(2,1)S(1)}, u32[]{:S(2)}, u32[]{:S(2)}) %all-to-all-start.2) | async-done | bytes 524320 | tf_op jit(solution)/shard_map/all_to_all | solution.py:59
  81.9 9.8 %all-to-all-start = ((bf16[32,2,4096]{2,1,0:T(2,128)(2,1)}), bf16[32,2,4096]{2,1,0:T(2,128)(2,1)S(1)}, u32[]{:S(2)}, u32[]{:S(2)}) async-start(bf16[32,2,4096]{2,1,0:T(2,128)(2,1)} %reshape.338), calls=%async_computation | async-start | bytes 1048576 | tf_op jit(solution)/shard_map/all_to_all | solution.py:59
  91.7 4.8 %collective-permute-start.10 = (bf16[32,2,4096]{2,1,0:T(2,128)(2,1)S(1)}, bf16[32,2,4096]{2,1,0:T(2,128)(2,1)}, u32[]{:S(2)}, u32[]{:S(2)}) collective-permute-start(bf16[32,2,4096]{2,1,0:T(2,128)(2,1)S(1)} %all-to-all-done.2), channel_id=1, source_target_pairs={{0,4},{2,6},{4,0},{6,2},{1,5},{3,7},{5,1},{7,3},{8,12},{10,14},{12... | collective-permute-start | bytes 1572872 | tf_op jit(solution)/shard_map/ppermute | solution.py:11
  101.8 16.6 %all-to-all-done = bf16[32,2,4096]{2,1,0:T(2,128)(2,1)S(1)} async-done(((bf16[32,2,4096]{2,1,0:T(2,128)(2,1)}), bf16[32,2,4096]{2,1,0:T(2,128)(2,1)S(1)}, u32[]{:S(2)}, u32[]{:S(2)}) %all-to-all-start) | async-done | bytes 524320 | tf_op jit(solution)/shard_map/all_to_all | solution.py:59
  121.6 4.5 %collective-permute-start.2 = (bf16[32,2,4096]{2,1,0:T(2,128)(2,1)S(1)}, bf16[32,2,4096]{2,1,0:T(2,128)(2,1)}, u32[]{:S(2)}, u32[]{:S(2)}) collective-permute-start(bf16[32,2,4096]{2,1,0:T(2,128)(2,1)S(1)} %all-to-all-done), channel_id=1, source_target_pairs={{0,4},{2,6},{4,0},{6,2},{1,5},{3,7},{5,1},{7,3},{8,12},{10,14},{12... | collective-permute-start | bytes 1572872 | tf_op jit(solution)/shard_map/ppermute | solution.py:11
  129.2 5.5 %pad_maximum_fusion.1 = bf16[128,2,4096]{2,1,0:T(2,128)(2,1)} fusion(bf16[32,2,4096]{2,1,0:T(2,128)(2,1)} %collective-permute-done.11, bf16[32,2,4096]{2,1,0:T(2,128)(2,1)} %collective-permute-done.10, bf16[32,2,4096]{2,1,0:T(2,128)(2,1)} %collective-permute-done.9, bf16[32,2,4096]{2,1,0:T(2,128)(2,1)S(1)} %all-to-all-done.2), kind=kLoop, calls=%fused_computation.10 | loop fusion | flops 3145728 | bytes 4194304 | tf_op jit(solution)/shard_map/concatenate | solution.py:61
  134.6 4.1 %reshape.346 = bf16[256,4096]{1,0:T(8,128)(2,1)} reshape(bf16[128,2,4096]{2,1,0:T(2,128)(2,1)} %pad_maximum_fusion.1) | data formatting | bytes 4194304 | tf_op jit(solution)/shard_map/reshape | solution.py:61
  138.8 6.0 %convolution_convert_fusion = bf16[256,4096]{1,0:T(8,128)(2,1)} fusion(bf16[1,1,256,4096]{3,2,1,0:T(8,128)(2,1)S(1)} %copy-done, bf16[256,4096]{1,0:T(8,128)(2,1)} %reshape.346, bf16[1,1,4096,256]{3,2,1,0:T(8,128)(2,1)} %param.9), kind=kOutput, calls=%fused_computation | convolution fusion | flops 1075380224 | bytes 8388608 | tf_op jit(solution)/shard_map/dot_general | solution.py:65
  149.3 4.1 %collective-permute-start.13 = (bf16[64,4096]{1,0:T(8,128)(2,1)}, bf16[64,4096]{1,0:T(8,128)(2,1)}, u32[]{:S(2)}, u32[]{:S(2)}) collective-permute-start(bf16[64,4096]{1,0:T(8,128)(2,1)} %get-tuple-element.11), channel_id=1, source_target_pairs={{0,4},{2,6},{4,0},{6,2},{1,5},{3,7},{5,1},{7,3},{8,12},{10,14},{12... | collective-permute-start | bytes 1572872 | tf_op jit(solution)/shard_map/ppermute | solution.py:11
  155.3 5.4 %pad_maximum_fusion = bf16[128,2,4096]{2,1,0:T(2,128)(2,1)} fusion(bf16[32,2,4096]{2,1,0:T(2,128)(2,1)} %collective-permute-done.3, bf16[32,2,4096]{2,1,0:T(2,128)(2,1)} %collective-permute-done.2, bf16[32,2,4096]{2,1,0:T(2,128)(2,1)} %collective-permute-done.1, bf16[32,2,4096]{2,1,0:T(2,128)(2,1)S(1)} %all-to-all-done), kind=kLoop, calls=%fused_computation.9 | loop fusion | flops 3145728 | bytes 4194304 | tf_op jit(solution)/shard_map/concatenate | solution.py:61
  160.8 4.1 %reshape.339 = bf16[256,4096]{1,0:T(8,128)(2,1)} reshape(bf16[128,2,4096]{2,1,0:T(2,128)(2,1)} %pad_maximum_fusion) | data formatting | bytes 4194304 | tf_op jit(solution)/shard_map/reshape | solution.py:61
  164.9 5.9 %convolution_convert_fusion.1 = bf16[256,4096]{1,0:T(8,128)(2,1)} fusion(bf16[1,1,256,4096]{3,2,1,0:T(8,128)(2,1)S(1)} %copy-done, bf16[256,4096]{1,0:T(8,128)(2,1)} %reshape.339, bf16[1,1,4096,256]{3,2,1,0:T(8,128)(2,1)} %param.9), kind=kOutput, calls=%fused_computation.1 | convolution fusion | flops 1075380224 | bytes 8388608 | tf_op jit(solution)/shard_map/dot_general | solution.py:65
  170.8 5.6 %collective-permute-done.14 = bf16[64,4096]{1,0:T(8,128)(2,1)} collective-permute-done((bf16[64,4096]{1,0:T(8,128)(2,1)}, bf16[64,4096]{1,0:T(8,128)(2,1)}, u32[]{:S(2)}, u32[]{:S(2)}) %collective-permute-start.14) | collective-permute-done | bytes 524320 | tf_op jit(solution)/shard_map/ppermute | solution.py:11
  179.2 10.4 %all-to-all-start.3 = ((bf16[32,2,4096]{2,1,0:T(2,128)(2,1)}), bf16[32,2,4096]{2,1,0:T(2,128)(2,1)S(1)}, u32[]{:S(2)}, u32[]{:S(2)}) async-start(bf16[32,2,4096]{2,1,0:T(2,128)(2,1)} %reshape.347), calls=%async_computation.3 | async-start | bytes 1048576 | tf_op jit(solution)/shard_map/all_to_all | solution.py:70
  199.9 5.8 %collective-permute-done.4 = bf16[64,4096]{1,0:T(8,128)(2,1)S(1)} collective-permute-done((bf16[64,4096]{1,0:T(8,128)(2,1)S(1)}, bf16[64,4096]{1,0:T(8,128)(2,1)S(1)}, u32[]{:S(2)}, u32[]{:S(2)}) %collective-permute-start.4) | collective-permute-done | bytes 524320 | tf_op jit(solution)/shard_map/ppermute | solution.py:11
  208.6 12.9 %collective-permute-done.6 = bf16[64,4096]{1,0:T(8,128)(2,1)S(1)} collective-permute-done((bf16[64,4096]{1,0:T(8,128)(2,1)S(1)}, bf16[64,4096]{1,0:T(8,128)(2,1)S(1)}, u32[]{:S(2)}, u32[]{:S(2)}) %collective-permute-start.6) | collective-permute-done | bytes 524320 | tf_op jit(solution)/shard_map/ppermute | solution.py:11
  224.0 12.1 %all-to-all-start.1 = ((bf16[32,2,4096]{2,1,0:T(2,128)(2,1)}), bf16[32,2,4096]{2,1,0:T(2,128)(2,1)}, u32[]{:S(2)}, u32[]{:S(2)}) async-start(bf16[32,2,4096]{2,1,0:T(2,128)(2,1)} %reshape.340), calls=%async_computation.1 | async-start | bytes 1048576 | tf_op jit(solution)/shard_map/all_to_all | solution.py:70
  236.7 10.0 %collective-permute-start.15 = (bf16[16,4096]{1,0:T(8,128)(2,1)S(1)}, bf16[16,4096]{1,0:T(8,128)(2,1)S(1)}, u32[]{:S(2)}, u32[]{:S(2)}) collective-permute-start(bf16[16,4096]{1,0:T(8,128)(2,1)S(1)} %convolution_convert_fusion.4), channel_id=1, source_target_pairs={{0,1},{1,0},{2,3},{3,2},{4,5},{5,4},{6,7},{7,6},{8,9},{9,8},{10,11... | collective-permute-start | bytes 393224 | tf_op jit(solution)/shard_map/ppermute | solution.py:11
  246.6 24.3 %all-to-all-done.1 = bf16[32,2,4096]{2,1,0:T(2,128)(2,1)} async-done(((bf16[32,2,4096]{2,1,0:T(2,128)(2,1)}), bf16[32,2,4096]{2,1,0:T(2,128)(2,1)}, u32[]{:S(2)}, u32[]{:S(2)}) %all-to-all-start.1) | async-done | bytes 524320 | tf_op jit(solution)/shard_map/all_to_all | solution.py:70
  272.5 7.7 %collective-permute-start.16 = (bf16[1,16,4096]{2,1,0:T(8,128)(2,1)S(1)}, bf16[1,16,4096]{2,1,0:T(8,128)(2,1)S(1)}, u32[]{:S(2)}, u32[]{:S(2)}) collective-permute-start(bf16[1,16,4096]{2,1,0:T(8,128)(2,1)S(1)} %fusion.2), channel_id=1, source_target_pairs={{0,256},{256,0},{1,257},{257,1},{2,258},{258,2},{3,259},{259,3},{4... | collective-permute-start | bytes 393224 | tf_op jit(solution)/shard_map/ppermute | solution.py:11
  (78 shorter events, 54.6 us)
Async XLA Ops:
  0.0 138.8 %copy-start = (bf16[1,1,256,4096]{3,2,1,0:T(8,128)(2,1)S(1)}, bf16[1,1,256,4096]{3,2,1,0:T(8,128)(2,1)}, u32[]{:S(2)}) copy-start(bf16[1,1,256,4096]{3,2,1,0:T(8,128)(2,1)} %param.10) | copy-start | bytes 6291460
  0.0 58.2 %copy-start.3 = (f32[1,4096]{1,0:T(1,128)S(1)}, f32[1,4096]{1,0:T(1,128)}, u32[]{:S(2)}) copy-start(f32[1,4096]{1,0:T(1,128)} %param.7) | copy-start | bytes 49156
  0.0 58.2 %copy-start.1 = (bf16[1,4096,32]{1,2,0:T(8,128)(2,1)S(1)}, bf16[1,4096,32]{1,2,0:T(8,128)(2,1)}, u32[]{:S(2)}) copy-start(bf16[1,4096,32]{1,2,0:T(8,128)(2,1)} %param.8) | copy-start | bytes 786436
  0.0 19.3 %collective-permute-start.7 = (s32[16,2]{0,1:T(2,128)}, s32[16,2]{0,1:T(2,128)S(1)}, u32[]{:S(2)}, u32[]{:S(2)}) collective-permute-start(s32[16,2]{0,1:T(2,128)} %bitcast.76), channel_id=1, source_target_pairs={{0,1},{1,0},{2,3},{3,2},{4,5},{5,4},{6,7},{7,6},{8,9},{9,8},{10,11... | collective-permute-start | bytes 392 | tf_op jit(solution)/shard_map/ppermute | solution.py:11
  16.4 4.0 %collective-permute-start = (bf16[1,16,4096]{2,1,0:T(8,128)(2,1)}, bf16[1,16,4096]{2,1,0:T(8,128)(2,1)S(1)}, u32[]{:S(2)}, u32[]{:S(2)}) collective-permute-start(bf16[1,16,4096]{2,1,0:T(8,128)(2,1)} %param.6), channel_id=1, source_target_pairs={{0,256},{256,0},{1,257},{257,1},{2,258},{258,2},{3,259},{259,3},{4... | collective-permute-start | bytes 393224 | tf_op jit(solution)/shard_map/ppermute | solution.py:11
  21.5 15.7 %collective-permute-start.8 = (bf16[16,4096]{1,0:T(8,128)(2,1)S(1)}, bf16[16,4096]{1,0:T(8,128)(2,1)S(1)}, u32[]{:S(2)}, u32[]{:S(2)}) collective-permute-start(bf16[16,4096]{1,0:T(8,128)(2,1)S(1)} %fusion.13), channel_id=1, source_target_pairs={{0,1},{1,0},{2,3},{3,2},{4,5},{5,4},{6,7},{7,6},{8,9},{9,8},{10,11... | collective-permute-start | bytes 393224 | tf_op jit(solution)/shard_map/ppermute | solution.py:11
  40.7 41.2 %all-to-all-start.2 = ((bf16[32,2,4096]{2,1,0:T(2,128)(2,1)}), bf16[32,2,4096]{2,1,0:T(2,128)(2,1)S(1)}, u32[]{:S(2)}, u32[]{:S(2)}) async-start(bf16[32,2,4096]{2,1,0:T(2,128)(2,1)} %reshape.345), calls=%async_computation.2 | async-start | bytes 1048576 | tf_op jit(solution)/shard_map/all_to_all | solution.py:59
  81.9 36.5 %all-to-all-start = ((bf16[32,2,4096]{2,1,0:T(2,128)(2,1)}), bf16[32,2,4096]{2,1,0:T(2,128)(2,1)S(1)}, u32[]{:S(2)}, u32[]{:S(2)}) async-start(bf16[32,2,4096]{2,1,0:T(2,128)(2,1)} %reshape.338), calls=%async_computation | async-start | bytes 1048576 | tf_op jit(solution)/shard_map/all_to_all | solution.py:59
  91.7 34.5 %collective-permute-start.10 = (bf16[32,2,4096]{2,1,0:T(2,128)(2,1)S(1)}, bf16[32,2,4096]{2,1,0:T(2,128)(2,1)}, u32[]{:S(2)}, u32[]{:S(2)}) collective-permute-start(bf16[32,2,4096]{2,1,0:T(2,128)(2,1)S(1)} %all-to-all-done.2), channel_id=1, source_target_pairs={{0,4},{2,6},{4,0},{6,2},{1,5},{3,7},{5,1},{7,3},{8,12},{10,14},{12... | collective-permute-start | bytes 1572872 | tf_op jit(solution)/shard_map/ppermute | solution.py:11
  96.5 32.7 %collective-permute-start.11 = (bf16[32,2,4096]{2,1,0:T(2,128)(2,1)S(1)}, bf16[32,2,4096]{2,1,0:T(2,128)(2,1)}, u32[]{:S(2)}, u32[]{:S(2)}) collective-permute-start(bf16[32,2,4096]{2,1,0:T(2,128)(2,1)S(1)} %all-to-all-done.2), channel_id=1, source_target_pairs={{0,6},{2,0},{4,2},{6,4},{1,7},{3,1},{5,3},{7,5},{8,14},{10,8},{12,... | collective-permute-start | bytes 1572872 | tf_op jit(solution)/shard_map/ppermute | solution.py:11
  99.2 30.0 %collective-permute-start.9 = (bf16[32,2,4096]{2,1,0:T(2,128)(2,1)S(1)}, bf16[32,2,4096]{2,1,0:T(2,128)(2,1)}, u32[]{:S(2)}, u32[]{:S(2)}) collective-permute-start(bf16[32,2,4096]{2,1,0:T(2,128)(2,1)S(1)} %all-to-all-done.2), channel_id=1, source_target_pairs={{0,2},{2,4},{4,6},{6,0},{1,3},{3,5},{5,7},{7,1},{8,10},{10,12},{12... | collective-permute-start | bytes 1572872 | tf_op jit(solution)/shard_map/ppermute | solution.py:11
  118.4 35.0 %collective-permute-start.1 = (bf16[32,2,4096]{2,1,0:T(2,128)(2,1)S(1)}, bf16[32,2,4096]{2,1,0:T(2,128)(2,1)}, u32[]{:S(2)}, u32[]{:S(2)}) collective-permute-start(bf16[32,2,4096]{2,1,0:T(2,128)(2,1)S(1)} %all-to-all-done), channel_id=1, source_target_pairs={{0,2},{2,4},{4,6},{6,0},{1,3},{3,5},{5,7},{7,1},{8,10},{10,12},{12... | collective-permute-start | bytes 1572872 | tf_op jit(solution)/shard_map/ppermute | solution.py:11
  121.6 33.7 %collective-permute-start.2 = (bf16[32,2,4096]{2,1,0:T(2,128)(2,1)S(1)}, bf16[32,2,4096]{2,1,0:T(2,128)(2,1)}, u32[]{:S(2)}, u32[]{:S(2)}) collective-permute-start(bf16[32,2,4096]{2,1,0:T(2,128)(2,1)S(1)} %all-to-all-done), channel_id=1, source_target_pairs={{0,4},{2,6},{4,0},{6,2},{1,5},{3,7},{5,1},{7,3},{8,12},{10,14},{12... | collective-permute-start | bytes 1572872 | tf_op jit(solution)/shard_map/ppermute | solution.py:11
  126.2 29.2 %collective-permute-start.3 = (bf16[32,2,4096]{2,1,0:T(2,128)(2,1)S(1)}, bf16[32,2,4096]{2,1,0:T(2,128)(2,1)}, u32[]{:S(2)}, u32[]{:S(2)}) collective-permute-start(bf16[32,2,4096]{2,1,0:T(2,128)(2,1)S(1)} %all-to-all-done), channel_id=1, source_target_pairs={{0,6},{2,0},{4,2},{6,4},{1,7},{3,1},{5,3},{7,5},{8,14},{10,8},{12,... | collective-permute-start | bytes 1572872 | tf_op jit(solution)/shard_map/ppermute | solution.py:11
  147.4 23.4 %collective-permute-start.12 = (bf16[64,4096]{1,0:T(8,128)(2,1)}, bf16[64,4096]{1,0:T(8,128)(2,1)S(1)}, u32[]{:S(2)}, u32[]{:S(2)}) collective-permute-start(bf16[64,4096]{1,0:T(8,128)(2,1)} %get-tuple-element.9), channel_id=1, source_target_pairs={{0,6},{2,0},{4,2},{6,4},{1,7},{3,1},{5,3},{7,5},{8,14},{10,8},{12,... | collective-permute-start | bytes 1572872 | tf_op jit(solution)/shard_map/ppermute | solution.py:11
  149.3 21.5 %collective-permute-start.13 = (bf16[64,4096]{1,0:T(8,128)(2,1)}, bf16[64,4096]{1,0:T(8,128)(2,1)}, u32[]{:S(2)}, u32[]{:S(2)}) collective-permute-start(bf16[64,4096]{1,0:T(8,128)(2,1)} %get-tuple-element.11), channel_id=1, source_target_pairs={{0,4},{2,6},{4,0},{6,2},{1,5},{3,7},{5,1},{7,3},{8,12},{10,14},{12... | collective-permute-start | bytes 1572872 | tf_op jit(solution)/shard_map/ppermute | solution.py:11
  153.4 23.1 %collective-permute-start.14 = (bf16[64,4096]{1,0:T(8,128)(2,1)}, bf16[64,4096]{1,0:T(8,128)(2,1)}, u32[]{:S(2)}, u32[]{:S(2)}) collective-permute-start(bf16[64,4096]{1,0:T(8,128)(2,1)} %get-tuple-element.10), channel_id=1, source_target_pairs={{0,2},{2,4},{4,6},{6,0},{1,3},{3,5},{5,7},{7,1},{8,10},{10,12},{12... | collective-permute-start | bytes 1572872 | tf_op jit(solution)/shard_map/ppermute | solution.py:11
  179.2 44.8 %all-to-all-start.3 = ((bf16[32,2,4096]{2,1,0:T(2,128)(2,1)}), bf16[32,2,4096]{2,1,0:T(2,128)(2,1)S(1)}, u32[]{:S(2)}, u32[]{:S(2)}) async-start(bf16[32,2,4096]{2,1,0:T(2,128)(2,1)} %reshape.347), calls=%async_computation.3 | async-start | bytes 1048576 | tf_op jit(solution)/shard_map/all_to_all | solution.py:70
  191.2 14.6 %collective-permute-start.4 = (bf16[64,4096]{1,0:T(8,128)(2,1)S(1)}, bf16[64,4096]{1,0:T(8,128)(2,1)S(1)}, u32[]{:S(2)}, u32[]{:S(2)}) collective-permute-start(bf16[64,4096]{1,0:T(8,128)(2,1)S(1)} %get-tuple-element.12), channel_id=1, source_target_pairs={{0,6},{2,0},{4,2},{6,4},{1,7},{3,1},{5,3},{7,5},{8,14},{10,8},{12,... | collective-permute-start | bytes 1572872 | tf_op jit(solution)/shard_map/ppermute | solution.py:11
  193.1 15.6 %collective-permute-start.5 = (bf16[64,4096]{1,0:T(8,128)(2,1)S(1)}, bf16[64,4096]{1,0:T(8,128)(2,1)S(1)}, u32[]{:S(2)}, u32[]{:S(2)}) collective-permute-start(bf16[64,4096]{1,0:T(8,128)(2,1)S(1)} %get-tuple-element.14), channel_id=1, source_target_pairs={{0,4},{2,6},{4,0},{6,2},{1,5},{3,7},{5,1},{7,3},{8,12},{10,14},{12... | collective-permute-start | bytes 1572872 | tf_op jit(solution)/shard_map/ppermute | solution.py:11
  197.2 24.4 %collective-permute-start.6 = (bf16[64,4096]{1,0:T(8,128)(2,1)S(1)}, bf16[64,4096]{1,0:T(8,128)(2,1)S(1)}, u32[]{:S(2)}, u32[]{:S(2)}) collective-permute-start(bf16[64,4096]{1,0:T(8,128)(2,1)S(1)} %get-tuple-element.13), channel_id=1, source_target_pairs={{0,2},{2,4},{4,6},{6,0},{1,3},{3,5},{5,7},{7,1},{8,10},{10,12},{12... | collective-permute-start | bytes 1572872 | tf_op jit(solution)/shard_map/ppermute | solution.py:11
  224.0 46.9 %all-to-all-start.1 = ((bf16[32,2,4096]{2,1,0:T(2,128)(2,1)}), bf16[32,2,4096]{2,1,0:T(2,128)(2,1)}, u32[]{:S(2)}, u32[]{:S(2)}) async-start(bf16[32,2,4096]{2,1,0:T(2,128)(2,1)} %reshape.340), calls=%async_computation.1 | async-start | bytes 1048576 | tf_op jit(solution)/shard_map/all_to_all | solution.py:70
  236.7 35.5 %collective-permute-start.15 = (bf16[16,4096]{1,0:T(8,128)(2,1)S(1)}, bf16[16,4096]{1,0:T(8,128)(2,1)S(1)}, u32[]{:S(2)}, u32[]{:S(2)}) collective-permute-start(bf16[16,4096]{1,0:T(8,128)(2,1)S(1)} %convolution_convert_fusion.4), channel_id=1, source_target_pairs={{0,1},{1,0},{2,3},{3,2},{4,5},{5,4},{6,7},{7,6},{8,9},{9,8},{10,11... | collective-permute-start | bytes 393224 | tf_op jit(solution)/shard_map/ppermute | solution.py:11
  272.5 8.6 %collective-permute-start.16 = (bf16[1,16,4096]{2,1,0:T(8,128)(2,1)S(1)}, bf16[1,16,4096]{2,1,0:T(8,128)(2,1)S(1)}, u32[]{:S(2)}, u32[]{:S(2)}) collective-permute-start(bf16[1,16,4096]{2,1,0:T(8,128)(2,1)S(1)} %fusion.2), channel_id=1, source_target_pairs={{0,256},{256,0},{1,257},{257,1},{2,258},{258,2},{3,259},{259,3},{4... | collective-permute-start | bytes 393224 | tf_op jit(solution)/shard_map/ppermute | solution.py:11
  (3 other events, 49.2 us)

commit v4 on v2

--- a/solution.py
+++ b/solution.py
@@ -41,7 +41,7 @@
     tok_count, model_width = rows.shape
     experts = router_mat.shape[1]
     gate_vals, pair_ranks, is_kept = route(rows, router_mat, pick, tok_count, capacity)
-    slot_ids = pick * capacity + pair_ranks
+    slot_ids = pair_ranks * experts + pick
     slot_count = experts * capacity
     slot_labels = jnp.arange(slot_count, dtype=jnp.int32)
     slot_hot = ((slot_ids[:, :, None] == slot_labels[None, None, :]) & is_kept[:, :, None]).astype(
@@ -50,28 +50,31 @@
     placement = jnp.transpose(jnp.sum(slot_hot, axis=1)).astype(jnp.bfloat16)
     combine_mat = jnp.sum(slot_hot * gate_vals[:, :, None], axis=1)
     send_rows = jnp.dot(placement, rows, preferred_element_type=jnp.float32).astype(jnp.bfloat16)
-    return send_rows.reshape(experts, capacity, model_width), combine_mat
+    return send_rows.reshape(capacity, experts, model_width), combine_mat
 
 
 def expert_pass(slot_grid, combine_mat, w_first, w_second):
-    experts, capacity, model_width = slot_grid.shape
+    capacity, experts, model_width = slot_grid.shape
     n_y = lax.axis_size("y")
-    received = lax.all_to_all(slot_grid, "expert", split_axis=0, concat_axis=0, tiled=True)
-    gathered = lax.all_gather(received[None], "y", axis=0, tiled=True)
-    rows_in = gathered.reshape(-1, model_width)
-    hidden = jax.nn.gelu(
-        jnp.dot(rows_in, w_first, preferred_element_type=jnp.float32)
-    ).astype(jnp.bfloat16)
-    partial = jnp.dot(hidden, w_second, preferred_element_type=jnp.float32).astype(jnp.bfloat16)
-    summed = lax.psum_scatter(
-        partial.reshape(n_y, -1, model_width), "y", scatter_dimension=0, tiled=True
-    )
+    received = lax.all_to_all(slot_grid, "expert", split_axis=1, concat_axis=1, tiled=True)
+    summed = None
+    for k in range(n_y):
+        rows_in = received if k == 0 else passed_along(received, "y", k)
+        hidden = jax.nn.gelu(
+            jnp.dot(rows_in.reshape(-1, model_width), w_first, preferred_element_type=jnp.float32)
+        ).astype(jnp.bfloat16)
+        partial = jnp.dot(hidden, w_second, preferred_element_type=jnp.float32).astype(jnp.bfloat16)
+        if k == 0:
+            summed = partial.astype(jnp.float32)
+        else:
+            summed = summed + passed_along(partial, "y", n_y - k).astype(jnp.float32)
     back = lax.all_to_all(
-        summed.reshape(experts, capacity, model_width), "expert", split_axis=0, concat_axis=0, tiled=True
+        summed.astype(jnp.bfloat16).reshape(capacity, experts, model_width),
+        "expert", split_axis=1, concat_axis=1, tiled=True,
     )
     return jnp.dot(
         combine_mat,
-        back.reshape(experts * capacity, model_width).astype(jnp.float32),
+        back.reshape(capacity * experts, model_width).astype(jnp.float32),
         precision=lax.Precision.HIGHEST,
     )
 
@@ -82,9 +85,17 @@
     experts = router.shape[2]
     top_count = expert_ids.shape[2]
     capacity = max(2, (5 * top_count * tok_count + 4 * experts - 1) // (4 * experts))
+    n_sec = lax.axis_size("section")
+    n_zh = lax.axis_size("zh")
+    crossed = [
+        (s * n_zh + h, ((s + 1) % n_sec) * n_zh + (h + 1) % n_zh)
+        for s in range(n_sec)
+        for h in range(n_zh)
+    ]
+    partner_arrived = lax.ppermute(sent, ("section", "zh"), crossed)[0]
     normed = normalize(arrived, norm_gain[0])
+    partner_rows = normalize(partner_arrived, norm_gain[0])
     own_pick = expert_ids[0]
-    partner_rows = passed_along(normed, "zh", 1)
     partner_pick = passed_along(own_pick, "zh", 1)
     w_first = w_in[0, 0]
     w_second = w_out[0, 0]

time: 317 us -> 253 us (0.80)
  waiting for transfers between devices: 145 us -> 72.8 us
  starting transfers between devices: 82.3 us -> 132 us
  blocking collectives: 36.4 us -> 0 us
  matrix products: 17.2 us -> 35 us
  between operations: 13.3 us -> 0.4 us
  local copies, waits for them, and re-layouts: 17.8 us -> 10.2 us
    reduce_scatter x2 -> x0, waiting for transfers between devices: 55.4 us -> none  [expert_pass(): lax.psum_scatter(partial.reshape(n_y, -1, model_width), 'y', scatter_dime...]
    all_to_all x1 -> x0, blocking collectives: 36.4 us -> none  [expert_pass(): lax.all_to_all(slot_grid, 'expert', split_axis=0, concat_axis=0, tiled=True)]
    ppermute x5 -> x16, starting transfers between devices: 41.3 us -> 75.1 us  [passed_along(): return lax.ppermute(value, axis, pairs)]
    all_gather x2 -> x0, waiting for transfers between devices: 30.8 us -> none  [expert_pass(): gathered = lax.all_gather(received[None], 'y', axis=0, tiled=True)]
    ppermute x5 -> x16, waiting for transfers between devices: 7.65 us -> 37.5 us  [passed_along(): return lax.ppermute(value, axis, pairs)]
    dot_general x2 -> x8, matrix products: 11.9 us -> 31.5 us  [expert_pass(): jnp.dot(hidden, w_second, preferred_element_type=jnp.float32)]
    ppermute x0 -> x1, starting transfers between devices: none -> 17 us  [on_device(): partner_arrived = lax.ppermute(sent, ('section', 'zh'), crossed)[0]]
    all_to_all x3 -> x4, waiting for transfers between devices: 51.4 us -> 35.4 us  [the longest x2 24.1 us: expert_pass(): lax.all_to_all(slot_grid, 'expert', split_axis=1, concat_axis=1, tiled=True)]
  transfers between devices with their start and end apart: 12 -> 21, of which waited for: 9 -> 9; matrix products, arithmetic and copies ran while one was open for 10% -> 18% of each run, Pallas kernels for 0% -> 0%
where the time goes in v4:
time: 253 us; the launch traced here: 252 us
  starting transfers between devices  132 us (52%)
  waiting for transfers between devices  72.8 us (29%)
  matrix products  35 us (14%)
  local copies, waits for them, and re-layouts  10.2 us (4%)
    ppermute x16, starting transfers between devices, passed_along(): return lax.ppermute(value, axis, pairs)  75.1 us
    ppermute x16, waiting for transfers between devices, passed_along(): return lax.ppermute(value, axis, pairs)  37.5 us
    dot_general x8, matrix products, expert_pass(): jnp.dot(hidden, w_second, preferred_element_type=jnp.float32)  31.5 us
    all_to_all x2, waiting for transfers between devices, expert_pass(): lax.all_to_all(slot_grid, 'expert', split_axis=1, concat_axis=1, tiled=True)  24.1 us
    all_to_all x2, starting transfers between devices, expert_pass(): lax.all_to_all(summed.astype(jnp.bfloat16).reshape(capacity, experts, mod...  23.5 us
    ppermute x1, starting transfers between devices, on_device(): partner_arrived = lax.ppermute(sent, ('section', 'zh'), crossed)[0]  17 us
    all_to_all x2, starting transfers between devices, expert_pass(): lax.all_to_all(slot_grid, 'expert', split_axis=1, concat_axis=1, tiled=True)  16.2 us
    all_to_all x2, waiting for transfers between devices, expert_pass(): lax.all_to_all(summed.astype(jnp.bfloat16).reshape(capacity, experts, mod...  11.3 us
  transfers between devices with their start and end apart: 21, of which 9 were waited for; matrix products, arithmetic and copies ran while one was open for 18% of the time, Pallas kernels for 0%

profile of v4, /device:TPU:1, one launch (start us, length us, event | category | flops | bytes accessed | tf_op | source)
XLA Modules:
  0.0 251.8 jit_solution(7287542065704016377)
XLA Ops:
  0.0 17.0 %collective-permute-start.8 = (bf16[1,16,4096]{2,1,0:T(8,128)(2,1)}, bf16[1,16,4096]{2,1,0:T(8,128)(2,1)S(1)}, u32[]{:S(2)}, u32[]{:S(2)}) collective-permute-start(bf16[1,16,4096]{2,1,0:T(8,128)(2,1)} %param.6), channel_id=1, source_target_pairs={{0,257},{1,256},{256,1},{257,0},{2,259},{3,258},{258,3},{259,2},{4... | collective-permute-start | bytes 393224 | tf_op jit(solution)/shard_map/ppermute | solution.py:95
  18.9 3.9 %collective-permute-start.7 = (s32[16,2]{0,1:T(2,128)}, s32[16,2]{0,1:T(2,128)S(1)}, u32[]{:S(2)}, u32[]{:S(2)}) collective-permute-start(s32[16,2]{0,1:T(2,128)} %bitcast.192), channel_id=1, source_target_pairs={{0,1},{1,0},{2,3},{3,2},{4,5},{5,4},{6,7},{7,6},{8,9},{9,8},{10,11... | collective-permute-start | bytes 392 | tf_op jit(solution)/shard_map/ppermute | solution.py:11
  23.9 8.4 %collective-permute-done.7 = s32[16,2]{0,1:T(2,128)S(1)} collective-permute-done((s32[16,2]{0,1:T(2,128)}, s32[16,2]{0,1:T(2,128)S(1)}, u32[]{:S(2)}, u32[]{:S(2)}) %collective-permute-start.7) | collective-permute-done | bytes 160 | tf_op jit(solution)/shard_map/ppermute | solution.py:11
  36.9 7.6 %all-to-all-start.2 = ((bf16[2,32,4096]{2,0,1:T(2,128)(2,1)}), bf16[2,32,4096]{2,0,1:T(2,128)(2,1)S(1)}, u32[]{:S(2)}, u32[]{:S(2)}) async-start(bf16[2,32,4096]{2,0,1:T(2,128)(2,1)} %copy.50), calls=%async_computation.2 | async-start | bytes 1048576 | tf_op jit(solution)/shard_map/all_to_all | solution.py:59
  47.2 24.1 %all-to-all-done.2 = bf16[2,32,4096]{2,0,1:T(2,128)(2,1)S(1)} async-done(((bf16[2,32,4096]{2,0,1:T(2,128)(2,1)}), bf16[2,32,4096]{2,0,1:T(2,128)(2,1)S(1)}, u32[]{:S(2)}, u32[]{:S(2)}) %all-to-all-start.2) | async-done | bytes 524320 | tf_op jit(solution)/shard_map/all_to_all | solution.py:59
  71.2 8.7 %all-to-all-start = ((bf16[2,32,4096]{2,0,1:T(2,128)(2,1)}), bf16[2,32,4096]{2,0,1:T(2,128)(2,1)S(1)}, u32[]{:S(2)}, u32[]{:S(2)}) async-start(bf16[2,32,4096]{2,0,1:T(2,128)(2,1)} %copy.43), calls=%async_computation | async-start | bytes 1048576 | tf_op jit(solution)/shard_map/all_to_all | solution.py:59
  84.2 4.5 %collective-permute-start.11 = (bf16[2,32,4096]{2,1,0:T(8,128)(2,1)}, bf16[2,32,4096]{2,1,0:T(8,128)(2,1)}, u32[]{:S(2)}, u32[]{:S(2)}) collective-permute-start(bf16[2,32,4096]{2,1,0:T(8,128)(2,1)} %copy.51), channel_id=1, source_target_pairs={{0,4},{2,6},{4,0},{6,2},{1,5},{3,7},{5,1},{7,3},{8,12},{10,14},{12... | collective-permute-start | bytes 1572872 | tf_op jit(solution)/shard_map/ppermute | solution.py:11
  91.7 5.0 %collective-permute-done.9 = bf16[2,32,4096]{2,1,0:T(8,128)(2,1)} collective-permute-done((bf16[2,32,4096]{2,1,0:T(8,128)(2,1)}, bf16[2,32,4096]{2,1,0:T(8,128)(2,1)}, u32[]{:S(2)}, u32[]{:S(2)}) %collective-permute-start.9) | collective-permute-done | bytes 524320 | tf_op jit(solution)/shard_map/ppermute | solution.py:11
  96.7 4.0 %convolution_convert_fusion.2 = bf16[64,4096]{1,0:T(8,128)(2,1)} fusion(bf16[1,1,256,4096]{3,2,1,0:T(8,128)(2,1)S(1)} %copy-done, bf16[64,4096]{1,0:T(8,128)(2,1)} %bitcast.29, bf16[1,1,4096,256]{3,2,1,0:T(8,128)(2,1)} %param.9), kind=kOutput, calls=%fused_computation.2 | convolution fusion | flops 268845056 | bytes 5242880 | tf_op jit(solution)/shard_map/dot_general | solution.py:66
  104.0 5.1 %collective-permute-done.11 = bf16[2,32,4096]{2,1,0:T(8,128)(2,1)} collective-permute-done((bf16[2,32,4096]{2,1,0:T(8,128)(2,1)}, bf16[2,32,4096]{2,1,0:T(8,128)(2,1)}, u32[]{:S(2)}, u32[]{:S(2)}) %collective-permute-start.11) | collective-permute-done | bytes 524320 | tf_op jit(solution)/shard_map/ppermute | solution.py:11
  109.0 4.0 %convolution_convert_fusion.1 = bf16[64,4096]{1,0:T(8,128)(2,1)} fusion(bf16[1,1,256,4096]{3,2,1,0:T(8,128)(2,1)S(1)} %copy-done, bf16[64,4096]{1,0:T(8,128)(2,1)} %bitcast.30, bf16[1,1,4096,256]{3,2,1,0:T(8,128)(2,1)} %param.9), kind=kOutput, calls=%fused_computation.1 | convolution fusion | flops 268845056 | bytes 5242880 | tf_op jit(solution)/shard_map/dot_general | solution.py:66
  121.4 4.1 %collective-permute-start.1 = (bf16[2,32,4096]{2,1,0:T(8,128)(2,1)S(1)}, bf16[2,32,4096]{2,1,0:T(8,128)(2,1)}, u32[]{:S(2)}, u32[]{:S(2)}) collective-permute-start(bf16[2,32,4096]{2,1,0:T(8,128)(2,1)S(1)} %copy.44), channel_id=1, source_target_pairs={{0,2},{2,4},{4,6},{6,0},{1,3},{3,5},{5,7},{7,1},{8,10},{10,12},{12... | collective-permute-start | bytes 1572872 | tf_op jit(solution)/shard_map/ppermute | solution.py:11
  129.1 8.6 %collective-permute-done.14 = bf16[64,4096]{1,0:T(8,128)(2,1)} collective-permute-done((bf16[64,4096]{1,0:T(8,128)(2,1)}, bf16[64,4096]{1,0:T(8,128)(2,1)}, u32[]{:S(2)}, u32[]{:S(2)}) %collective-permute-start.14) | collective-permute-done | bytes 524320 | tf_op jit(solution)/shard_map/ppermute | solution.py:11
  142.5 11.5 %all-to-all-start.3 = ((bf16[2,32,4096]{2,0,1:T(2,128)(2,1)}), bf16[2,32,4096]{2,0,1:T(2,128)(2,1)S(1)}, u32[]{:S(2)}, u32[]{:S(2)}) async-start(bf16[2,32,4096]{2,0,1:T(2,128)(2,1)} %copy.55), calls=%async_computation.3 | async-start | bytes 1048576 | tf_op jit(solution)/shard_map/all_to_all | solution.py:71
  155.9 4.0 %convolution_convert_fusion.7 = bf16[64,4096]{1,0:T(8,128)(2,1)} fusion(bf16[1,1,256,4096]{3,2,1,0:T(8,128)(2,1)S(1)} %copy-done, bf16[64,4096]{1,0:T(8,128)(2,1)} %bitcast.14, bf16[1,1,4096,256]{3,2,1,0:T(8,128)(2,1)} %param.9), kind=kOutput, calls=%fused_computation.8 | convolution fusion | flops 268845056 | bytes 5242880 | tf_op jit(solution)/shard_map/dot_general | solution.py:66
  161.8 4.0 %convolution_convert_fusion.6 = bf16[64,4096]{1,0:T(8,128)(2,1)} fusion(bf16[1,1,256,4096]{3,2,1,0:T(8,128)(2,1)S(1)} %copy-done, bf16[64,4096]{1,0:T(8,128)(2,1)} %bitcast.15, bf16[1,1,4096,256]{3,2,1,0:T(8,128)(2,1)} %param.9), kind=kOutput, calls=%fused_computation.7 | convolution fusion | flops 268845056 | bytes 5242880 | tf_op jit(solution)/shard_map/dot_general | solution.py:66
  165.8 5.3 %collective-permute-start.4 = (bf16[64,4096]{1,0:T(8,128)(2,1)}, bf16[64,4096]{1,0:T(8,128)(2,1)}, u32[]{:S(2)}, u32[]{:S(2)}) collective-permute-start(bf16[64,4096]{1,0:T(8,128)(2,1)} %convolution_convert_fusion.6), channel_id=1, source_target_pairs={{0,4},{2,6},{4,0},{6,2},{1,5},{3,7},{5,1},{7,3},{8,12},{10,14},{12... | collective-permute-start | bytes 1572872 | tf_op jit(solution)/shard_map/ppermute | solution.py:11
  171.1 4.0 %convolution_convert_fusion.5 = bf16[64,4096]{1,0:T(8,128)(2,1)} fusion(bf16[1,1,256,4096]{3,2,1,0:T(8,128)(2,1)S(1)} %copy-done, bf16[64,4096]{1,0:T(8,128)(2,1)} %bitcast.16, bf16[1,1,4096,256]{3,2,1,0:T(8,128)(2,1)} %param.9), kind=kOutput, calls=%fused_computation.6 | convolution fusion | flops 268845056 | bytes 5242880 | tf_op jit(solution)/shard_map/dot_general | solution.py:66
  178.0 8.6 %collective-permute-done.6 = bf16[64,4096]{1,0:T(8,128)(2,1)} collective-permute-done((bf16[64,4096]{1,0:T(8,128)(2,1)}, bf16[64,4096]{1,0:T(8,128)(2,1)}, u32[]{:S(2)}, u32[]{:S(2)}) %collective-permute-start.6) | collective-permute-done | bytes 524320 | tf_op jit(solution)/shard_map/ppermute | solution.py:11
  186.6 4.2 %add_convert_fusion.1 = bf16[64,4096]{1,0:T(8,128)(2,1)} fusion(bf16[64,4096]{1,0:T(8,128)(2,1)} %collective-permute-done.6, bf16[64,4096]{1,0:T(8,128)(2,1)} %collective-permute-done.4, bf16[64,4096]{1,0:T(8,128)(2,1)} %collective-permute-done.2, bf16[1,1,256,4096]{3,2,1,0:T(8,128)(2,1)S(1)} %copy-done, bf16[64,4096]{1,0:T(8,128)(2,1)S(1)} %bitcast.184, ...), kind=kOutput, calls=%fused_computation.42 | convolution fusion | flops 270942208 | bytes 6815744 | tf_op jit(solution)/shard_map/dot_general | solution.py:66
  193.2 12.0 %all-to-all-start.1 = ((bf16[2,32,4096]{2,0,1:T(2,128)(2,1)}), bf16[2,32,4096]{2,0,1:T(2,128)(2,1)S(1)}, u32[]{:S(2)}, u32[]{:S(2)}) async-start(bf16[2,32,4096]{2,0,1:T(2,128)(2,1)} %copy.48), calls=%async_computation.1 | async-start | bytes 1048576 | tf_op jit(solution)/shard_map/all_to_all | solution.py:71
  205.8 9.1 %collective-permute-start.15 = (bf16[16,4096]{1,0:T(8,128)(2,1)S(1)}, bf16[16,4096]{1,0:T(8,128)(2,1)S(1)}, u32[]{:S(2)}, u32[]{:S(2)}) collective-permute-start(bf16[16,4096]{1,0:T(8,128)(2,1)S(1)} %convolution_convert_fusion.10), channel_id=1, source_target_pairs={{0,1},{1,0},{2,3},{3,2},{4,5},{5,4},{6,7},{7,6},{8,9},{9,8},{10,11... | collective-permute-start | bytes 393224 | tf_op jit(solution)/shard_map/ppermute | solution.py:11
  214.9 11.3 %all-to-all-done.1 = bf16[2,32,4096]{2,0,1:T(2,128)(2,1)S(1)} async-done(((bf16[2,32,4096]{2,0,1:T(2,128)(2,1)}), bf16[2,32,4096]{2,0,1:T(2,128)(2,1)S(1)}, u32[]{:S(2)}, u32[]{:S(2)}) %all-to-all-start.1) | async-done | bytes 524320 | tf_op jit(solution)/shard_map/all_to_all | solution.py:71
  226.9 23.3 %collective-permute-start.16 = (bf16[1,16,4096]{2,1,0:T(8,128)(2,1)S(1)}, bf16[1,16,4096]{2,1,0:T(8,128)(2,1)S(1)}, u32[]{:S(2)}, u32[]{:S(2)}) collective-permute-start(bf16[1,16,4096]{2,1,0:T(8,128)(2,1)S(1)} %fusion.4), channel_id=1, source_target_pairs={{0,256},{256,0},{1,257},{257,1},{2,258},{258,2},{3,259},{259,3},{4... | collective-permute-start | bytes 393224 | tf_op jit(solution)/shard_map/ppermute | solution.py:11
  (79 shorter events, 49.4 us)
Async XLA Ops:
  0.0 96.7 %copy-start = (bf16[1,1,256,4096]{3,2,1,0:T(8,128)(2,1)S(1)}, bf16[1,1,256,4096]{3,2,1,0:T(8,128)(2,1)}, u32[]{:S(2)}) copy-start(bf16[1,1,256,4096]{3,2,1,0:T(8,128)(2,1)} %param.10) | copy-start | bytes 6291460
  0.0 44.9 %copy-start.2 = (f32[1,4096]{1,0:T(1,128)S(1)}, f32[1,4096]{1,0:T(1,128)}, u32[]{:S(2)}) copy-start(f32[1,4096]{1,0:T(1,128)} %param.7) | copy-start | bytes 49156
  0.0 44.9 %copy-start.1 = (bf16[1,4096,32]{1,2,0:T(8,128)(2,1)S(1)}, bf16[1,4096,32]{1,2,0:T(8,128)(2,1)}, u32[]{:S(2)}) copy-start(bf16[1,4096,32]{1,2,0:T(8,128)(2,1)} %param.8) | copy-start | bytes 786436
  0.0 32.8 %collective-permute-start.8 = (bf16[1,16,4096]{2,1,0:T(8,128)(2,1)}, bf16[1,16,4096]{2,1,0:T(8,128)(2,1)S(1)}, u32[]{:S(2)}, u32[]{:S(2)}) collective-permute-start(bf16[1,16,4096]{2,1,0:T(8,128)(2,1)} %param.6), channel_id=1, source_target_pairs={{0,257},{1,256},{256,1},{257,0},{2,259},{3,258},{258,3},{259,2},{4... | collective-permute-start | bytes 393224 | tf_op jit(solution)/shard_map/ppermute | solution.py:95
  17.0 27.8 %collective-permute-start = (bf16[1,16,4096]{2,1,0:T(8,128)(2,1)}, bf16[1,16,4096]{2,1,0:T(8,128)(2,1)S(1)}, u32[]{:S(2)}, u32[]{:S(2)}) collective-permute-start(bf16[1,16,4096]{2,1,0:T(8,128)(2,1)} %param.6), channel_id=1, source_target_pairs={{0,256},{256,0},{1,257},{257,1},{2,258},{258,2},{3,259},{259,3},{4... | collective-permute-start | bytes 393224 | tf_op jit(solution)/shard_map/ppermute | solution.py:11
  18.9 13.3 %collective-permute-start.7 = (s32[16,2]{0,1:T(2,128)}, s32[16,2]{0,1:T(2,128)S(1)}, u32[]{:S(2)}, u32[]{:S(2)}) collective-permute-start(s32[16,2]{0,1:T(2,128)} %bitcast.192), channel_id=1, source_target_pairs={{0,1},{1,0},{2,3},{3,2},{4,5},{5,4},{6,7},{7,6},{8,9},{9,8},{10,11... | collective-permute-start | bytes 392 | tf_op jit(solution)/shard_map/ppermute | solution.py:11
  36.9 34.3 %all-to-all-start.2 = ((bf16[2,32,4096]{2,0,1:T(2,128)(2,1)}), bf16[2,32,4096]{2,0,1:T(2,128)(2,1)S(1)}, u32[]{:S(2)}, u32[]{:S(2)}) async-start(bf16[2,32,4096]{2,0,1:T(2,128)(2,1)} %copy.50), calls=%async_computation.2 | async-start | bytes 1048576 | tf_op jit(solution)/shard_map/all_to_all | solution.py:59
  71.2 49.8 %all-to-all-start = ((bf16[2,32,4096]{2,0,1:T(2,128)(2,1)}), bf16[2,32,4096]{2,0,1:T(2,128)(2,1)S(1)}, u32[]{:S(2)}, u32[]{:S(2)}) async-start(bf16[2,32,4096]{2,0,1:T(2,128)(2,1)} %copy.43), calls=%async_computation | async-start | bytes 1048576 | tf_op jit(solution)/shard_map/all_to_all | solution.py:59
  81.0 15.7 %collective-permute-start.9 = (bf16[2,32,4096]{2,1,0:T(8,128)(2,1)}, bf16[2,32,4096]{2,1,0:T(8,128)(2,1)}, u32[]{:S(2)}, u32[]{:S(2)}) collective-permute-start(bf16[2,32,4096]{2,1,0:T(8,128)(2,1)} %copy.51), channel_id=1, source_target_pairs={{0,2},{2,4},{4,6},{6,0},{1,3},{3,5},{5,7},{7,1},{8,10},{10,12},{12... | collective-permute-start | bytes 1572872 | tf_op jit(solution)/shard_map/ppermute | solution.py:11
  84.2 24.8 %collective-permute-start.11 = (bf16[2,32,4096]{2,1,0:T(8,128)(2,1)}, bf16[2,32,4096]{2,1,0:T(8,128)(2,1)}, u32[]{:S(2)}, u32[]{:S(2)}) collective-permute-start(bf16[2,32,4096]{2,1,0:T(8,128)(2,1)} %copy.51), channel_id=1, source_target_pairs={{0,4},{2,6},{4,0},{6,2},{1,5},{3,7},{5,1},{7,3},{8,12},{10,14},{12... | collective-permute-start | bytes 1572872 | tf_op jit(solution)/shard_map/ppermute | solution.py:11
  88.7 26.6 %collective-permute-start.13 = (bf16[2,32,4096]{2,1,0:T(8,128)(2,1)}, bf16[2,32,4096]{2,1,0:T(8,128)(2,1)S(1)}, u32[]{:S(2)}, u32[]{:S(2)}) collective-permute-start(bf16[2,32,4096]{2,1,0:T(8,128)(2,1)} %copy.51), channel_id=1, source_target_pairs={{0,6},{2,0},{4,2},{6,4},{1,7},{3,1},{5,3},{7,5},{8,14},{10,8},{12,... | collective-permute-start | bytes 1572872 | tf_op jit(solution)/shard_map/ppermute | solution.py:11
  100.7 28.4 %collective-permute-start.10 = (bf16[64,4096]{1,0:T(8,128)(2,1)}, bf16[64,4096]{1,0:T(8,128)(2,1)}, u32[]{:S(2)}, u32[]{:S(2)}) collective-permute-start(bf16[64,4096]{1,0:T(8,128)(2,1)} %convolution_convert_fusion.2), channel_id=1, source_target_pairs={{0,6},{2,0},{4,2},{6,4},{1,7},{3,1},{5,3},{7,5},{8,14},{10,8},{12,... | collective-permute-start | bytes 1572872 | tf_op jit(solution)/shard_map/ppermute | solution.py:11
  113.0 16.0 %collective-permute-start.12 = (bf16[64,4096]{1,0:T(8,128)(2,1)}, bf16[64,4096]{1,0:T(8,128)(2,1)}, u32[]{:S(2)}, u32[]{:S(2)}) collective-permute-start(bf16[64,4096]{1,0:T(8,128)(2,1)} %convolution_convert_fusion.1), channel_id=1, source_target_pairs={{0,4},{2,6},{4,0},{6,2},{1,5},{3,7},{5,1},{7,3},{8,12},{10,14},{12... | collective-permute-start | bytes 1572872 | tf_op jit(solution)/shard_map/ppermute | solution.py:11
  119.1 18.5 %collective-permute-start.14 = (bf16[64,4096]{1,0:T(8,128)(2,1)}, bf16[64,4096]{1,0:T(8,128)(2,1)}, u32[]{:S(2)}, u32[]{:S(2)}) collective-permute-start(bf16[64,4096]{1,0:T(8,128)(2,1)} %convolution_convert_fusion), channel_id=1, source_target_pairs={{0,2},{2,4},{4,6},{6,0},{1,3},{3,5},{5,7},{7,1},{8,10},{10,12},{12... | collective-permute-start | bytes 1572872 | tf_op jit(solution)/shard_map/ppermute | solution.py:11
  121.4 34.6 %collective-permute-start.1 = (bf16[2,32,4096]{2,1,0:T(8,128)(2,1)S(1)}, bf16[2,32,4096]{2,1,0:T(8,128)(2,1)}, u32[]{:S(2)}, u32[]{:S(2)}) collective-permute-start(bf16[2,32,4096]{2,1,0:T(8,128)(2,1)S(1)} %copy.44), channel_id=1, source_target_pairs={{0,2},{2,4},{4,6},{6,0},{1,3},{3,5},{5,7},{7,1},{8,10},{10,12},{12... | collective-permute-start | bytes 1572872 | tf_op jit(solution)/shard_map/ppermute | solution.py:11
  125.5 36.3 %collective-permute-start.3 = (bf16[2,32,4096]{2,1,0:T(8,128)(2,1)S(1)}, bf16[2,32,4096]{2,1,0:T(8,128)(2,1)}, u32[]{:S(2)}, u32[]{:S(2)}) collective-permute-start(bf16[2,32,4096]{2,1,0:T(8,128)(2,1)S(1)} %copy.44), channel_id=1, source_target_pairs={{0,4},{2,6},{4,0},{6,2},{1,5},{3,7},{5,1},{7,3},{8,12},{10,14},{12... | collective-permute-start | bytes 1572872 | tf_op jit(solution)/shard_map/ppermute | solution.py:11
  142.5 50.6 %all-to-all-start.3 = ((bf16[2,32,4096]{2,0,1:T(2,128)(2,1)}), bf16[2,32,4096]{2,0,1:T(2,128)(2,1)S(1)}, u32[]{:S(2)}, u32[]{:S(2)}) async-start(bf16[2,32,4096]{2,0,1:T(2,128)(2,1)} %copy.55), calls=%async_computation.3 | async-start | bytes 1048576 | tf_op jit(solution)/shard_map/all_to_all | solution.py:71
  154.0 17.1 %collective-permute-start.5 = (bf16[2,32,4096]{2,1,0:T(8,128)(2,1)S(1)}, bf16[2,32,4096]{2,1,0:T(8,128)(2,1)}, u32[]{:S(2)}, u32[]{:S(2)}) collective-permute-start(bf16[2,32,4096]{2,1,0:T(8,128)(2,1)S(1)} %copy.44), channel_id=1, source_target_pairs={{0,6},{2,0},{4,2},{6,4},{1,7},{3,1},{5,3},{7,5},{8,14},{10,8},{12,... | collective-permute-start | bytes 1572872 | tf_op jit(solution)/shard_map/ppermute | solution.py:11
  159.9 17.1 %collective-permute-start.2 = (bf16[64,4096]{1,0:T(8,128)(2,1)}, bf16[64,4096]{1,0:T(8,128)(2,1)}, u32[]{:S(2)}, u32[]{:S(2)}) collective-permute-start(bf16[64,4096]{1,0:T(8,128)(2,1)} %convolution_convert_fusion.7), channel_id=1, source_target_pairs={{0,6},{2,0},{4,2},{6,4},{1,7},{3,1},{5,3},{7,5},{8,14},{10,8},{12,... | collective-permute-start | bytes 1572872 | tf_op jit(solution)/shard_map/ppermute | solution.py:11
  165.8 12.2 %collective-permute-start.4 = (bf16[64,4096]{1,0:T(8,128)(2,1)}, bf16[64,4096]{1,0:T(8,128)(2,1)}, u32[]{:S(2)}, u32[]{:S(2)}) collective-permute-start(bf16[64,4096]{1,0:T(8,128)(2,1)} %convolution_convert_fusion.6), channel_id=1, source_target_pairs={{0,4},{2,6},{4,0},{6,2},{1,5},{3,7},{5,1},{7,3},{8,12},{10,14},{12... | collective-permute-start | bytes 1572872 | tf_op jit(solution)/shard_map/ppermute | solution.py:11
  175.1 11.4 %collective-permute-start.6 = (bf16[64,4096]{1,0:T(8,128)(2,1)}, bf16[64,4096]{1,0:T(8,128)(2,1)}, u32[]{:S(2)}, u32[]{:S(2)}) collective-permute-start(bf16[64,4096]{1,0:T(8,128)(2,1)} %convolution_convert_fusion.5), channel_id=1, source_target_pairs={{0,2},{2,4},{4,6},{6,0},{1,3},{3,5},{5,7},{7,1},{8,10},{10,12},{12... | collective-permute-start | bytes 1572872 | tf_op jit(solution)/shard_map/ppermute | solution.py:11
  193.2 33.0 %all-to-all-start.1 = ((bf16[2,32,4096]{2,0,1:T(2,128)(2,1)}), bf16[2,32,4096]{2,0,1:T(2,128)(2,1)S(1)}, u32[]{:S(2)}, u32[]{:S(2)}) async-start(bf16[2,32,4096]{2,0,1:T(2,128)(2,1)} %copy.48), calls=%async_computation.1 | async-start | bytes 1048576 | tf_op jit(solution)/shard_map/all_to_all | solution.py:71
  205.8 20.7 %collective-permute-start.15 = (bf16[16,4096]{1,0:T(8,128)(2,1)S(1)}, bf16[16,4096]{1,0:T(8,128)(2,1)S(1)}, u32[]{:S(2)}, u32[]{:S(2)}) collective-permute-start(bf16[16,4096]{1,0:T(8,128)(2,1)S(1)} %convolution_convert_fusion.10), channel_id=1, source_target_pairs={{0,1},{1,0},{2,3},{3,2},{4,5},{5,4},{6,7},{7,6},{8,9},{9,8},{10,11... | collective-permute-start | bytes 393224 | tf_op jit(solution)/shard_map/ppermute | solution.py:11
  226.9 24.2 %collective-permute-start.16 = (bf16[1,16,4096]{2,1,0:T(8,128)(2,1)S(1)}, bf16[1,16,4096]{2,1,0:T(8,128)(2,1)S(1)}, u32[]{:S(2)}, u32[]{:S(2)}) collective-permute-start(bf16[1,16,4096]{2,1,0:T(8,128)(2,1)S(1)} %fusion.4), channel_id=1, source_target_pairs={{0,256},{256,0},{1,257},{257,1},{2,258},{258,2},{3,259},{259,3},{4... | collective-permute-start | bytes 393224 | tf_op jit(solution)/shard_map/ppermute | solution.py:11
  (1 other events, 44.7 us)

commit v5 on v4

--- a/solution.py
+++ b/solution.py
@@ -57,17 +57,15 @@
     capacity, experts, model_width = slot_grid.shape
     n_y = lax.axis_size("y")
     received = lax.all_to_all(slot_grid, "expert", split_axis=1, concat_axis=1, tiled=True)
-    summed = None
-    for k in range(n_y):
-        rows_in = received if k == 0 else passed_along(received, "y", k)
-        hidden = jax.nn.gelu(
-            jnp.dot(rows_in.reshape(-1, model_width), w_first, preferred_element_type=jnp.float32)
-        ).astype(jnp.bfloat16)
-        partial = jnp.dot(hidden, w_second, preferred_element_type=jnp.float32).astype(jnp.bfloat16)
-        if k == 0:
-            summed = partial.astype(jnp.float32)
-        else:
-            summed = summed + passed_along(partial, "y", n_y - k).astype(jnp.float32)
+    copies = jnp.broadcast_to(received[None], (n_y,) + received.shape)
+    rows_in = lax.all_to_all(copies, "y", split_axis=0, concat_axis=0, tiled=True)
+    hidden = jax.nn.gelu(
+        jnp.dot(rows_in.reshape(-1, model_width), w_first, preferred_element_type=jnp.float32)
+    ).astype(jnp.bfloat16)
+    partial = jnp.dot(hidden, w_second, preferred_element_type=jnp.float32).astype(jnp.bfloat16)
+    partial = partial.reshape(n_y, capacity * experts, model_width)
+    parts = lax.all_to_all(partial, "y", split_axis=0, concat_axis=0, tiled=True)
+    summed = jnp.sum(parts.astype(jnp.float32), axis=0)
     back = lax.all_to_all(
         summed.astype(jnp.bfloat16).reshape(capacity, experts, model_width),
         "expert", split_axis=1, concat_axis=1, tiled=True,

time: 253 us -> 315 us (1.25)
  waiting for transfers between devices: 72.8 us -> 173 us
  starting transfers between devices: 132 us -> 107 us
  matrix products: 35 us -> 15.4 us
  other arithmetic: 1.56 us -> 5.51 us
    all_to_all x0 -> x4, waiting for transfers between devices: none -> 67.8 us  [the longest x2 37 us: expert_pass(): lax.all_to_all(copies, 'y', split_axis=0, concat_axis=0, tiled=True)]
    ppermute x16 -> x4, starting transfers between devices: 75.1 us -> 22 us  [passed_along(): return lax.ppermute(value, axis, pairs)]
    all_to_all x2, waiting for transfers between devices: 11.3 us -> 45.8 us  [expert_pass(): lax.all_to_all(summed.astype(jnp.bfloat16).reshape(capacity, experts, mod...]
    ppermute x16 -> x4, waiting for transfers between devices: 37.5 us -> 9.34 us  [passed_along(): return lax.ppermute(value, axis, pairs)]
    all_to_all x2, waiting for transfers between devices: 24.1 us -> 50.5 us  [expert_pass(): lax.all_to_all(slot_grid, 'expert', split_axis=1, concat_axis=1, tiled=True)]
    dot_general x8 -> x2, matrix products: 31.5 us -> 11.9 us  [expert_pass(): jnp.dot(hidden, w_second, preferred_element_type=jnp.float32)]
    all_to_all x0 -> x4, starting transfers between devices: none -> 17.8 us  [the longest x2 8.9 us: expert_pass(): lax.all_to_all(partial, 'y', split_axis=0, concat_axis=0, tiled=True)]
    all_to_all x2, starting transfers between devices: 23.5 us -> 33.6 us  [expert_pass(): lax.all_to_all(summed.astype(jnp.bfloat16).reshape(capacity, experts, mod...]
  transfers between devices with their start and end apart: 21 -> 13, of which waited for: 9 -> 10; matrix products, arithmetic and copies ran while one was open for 18% -> 9% of each run, Pallas kernels for 0% -> 0%
where the time goes in v5:
time: 315 us; the launch traced here: 314 us
  waiting for transfers between devices  173 us (55%)
  starting transfers between devices  107 us (34%)
  matrix products  15.4 us (5%)
  local copies, waits for them, and re-layouts  12.6 us (4%)
  other arithmetic  5.51 us (2%)
    all_to_all x2, waiting for transfers between devices, expert_pass(): lax.all_to_all(slot_grid, 'expert', split_axis=1, concat_axis=1, tiled=True)  50.5 us
    all_to_all x2, waiting for transfers between devices, expert_pass(): lax.all_to_all(summed.astype(jnp.bfloat16).reshape(capacity, experts, mod...  45.8 us
    all_to_all x2, waiting for transfers between devices, expert_pass(): lax.all_to_all(copies, 'y', split_axis=0, concat_axis=0, tiled=True)  37 us
    all_to_all x2, starting transfers between devices, expert_pass(): lax.all_to_all(summed.astype(jnp.bfloat16).reshape(capacity, experts, mod...  33.6 us
    all_to_all x2, waiting for transfers between devices, expert_pass(): lax.all_to_all(partial, 'y', split_axis=0, concat_axis=0, tiled=True)  30.8 us
    ppermute x4, starting transfers between devices, passed_along(): return lax.ppermute(value, axis, pairs)  22 us
    ppermute x1, starting transfers between devices, on_device(): partner_arrived = lax.ppermute(sent, ('section', 'zh'), crossed)[0]  17 us
    all_to_all x2, starting transfers between devices, expert_pass(): lax.all_to_all(slot_grid, 'expert', split_axis=1, concat_axis=1, tiled=True)  16.4 us
  transfers between devices with their start and end apart: 13, of which 10 were waited for; matrix products, arithmetic and copies ran while one was open for 9% of the time, Pallas kernels for 0%

profile of v5, /device:TPU:1, one launch (start us, length us, event | category | flops | bytes accessed | tf_op | source)
XLA Modules:
  0.0 313.9 jit_solution(7121927325626330771)
XLA Ops:
  0.0 17.0 %collective-permute-start.2 = (bf16[1,16,4096]{2,1,0:T(8,128)(2,1)}, bf16[1,16,4096]{2,1,0:T(8,128)(2,1)S(1)}, u32[]{:S(2)}, u32[]{:S(2)}) collective-permute-start(bf16[1,16,4096]{2,1,0:T(8,128)(2,1)} %param.6), channel_id=1, source_target_pairs={{0,257},{1,256},{256,1},{257,0},{2,259},{3,258},{258,3},{259,2},{4... | collective-permute-start | bytes 393224 | tf_op jit(solution)/shard_map/ppermute | solution.py:93
  18.9 3.9 %collective-permute-start.1 = (s32[16,2]{0,1:T(2,128)}, s32[16,2]{0,1:T(2,128)S(1)}, u32[]{:S(2)}, u32[]{:S(2)}) collective-permute-start(s32[16,2]{0,1:T(2,128)} %bitcast.114), channel_id=1, source_target_pairs={{0,1},{1,0},{2,3},{3,2},{4,5},{5,4},{6,7},{7,6},{8,9},{9,8},{10,11... | collective-permute-start | bytes 392 | tf_op jit(solution)/shard_map/ppermute | solution.py:11
  23.9 8.4 %collective-permute-done.1 = s32[16,2]{0,1:T(2,128)S(1)} collective-permute-done((s32[16,2]{0,1:T(2,128)}, s32[16,2]{0,1:T(2,128)S(1)}, u32[]{:S(2)}, u32[]{:S(2)}) %collective-permute-start.1) | collective-permute-done | bytes 160 | tf_op jit(solution)/shard_map/ppermute | solution.py:11
  37.0 7.6 %all-to-all-start.4 = ((bf16[2,32,4096]{2,0,1:T(2,128)(2,1)}), bf16[2,32,4096]{2,0,1:T(2,128)(2,1)S(1)}, u32[]{:S(2)}, u32[]{:S(2)}) async-start(bf16[2,32,4096]{2,0,1:T(2,128)(2,1)} %copy.41), calls=%async_computation.4 | async-start | bytes 1048576 | tf_op jit(solution)/shard_map/all_to_all | solution.py:59
  47.2 24.1 %all-to-all-done.4 = bf16[2,32,4096]{2,0,1:T(2,128)(2,1)S(1)} async-done(((bf16[2,32,4096]{2,0,1:T(2,128)(2,1)}), bf16[2,32,4096]{2,0,1:T(2,128)(2,1)S(1)}, u32[]{:S(2)}, u32[]{:S(2)}) %all-to-all-start.4) | async-done | bytes 524320 | tf_op jit(solution)/shard_map/all_to_all | solution.py:59
  71.3 8.8 %all-to-all-start = ((bf16[2,32,4096]{2,0,1:T(2,128)(2,1)}), bf16[2,32,4096]{2,0,1:T(2,128)(2,1)}, u32[]{:S(2)}, u32[]{:S(2)}) async-start(bf16[2,32,4096]{2,0,1:T(2,128)(2,1)} %copy.37), calls=%async_computation | async-start | bytes 1048576 | tf_op jit(solution)/shard_map/all_to_all | solution.py:59
  80.4 26.4 %all-to-all-done = bf16[2,32,4096]{2,0,1:T(2,128)(2,1)} async-done(((bf16[2,32,4096]{2,0,1:T(2,128)(2,1)}), bf16[2,32,4096]{2,0,1:T(2,128)(2,1)}, u32[]{:S(2)}, u32[]{:S(2)}) %all-to-all-start) | async-done | bytes 524320 | tf_op jit(solution)/shard_map/all_to_all | solution.py:59
  108.4 4.4 %all-to-all-start.5 = ((bf16[4,2,32,4096]{3,2,1,0:T(8,128)(2,1)}), bf16[4,2,32,4096]{3,2,1,0:T(8,128)(2,1)}, u32[]{:S(2)}, u32[]{:S(2)}) async-start(bf16[4,2,32,4096]{3,2,1,0:T(8,128)(2,1)} %broadcast_in_dim.7), calls=%async_computation.5 | async-start | bytes 4194304 | tf_op jit(solution)/shard_map/all_to_all | solution.py:61
  114.2 21.3 %all-to-all-done.5 = bf16[4,2,32,4096]{3,2,1,0:T(8,128)(2,1)} async-done(((bf16[4,2,32,4096]{3,2,1,0:T(8,128)(2,1)}), bf16[4,2,32,4096]{3,2,1,0:T(8,128)(2,1)}, u32[]{:S(2)}, u32[]{:S(2)}) %all-to-all-start.5) | async-done | bytes 2097184 | tf_op jit(solution)/shard_map/all_to_all | solution.py:61
  137.0 4.4 %all-to-all-start.1 = ((bf16[4,2,32,4096]{3,2,1,0:T(8,128)(2,1)}), bf16[4,2,32,4096]{3,2,1,0:T(8,128)(2,1)}, u32[]{:S(2)}, u32[]{:S(2)}) async-start(bf16[4,2,32,4096]{3,2,1,0:T(8,128)(2,1)} %broadcast_in_dim.6), calls=%async_computation.1 | async-start | bytes 4194304 | tf_op jit(solution)/shard_map/all_to_all | solution.py:61
  141.5 6.0 %convolution_convert_fusion = bf16[256,4096]{1,0:T(8,128)(2,1)} fusion(bf16[1,1,256,4096]{3,2,1,0:T(8,128)(2,1)S(1)} %copy-done, bf16[256,4096]{1,0:T(8,128)(2,1)} %bitcast.26, bf16[1,1,4096,256]{3,2,1,0:T(8,128)(2,1)} %param.9), kind=kOutput, calls=%fused_computation | convolution fusion | flops 1075380224 | bytes 8388608 | tf_op jit(solution)/shard_map/dot_general | solution.py:65
  147.4 15.8 %all-to-all-done.1 = bf16[4,2,32,4096]{3,2,1,0:T(8,128)(2,1)} async-done(((bf16[4,2,32,4096]{3,2,1,0:T(8,128)(2,1)}), bf16[4,2,32,4096]{3,2,1,0:T(8,128)(2,1)}, u32[]{:S(2)}, u32[]{:S(2)}) %all-to-all-start.1) | async-done | bytes 2097184 | tf_op jit(solution)/shard_map/all_to_all | solution.py:61
  163.2 4.5 %all-to-all-start.6 = ((bf16[4,64,4096]{2,1,0:T(8,128)(2,1)}), bf16[4,64,4096]{2,1,0:T(8,128)(2,1)}, u32[]{:S(2)}, u32[]{:S(2)}) async-start(bf16[4,64,4096]{2,1,0:T(8,128)(2,1)} %bitcast.103), calls=%async_computation.6 | async-start | bytes 4194304 | tf_op jit(solution)/shard_map/all_to_all | solution.py:67
  167.7 5.9 %convolution_convert_fusion.1 = bf16[256,4096]{1,0:T(8,128)(2,1)} fusion(bf16[1,1,256,4096]{3,2,1,0:T(8,128)(2,1)S(1)} %copy-done, bf16[256,4096]{1,0:T(8,128)(2,1)} %bitcast.11, bf16[1,1,4096,256]{3,2,1,0:T(8,128)(2,1)} %param.9), kind=kOutput, calls=%fused_computation.1 | convolution fusion | flops 1075380224 | bytes 8388608 | tf_op jit(solution)/shard_map/dot_general | solution.py:65
  173.6 14.7 %all-to-all-done.6 = bf16[4,64,4096]{2,1,0:T(8,128)(2,1)} async-done(((bf16[4,64,4096]{2,1,0:T(8,128)(2,1)}), bf16[4,64,4096]{2,1,0:T(8,128)(2,1)}, u32[]{:S(2)}, u32[]{:S(2)}) %all-to-all-start.6) | async-done | bytes 2097184 | tf_op jit(solution)/shard_map/all_to_all | solution.py:67
  188.2 4.4 %all-to-all-start.2 = ((bf16[4,64,4096]{2,1,0:T(8,128)(2,1)}), bf16[4,64,4096]{2,1,0:T(8,128)(2,1)}, u32[]{:S(2)}, u32[]{:S(2)}) async-start(bf16[4,64,4096]{2,1,0:T(8,128)(2,1)} %bitcast.102), calls=%async_computation.2 | async-start | bytes 4194304 | tf_op jit(solution)/shard_map/all_to_all | solution.py:67
  196.0 16.1 %all-to-all-done.2 = bf16[4,64,4096]{2,1,0:T(8,128)(2,1)} async-done(((bf16[4,64,4096]{2,1,0:T(8,128)(2,1)}), bf16[4,64,4096]{2,1,0:T(8,128)(2,1)}, u32[]{:S(2)}, u32[]{:S(2)}) %all-to-all-start.2) | async-done | bytes 2097184 | tf_op jit(solution)/shard_map/all_to_all | solution.py:67
  212.1 21.9 %all-to-all-start.7 = ((bf16[2,32,4096]{2,0,1:T(2,128)(2,1)}), bf16[2,32,4096]{2,0,1:T(2,128)(2,1)S(1)}, u32[]{:S(2)}, u32[]{:S(2)}) async-start(bf16[2,32,4096]{2,0,1:T(2,128)(2,1)} %copy.43), calls=%async_computation.7 | async-start | bytes 1048576 | tf_op jit(solution)/shard_map/all_to_all | solution.py:69
  234.0 2.0 reduce_sum.138
  237.3 20.1 %all-to-all-done.7 = bf16[2,32,4096]{2,0,1:T(2,128)(2,1)S(1)} async-done(((bf16[2,32,4096]{2,0,1:T(2,128)(2,1)}), bf16[2,32,4096]{2,0,1:T(2,128)(2,1)S(1)}, u32[]{:S(2)}, u32[]{:S(2)}) %all-to-all-start.7) | async-done | bytes 524320 | tf_op jit(solution)/shard_map/all_to_all | solution.py:69
  257.4 11.7 %all-to-all-start.3 = ((bf16[2,32,4096]{2,0,1:T(2,128)(2,1)}), bf16[2,32,4096]{2,0,1:T(2,128)(2,1)S(1)}, u32[]{:S(2)}, u32[]{:S(2)}) async-start(bf16[2,32,4096]{2,0,1:T(2,128)(2,1)} %copy.39), calls=%async_computation.3 | async-start | bytes 1048576 | tf_op jit(solution)/shard_map/all_to_all | solution.py:69
  269.8 8.7 %collective-permute-start.3 = (bf16[16,4096]{1,0:T(8,128)(2,1)S(1)}, bf16[16,4096]{1,0:T(8,128)(2,1)S(1)}, u32[]{:S(2)}, u32[]{:S(2)}) collective-permute-start(bf16[16,4096]{1,0:T(8,128)(2,1)S(1)} %convolution_convert_fusion.4), channel_id=1, source_target_pairs={{0,1},{1,0},{2,3},{3,2},{4,5},{5,4},{6,7},{7,6},{8,9},{9,8},{10,11... | collective-permute-start | bytes 393224 | tf_op jit(solution)/shard_map/ppermute | solution.py:11
  278.5 25.7 %all-to-all-done.3 = bf16[2,32,4096]{2,0,1:T(2,128)(2,1)S(1)} async-done(((bf16[2,32,4096]{2,0,1:T(2,128)(2,1)}), bf16[2,32,4096]{2,0,1:T(2,128)(2,1)S(1)}, u32[]{:S(2)}, u32[]{:S(2)}) %all-to-all-start.3) | async-done | bytes 524320 | tf_op jit(solution)/shard_map/all_to_all | solution.py:69
  304.8 7.5 %collective-permute-start.4 = (bf16[1,16,4096]{2,1,0:T(8,128)(2,1)S(1)}, bf16[1,16,4096]{2,1,0:T(8,128)(2,1)S(1)}, u32[]{:S(2)}, u32[]{:S(2)}) collective-permute-start(bf16[1,16,4096]{2,1,0:T(8,128)(2,1)S(1)} %fusion.2), channel_id=1, source_target_pairs={{0,256},{256,0},{1,257},{257,1},{2,258},{258,2},{3,259},{259,3},{4... | collective-permute-start | bytes 393224 | tf_op jit(solution)/shard_map/ppermute | solution.py:11
  (61 shorter events, 22.5 us)
Async XLA Ops:
  0.0 141.5 %copy-start = (bf16[1,1,256,4096]{3,2,1,0:T(8,128)(2,1)S(1)}, bf16[1,1,256,4096]{3,2,1,0:T(8,128)(2,1)}, u32[]{:S(2)}) copy-start(bf16[1,1,256,4096]{3,2,1,0:T(8,128)(2,1)} %param.10) | copy-start | bytes 6291460
  0.0 44.8 %copy-start.3 = (s32[1,16,2]{1,2,0:T(2,128)S(1)}, s32[1,16,2]{1,2,0:T(2,128)}, u32[]{:S(2)}) copy-start(s32[1,16,2]{1,2,0:T(2,128)} %param.11) | copy-start | bytes 388
  0.0 44.9 %copy-start.2 = (f32[1,4096]{1,0:T(1,128)S(1)}, f32[1,4096]{1,0:T(1,128)}, u32[]{:S(2)}) copy-start(f32[1,4096]{1,0:T(1,128)} %param.7) | copy-start | bytes 49156
  0.0 44.9 %copy-start.1 = (bf16[1,4096,32]{1,2,0:T(8,128)(2,1)S(1)}, bf16[1,4096,32]{1,2,0:T(8,128)(2,1)}, u32[]{:S(2)}) copy-start(bf16[1,4096,32]{1,2,0:T(8,128)(2,1)} %param.8) | copy-start | bytes 786436
  0.0 32.8 %collective-permute-start.2 = (bf16[1,16,4096]{2,1,0:T(8,128)(2,1)}, bf16[1,16,4096]{2,1,0:T(8,128)(2,1)S(1)}, u32[]{:S(2)}, u32[]{:S(2)}) collective-permute-start(bf16[1,16,4096]{2,1,0:T(8,128)(2,1)} %param.6), channel_id=1, source_target_pairs={{0,257},{1,256},{256,1},{257,0},{2,259},{3,258},{258,3},{259,2},{4... | collective-permute-start | bytes 393224 | tf_op jit(solution)/shard_map/ppermute | solution.py:93
  17.0 27.8 %collective-permute-start = (bf16[1,16,4096]{2,1,0:T(8,128)(2,1)}, bf16[1,16,4096]{2,1,0:T(8,128)(2,1)S(1)}, u32[]{:S(2)}, u32[]{:S(2)}) collective-permute-start(bf16[1,16,4096]{2,1,0:T(8,128)(2,1)} %param.6), channel_id=1, source_target_pairs={{0,256},{256,0},{1,257},{257,1},{2,258},{258,2},{3,259},{259,3},{4... | collective-permute-start | bytes 393224 | tf_op jit(solution)/shard_map/ppermute | solution.py:11
  18.9 13.3 %collective-permute-start.1 = (s32[16,2]{0,1:T(2,128)}, s32[16,2]{0,1:T(2,128)S(1)}, u32[]{:S(2)}, u32[]{:S(2)}) collective-permute-start(s32[16,2]{0,1:T(2,128)} %bitcast.114), channel_id=1, source_target_pairs={{0,1},{1,0},{2,3},{3,2},{4,5},{5,4},{6,7},{7,6},{8,9},{9,8},{10,11... | collective-permute-start | bytes 392 | tf_op jit(solution)/shard_map/ppermute | solution.py:11
  37.0 34.3 %all-to-all-start.4 = ((bf16[2,32,4096]{2,0,1:T(2,128)(2,1)}), bf16[2,32,4096]{2,0,1:T(2,128)(2,1)S(1)}, u32[]{:S(2)}, u32[]{:S(2)}) async-start(bf16[2,32,4096]{2,0,1:T(2,128)(2,1)} %copy.41), calls=%async_computation.4 | async-start | bytes 1048576 | tf_op jit(solution)/shard_map/all_to_all | solution.py:59
  71.3 35.5 %all-to-all-start = ((bf16[2,32,4096]{2,0,1:T(2,128)(2,1)}), bf16[2,32,4096]{2,0,1:T(2,128)(2,1)}, u32[]{:S(2)}, u32[]{:S(2)}) async-start(bf16[2,32,4096]{2,0,1:T(2,128)(2,1)} %copy.37), calls=%async_computation | async-start | bytes 1048576 | tf_op jit(solution)/shard_map/all_to_all | solution.py:59
  108.4 27.0 %all-to-all-start.5 = ((bf16[4,2,32,4096]{3,2,1,0:T(8,128)(2,1)}), bf16[4,2,32,4096]{3,2,1,0:T(8,128)(2,1)}, u32[]{:S(2)}, u32[]{:S(2)}) async-start(bf16[4,2,32,4096]{3,2,1,0:T(8,128)(2,1)} %broadcast_in_dim.7), calls=%async_computation.5 | async-start | bytes 4194304 | tf_op jit(solution)/shard_map/all_to_all | solution.py:61
  137.0 26.2 %all-to-all-start.1 = ((bf16[4,2,32,4096]{3,2,1,0:T(8,128)(2,1)}), bf16[4,2,32,4096]{3,2,1,0:T(8,128)(2,1)}, u32[]{:S(2)}, u32[]{:S(2)}) async-start(bf16[4,2,32,4096]{3,2,1,0:T(8,128)(2,1)} %broadcast_in_dim.6), calls=%async_computation.1 | async-start | bytes 4194304 | tf_op jit(solution)/shard_map/all_to_all | solution.py:61
  163.2 25.1 %all-to-all-start.6 = ((bf16[4,64,4096]{2,1,0:T(8,128)(2,1)}), bf16[4,64,4096]{2,1,0:T(8,128)(2,1)}, u32[]{:S(2)}, u32[]{:S(2)}) async-start(bf16[4,64,4096]{2,1,0:T(8,128)(2,1)} %bitcast.103), calls=%async_computation.6 | async-start | bytes 4194304 | tf_op jit(solution)/shard_map/all_to_all | solution.py:67
  188.2 23.9 %all-to-all-start.2 = ((bf16[4,64,4096]{2,1,0:T(8,128)(2,1)}), bf16[4,64,4096]{2,1,0:T(8,128)(2,1)}, u32[]{:S(2)}, u32[]{:S(2)}) async-start(bf16[4,64,4096]{2,1,0:T(8,128)(2,1)} %bitcast.102), calls=%async_computation.2 | async-start | bytes 4194304 | tf_op jit(solution)/shard_map/all_to_all | solution.py:67
  212.1 45.3 %all-to-all-start.7 = ((bf16[2,32,4096]{2,0,1:T(2,128)(2,1)}), bf16[2,32,4096]{2,0,1:T(2,128)(2,1)S(1)}, u32[]{:S(2)}, u32[]{:S(2)}) async-start(bf16[2,32,4096]{2,0,1:T(2,128)(2,1)} %copy.43), calls=%async_computation.7 | async-start | bytes 1048576 | tf_op jit(solution)/shard_map/all_to_all | solution.py:69
  257.4 46.8 %all-to-all-start.3 = ((bf16[2,32,4096]{2,0,1:T(2,128)(2,1)}), bf16[2,32,4096]{2,0,1:T(2,128)(2,1)S(1)}, u32[]{:S(2)}, u32[]{:S(2)}) async-start(bf16[2,32,4096]{2,0,1:T(2,128)(2,1)} %copy.39), calls=%async_computation.3 | async-start | bytes 1048576 | tf_op jit(solution)/shard_map/all_to_all | solution.py:69
  269.8 34.7 %collective-permute-start.3 = (bf16[16,4096]{1,0:T(8,128)(2,1)S(1)}, bf16[16,4096]{1,0:T(8,128)(2,1)S(1)}, u32[]{:S(2)}, u32[]{:S(2)}) collective-permute-start(bf16[16,4096]{1,0:T(8,128)(2,1)S(1)} %convolution_convert_fusion.4), channel_id=1, source_target_pairs={{0,1},{1,0},{2,3},{3,2},{4,5},{5,4},{6,7},{7,6},{8,9},{9,8},{10,11... | collective-permute-start | bytes 393224 | tf_op jit(solution)/shard_map/ppermute | solution.py:11
  304.8 8.4 %collective-permute-start.4 = (bf16[1,16,4096]{2,1,0:T(8,128)(2,1)S(1)}, bf16[1,16,4096]{2,1,0:T(8,128)(2,1)S(1)}, u32[]{:S(2)}, u32[]{:S(2)}) collective-permute-start(bf16[1,16,4096]{2,1,0:T(8,128)(2,1)S(1)} %fusion.2), channel_id=1, source_target_pairs={{0,256},{256,0},{1,257},{257,1},{2,258},{258,2},{3,259},{259,3},{4... | collective-permute-start | bytes 393224 | tf_op jit(solution)/shard_map/ppermute | solution.py:11

commit v6 on v5

--- a/solution.py
+++ b/solution.py
@@ -57,15 +57,17 @@
     capacity, experts, model_width = slot_grid.shape
     n_y = lax.axis_size("y")
     received = lax.all_to_all(slot_grid, "expert", split_axis=1, concat_axis=1, tiled=True)
-    copies = jnp.broadcast_to(received[None], (n_y,) + received.shape)
-    rows_in = lax.all_to_all(copies, "y", split_axis=0, concat_axis=0, tiled=True)
+    gathered = lax.all_gather(received, "y", axis=0, tiled=False)
     hidden = jax.nn.gelu(
-        jnp.dot(rows_in.reshape(-1, model_width), w_first, preferred_element_type=jnp.float32)
+        jnp.dot(gathered.reshape(-1, model_width), w_first, preferred_element_type=jnp.float32)
     ).astype(jnp.bfloat16)
     partial = jnp.dot(hidden, w_second, preferred_element_type=jnp.float32).astype(jnp.bfloat16)
     partial = partial.reshape(n_y, capacity * experts, model_width)
-    parts = lax.all_to_all(partial, "y", split_axis=0, concat_axis=0, tiled=True)
-    summed = jnp.sum(parts.astype(jnp.float32), axis=0)
+    me = lax.axis_index("y")
+    summed = lax.dynamic_index_in_dim(partial, me, axis=0, keepdims=False).astype(jnp.float32)
+    for k in range(1, n_y):
+        block = lax.dynamic_index_in_dim(partial, (me + k) % n_y, axis=0, keepdims=False)
+        summed = summed + passed_along(block, "y", k).astype(jnp.float32)
     back = lax.all_to_all(
         summed.astype(jnp.bfloat16).reshape(capacity, experts, model_width),
         "expert", split_axis=1, concat_axis=1, tiled=True,

time: 315 us -> 309 us (0.981)
  the two profiles are of different devices: /device:TPU:1 before, /device:TPU:9 now
where the time goes in v6:
time: 309 us; the launch traced here: 308 us
  waiting for transfers between devices  136 us (44%)
  starting transfers between devices  81.2 us (26%)
  blocking collectives  42.1 us (14%)
  matrix products  15.4 us (5%)
  local copies, waits for them, and re-layouts  14.1 us (5%)
  between operations  13.8 us (4%)
  other arithmetic  5.72 us (2%)
    all_to_all x2, waiting for transfers between devices, expert_pass(): lax.all_to_all(summed.astype(jnp.bfloat16).reshape(capacity, experts, mod...  53.8 us
    ppermute x10, starting transfers between devices, passed_along(): return lax.ppermute(value, axis, pairs)  43.1 us
    all_to_all x1, blocking collectives, expert_pass(): lax.all_to_all(slot_grid, 'expert', split_axis=1, concat_axis=1, tiled=True)  42.1 us
    ppermute x10, waiting for transfers between devices, passed_along(): return lax.ppermute(value, axis, pairs)  34.3 us
    all_gather x2, waiting for transfers between devices, expert_pass(): gathered = lax.all_gather(received, 'y', axis=0, tiled=False)  29.4 us
    all_to_all x2, starting transfers between devices, expert_pass(): lax.all_to_all(summed.astype(jnp.bfloat16).reshape(capacity, experts, mod...  16.4 us
    all_to_all x1, starting transfers between devices, expert_pass(): lax.all_to_all(slot_grid, 'expert', split_axis=1, concat_axis=1, tiled=True)  15.1 us
    dot_general x2, matrix products, expert_pass(): jnp.dot(hidden, w_second, preferred_element_type=jnp.float32)  11.9 us
  transfers between devices with their start and end apart: 16, of which 11 were waited for; matrix products, arithmetic and copies ran while one was open for 8% of the time, Pallas kernels for 0%

profile of v6, /device:TPU:9, one launch (start us, length us, event | category | flops | bytes accessed | tf_op | source)
XLA Modules:
  0.0 308.1 jit_solution(9929364722035735307)
XLA Ops:
  16.0 15.1 %all-to-all-start = ((bf16[2,32,4096]{2,0,1:T(2,128)(2,1)}), bf16[2,32,4096]{2,0,1:T(2,128)(2,1)S(1)}, u32[]{:S(2)}, u32[]{:S(2)}) async-start(bf16[2,32,4096]{2,0,1:T(2,128)(2,1)} %copy.37), calls=%async_computation | async-start | bytes 1048576 | tf_op jit(solution)/shard_map/all_to_all | solution.py:59
  31.2 7.9 %collective-permute-start.4 = (s32[16,2]{0,1:T(2,128)S(1)}, s32[16,2]{0,1:T(2,128)S(1)}, u32[]{:S(2)}, u32[]{:S(2)}) collective-permute-start(s32[16,2]{0,1:T(2,128)S(1)} %bitcast.138), channel_id=1, source_target_pairs={{0,1},{1,0},{2,3},{3,2},{4,5},{5,4},{6,7},{7,6},{8,9},{9,8},{10,11... | collective-permute-start | bytes 392 | tf_op jit(solution)/shard_map/ppermute | solution.py:11
  39.1 6.5 %collective-permute-start.5 = (bf16[1,16,4096]{2,1,0:T(8,128)(2,1)S(1)}, bf16[1,16,4096]{2,1,0:T(8,128)(2,1)S(1)}, u32[]{:S(2)}, u32[]{:S(2)}) collective-permute-start(bf16[1,16,4096]{2,1,0:T(8,128)(2,1)S(1)} %copy-done.4), channel_id=1, source_target_pairs={{0,257},{1,256},{256,1},{257,0},{2,259},{3,258},{258,3},{259,2},{4... | collective-permute-start | bytes 393224 | tf_op jit(solution)/shard_map/ppermute | solution.py:95
  48.0 7.6 %collective-permute-done.5 = bf16[1,16,4096]{2,1,0:T(8,128)(2,1)S(1)} collective-permute-done((bf16[1,16,4096]{2,1,0:T(8,128)(2,1)S(1)}, bf16[1,16,4096]{2,1,0:T(8,128)(2,1)S(1)}, u32[]{:S(2)}, u32[]{:S(2)}) %collective-permute-start.5) | collective-permute-done | bytes 131104 | tf_op jit(solution)/shard_map/ppermute | solution.py:95
  55.8 10.6 %all-to-all-done = bf16[2,32,4096]{2,0,1:T(2,128)(2,1)S(1)} async-done(((bf16[2,32,4096]{2,0,1:T(2,128)(2,1)}), bf16[2,32,4096]{2,0,1:T(2,128)(2,1)S(1)}, u32[]{:S(2)}, u32[]{:S(2)}) %all-to-all-start) | async-done | bytes 524320 | tf_op jit(solution)/shard_map/all_to_all | solution.py:59
  69.0 42.1 %all_to_all.20 = bf16[2,32,4096]{2,0,1:T(2,128)(2,1)S(1)} all-to-all(bf16[2,32,4096]{2,0,1:T(2,128)(2,1)S(1)} %copy.41), channel_id=1, replica_groups=mesh['section'=2,'expert'=32,'y'=4,'zh'=2] {'expert'}, dimensions={1} | all-to-all | bytes 1048576 | tf_op jit(solution)/shard_map/all_to_all | solution.py:59
  112.3 6.0 %convolution_convert_fusion.1 = bf16[256,4096]{1,0:T(8,128)(2,1)} fusion(bf16[1,1,256,4096]{3,2,1,0:T(8,128)(2,1)S(1)} %copy-done, bf16[256,4096]{1,0:T(8,128)(2,1)} %bitcast.128, bf16[1,1,4096,256]{3,2,1,0:T(8,128)(2,1)} %param.9), kind=kOutput, calls=%fused_computation.1 | convolution fusion | flops 1075380224 | bytes 8388608 | tf_op jit(solution)/shard_map/dot_general | solution.py:64
  120.6 3.2 %collective-permute-start.1 = (bf16[64,4096]{1,0:T(8,128)(2,1)}, bf16[64,4096]{1,0:T(8,128)(2,1)}, u32[]{:S(2)}, u32[]{:S(2)}) collective-permute-start(bf16[64,4096]{1,0:T(8,128)(2,1)} %get-tuple-element.12), channel_id=1, source_target_pairs={{0,2},{2,4},{4,6},{6,0},{1,3},{3,5},{5,7},{7,1},{8,10},{10,12},{12... | collective-permute-start | bytes 1572872 | tf_op jit(solution)/shard_map/ppermute | solution.py:11
  123.8 29.4 %all-gather.7.cloned.1.call-done = bf16[8,32,4096]{2,1,0:T(8,128)(2,1)} async-done(((bf16[2,32,4096]{2,1,0:T(8,128)(2,1)}), bf16[8,32,4096]{2,1,0:T(8,128)(2,1)}) %all-gather.7.cloned.1.call-update) | async-done | bytes 2097168 | tf_op jit(solution)/shard_map/all_gather | solution.py:60
  153.2 5.9 %convolution_convert_fusion = bf16[256,4096]{1,0:T(8,128)(2,1)} fusion(bf16[1,1,256,4096]{3,2,1,0:T(8,128)(2,1)S(1)} %copy-done, bf16[256,4096]{1,0:T(8,128)(2,1)} %bitcast.129, bf16[1,1,4096,256]{3,2,1,0:T(8,128)(2,1)} %param.9), kind=kOutput, calls=%fused_computation | convolution fusion | flops 1075380224 | bytes 8388608 | tf_op jit(solution)/shard_map/dot_general | solution.py:64
  159.1 3.8 %collective-permute-start.3 = (bf16[64,4096]{1,0:T(8,128)(2,1)S(1)}, bf16[64,4096]{1,0:T(8,128)(2,1)}, u32[]{:S(2)}, u32[]{:S(2)}) collective-permute-start(bf16[64,4096]{1,0:T(8,128)(2,1)S(1)} %get-tuple-element.13), channel_id=1, source_target_pairs={{0,6},{2,0},{4,2},{6,4},{1,7},{3,1},{5,3},{7,5},{8,14},{10,8},{12,... | collective-permute-start | bytes 1572872 | tf_op jit(solution)/shard_map/ppermute | solution.py:11
  162.9 2.9 collective-permute-start.2
  168.5 3.5 %collective-permute-start.6 = (bf16[64,4096]{1,0:T(8,128)(2,1)}, bf16[64,4096]{1,0:T(8,128)(2,1)}, u32[]{:S(2)}, u32[]{:S(2)}) collective-permute-start(bf16[64,4096]{1,0:T(8,128)(2,1)} %get-tuple-element.9), channel_id=1, source_target_pairs={{0,2},{2,4},{4,6},{6,0},{1,3},{3,5},{5,7},{7,1},{8,10},{10,12},{12... | collective-permute-start | bytes 1572872 | tf_op jit(solution)/shard_map/ppermute | solution.py:11
  174.0 3.7 %collective-permute-start.7 = (bf16[64,4096]{1,0:T(8,128)(2,1)}, bf16[64,4096]{1,0:T(8,128)(2,1)}, u32[]{:S(2)}, u32[]{:S(2)}) collective-permute-start(bf16[64,4096]{1,0:T(8,128)(2,1)} %get-tuple-element.11), channel_id=1, source_target_pairs={{0,4},{2,6},{4,0},{6,2},{1,5},{3,7},{5,1},{7,3},{8,12},{10,14},{12... | collective-permute-start | bytes 1572872 | tf_op jit(solution)/shard_map/ppermute | solution.py:11
  177.7 9.1 %collective-permute-done.2 = bf16[64,4096]{1,0:T(8,128)(2,1)} collective-permute-done((bf16[64,4096]{1,0:T(8,128)(2,1)S(1)}, bf16[64,4096]{1,0:T(8,128)(2,1)}, u32[]{:S(2)}, u32[]{:S(2)}) %collective-permute-start.2) | collective-permute-done | bytes 524320 | tf_op jit(solution)/shard_map/ppermute | solution.py:11
  186.8 3.2 %collective-permute-done.6 = bf16[64,4096]{1,0:T(8,128)(2,1)} collective-permute-done((bf16[64,4096]{1,0:T(8,128)(2,1)}, bf16[64,4096]{1,0:T(8,128)(2,1)}, u32[]{:S(2)}, u32[]{:S(2)}) %collective-permute-start.6) | collective-permute-done | bytes 524320 | tf_op jit(solution)/shard_map/ppermute | solution.py:11
  190.0 8.6 %collective-permute-done.8 = bf16[64,4096]{1,0:T(8,128)(2,1)} collective-permute-done((bf16[64,4096]{1,0:T(8,128)(2,1)}, bf16[64,4096]{1,0:T(8,128)(2,1)}, u32[]{:S(2)}, u32[]{:S(2)}) %collective-permute-start.8) | collective-permute-done | bytes 524320 | tf_op jit(solution)/shard_map/ppermute | solution.py:11
  198.6 10.7 %collective-permute-done.7 = bf16[64,4096]{1,0:T(8,128)(2,1)} collective-permute-done((bf16[64,4096]{1,0:T(8,128)(2,1)}, bf16[64,4096]{1,0:T(8,128)(2,1)}, u32[]{:S(2)}, u32[]{:S(2)}) %collective-permute-start.7) | collective-permute-done | bytes 524320 | tf_op jit(solution)/shard_map/ppermute | solution.py:11
  213.4 7.7 %all-to-all-start.3 = ((bf16[2,32,4096]{2,0,1:T(2,128)(2,1)}), bf16[2,32,4096]{2,0,1:T(2,128)(2,1)S(1)}, u32[]{:S(2)}, u32[]{:S(2)}) async-start(bf16[2,32,4096]{2,0,1:T(2,128)(2,1)} %copy.43), calls=%async_computation.3 | async-start | bytes 1048576 | tf_op jit(solution)/shard_map/all_to_all | solution.py:71
  222.5 25.4 %all-to-all-done.3 = bf16[2,32,4096]{2,0,1:T(2,128)(2,1)S(1)} async-done(((bf16[2,32,4096]{2,0,1:T(2,128)(2,1)}), bf16[2,32,4096]{2,0,1:T(2,128)(2,1)S(1)}, u32[]{:S(2)}, u32[]{:S(2)}) %all-to-all-start.3) | async-done | bytes 524320 | tf_op jit(solution)/shard_map/all_to_all | solution.py:71
  247.9 8.7 %all-to-all-start.1 = ((bf16[2,32,4096]{2,0,1:T(2,128)(2,1)}), bf16[2,32,4096]{2,0,1:T(2,128)(2,1)S(1)}, u32[]{:S(2)}, u32[]{:S(2)}) async-start(bf16[2,32,4096]{2,0,1:T(2,128)(2,1)} %copy.39), calls=%async_computation.1 | async-start | bytes 1048576 | tf_op jit(solution)/shard_map/all_to_all | solution.py:71
  257.2 6.1 %collective-permute-start.9 = (bf16[16,4096]{1,0:T(8,128)(2,1)S(1)}, bf16[16,4096]{1,0:T(8,128)(2,1)S(1)}, u32[]{:S(2)}, u32[]{:S(2)}) collective-permute-start(bf16[16,4096]{1,0:T(8,128)(2,1)S(1)} %convolution_convert_fusion.4), channel_id=1, source_target_pairs={{0,1},{1,0},{2,3},{3,2},{4,5},{5,4},{6,7},{7,6},{8,9},{9,8},{10,11... | collective-permute-start | bytes 393224 | tf_op jit(solution)/shard_map/ppermute | solution.py:11
  263.2 28.5 %all-to-all-done.1 = bf16[2,32,4096]{2,0,1:T(2,128)(2,1)S(1)} async-done(((bf16[2,32,4096]{2,0,1:T(2,128)(2,1)}), bf16[2,32,4096]{2,0,1:T(2,128)(2,1)S(1)}, u32[]{:S(2)}, u32[]{:S(2)}) %all-to-all-start.1) | async-done | bytes 524320 | tf_op jit(solution)/shard_map/all_to_all | solution.py:71
  292.3 7.3 %collective-permute-start.10 = (bf16[1,16,4096]{2,1,0:T(8,128)(2,1)S(1)}, bf16[1,16,4096]{2,1,0:T(8,128)(2,1)S(1)}, u32[]{:S(2)}, u32[]{:S(2)}) collective-permute-start(bf16[1,16,4096]{2,1,0:T(8,128)(2,1)S(1)} %fusion.2), channel_id=1, source_target_pairs={{0,256},{256,0},{1,257},{257,1},{2,258},{258,2},{3,259},{259,3},{4... | collective-permute-start | bytes 393224 | tf_op jit(solution)/shard_map/ppermute | solution.py:11
  (71 shorter events, 30.9 us)
Async XLA Ops:
  6.5 105.8 %copy-start = (bf16[1,1,256,4096]{3,2,1,0:T(8,128)(2,1)S(1)}, bf16[1,1,256,4096]{3,2,1,0:T(8,128)(2,1)}, u32[]{:S(2)}) copy-start(bf16[1,1,256,4096]{3,2,1,0:T(8,128)(2,1)} %param.10) | copy-start | bytes 6291460
  6.5 32.6 %copy-start.4 = (bf16[1,16,4096]{2,1,0:T(8,128)(2,1)S(1)}, bf16[1,16,4096]{2,1,0:T(8,128)(2,1)}, u32[]{:S(2)}) copy-start(bf16[1,16,4096]{2,1,0:T(8,128)(2,1)} %param.6) | copy-start | bytes 393220
  6.5 24.6 %copy-start.3 = (s32[1,16,2]{1,2,0:T(2,128)S(1)}, s32[1,16,2]{1,2,0:T(2,128)}, u32[]{:S(2)}) copy-start(s32[1,16,2]{1,2,0:T(2,128)} %param.11) | copy-start | bytes 388
  6.5 4.7 %collective-permute-start = (bf16[1,16,4096]{2,1,0:T(8,128)(2,1)}, bf16[1,16,4096]{2,1,0:T(8,128)(2,1)S(1)}, u32[]{:S(2)}, u32[]{:S(2)}) collective-permute-start(bf16[1,16,4096]{2,1,0:T(8,128)(2,1)} %param.6), channel_id=1, source_target_pairs={{0,256},{256,0},{1,257},{257,1},{2,258},{258,2},{3,259},{259,3},{4... | collective-permute-start | bytes 393224 | tf_op jit(solution)/shard_map/ppermute | solution.py:11
  14.6 52.9 %copy-start.1 = (bf16[1,4096,32]{1,2,0:T(8,128)(2,1)S(1)}, bf16[1,4096,32]{1,2,0:T(8,128)(2,1)}, u32[]{:S(2)}) copy-start(bf16[1,4096,32]{1,2,0:T(8,128)(2,1)} %param.8) | copy-start | bytes 786436
  14.6 52.9 %copy-start.2 = (f32[1,4096]{1,0:T(1,128)S(1)}, f32[1,4096]{1,0:T(1,128)}, u32[]{:S(2)}) copy-start(f32[1,4096]{1,0:T(1,128)} %param.7) | copy-start | bytes 49156
  16.0 50.4 %all-to-all-start = ((bf16[2,32,4096]{2,0,1:T(2,128)(2,1)}), bf16[2,32,4096]{2,0,1:T(2,128)(2,1)S(1)}, u32[]{:S(2)}, u32[]{:S(2)}) async-start(bf16[2,32,4096]{2,0,1:T(2,128)(2,1)} %copy.37), calls=%async_computation | async-start | bytes 1048576 | tf_op jit(solution)/shard_map/all_to_all | solution.py:59
  31.1 81.2 %all-gather.5.cloned.1.call-start = ((), (), s32[]{:S(2)}) async-start(), calls=%async_computation.4 | async-start | bytes 2621440 | tf_op jit(solution)/shard_map/all_gather | solution.py:60
  31.2 16.3 %collective-permute-start.4 = (s32[16,2]{0,1:T(2,128)S(1)}, s32[16,2]{0,1:T(2,128)S(1)}, u32[]{:S(2)}, u32[]{:S(2)}) collective-permute-start(s32[16,2]{0,1:T(2,128)S(1)} %bitcast.138), channel_id=1, source_target_pairs={{0,1},{1,0},{2,3},{3,2},{4,5},{5,4},{6,7},{7,6},{8,9},{9,8},{10,11... | collective-permute-start | bytes 392 | tf_op jit(solution)/shard_map/ppermute | solution.py:11
  39.1 16.5 %collective-permute-start.5 = (bf16[1,16,4096]{2,1,0:T(8,128)(2,1)S(1)}, bf16[1,16,4096]{2,1,0:T(8,128)(2,1)S(1)}, u32[]{:S(2)}, u32[]{:S(2)}) collective-permute-start(bf16[1,16,4096]{2,1,0:T(8,128)(2,1)S(1)} %copy-done.4), channel_id=1, source_target_pairs={{0,257},{1,256},{256,1},{257,0},{2,259},{3,258},{258,3},{259,2},{4... | collective-permute-start | bytes 393224 | tf_op jit(solution)/shard_map/ppermute | solution.py:95
  67.5 85.7 %all-gather.7.cloned.1.call-start = ((), (), s32[]{:S(2)}) async-start(), calls=%async_computation.5 | async-start | bytes 2621440 | tf_op jit(solution)/shard_map/all_gather | solution.py:60
  120.6 53.4 %collective-permute-start.1 = (bf16[64,4096]{1,0:T(8,128)(2,1)}, bf16[64,4096]{1,0:T(8,128)(2,1)}, u32[]{:S(2)}, u32[]{:S(2)}) collective-permute-start(bf16[64,4096]{1,0:T(8,128)(2,1)} %get-tuple-element.12), channel_id=1, source_target_pairs={{0,2},{2,4},{4,6},{6,0},{1,3},{3,5},{5,7},{7,1},{8,10},{10,12},{12... | collective-permute-start | bytes 1572872 | tf_op jit(solution)/shard_map/ppermute | solution.py:11
  159.1 18.6 %collective-permute-start.3 = (bf16[64,4096]{1,0:T(8,128)(2,1)S(1)}, bf16[64,4096]{1,0:T(8,128)(2,1)}, u32[]{:S(2)}, u32[]{:S(2)}) collective-permute-start(bf16[64,4096]{1,0:T(8,128)(2,1)S(1)} %get-tuple-element.13), channel_id=1, source_target_pairs={{0,6},{2,0},{4,2},{6,4},{1,7},{3,1},{5,3},{7,5},{8,14},{10,8},{12,... | collective-permute-start | bytes 1572872 | tf_op jit(solution)/shard_map/ppermute | solution.py:11
  162.9 23.8 %collective-permute-start.2 = (bf16[64,4096]{1,0:T(8,128)(2,1)S(1)}, bf16[64,4096]{1,0:T(8,128)(2,1)}, u32[]{:S(2)}, u32[]{:S(2)}) collective-permute-start(bf16[64,4096]{1,0:T(8,128)(2,1)S(1)} %get-tuple-element.14), channel_id=1, source_target_pairs={{0,4},{2,6},{4,0},{6,2},{1,5},{3,7},{5,1},{7,3},{8,12},{10,14},{12... | collective-permute-start | bytes 1572872 | tf_op jit(solution)/shard_map/ppermute | solution.py:11
  168.5 21.5 %collective-permute-start.6 = (bf16[64,4096]{1,0:T(8,128)(2,1)}, bf16[64,4096]{1,0:T(8,128)(2,1)}, u32[]{:S(2)}, u32[]{:S(2)}) collective-permute-start(bf16[64,4096]{1,0:T(8,128)(2,1)} %get-tuple-element.9), channel_id=1, source_target_pairs={{0,2},{2,4},{4,6},{6,0},{1,3},{3,5},{5,7},{7,1},{8,10},{10,12},{12... | collective-permute-start | bytes 1572872 | tf_op jit(solution)/shard_map/ppermute | solution.py:11
  172.0 26.6 %collective-permute-start.8 = (bf16[64,4096]{1,0:T(8,128)(2,1)}, bf16[64,4096]{1,0:T(8,128)(2,1)}, u32[]{:S(2)}, u32[]{:S(2)}) collective-permute-start(bf16[64,4096]{1,0:T(8,128)(2,1)} %get-tuple-element.10), channel_id=1, source_target_pairs={{0,6},{2,0},{4,2},{6,4},{1,7},{3,1},{5,3},{7,5},{8,14},{10,8},{12,... | collective-permute-start | bytes 1572872 | tf_op jit(solution)/shard_map/ppermute | solution.py:11
  174.0 35.3 %collective-permute-start.7 = (bf16[64,4096]{1,0:T(8,128)(2,1)}, bf16[64,4096]{1,0:T(8,128)(2,1)}, u32[]{:S(2)}, u32[]{:S(2)}) collective-permute-start(bf16[64,4096]{1,0:T(8,128)(2,1)} %get-tuple-element.11), channel_id=1, source_target_pairs={{0,4},{2,6},{4,0},{6,2},{1,5},{3,7},{5,1},{7,3},{8,12},{10,14},{12... | collective-permute-start | bytes 1572872 | tf_op jit(solution)/shard_map/ppermute | solution.py:11
  213.4 34.4 %all-to-all-start.3 = ((bf16[2,32,4096]{2,0,1:T(2,128)(2,1)}), bf16[2,32,4096]{2,0,1:T(2,128)(2,1)S(1)}, u32[]{:S(2)}, u32[]{:S(2)}) async-start(bf16[2,32,4096]{2,0,1:T(2,128)(2,1)} %copy.43), calls=%async_computation.3 | async-start | bytes 1048576 | tf_op jit(solution)/shard_map/all_to_all | solution.py:71
  247.9 43.8 %all-to-all-start.1 = ((bf16[2,32,4096]{2,0,1:T(2,128)(2,1)}), bf16[2,32,4096]{2,0,1:T(2,128)(2,1)S(1)}, u32[]{:S(2)}, u32[]{:S(2)}) async-start(bf16[2,32,4096]{2,0,1:T(2,128)(2,1)} %copy.39), calls=%async_computation.1 | async-start | bytes 1048576 | tf_op jit(solution)/shard_map/all_to_all | solution.py:71
  257.2 34.8 %collective-permute-start.9 = (bf16[16,4096]{1,0:T(8,128)(2,1)S(1)}, bf16[16,4096]{1,0:T(8,128)(2,1)S(1)}, u32[]{:S(2)}, u32[]{:S(2)}) collective-permute-start(bf16[16,4096]{1,0:T(8,128)(2,1)S(1)} %convolution_convert_fusion.4), channel_id=1, source_target_pairs={{0,1},{1,0},{2,3},{3,2},{4,5},{5,4},{6,7},{7,6},{8,9},{9,8},{10,11... | collective-permute-start | bytes 393224 | tf_op jit(solution)/shard_map/ppermute | solution.py:11
  292.3 8.3 %collective-permute-start.10 = (bf16[1,16,4096]{2,1,0:T(8,128)(2,1)S(1)}, bf16[1,16,4096]{2,1,0:T(8,128)(2,1)S(1)}, u32[]{:S(2)}, u32[]{:S(2)}) collective-permute-start(bf16[1,16,4096]{2,1,0:T(8,128)(2,1)S(1)} %fusion.2), channel_id=1, source_target_pairs={{0,256},{256,0},{1,257},{257,1},{2,258},{258,2},{3,259},{259,3},{4... | collective-permute-start | bytes 393224 | tf_op jit(solution)/shard_map/ppermute | solution.py:11
Sparse Core Ops, SparseCore 0:
  67.6 38.8 all-gather.4
  112.3 40.7 all-gather.6

commit v7 on v4

v7 whole, which is shorter than its diff:
```python
import jax
import jax.numpy as jnp
from jax import lax
from jax.sharding import Mesh
from jax.sharding import PartitionSpec as P

TOK_BLOCK = 16
QUARTER = ("r", "x")


def passed_along(value, axis, steps):
    count = lax.axis_size(axis)
    pairs = [(source, (source + steps) % count) for source in range(count)]
    return lax.ppermute(value, axis, pairs)


def normalize(inputs, gain_row):
    widened = inputs.astype(jnp.float32)
    mean_sq = jnp.mean(widened * widened, axis=-1, keepdims=True)
    return (widened * lax.rsqrt(mean_sq + 1e-05) * gain_row).astype(jnp.bfloat16)


def route(normed, router_mat, expert_pick, tok_block, capacity):
    logits = jnp.dot(normed, router_mat, preferred_element_type=jnp.float32)
    experts = router_mat.shape[1]
    labels = jnp.arange(experts, dtype=jnp.int32)
    pair_hot = (expert_pick[:, :, None] == labels[None, None, :]).astype(jnp.float32)
    picked = jnp.sum(pair_hot * logits[:, None, :], axis=-1)
    squashed = jax.nn.sigmoid(picked)
    gate_vals = squashed / jnp.sum(squashed, axis=-1, keepdims=True)
    blocks = expert_pick.shape[0] // tok_block
    pair_order = jnp.transpose(expert_pick.reshape(blocks, tok_block, 2), (0, 2, 1)).reshape(
        blocks, 2 * tok_block
    )
    one_hot = (pair_order[:, :, None] == labels[None, None, :]).astype(jnp.int32)
    before = jnp.cumsum(one_hot, axis=1) - one_hot
    pair_ranks = jnp.sum(before * one_hot, axis=-1)
    pair_ranks = jnp.transpose(pair_ranks.reshape(blocks, 2, tok_block), (0, 2, 1)).reshape(-1, 2)
    is_kept = pair_ranks < capacity
    return (gate_vals, pair_ranks, is_kept)


def dispatch(rows, pick, router_mat, capacity, home_q, n_local):
    tok_count, model_width = rows.shape
    tok_block = TOK_BLOCK
    blocks = tok_count // tok_block
    gate_vals, pair_ranks, is_kept = route(rows, router_mat, pick, tok_block, capacity)
    block_of = (jnp.arange(tok_count, dtype=jnp.int32) // tok_block)[:, None]
    here = is_kept & (pick // n_local == home_q)
    slot_ids = (block_of * capacity + pair_ranks) * n_local + pick % n_local
    slot_count = blocks * capacity * n_local
    slot_labels = jnp.arange(slot_count, dtype=jnp.int32)
    slot_hot = ((slot_ids[:, :, None] == slot_labels[None, None, :]) & here[:, :, None]).astype(
        jnp.float32
    )
    placement = jnp.transpose(jnp.sum(slot_hot, axis=1)).astype(jnp.bfloat16)
    combine_mat = jnp.sum(slot_hot * gate_vals[:, :, None], axis=1)
    send_rows = jnp.dot(placement, rows, preferred_element_type=jnp.float32).astype(jnp.bfloat16)
    return send_rows.reshape(blocks * capacity, n_local, model_width), combine_mat


def expert_pass(slot_grid, combine_mat, w_first, w_second):
    lead, n_local, model_width = slot_grid.shape
    n_y = lax.axis_size("y")
    received = lax.all_to_all(slot_grid, QUARTER, split_axis=1, concat_axis=1, tiled=True)
    summed = None
    for k in range(n_y):
        rows_in = received if k == 0 else passed_along(received, "y", k)
        hidden = jax.nn.gelu(
            jnp.dot(rows_in.reshape(-1, model_width), w_first, preferred_element_type=jnp.float32)
        ).astype(jnp.bfloat16)
        partial = jnp.dot(hidden, w_second, preferred_element_type=jnp.float32).astype(jnp.bfloat16)
        if k == 0:
            summed = partial.astype(jnp.float32)
        else:
            summed = summed + passed_along(partial, "y", n_y - k).astype(jnp.float32)
    back = lax.all_to_all(
        summed.astype(jnp.bfloat16).reshape(lead, n_local, model_width),
        QUARTER, split_axis=1, concat_axis=1, tiled=True,
    )
    return jnp.dot(
        combine_mat,
        back.reshape(lead * n_local, model_width).astype(jnp.float32),
        precision=lax.Precision.HIGHEST,
    )


def shifted_pairs(sizes, steps):
    total = 1
    for size in sizes:
        total *= size
    pairs = []
    for source in range(total):
        digits, rest = [], source
        for size in reversed(sizes):
            digits.append(rest % size)
            rest //= size
        digits = digits[::-1]
        dest = 0
        for digit, size, step in zip(digits, sizes, steps):
            dest = dest * size + (digit + step) % size
        pairs.append((source, dest))
    return pairs


def on_device(sent, norm_gain, router, w_in, w_out, expert_ids):
    arrived = passed_along(sent, "section", 1)[0]
    tok_count = arrived.shape[0]
    experts = router.shape[2]
    top_count = expert_ids.shape[2]
    capacity = max(2, (5 * top_count * tok_count + 4 * experts - 1) // (4 * experts))
    n_sec, n_q, n_zh = (lax.axis_size(a) for a in ("section", "q2", "zh"))
    n_local = experts // n_q
    home_q = lax.axis_index("q2")
    offsets = [(a, c) for a in range(n_q) for c in range(n_zh) if (a, c) != (0, 0)]
    rows = [normalize(arrived, norm_gain[0])]
    picks = [expert_ids[0]]
    for a, c in offsets:
        far = lax.ppermute(sent, ("section", "q2", "zh"), shifted_pairs((n_sec, n_q, n_zh), (1, a, c)))
        rows.append(normalize(far[0], norm_gain[0]))
        picks.append(lax.ppermute(expert_ids[0], ("q2", "zh"), shifted_pairs((n_q, n_zh), (a, c))))
    w_first = w_in[0, 0]
    w_second = w_out[0, 0]
    chunk = len(rows) // 2
    halves = []
    for part in (slice(0, chunk), slice(chunk, len(rows))):
        slots, combine = dispatch(
            jnp.concatenate(rows[part], axis=0), jnp.concatenate(picks[part], axis=0),
            router[0], capacity, home_q, n_local,
        )
        halves.append(expert_pass(slots, combine, w_first, w_second))
    sums = jnp.concatenate(halves, axis=0).reshape(len(rows), tok_count, -1)
    combined = arrived.astype(jnp.float32) + sums[0]
    for j, (a, c) in enumerate(offsets, start=1):
        home = shifted_pairs((n_q, n_zh), (-a, -c))
        combined = combined + lax.ppermute(sums[j].astype(jnp.bfloat16), ("q2", "zh"), home).astype(
            jnp.float32
        )
    return passed_along(combined.astype(jnp.bfloat16)[None], "section", 1)


def solution(mesh):
    sizes = dict(mesh.shape)
    n_expert, n_tensor = sizes["expert"], sizes["tensor"]
    n_x = 4
    fine = Mesh(
        mesh.devices.reshape(sizes["section"], 2, n_expert // (2 * n_x), n_x, n_tensor // 2, 2),
        ("section", "q2", "r", "x", "y", "zh"),
    )
    experts_at = ("q2", "r", "x")
    hidden_units = ("y", "zh")
    tokens = experts_at + hidden_units
    return jax.shard_map(
        on_device,
        mesh=fine,
        in_specs=(
            P("section", tokens, None),
            P("section", None),
            P("section", None, None),
            P("section", experts_at, None, hidden_units),
            P("section", experts_at, hidden_units, None),
            P("section", tokens, None),
        ),
        out_specs=P("section", tokens, None),
        check_vma=False,
    )
```

time: 253 us -> 262 us (1.036)
  the two profiles are of different devices: /device:TPU:1 before, /device:TPU:57 now
where the time goes in v7:
time: 262 us; the launch traced here: 261 us
  starting transfers between devices  116 us (44%)
  waiting for transfers between devices  78.4 us (30%)
  matrix products  32.7 us (12%)
  blocking collectives  21.3 us (8%)
  local copies, waits for them, and re-layouts  8.19 us (3%)
  other arithmetic  3.68 us (1%)
    ppermute x14, starting transfers between devices, passed_along(): return lax.ppermute(value, axis, pairs)  42.1 us
    ppermute x14, waiting for transfers between devices, passed_along(): return lax.ppermute(value, axis, pairs)  38.2 us
    dot_general x8, matrix products, expert_pass(): jnp.dot(hidden, w_second, preferred_element_type=jnp.float32)  30.1 us
    all_to_all x1, blocking collectives, expert_pass(): lax.all_to_all(slot_grid, QUARTER, split_axis=1, concat_axis=1, tiled=True)  21.3 us
    ppermute x3, starting transfers between devices, on_device(): lax.ppermute(expert_ids[0], ('q2', 'zh'), shifted_pairs((n_q, n_zh), (a,...  20.6 us
    ppermute x3, starting transfers between devices, on_device(): lax.ppermute(sums[j].astype(jnp.bfloat16), ('q2', 'zh'), home)  19.7 us
    ppermute x3, starting transfers between devices, on_device(): lax.ppermute(sent, ('section', 'q2', 'zh'), shifted_pairs((n_sec, n_q, n_...  16.8 us
    ppermute x3, waiting for transfers between devices, on_device(): lax.ppermute(sums[j].astype(jnp.bfloat16), ('q2', 'zh'), home)  15.2 us
  transfers between devices with their start and end apart: 26, of which 12 were waited for; matrix products, arithmetic and copies ran while one was open for 15% of the time, Pallas kernels for 0%

profile of v7, /device:TPU:57, one launch (start us, length us, event | category | flops | bytes accessed | tf_op | source)
XLA Modules:
  0.0 260.8 jit_solution(11981180788715168619)
XLA Ops:
  0.0 14.7 %collective-permute-start.1 = (s32[16,2]{0,1:T(2,128)}, s32[16,2]{0,1:T(2,128)S(1)}, u32[]{:S(2)}, u32[]{:S(2)}) collective-permute-start(s32[16,2]{0,1:T(2,128)} %bitcast.168), channel_id=1, source_target_pairs={{0,1},{1,0},{128,129},{129,128},{2,3},{3,2},{130,131},{131,130},{4... | collective-permute-start | bytes 392 | tf_op jit(solution)/shard_map/ppermute | solution.py:121
  16.6 4.0 %collective-permute-start.10 = (s32[16,2]{0,1:T(2,128)}, s32[16,2]{0,1:T(2,128)S(1)}, u32[]{:S(2)}, u32[]{:S(2)}) collective-permute-start(s32[16,2]{0,1:T(2,128)} %bitcast.170), channel_id=1, source_target_pairs={{0,128},{1,129},{128,0},{129,1},{2,130},{3,131},{130,2},{131,3},{4... | collective-permute-start | bytes 392 | tf_op jit(solution)/shard_map/ppermute | solution.py:121
  23.8 10.4 %collective-permute-start.2 = (bf16[1,16,4096]{2,1,0:T(8,128)(2,1)}, bf16[1,16,4096]{2,1,0:T(8,128)(2,1)S(1)}, u32[]{:S(2)}, u32[]{:S(2)}) collective-permute-start(bf16[1,16,4096]{2,1,0:T(8,128)(2,1)} %param.6), channel_id=1, source_target_pairs={{0,257},{1,256},{128,385},{129,384},{256,1},{257,0},{384,129},{385... | collective-permute-start | bytes 393224 | tf_op jit(solution)/shard_map/ppermute | solution.py:119
  34.3 4.4 %collective-permute-start.12 = (bf16[1,16,4096]{2,1,0:T(8,128)(2,1)}, bf16[1,16,4096]{2,1,0:T(8,128)(2,1)S(1)}, u32[]{:S(2)}, u32[]{:S(2)}) collective-permute-start(bf16[1,16,4096]{2,1,0:T(8,128)(2,1)} %param.6), channel_id=1, source_target_pairs={{0,384},{1,385},{128,256},{129,257},{256,128},{257,129},{384,0},{3... | collective-permute-start | bytes 393224 | tf_op jit(solution)/shard_map/ppermute | solution.py:119
  43.0 5.4 %collective-permute-done.2 = bf16[1,16,4096]{2,1,0:T(8,128)(2,1)S(1)} collective-permute-done((bf16[1,16,4096]{2,1,0:T(8,128)(2,1)}, bf16[1,16,4096]{2,1,0:T(8,128)(2,1)S(1)}, u32[]{:S(2)}, u32[]{:S(2)}) %collective-permute-start.2) | collective-permute-done | bytes 131104 | tf_op jit(solution)/shard_map/ppermute | solution.py:119
  48.6 8.8 %collective-permute-done.12 = bf16[1,16,4096]{2,1,0:T(8,128)(2,1)S(1)} collective-permute-done((bf16[1,16,4096]{2,1,0:T(8,128)(2,1)}, bf16[1,16,4096]{2,1,0:T(8,128)(2,1)S(1)}, u32[]{:S(2)}, u32[]{:S(2)}) %collective-permute-start.12) | collective-permute-done | bytes 131104 | tf_op jit(solution)/shard_map/ppermute | solution.py:119
  61.4 21.3 %all_to_all.20 = bf16[4,16,4096]{2,0,1:T(4,128)(2,1)S(1)} all-to-all(bf16[4,16,4096]{2,0,1:T(4,128)(2,1)S(1)} %copy.66), channel_id=1, replica_groups=mesh['section'=2,'q2'=2,'r'=4,'x'=4,'y'=4,'zh'=2] {'r','x'}, dimensions={1} | all-to-all | bytes 1048576 | tf_op jit(solution)/shard_map/all_to_all | solution.py:65
  86.8 5.1 %all-to-all-start = ((bf16[4,16,4096]{2,0,1:T(4,128)(2,1)}), bf16[4,16,4096]{2,0,1:T(4,128)(2,1)S(1)}, u32[]{:S(2)}, u32[]{:S(2)}) async-start(bf16[4,16,4096]{2,0,1:T(4,128)(2,1)} %copy.57), calls=%async_computation | async-start | bytes 1048576 | tf_op jit(solution)/shard_map/all_to_all | solution.py:65
  98.3 4.0 %convolution_convert_fusion.2 = bf16[64,4096]{1,0:T(8,128)(2,1)} fusion(bf16[1,1,256,4096]{3,2,1,0:T(8,128)(2,1)S(1)} %copy-done, bf16[64,4096]{1,0:T(8,128)(2,1)} %bitcast.28, bf16[1,1,4096,256]{3,2,1,0:T(8,128)(2,1)} %param.9), kind=kOutput, calls=%fused_computation.2 | convolution fusion | flops 268845056 | bytes 5242880 | tf_op jit(solution)/shard_map/dot_general | solution.py:72
  111.4 4.5 %collective-permute-start.17 = (bf16[64,4096]{1,0:T(8,128)(2,1)}, bf16[64,4096]{1,0:T(8,128)(2,1)}, u32[]{:S(2)}, u32[]{:S(2)}) collective-permute-start(bf16[64,4096]{1,0:T(8,128)(2,1)} %convolution_convert_fusion.3), channel_id=1, source_target_pairs={{0,4},{2,6},{4,0},{6,2},{1,5},{3,7},{5,1},{7,3},{8,12},{10,14},{12... | collective-permute-start | bytes 1572872 | tf_op jit(solution)/shard_map/ppermute | solution.py:14
  119.2 4.0 %convolution_convert_fusion.4 = bf16[64,4096]{1,0:T(8,128)(2,1)} fusion(bf16[1,1,256,4096]{3,2,1,0:T(8,128)(2,1)S(1)} %copy-done, bf16[64,4096]{1,0:T(8,128)(2,1)} %bitcast.26, bf16[1,1,4096,256]{3,2,1,0:T(8,128)(2,1)} %param.9), kind=kOutput, calls=%fused_computation.4 | convolution fusion | flops 268845056 | bytes 5242880 | tf_op jit(solution)/shard_map/dot_general | solution.py:72
  129.6 5.1 %collective-permute-start.5 = (bf16[4,16,4096]{2,1,0:T(8,128)(2,1)}, bf16[4,16,4096]{2,1,0:T(8,128)(2,1)}, u32[]{:S(2)}, u32[]{:S(2)}) collective-permute-start(bf16[4,16,4096]{2,1,0:T(8,128)(2,1)} %copy.58), channel_id=1, source_target_pairs={{0,4},{2,6},{4,0},{6,2},{1,5},{3,7},{5,1},{7,3},{8,12},{10,14},{12... | collective-permute-start | bytes 1572872 | tf_op jit(solution)/shard_map/ppermute | solution.py:14
  138.7 4.5 %collective-permute-done.15 = bf16[64,4096]{1,0:T(8,128)(2,1)} collective-permute-done((bf16[64,4096]{1,0:T(8,128)(2,1)}, bf16[64,4096]{1,0:T(8,128)(2,1)}, u32[]{:S(2)}, u32[]{:S(2)}) %collective-permute-start.15) | collective-permute-done | bytes 524320 | tf_op jit(solution)/shard_map/ppermute | solution.py:14
  147.8 4.8 %all-to-all-start.3 = ((bf16[4,16,4096]{2,0,1:T(4,128)(2,1)}), bf16[4,16,4096]{2,0,1:T(4,128)(2,1)S(1)}, u32[]{:S(2)}, u32[]{:S(2)}) async-start(bf16[4,16,4096]{2,0,1:T(4,128)(2,1)} %copy.71), calls=%async_computation.3 | async-start | bytes 1048576 | tf_op jit(solution)/shard_map/all_to_all | solution.py:77
  160.3 4.5 %collective-permute-done.5 = bf16[4,16,4096]{2,1,0:T(8,128)(2,1)} collective-permute-done((bf16[4,16,4096]{2,1,0:T(8,128)(2,1)}, bf16[4,16,4096]{2,1,0:T(8,128)(2,1)}, u32[]{:S(2)}, u32[]{:S(2)}) %collective-permute-start.5) | collective-permute-done | bytes 524320 | tf_op jit(solution)/shard_map/ppermute | solution.py:14
  171.0 4.0 %convolution_convert_fusion.8 = bf16[64,4096]{1,0:T(8,128)(2,1)} fusion(bf16[1,1,256,4096]{3,2,1,0:T(8,128)(2,1)S(1)} %copy-done, bf16[64,4096]{1,0:T(8,128)(2,1)} %bitcast.13, bf16[1,1,4096,256]{3,2,1,0:T(8,128)(2,1)} %param.9), kind=kOutput, calls=%fused_computation.9 | convolution fusion | flops 268845056 | bytes 5242880 | tf_op jit(solution)/shard_map/dot_general | solution.py:72
  176.9 5.9 %collective-permute-done.6 = bf16[64,4096]{1,0:T(8,128)(2,1)} collective-permute-done((bf16[64,4096]{1,0:T(8,128)(2,1)}, bf16[64,4096]{1,0:T(8,128)(2,1)}, u32[]{:S(2)}, u32[]{:S(2)}) %collective-permute-start.6) | collective-permute-done | bytes 524320 | tf_op jit(solution)/shard_map/ppermute | solution.py:14
  182.7 13.8 %collective-permute-done.4 = bf16[64,4096]{1,0:T(8,128)(2,1)S(1)} collective-permute-done((bf16[64,4096]{1,0:T(8,128)(2,1)}, bf16[64,4096]{1,0:T(8,128)(2,1)S(1)}, u32[]{:S(2)}, u32[]{:S(2)}) %collective-permute-start.4) | collective-permute-done | bytes 524320 | tf_op jit(solution)/shard_map/ppermute | solution.py:14
  202.1 7.0 %all-to-all-start.1 = ((bf16[4,16,4096]{2,0,1:T(4,128)(2,1)}), bf16[4,16,4096]{2,0,1:T(4,128)(2,1)S(1)}, u32[]{:S(2)}, u32[]{:S(2)}) async-start(bf16[4,16,4096]{2,0,1:T(4,128)(2,1)} %copy.62), calls=%async_computation.1 | async-start | bytes 1048576 | tf_op jit(solution)/shard_map/all_to_all | solution.py:77
  209.9 5.5 %collective-permute-start.21 = (bf16[16,4096]{1,0:T(8,128)(2,1)S(1)}, bf16[16,4096]{1,0:T(8,128)(2,1)S(1)}, u32[]{:S(2)}, u32[]{:S(2)}) collective-permute-start(bf16[16,4096]{1,0:T(8,128)(2,1)S(1)} %get-tuple-element.10), channel_id=1, source_target_pairs={{0,129},{1,128},{128,1},{129,0},{2,131},{3,130},{130,3},{131,2},{4... | collective-permute-start | bytes 393224 | tf_op jit(solution)/shard_map/ppermute | solution.py:136
  215.4 5.4 %collective-permute-start.20 = (bf16[16,4096]{1,0:T(8,128)(2,1)S(1)}, bf16[16,4096]{1,0:T(8,128)(2,1)S(1)}, u32[]{:S(2)}, u32[]{:S(2)}) collective-permute-start(bf16[16,4096]{1,0:T(8,128)(2,1)S(1)} %get-tuple-element.9), channel_id=1, source_target_pairs={{0,128},{1,129},{128,0},{129,1},{2,130},{3,131},{130,2},{131,3},{4... | collective-permute-start | bytes 393224 | tf_op jit(solution)/shard_map/ppermute | solution.py:136
  220.8 10.8 %all-to-all-done.1 = bf16[4,16,4096]{2,0,1:T(4,128)(2,1)S(1)} async-done(((bf16[4,16,4096]{2,0,1:T(4,128)(2,1)}), bf16[4,16,4096]{2,0,1:T(4,128)(2,1)S(1)}, u32[]{:S(2)}, u32[]{:S(2)}) %all-to-all-start.1) | async-done | bytes 524320 | tf_op jit(solution)/shard_map/all_to_all | solution.py:77
  232.3 8.7 %collective-permute-start.9 = (bf16[16,4096]{1,0:T(8,128)(2,1)S(1)}, bf16[16,4096]{1,0:T(8,128)(2,1)S(1)}, u32[]{:S(2)}, u32[]{:S(2)}) collective-permute-start(bf16[16,4096]{1,0:T(8,128)(2,1)S(1)} %slice.35), channel_id=1, source_target_pairs={{0,1},{1,0},{128,129},{129,128},{2,3},{3,2},{130,131},{131,130},{4... | collective-permute-start | bytes 393224 | tf_op jit(solution)/shard_map/ppermute | solution.py:136
  241.0 15.2 %collective-permute-done.9 = bf16[16,4096]{1,0:T(8,128)(2,1)S(1)} collective-permute-done((bf16[16,4096]{1,0:T(8,128)(2,1)S(1)}, bf16[16,4096]{1,0:T(8,128)(2,1)S(1)}, u32[]{:S(2)}, u32[]{:S(2)}) %collective-permute-start.9) | collective-permute-done | bytes 131104 | tf_op jit(solution)/shard_map/ppermute | solution.py:136
  (101 shorter events, 78.5 us)
Async XLA Ops:
  0.0 34.2 %collective-permute-start.1 = (s32[16,2]{0,1:T(2,128)}, s32[16,2]{0,1:T(2,128)S(1)}, u32[]{:S(2)}, u32[]{:S(2)}) collective-permute-start(s32[16,2]{0,1:T(2,128)} %bitcast.168), channel_id=1, source_target_pairs={{0,1},{1,0},{128,129},{129,128},{2,3},{3,2},{130,131},{131,130},{4... | collective-permute-start | bytes 392 | tf_op jit(solution)/shard_map/ppermute | solution.py:121
  14.7 25.4 %collective-permute-start.11 = (s32[16,2]{0,1:T(2,128)}, s32[16,2]{0,1:T(2,128)S(1)}, u32[]{:S(2)}, u32[]{:S(2)}) collective-permute-start(s32[16,2]{0,1:T(2,128)} %bitcast.169), channel_id=1, source_target_pairs={{0,129},{1,128},{128,1},{129,0},{2,131},{3,130},{130,3},{131,2},{4... | collective-permute-start | bytes 392 | tf_op jit(solution)/shard_map/ppermute | solution.py:121
  16.6 25.4 %collective-permute-start.10 = (s32[16,2]{0,1:T(2,128)}, s32[16,2]{0,1:T(2,128)S(1)}, u32[]{:S(2)}, u32[]{:S(2)}) collective-permute-start(s32[16,2]{0,1:T(2,128)} %bitcast.170), channel_id=1, source_target_pairs={{0,128},{1,129},{128,0},{129,1},{2,130},{3,131},{130,2},{131,3},{4... | collective-permute-start | bytes 392 | tf_op jit(solution)/shard_map/ppermute | solution.py:121
  20.6 22.2 %collective-permute-start = (bf16[1,16,4096]{2,1,0:T(8,128)(2,1)}, bf16[1,16,4096]{2,1,0:T(8,128)(2,1)S(1)}, u32[]{:S(2)}, u32[]{:S(2)}) collective-permute-start(bf16[1,16,4096]{2,1,0:T(8,128)(2,1)} %param.6), channel_id=1, source_target_pairs={{0,256},{256,0},{1,257},{257,1},{2,258},{258,2},{3,259},{259,3},{4... | collective-permute-start | bytes 393224 | tf_op jit(solution)/shard_map/ppermute | solution.py:14
  23.8 24.6 %collective-permute-start.2 = (bf16[1,16,4096]{2,1,0:T(8,128)(2,1)}, bf16[1,16,4096]{2,1,0:T(8,128)(2,1)S(1)}, u32[]{:S(2)}, u32[]{:S(2)}) collective-permute-start(bf16[1,16,4096]{2,1,0:T(8,128)(2,1)} %param.6), channel_id=1, source_target_pairs={{0,257},{1,256},{128,385},{129,384},{256,1},{257,0},{384,129},{385... | collective-permute-start | bytes 393224 | tf_op jit(solution)/shard_map/ppermute | solution.py:119
  34.3 23.2 %collective-permute-start.12 = (bf16[1,16,4096]{2,1,0:T(8,128)(2,1)}, bf16[1,16,4096]{2,1,0:T(8,128)(2,1)S(1)}, u32[]{:S(2)}, u32[]{:S(2)}) collective-permute-start(bf16[1,16,4096]{2,1,0:T(8,128)(2,1)} %param.6), channel_id=1, source_target_pairs={{0,384},{1,385},{128,256},{129,257},{256,128},{257,129},{384,0},{3... | collective-permute-start | bytes 393224 | tf_op jit(solution)/shard_map/ppermute | solution.py:119
  40.1 17.5 %collective-permute-start.13 = (bf16[1,16,4096]{2,1,0:T(8,128)(2,1)}, bf16[1,16,4096]{2,1,0:T(8,128)(2,1)S(1)}, u32[]{:S(2)}, u32[]{:S(2)}) collective-permute-start(bf16[1,16,4096]{2,1,0:T(8,128)(2,1)} %param.6), channel_id=1, source_target_pairs={{0,385},{1,384},{128,257},{129,256},{256,129},{257,128},{384,1},{3... | collective-permute-start | bytes 393224 | tf_op jit(solution)/shard_map/ppermute | solution.py:119
  82.9 15.4 %collective-permute-start.18 = (bf16[4,16,4096]{2,1,0:T(8,128)(2,1)S(1)}, bf16[4,16,4096]{2,1,0:T(8,128)(2,1)}, u32[]{:S(2)}, u32[]{:S(2)}) collective-permute-start(bf16[4,16,4096]{2,1,0:T(8,128)(2,1)S(1)} %copy.67), channel_id=1, source_target_pairs={{0,6},{2,0},{4,2},{6,4},{1,7},{3,1},{5,3},{7,5},{8,14},{10,8},{12,... | collective-permute-start | bytes 1572872 | tf_op jit(solution)/shard_map/ppermute | solution.py:14
  86.8 39.8 %all-to-all-start = ((bf16[4,16,4096]{2,0,1:T(4,128)(2,1)}), bf16[4,16,4096]{2,0,1:T(4,128)(2,1)S(1)}, u32[]{:S(2)}, u32[]{:S(2)}) async-start(bf16[4,16,4096]{2,0,1:T(4,128)(2,1)} %copy.57), calls=%async_computation | async-start | bytes 1048576 | tf_op jit(solution)/shard_map/all_to_all | solution.py:65
  91.9 15.5 %collective-permute-start.16 = (bf16[4,16,4096]{2,1,0:T(8,128)(2,1)S(1)}, bf16[4,16,4096]{2,1,0:T(8,128)(2,1)}, u32[]{:S(2)}, u32[]{:S(2)}) collective-permute-start(bf16[4,16,4096]{2,1,0:T(8,128)(2,1)S(1)} %copy.67), channel_id=1, source_target_pairs={{0,4},{2,6},{4,0},{6,2},{1,5},{3,7},{5,1},{7,3},{8,12},{10,14},{12... | collective-permute-start | bytes 1572872 | tf_op jit(solution)/shard_map/ppermute | solution.py:14
  94.5 24.7 %collective-permute-start.14 = (bf16[4,16,4096]{2,1,0:T(8,128)(2,1)S(1)}, bf16[4,16,4096]{2,1,0:T(8,128)(2,1)}, u32[]{:S(2)}, u32[]{:S(2)}) collective-permute-start(bf16[4,16,4096]{2,1,0:T(8,128)(2,1)S(1)} %copy.67), channel_id=1, source_target_pairs={{0,2},{2,4},{4,6},{6,0},{1,3},{3,5},{5,7},{7,1},{8,10},{10,12},{12... | collective-permute-start | bytes 1572872 | tf_op jit(solution)/shard_map/ppermute | solution.py:14
  102.3 32.4 %collective-permute-start.19 = (bf16[64,4096]{1,0:T(8,128)(2,1)}, bf16[64,4096]{1,0:T(8,128)(2,1)}, u32[]{:S(2)}, u32[]{:S(2)}) collective-permute-start(bf16[64,4096]{1,0:T(8,128)(2,1)} %convolution_convert_fusion.2), channel_id=1, source_target_pairs={{0,2},{2,4},{4,6},{6,0},{1,3},{3,5},{5,7},{7,1},{8,10},{10,12},{12... | collective-permute-start | bytes 1572872 | tf_op jit(solution)/shard_map/ppermute | solution.py:14
  111.4 27.3 %collective-permute-start.17 = (bf16[64,4096]{1,0:T(8,128)(2,1)}, bf16[64,4096]{1,0:T(8,128)(2,1)}, u32[]{:S(2)}, u32[]{:S(2)}) collective-permute-start(bf16[64,4096]{1,0:T(8,128)(2,1)} %convolution_convert_fusion.3), channel_id=1, source_target_pairs={{0,4},{2,6},{4,0},{6,2},{1,5},{3,7},{5,1},{7,3},{8,12},{10,14},{12... | collective-permute-start | bytes 1572872 | tf_op jit(solution)/shard_map/ppermute | solution.py:14
  123.2 20.0 %collective-permute-start.15 = (bf16[64,4096]{1,0:T(8,128)(2,1)}, bf16[64,4096]{1,0:T(8,128)(2,1)}, u32[]{:S(2)}, u32[]{:S(2)}) collective-permute-start(bf16[64,4096]{1,0:T(8,128)(2,1)} %convolution_convert_fusion.4), channel_id=1, source_target_pairs={{0,6},{2,0},{4,2},{6,4},{1,7},{3,1},{5,3},{7,5},{8,14},{10,8},{12,... | collective-permute-start | bytes 1572872 | tf_op jit(solution)/shard_map/ppermute | solution.py:14
  127.7 27.6 %collective-permute-start.7 = (bf16[4,16,4096]{2,1,0:T(8,128)(2,1)}, bf16[4,16,4096]{2,1,0:T(8,128)(2,1)}, u32[]{:S(2)}, u32[]{:S(2)}) collective-permute-start(bf16[4,16,4096]{2,1,0:T(8,128)(2,1)} %copy.58), channel_id=1, source_target_pairs={{0,6},{2,0},{4,2},{6,4},{1,7},{3,1},{5,3},{7,5},{8,14},{10,8},{12,... | collective-permute-start | bytes 1572872 | tf_op jit(solution)/shard_map/ppermute | solution.py:14
  129.6 35.3 %collective-permute-start.5 = (bf16[4,16,4096]{2,1,0:T(8,128)(2,1)}, bf16[4,16,4096]{2,1,0:T(8,128)(2,1)}, u32[]{:S(2)}, u32[]{:S(2)}) collective-permute-start(bf16[4,16,4096]{2,1,0:T(8,128)(2,1)} %copy.58), channel_id=1, source_target_pairs={{0,4},{2,6},{4,0},{6,2},{1,5},{3,7},{5,1},{7,3},{8,12},{10,14},{12... | collective-permute-start | bytes 1572872 | tf_op jit(solution)/shard_map/ppermute | solution.py:14
  134.7 36.2 %collective-permute-start.3 = (bf16[4,16,4096]{2,1,0:T(8,128)(2,1)}, bf16[4,16,4096]{2,1,0:T(8,128)(2,1)}, u32[]{:S(2)}, u32[]{:S(2)}) collective-permute-start(bf16[4,16,4096]{2,1,0:T(8,128)(2,1)} %copy.58), channel_id=1, source_target_pairs={{0,2},{2,4},{4,6},{6,0},{1,3},{3,5},{5,7},{7,1},{8,10},{10,12},{12... | collective-permute-start | bytes 1572872 | tf_op jit(solution)/shard_map/ppermute | solution.py:14
  147.8 54.3 %all-to-all-start.3 = ((bf16[4,16,4096]{2,0,1:T(4,128)(2,1)}), bf16[4,16,4096]{2,0,1:T(4,128)(2,1)S(1)}, u32[]{:S(2)}, u32[]{:S(2)}) async-start(bf16[4,16,4096]{2,0,1:T(4,128)(2,1)} %copy.71), calls=%async_computation.3 | async-start | bytes 1048576 | tf_op jit(solution)/shard_map/all_to_all | solution.py:77
  158.4 18.5 %collective-permute-start.8 = (bf16[64,4096]{1,0:T(8,128)(2,1)S(1)}, bf16[64,4096]{1,0:T(8,128)(2,1)}, u32[]{:S(2)}, u32[]{:S(2)}) collective-permute-start(bf16[64,4096]{1,0:T(8,128)(2,1)S(1)} %convolution_convert_fusion.6), channel_id=1, source_target_pairs={{0,2},{2,4},{4,6},{6,0},{1,3},{3,5},{5,7},{7,1},{8,10},{10,12},{12... | collective-permute-start | bytes 1572872 | tf_op jit(solution)/shard_map/ppermute | solution.py:14
  175.0 21.6 %collective-permute-start.4 = (bf16[64,4096]{1,0:T(8,128)(2,1)}, bf16[64,4096]{1,0:T(8,128)(2,1)S(1)}, u32[]{:S(2)}, u32[]{:S(2)}) collective-permute-start(bf16[64,4096]{1,0:T(8,128)(2,1)} %convolution_convert_fusion.8), channel_id=1, source_target_pairs={{0,6},{2,0},{4,2},{6,4},{1,7},{3,1},{5,3},{7,5},{8,14},{10,8},{12,... | collective-permute-start | bytes 1572872 | tf_op jit(solution)/shard_map/ppermute | solution.py:14
  202.1 29.4 %all-to-all-start.1 = ((bf16[4,16,4096]{2,0,1:T(4,128)(2,1)}), bf16[4,16,4096]{2,0,1:T(4,128)(2,1)S(1)}, u32[]{:S(2)}, u32[]{:S(2)}) async-start(bf16[4,16,4096]{2,0,1:T(4,128)(2,1)} %copy.62), calls=%async_computation.1 | async-start | bytes 1048576 | tf_op jit(solution)/shard_map/all_to_all | solution.py:77
  209.9 31.1 %collective-permute-start.21 = (bf16[16,4096]{1,0:T(8,128)(2,1)S(1)}, bf16[16,4096]{1,0:T(8,128)(2,1)S(1)}, u32[]{:S(2)}, u32[]{:S(2)}) collective-permute-start(bf16[16,4096]{1,0:T(8,128)(2,1)S(1)} %get-tuple-element.10), channel_id=1, source_target_pairs={{0,129},{1,128},{128,1},{129,0},{2,131},{3,130},{130,3},{131,2},{4... | collective-permute-start | bytes 393224 | tf_op jit(solution)/shard_map/ppermute | solution.py:136
  215.4 25.6 %collective-permute-start.20 = (bf16[16,4096]{1,0:T(8,128)(2,1)S(1)}, bf16[16,4096]{1,0:T(8,128)(2,1)S(1)}, u32[]{:S(2)}, u32[]{:S(2)}) collective-permute-start(bf16[16,4096]{1,0:T(8,128)(2,1)S(1)} %get-tuple-element.9), channel_id=1, source_target_pairs={{0,128},{1,129},{128,0},{129,1},{2,130},{3,131},{130,2},{131,3},{4... | collective-permute-start | bytes 393224 | tf_op jit(solution)/shard_map/ppermute | solution.py:136
  232.3 24.0 %collective-permute-start.9 = (bf16[16,4096]{1,0:T(8,128)(2,1)S(1)}, bf16[16,4096]{1,0:T(8,128)(2,1)S(1)}, u32[]{:S(2)}, u32[]{:S(2)}) collective-permute-start(bf16[16,4096]{1,0:T(8,128)(2,1)S(1)} %slice.35), channel_id=1, source_target_pairs={{0,1},{1,0},{128,129},{129,128},{2,3},{3,2},{130,131},{131,130},{4... | collective-permute-start | bytes 393224 | tf_op jit(solution)/shard_map/ppermute | solution.py:136
  (5 other events, 176.9 us)

commit v8 on v7

--- a/solution.py
+++ b/solution.py
@@ -112,7 +112,10 @@
     n_sec, n_q, n_zh = (lax.axis_size(a) for a in ("section", "q2", "zh"))
     n_local = experts // n_q
     home_q = lax.axis_index("q2")
-    offsets = [(a, c) for a in range(n_q) for c in range(n_zh) if (a, c) != (0, 0)]
+    offsets = sorted(
+        ((a, c) for a in range(n_q) for c in range(n_zh) if (a, c) != (0, 0)),
+        key=lambda step: (step[1], -step[0]),
+    )
     rows = [normalize(arrived, norm_gain[0])]
     picks = [expert_ids[0]]
     for a, c in offsets:

time: 262 us -> 261 us (level)
  the two profiles are of different devices: /device:TPU:57 before, /device:TPU:1 now
where the time goes in v8:
time: 261 us; the launch traced here: 256 us
  starting transfers between devices  125 us (48%)
  waiting for transfers between devices  66.1 us (25%)
  matrix products  32.8 us (13%)
  blocking collectives  19.6 us (8%)
  local copies, waits for them, and re-layouts  8.19 us (3%)
  other arithmetic  3.68 us (1%)
    ppermute x14, starting transfers between devices, passed_along(): return lax.ppermute(value, axis, pairs)  51 us
    ppermute x14, waiting for transfers between devices, passed_along(): return lax.ppermute(value, axis, pairs)  31.3 us
    dot_general x8, matrix products, expert_pass(): jnp.dot(hidden, w_second, preferred_element_type=jnp.float32)  30.1 us
    ppermute x3, starting transfers between devices, on_device(): lax.ppermute(expert_ids[0], ('q2', 'zh'), shifted_pairs((n_q, n_zh), (a,...  22.3 us
    all_to_all x1, blocking collectives, expert_pass(): lax.all_to_all(slot_grid, QUARTER, split_axis=1, concat_axis=1, tiled=True)  19.6 us
    ppermute x3, waiting for transfers between devices, on_device(): lax.ppermute(sent, ('section', 'q2', 'zh'), shifted_pairs((n_sec, n_q, n_...  18.5 us
    ppermute x3, starting transfers between devices, on_device(): lax.ppermute(sums[j].astype(jnp.bfloat16), ('q2', 'zh'), home)  16.5 us
    ppermute x3, starting transfers between devices, on_device(): lax.ppermute(sent, ('section', 'q2', 'zh'), shifted_pairs((n_sec, n_q, n_...  16.4 us
  transfers between devices with their start and end apart: 26, of which 12 were waited for; matrix products, arithmetic and copies ran while one was open for 15% of the time, Pallas kernels for 0%

profile of v8, /device:TPU:1, one launch (start us, length us, event | category | flops | bytes accessed | tf_op | source)
XLA Modules:
  0.0 255.5 jit_solution(2713185671874995278)
XLA Ops:
  0.0 9.8 %collective-permute-start.1 = (s32[16,2]{0,1:T(2,128)}, s32[16,2]{0,1:T(2,128)S(1)}, u32[]{:S(2)}, u32[]{:S(2)}) collective-permute-start(s32[16,2]{0,1:T(2,128)} %bitcast.168), channel_id=1, source_target_pairs={{0,128},{1,129},{128,0},{129,1},{2,130},{3,131},{130,2},{131,3},{4... | collective-permute-start | bytes 392 | tf_op jit(solution)/shard_map/ppermute | solution.py:124
  9.8 10.6 %collective-permute-start.11 = (s32[16,2]{0,1:T(2,128)}, s32[16,2]{0,1:T(2,128)S(1)}, u32[]{:S(2)}, u32[]{:S(2)}) collective-permute-start(s32[16,2]{0,1:T(2,128)} %bitcast.169), channel_id=1, source_target_pairs={{0,1},{1,0},{128,129},{129,128},{2,3},{3,2},{130,131},{131,130},{4... | collective-permute-start | bytes 392 | tf_op jit(solution)/shard_map/ppermute | solution.py:124
  25.9 4.6 %collective-permute-start.2 = (bf16[1,16,4096]{2,1,0:T(8,128)(2,1)}, bf16[1,16,4096]{2,1,0:T(8,128)(2,1)S(1)}, u32[]{:S(2)}, u32[]{:S(2)}) collective-permute-start(bf16[1,16,4096]{2,1,0:T(8,128)(2,1)} %param.6), channel_id=1, source_target_pairs={{0,384},{1,385},{128,256},{129,257},{256,128},{257,129},{384,0},{3... | collective-permute-start | bytes 393224 | tf_op jit(solution)/shard_map/ppermute | solution.py:122
  30.6 7.9 %collective-permute-start.12 = (bf16[1,16,4096]{2,1,0:T(8,128)(2,1)}, bf16[1,16,4096]{2,1,0:T(8,128)(2,1)S(1)}, u32[]{:S(2)}, u32[]{:S(2)}) collective-permute-start(bf16[1,16,4096]{2,1,0:T(8,128)(2,1)} %param.6), channel_id=1, source_target_pairs={{0,385},{1,384},{128,257},{129,256},{256,129},{257,128},{384,1},{3... | collective-permute-start | bytes 393224 | tf_op jit(solution)/shard_map/ppermute | solution.py:122
  46.1 17.5 %collective-permute-done.13 = bf16[1,16,4096]{2,1,0:T(8,128)(2,1)S(1)} collective-permute-done((bf16[1,16,4096]{2,1,0:T(8,128)(2,1)}, bf16[1,16,4096]{2,1,0:T(8,128)(2,1)S(1)}, u32[]{:S(2)}, u32[]{:S(2)}) %collective-permute-start.13) | collective-permute-done | bytes 131104 | tf_op jit(solution)/shard_map/ppermute | solution.py:122
  67.4 19.6 %all_to_all.20 = bf16[4,16,4096]{2,0,1:T(4,128)(2,1)S(1)} all-to-all(bf16[4,16,4096]{2,0,1:T(4,128)(2,1)S(1)} %copy.66), channel_id=1, replica_groups=mesh['section'=2,'q2'=2,'r'=4,'x'=4,'y'=4,'zh'=2] {'r','x'}, dimensions={1} | all-to-all | bytes 1048576 | tf_op jit(solution)/shard_map/all_to_all | solution.py:65
  87.3 4.6 %collective-permute-start.18 = (bf16[4,16,4096]{2,1,0:T(8,128)(2,1)S(1)}, bf16[4,16,4096]{2,1,0:T(8,128)(2,1)}, u32[]{:S(2)}, u32[]{:S(2)}) collective-permute-start(bf16[4,16,4096]{2,1,0:T(8,128)(2,1)S(1)} %copy.67), channel_id=1, source_target_pairs={{0,6},{2,0},{4,2},{6,4},{1,7},{3,1},{5,3},{7,5},{8,14},{10,8},{12,... | collective-permute-start | bytes 1572872 | tf_op jit(solution)/shard_map/ppermute | solution.py:14
  93.4 4.6 %all-to-all-start = ((bf16[4,16,4096]{2,0,1:T(4,128)(2,1)}), bf16[4,16,4096]{2,0,1:T(4,128)(2,1)S(1)}, u32[]{:S(2)}, u32[]{:S(2)}) async-start(bf16[4,16,4096]{2,0,1:T(4,128)(2,1)} %copy.57), calls=%async_computation | async-start | bytes 1048576 | tf_op jit(solution)/shard_map/all_to_all | solution.py:65
  103.0 4.0 %convolution_convert_fusion.2 = bf16[64,4096]{1,0:T(8,128)(2,1)} fusion(bf16[1,1,256,4096]{3,2,1,0:T(8,128)(2,1)S(1)} %copy-done, bf16[64,4096]{1,0:T(8,128)(2,1)} %bitcast.28, bf16[1,1,4096,256]{3,2,1,0:T(8,128)(2,1)} %param.9), kind=kOutput, calls=%fused_computation.2 | convolution fusion | flops 268845056 | bytes 5242880 | tf_op jit(solution)/shard_map/dot_general | solution.py:72
  119.3 7.4 %collective-permute-done.14 = bf16[4,16,4096]{2,1,0:T(8,128)(2,1)} collective-permute-done((bf16[4,16,4096]{2,1,0:T(8,128)(2,1)S(1)}, bf16[4,16,4096]{2,1,0:T(8,128)(2,1)}, u32[]{:S(2)}, u32[]{:S(2)}) %collective-permute-start.14) | collective-permute-done | bytes 524320 | tf_op jit(solution)/shard_map/ppermute | solution.py:14
  126.7 4.0 %convolution_convert_fusion.4 = bf16[64,4096]{1,0:T(8,128)(2,1)} fusion(bf16[1,1,256,4096]{3,2,1,0:T(8,128)(2,1)S(1)} %copy-done, bf16[64,4096]{1,0:T(8,128)(2,1)} %bitcast.26, bf16[1,1,4096,256]{3,2,1,0:T(8,128)(2,1)} %param.9), kind=kOutput, calls=%fused_computation.4 | convolution fusion | flops 268845056 | bytes 5242880 | tf_op jit(solution)/shard_map/dot_general | solution.py:72
  136.2 4.5 %collective-permute-start.5 = (bf16[4,16,4096]{2,1,0:T(8,128)(2,1)}, bf16[4,16,4096]{2,1,0:T(8,128)(2,1)}, u32[]{:S(2)}, u32[]{:S(2)}) collective-permute-start(bf16[4,16,4096]{2,1,0:T(8,128)(2,1)} %copy.58), channel_id=1, source_target_pairs={{0,4},{2,6},{4,0},{6,2},{1,5},{3,7},{5,1},{7,3},{8,12},{10,14},{12... | collective-permute-start | bytes 1572872 | tf_op jit(solution)/shard_map/ppermute | solution.py:14
  142.7 4.1 %collective-permute-done.17 = bf16[64,4096]{1,0:T(8,128)(2,1)} collective-permute-done((bf16[64,4096]{1,0:T(8,128)(2,1)}, bf16[64,4096]{1,0:T(8,128)(2,1)}, u32[]{:S(2)}, u32[]{:S(2)}) %collective-permute-start.17) | collective-permute-done | bytes 524320 | tf_op jit(solution)/shard_map/ppermute | solution.py:14
  151.4 6.6 %all-to-all-start.3 = ((bf16[4,16,4096]{2,0,1:T(4,128)(2,1)}), bf16[4,16,4096]{2,0,1:T(4,128)(2,1)S(1)}, u32[]{:S(2)}, u32[]{:S(2)}) async-start(bf16[4,16,4096]{2,0,1:T(4,128)(2,1)} %copy.71), calls=%async_computation.3 | async-start | bytes 1048576 | tf_op jit(solution)/shard_map/all_to_all | solution.py:77
  167.8 6.8 %collective-permute-start.6 = (bf16[64,4096]{1,0:T(8,128)(2,1)}, bf16[64,4096]{1,0:T(8,128)(2,1)}, u32[]{:S(2)}, u32[]{:S(2)}) collective-permute-start(bf16[64,4096]{1,0:T(8,128)(2,1)} %convolution_convert_fusion.7), channel_id=1, source_target_pairs={{0,4},{2,6},{4,0},{6,2},{1,5},{3,7},{5,1},{7,3},{8,12},{10,14},{12... | collective-permute-start | bytes 1572872 | tf_op jit(solution)/shard_map/ppermute | solution.py:14
  174.5 4.0 %convolution_convert_fusion.8 = bf16[64,4096]{1,0:T(8,128)(2,1)} fusion(bf16[1,1,256,4096]{3,2,1,0:T(8,128)(2,1)S(1)} %copy-done, bf16[64,4096]{1,0:T(8,128)(2,1)} %bitcast.13, bf16[1,1,4096,256]{3,2,1,0:T(8,128)(2,1)} %param.9), kind=kOutput, calls=%fused_computation.9 | convolution fusion | flops 268845056 | bytes 5242880 | tf_op jit(solution)/shard_map/dot_general | solution.py:72
  178.5 5.1 %collective-permute-start.4 = (bf16[64,4096]{1,0:T(8,128)(2,1)}, bf16[64,4096]{1,0:T(8,128)(2,1)S(1)}, u32[]{:S(2)}, u32[]{:S(2)}) collective-permute-start(bf16[64,4096]{1,0:T(8,128)(2,1)} %convolution_convert_fusion.8), channel_id=1, source_target_pairs={{0,6},{2,0},{4,2},{6,4},{1,7},{3,1},{5,3},{7,5},{8,14},{10,8},{12,... | collective-permute-start | bytes 1572872 | tf_op jit(solution)/shard_map/ppermute | solution.py:14
  183.6 7.1 %collective-permute-done.6 = bf16[64,4096]{1,0:T(8,128)(2,1)} collective-permute-done((bf16[64,4096]{1,0:T(8,128)(2,1)}, bf16[64,4096]{1,0:T(8,128)(2,1)}, u32[]{:S(2)}, u32[]{:S(2)}) %collective-permute-start.6) | collective-permute-done | bytes 524320 | tf_op jit(solution)/shard_map/ppermute | solution.py:14
  190.7 9.0 %collective-permute-done.4 = bf16[64,4096]{1,0:T(8,128)(2,1)S(1)} collective-permute-done((bf16[64,4096]{1,0:T(8,128)(2,1)}, bf16[64,4096]{1,0:T(8,128)(2,1)S(1)}, u32[]{:S(2)}, u32[]{:S(2)}) %collective-permute-start.4) | collective-permute-done | bytes 524320 | tf_op jit(solution)/shard_map/ppermute | solution.py:14
  205.3 7.2 %all-to-all-start.1 = ((bf16[4,16,4096]{2,0,1:T(4,128)(2,1)}), bf16[4,16,4096]{2,0,1:T(4,128)(2,1)S(1)}, u32[]{:S(2)}, u32[]{:S(2)}) async-start(bf16[4,16,4096]{2,0,1:T(4,128)(2,1)} %copy.62), calls=%async_computation.1 | async-start | bytes 1048576 | tf_op jit(solution)/shard_map/all_to_all | solution.py:77
  213.2 9.5 %collective-permute-start.21 = (bf16[16,4096]{1,0:T(8,128)(2,1)S(1)}, bf16[16,4096]{1,0:T(8,128)(2,1)S(1)}, u32[]{:S(2)}, u32[]{:S(2)}) collective-permute-start(bf16[16,4096]{1,0:T(8,128)(2,1)S(1)} %get-tuple-element.10), channel_id=1, source_target_pairs={{0,1},{1,0},{128,129},{129,128},{2,3},{3,2},{130,131},{131,130},{4... | collective-permute-start | bytes 393224 | tf_op jit(solution)/shard_map/ppermute | solution.py:139
  226.4 4.8 %collective-permute-start.9 = (bf16[16,4096]{1,0:T(8,128)(2,1)S(1)}, bf16[16,4096]{1,0:T(8,128)(2,1)S(1)}, u32[]{:S(2)}, u32[]{:S(2)}) collective-permute-start(bf16[16,4096]{1,0:T(8,128)(2,1)S(1)} %slice.35), channel_id=1, source_target_pairs={{0,128},{1,129},{128,0},{129,1},{2,130},{3,131},{130,2},{131,3},{4... | collective-permute-start | bytes 393224 | tf_op jit(solution)/shard_map/ppermute | solution.py:139
  232.2 14.5 %collective-permute-done.20 = bf16[16,4096]{1,0:T(8,128)(2,1)S(1)} collective-permute-done((bf16[16,4096]{1,0:T(8,128)(2,1)S(1)}, bf16[16,4096]{1,0:T(8,128)(2,1)S(1)}, u32[]{:S(2)}, u32[]{:S(2)}) %collective-permute-start.20) | collective-permute-done | bytes 131104 | tf_op jit(solution)/shard_map/ppermute | solution.py:139
  246.8 7.1 %collective-permute-start.22 = (bf16[1,16,4096]{2,1,0:T(8,128)(2,1)S(1)}, bf16[1,16,4096]{2,1,0:T(8,128)(2,1)S(1)}, u32[]{:S(2)}, u32[]{:S(2)}) collective-permute-start(bf16[1,16,4096]{2,1,0:T(8,128)(2,1)S(1)} %fusion.46), channel_id=1, source_target_pairs={{0,256},{256,0},{1,257},{257,1},{2,258},{258,2},{3,259},{259,3},{4... | collective-permute-start | bytes 393224 | tf_op jit(solution)/shard_map/ppermute | solution.py:14
  (101 shorter events, 70.1 us)
Async XLA Ops:
  0.0 30.6 %collective-permute-start.1 = (s32[16,2]{0,1:T(2,128)}, s32[16,2]{0,1:T(2,128)S(1)}, u32[]{:S(2)}, u32[]{:S(2)}) collective-permute-start(s32[16,2]{0,1:T(2,128)} %bitcast.168), channel_id=1, source_target_pairs={{0,128},{1,129},{128,0},{129,1},{2,130},{3,131},{130,2},{131,3},{4... | collective-permute-start | bytes 392 | tf_op jit(solution)/shard_map/ppermute | solution.py:124
  9.8 30.2 %collective-permute-start.11 = (s32[16,2]{0,1:T(2,128)}, s32[16,2]{0,1:T(2,128)S(1)}, u32[]{:S(2)}, u32[]{:S(2)}) collective-permute-start(s32[16,2]{0,1:T(2,128)} %bitcast.169), channel_id=1, source_target_pairs={{0,1},{1,0},{128,129},{129,128},{2,3},{3,2},{130,131},{131,130},{4... | collective-permute-start | bytes 392 | tf_op jit(solution)/shard_map/ppermute | solution.py:124
  20.4 23.4 %collective-permute-start.10 = (s32[16,2]{0,1:T(2,128)}, s32[16,2]{0,1:T(2,128)S(1)}, u32[]{:S(2)}, u32[]{:S(2)}) collective-permute-start(s32[16,2]{0,1:T(2,128)} %bitcast.170), channel_id=1, source_target_pairs={{0,129},{1,128},{128,1},{129,0},{2,131},{3,130},{130,3},{131,2},{4... | collective-permute-start | bytes 392 | tf_op jit(solution)/shard_map/ppermute | solution.py:124
  22.3 22.3 %collective-permute-start = (bf16[1,16,4096]{2,1,0:T(8,128)(2,1)}, bf16[1,16,4096]{2,1,0:T(8,128)(2,1)S(1)}, u32[]{:S(2)}, u32[]{:S(2)}) collective-permute-start(bf16[1,16,4096]{2,1,0:T(8,128)(2,1)} %param.6), channel_id=1, source_target_pairs={{0,256},{256,0},{1,257},{257,1},{2,258},{258,2},{3,259},{259,3},{4... | collective-permute-start | bytes 393224 | tf_op jit(solution)/shard_map/ppermute | solution.py:14
  25.9 19.8 %collective-permute-start.2 = (bf16[1,16,4096]{2,1,0:T(8,128)(2,1)}, bf16[1,16,4096]{2,1,0:T(8,128)(2,1)S(1)}, u32[]{:S(2)}, u32[]{:S(2)}) collective-permute-start(bf16[1,16,4096]{2,1,0:T(8,128)(2,1)} %param.6), channel_id=1, source_target_pairs={{0,384},{1,385},{128,256},{129,257},{256,128},{257,129},{384,0},{3... | collective-permute-start | bytes 393224 | tf_op jit(solution)/shard_map/ppermute | solution.py:122
  30.6 15.3 %collective-permute-start.12 = (bf16[1,16,4096]{2,1,0:T(8,128)(2,1)}, bf16[1,16,4096]{2,1,0:T(8,128)(2,1)S(1)}, u32[]{:S(2)}, u32[]{:S(2)}) collective-permute-start(bf16[1,16,4096]{2,1,0:T(8,128)(2,1)} %param.6), channel_id=1, source_target_pairs={{0,385},{1,384},{128,257},{129,256},{256,129},{257,128},{384,1},{3... | collective-permute-start | bytes 393224 | tf_op jit(solution)/shard_map/ppermute | solution.py:122
  40.0 23.6 %collective-permute-start.13 = (bf16[1,16,4096]{2,1,0:T(8,128)(2,1)}, bf16[1,16,4096]{2,1,0:T(8,128)(2,1)S(1)}, u32[]{:S(2)}, u32[]{:S(2)}) collective-permute-start(bf16[1,16,4096]{2,1,0:T(8,128)(2,1)} %param.6), channel_id=1, source_target_pairs={{0,257},{1,256},{128,385},{129,384},{256,1},{257,0},{384,129},{385... | collective-permute-start | bytes 393224 | tf_op jit(solution)/shard_map/ppermute | solution.py:122
  87.3 15.7 %collective-permute-start.18 = (bf16[4,16,4096]{2,1,0:T(8,128)(2,1)S(1)}, bf16[4,16,4096]{2,1,0:T(8,128)(2,1)}, u32[]{:S(2)}, u32[]{:S(2)}) collective-permute-start(bf16[4,16,4096]{2,1,0:T(8,128)(2,1)S(1)} %copy.67), channel_id=1, source_target_pairs={{0,6},{2,0},{4,2},{6,4},{1,7},{3,1},{5,3},{7,5},{8,14},{10,8},{12,... | collective-permute-start | bytes 1572872 | tf_op jit(solution)/shard_map/ppermute | solution.py:14
  93.4 39.1 %all-to-all-start = ((bf16[4,16,4096]{2,0,1:T(4,128)(2,1)}), bf16[4,16,4096]{2,0,1:T(4,128)(2,1)S(1)}, u32[]{:S(2)}, u32[]{:S(2)}) async-start(bf16[4,16,4096]{2,0,1:T(4,128)(2,1)} %copy.57), calls=%async_computation | async-start | bytes 1048576 | tf_op jit(solution)/shard_map/all_to_all | solution.py:65
  100.3 26.3 %collective-permute-start.14 = (bf16[4,16,4096]{2,1,0:T(8,128)(2,1)S(1)}, bf16[4,16,4096]{2,1,0:T(8,128)(2,1)}, u32[]{:S(2)}, u32[]{:S(2)}) collective-permute-start(bf16[4,16,4096]{2,1,0:T(8,128)(2,1)S(1)} %copy.67), channel_id=1, source_target_pairs={{0,2},{2,4},{4,6},{6,0},{1,3},{3,5},{5,7},{7,1},{8,10},{10,12},{12... | collective-permute-start | bytes 1572872 | tf_op jit(solution)/shard_map/ppermute | solution.py:14
  107.0 33.8 %collective-permute-start.19 = (bf16[64,4096]{1,0:T(8,128)(2,1)}, bf16[64,4096]{1,0:T(8,128)(2,1)}, u32[]{:S(2)}, u32[]{:S(2)}) collective-permute-start(bf16[64,4096]{1,0:T(8,128)(2,1)} %convolution_convert_fusion.2), channel_id=1, source_target_pairs={{0,2},{2,4},{4,6},{6,0},{1,3},{3,5},{5,7},{7,1},{8,10},{10,12},{12... | collective-permute-start | bytes 1572872 | tf_op jit(solution)/shard_map/ppermute | solution.py:14
  117.0 29.7 %collective-permute-start.17 = (bf16[64,4096]{1,0:T(8,128)(2,1)}, bf16[64,4096]{1,0:T(8,128)(2,1)}, u32[]{:S(2)}, u32[]{:S(2)}) collective-permute-start(bf16[64,4096]{1,0:T(8,128)(2,1)} %convolution_convert_fusion.3), channel_id=1, source_target_pairs={{0,4},{2,6},{4,0},{6,2},{1,5},{3,7},{5,1},{7,3},{8,12},{10,14},{12... | collective-permute-start | bytes 1572872 | tf_op jit(solution)/shard_map/ppermute | solution.py:14
  130.7 16.1 %collective-permute-start.15 = (bf16[64,4096]{1,0:T(8,128)(2,1)}, bf16[64,4096]{1,0:T(8,128)(2,1)}, u32[]{:S(2)}, u32[]{:S(2)}) collective-permute-start(bf16[64,4096]{1,0:T(8,128)(2,1)} %convolution_convert_fusion.4), channel_id=1, source_target_pairs={{0,6},{2,0},{4,2},{6,4},{1,7},{3,1},{5,3},{7,5},{8,14},{10,8},{12,... | collective-permute-start | bytes 1572872 | tf_op jit(solution)/shard_map/ppermute | solution.py:14
  133.7 24.6 %collective-permute-start.7 = (bf16[4,16,4096]{2,1,0:T(8,128)(2,1)}, bf16[4,16,4096]{2,1,0:T(8,128)(2,1)}, u32[]{:S(2)}, u32[]{:S(2)}) collective-permute-start(bf16[4,16,4096]{2,1,0:T(8,128)(2,1)} %copy.58), channel_id=1, source_target_pairs={{0,6},{2,0},{4,2},{6,4},{1,7},{3,1},{5,3},{7,5},{8,14},{10,8},{12,... | collective-permute-start | bytes 1572872 | tf_op jit(solution)/shard_map/ppermute | solution.py:14
  136.2 27.6 %collective-permute-start.5 = (bf16[4,16,4096]{2,1,0:T(8,128)(2,1)}, bf16[4,16,4096]{2,1,0:T(8,128)(2,1)}, u32[]{:S(2)}, u32[]{:S(2)}) collective-permute-start(bf16[4,16,4096]{2,1,0:T(8,128)(2,1)} %copy.58), channel_id=1, source_target_pairs={{0,4},{2,6},{4,0},{6,2},{1,5},{3,7},{5,1},{7,3},{8,12},{10,14},{12... | collective-permute-start | bytes 1572872 | tf_op jit(solution)/shard_map/ppermute | solution.py:14
  140.7 33.8 %collective-permute-start.3 = (bf16[4,16,4096]{2,1,0:T(8,128)(2,1)}, bf16[4,16,4096]{2,1,0:T(8,128)(2,1)}, u32[]{:S(2)}, u32[]{:S(2)}) collective-permute-start(bf16[4,16,4096]{2,1,0:T(8,128)(2,1)} %copy.58), channel_id=1, source_target_pairs={{0,2},{2,4},{4,6},{6,0},{1,3},{3,5},{5,7},{7,1},{8,10},{10,12},{12... | collective-permute-start | bytes 1572872 | tf_op jit(solution)/shard_map/ppermute | solution.py:14
  151.4 53.9 %all-to-all-start.3 = ((bf16[4,16,4096]{2,0,1:T(4,128)(2,1)}), bf16[4,16,4096]{2,0,1:T(4,128)(2,1)S(1)}, u32[]{:S(2)}, u32[]{:S(2)}) async-start(bf16[4,16,4096]{2,0,1:T(4,128)(2,1)} %copy.71), calls=%async_computation.3 | async-start | bytes 1048576 | tf_op jit(solution)/shard_map/all_to_all | solution.py:77
  161.5 22.2 %collective-permute-start.8 = (bf16[64,4096]{1,0:T(8,128)(2,1)S(1)}, bf16[64,4096]{1,0:T(8,128)(2,1)}, u32[]{:S(2)}, u32[]{:S(2)}) collective-permute-start(bf16[64,4096]{1,0:T(8,128)(2,1)S(1)} %convolution_convert_fusion.6), channel_id=1, source_target_pairs={{0,2},{2,4},{4,6},{6,0},{1,3},{3,5},{5,7},{7,1},{8,10},{10,12},{12... | collective-permute-start | bytes 1572872 | tf_op jit(solution)/shard_map/ppermute | solution.py:14
  167.8 23.0 %collective-permute-start.6 = (bf16[64,4096]{1,0:T(8,128)(2,1)}, bf16[64,4096]{1,0:T(8,128)(2,1)}, u32[]{:S(2)}, u32[]{:S(2)}) collective-permute-start(bf16[64,4096]{1,0:T(8,128)(2,1)} %convolution_convert_fusion.7), channel_id=1, source_target_pairs={{0,4},{2,6},{4,0},{6,2},{1,5},{3,7},{5,1},{7,3},{8,12},{10,14},{12... | collective-permute-start | bytes 1572872 | tf_op jit(solution)/shard_map/ppermute | solution.py:14
  178.5 21.2 %collective-permute-start.4 = (bf16[64,4096]{1,0:T(8,128)(2,1)}, bf16[64,4096]{1,0:T(8,128)(2,1)S(1)}, u32[]{:S(2)}, u32[]{:S(2)}) collective-permute-start(bf16[64,4096]{1,0:T(8,128)(2,1)} %convolution_convert_fusion.8), channel_id=1, source_target_pairs={{0,6},{2,0},{4,2},{6,4},{1,7},{3,1},{5,3},{7,5},{8,14},{10,8},{12,... | collective-permute-start | bytes 1572872 | tf_op jit(solution)/shard_map/ppermute | solution.py:14
  205.3 20.4 %all-to-all-start.1 = ((bf16[4,16,4096]{2,0,1:T(4,128)(2,1)}), bf16[4,16,4096]{2,0,1:T(4,128)(2,1)S(1)}, u32[]{:S(2)}, u32[]{:S(2)}) async-start(bf16[4,16,4096]{2,0,1:T(4,128)(2,1)} %copy.62), calls=%async_computation.1 | async-start | bytes 1048576 | tf_op jit(solution)/shard_map/all_to_all | solution.py:77
  213.2 19.0 %collective-permute-start.21 = (bf16[16,4096]{1,0:T(8,128)(2,1)S(1)}, bf16[16,4096]{1,0:T(8,128)(2,1)S(1)}, u32[]{:S(2)}, u32[]{:S(2)}) collective-permute-start(bf16[16,4096]{1,0:T(8,128)(2,1)S(1)} %get-tuple-element.10), channel_id=1, source_target_pairs={{0,1},{1,0},{128,129},{129,128},{2,3},{3,2},{130,131},{131,130},{4... | collective-permute-start | bytes 393224 | tf_op jit(solution)/shard_map/ppermute | solution.py:139
  222.7 24.0 %collective-permute-start.20 = (bf16[16,4096]{1,0:T(8,128)(2,1)S(1)}, bf16[16,4096]{1,0:T(8,128)(2,1)S(1)}, u32[]{:S(2)}, u32[]{:S(2)}) collective-permute-start(bf16[16,4096]{1,0:T(8,128)(2,1)S(1)} %get-tuple-element.9), channel_id=1, source_target_pairs={{0,129},{1,128},{128,1},{129,0},{2,131},{3,130},{130,3},{131,2},{4... | collective-permute-start | bytes 393224 | tf_op jit(solution)/shard_map/ppermute | solution.py:139
  226.4 20.3 %collective-permute-start.9 = (bf16[16,4096]{1,0:T(8,128)(2,1)S(1)}, bf16[16,4096]{1,0:T(8,128)(2,1)S(1)}, u32[]{:S(2)}, u32[]{:S(2)}) collective-permute-start(bf16[16,4096]{1,0:T(8,128)(2,1)S(1)} %slice.35), channel_id=1, source_target_pairs={{0,128},{1,129},{128,0},{129,1},{2,130},{3,131},{130,2},{131,3},{4... | collective-permute-start | bytes 393224 | tf_op jit(solution)/shard_map/ppermute | solution.py:139
  (5 other events, 192.9 us)

commit v9 on v4

--- a/solution.py
+++ b/solution.py
@@ -9,6 +9,11 @@
     count = lax.axis_size(axis)
     pairs = [(source, (source + steps) % count) for source in range(count)]
     return lax.ppermute(value, axis, pairs)
+
+
+def swapped(value, axis, mask):
+    count = lax.axis_size(axis)
+    return lax.ppermute(value, axis, [(source, source ^ mask) for source in range(count)])
 
 
 def normalize(inputs, gain_row):
@@ -57,17 +62,22 @@
     capacity, experts, model_width = slot_grid.shape
     n_y = lax.axis_size("y")
     received = lax.all_to_all(slot_grid, "expert", split_axis=1, concat_axis=1, tiled=True)
-    summed = None
-    for k in range(n_y):
-        rows_in = received if k == 0 else passed_along(received, "y", k)
+    def ffn(rows_in):
         hidden = jax.nn.gelu(
             jnp.dot(rows_in.reshape(-1, model_width), w_first, preferred_element_type=jnp.float32)
         ).astype(jnp.bfloat16)
-        partial = jnp.dot(hidden, w_second, preferred_element_type=jnp.float32).astype(jnp.bfloat16)
-        if k == 0:
-            summed = partial.astype(jnp.float32)
-        else:
-            summed = summed + passed_along(partial, "y", n_y - k).astype(jnp.float32)
+        return jnp.dot(hidden, w_second, preferred_element_type=jnp.float32).astype(jnp.bfloat16)
+
+    near = swapped(received, "y", 1)
+    pair = jnp.stack([received, near])
+    far = swapped(pair, "y", 2)
+    own_part = ffn(received)
+    near_part = ffn(near)
+    far_part = ffn(far).reshape(2, -1, model_width)
+    far_back = swapped(far_part, "y", 2)
+    summed = own_part.astype(jnp.float32) + far_back[0].astype(jnp.float32)
+    near_sum = near_part.astype(jnp.float32) + far_back[1].astype(jnp.float32)
+    summed = summed + swapped(near_sum.astype(jnp.bfloat16), "y", 1).astype(jnp.float32)
     back = lax.all_to_all(
         summed.astype(jnp.bfloat16).reshape(capacity, experts, model_width),
         "expert", split_axis=1, concat_axis=1, tiled=True,

time: 253 us -> 283 us (1.12)
  waiting for transfers between devices: 72.8 us -> 124 us
  starting transfers between devices: 132 us -> 112 us
  matrix products: 35 us -> 28.1 us
  other arithmetic: 1.56 us -> 8.22 us
    ppermute x16 -> x4, starting transfers between devices: 75.1 us -> 25.7 us  [passed_along(): return lax.ppermute(value, axis, pairs)]
    ppermute x0 -> x8, waiting for transfers between devices: none -> 45.8 us  [swapped(): lax.ppermute(value, axis, [(source, source ^ mask) for source in range(co...]
    ppermute x0 -> x8, starting transfers between devices: none -> 28.3 us  [swapped(): lax.ppermute(value, axis, [(source, source ^ mask) for source in range(co...]
    ppermute x16 -> x4, waiting for transfers between devices: 37.5 us -> 9.66 us  [passed_along(): return lax.ppermute(value, axis, pairs)]
    all_to_all x2, waiting for transfers between devices: 24.1 us -> 46.4 us  [expert_pass(): lax.all_to_all(slot_grid, 'expert', split_axis=1, concat_axis=1, tiled=True)]
    all_to_all x2, waiting for transfers between devices: 11.3 us -> 22 us  [expert_pass(): lax.all_to_all(summed.astype(jnp.bfloat16).reshape(capacity, experts, mod...]
    dot_general x8 -> x6, matrix products: 31.5 us -> 24.6 us  [ffn(): jnp.dot(hidden, w_second, preferred_element_type=jnp.float32)]
    convert_element_type x0 -> x2, other arithmetic: none -> 3.35 us  [expert_pass(): summed.astype(jnp.bfloat16).reshape(capacity, experts, model_width)]
  transfers between devices with their start and end apart: 21 -> 17, of which waited for: 9 -> 11; matrix products, arithmetic and copies ran while one was open for 18% -> 16% of each run, Pallas kernels for 0% -> 0%
where the time goes in v9:
time: 283 us; the launch traced here: 282 us
  waiting for transfers between devices  124 us (44%)
  starting transfers between devices  112 us (40%)
  matrix products  28.1 us (10%)
  local copies, waits for them, and re-layouts  9.43 us (3%)
  other arithmetic  8.22 us (3%)
    all_to_all x2, waiting for transfers between devices, expert_pass(): lax.all_to_all(slot_grid, 'expert', split_axis=1, concat_axis=1, tiled=True)  46.4 us
    ppermute x8, waiting for transfers between devices, swapped(): lax.ppermute(value, axis, [(source, source ^ mask) for source in range(co...  45.8 us
    ppermute x8, starting transfers between devices, swapped(): lax.ppermute(value, axis, [(source, source ^ mask) for source in range(co...  28.3 us
    ppermute x4, starting transfers between devices, passed_along(): return lax.ppermute(value, axis, pairs)  25.7 us
    all_to_all x2, starting transfers between devices, expert_pass(): lax.all_to_all(summed.astype(jnp.bfloat16).reshape(capacity, experts, mod...  24.6 us
    dot_general x6, matrix products, ffn(): jnp.dot(hidden, w_second, preferred_element_type=jnp.float32)  24.6 us
    all_to_all x2, waiting for transfers between devices, expert_pass(): lax.all_to_all(summed.astype(jnp.bfloat16).reshape(capacity, experts, mod...  22 us
    ppermute x1, starting transfers between devices, on_device(): partner_arrived = lax.ppermute(sent, ('section', 'zh'), crossed)[0]  17 us
  transfers between devices with their start and end apart: 17, of which 11 were waited for; matrix products, arithmetic and copies ran while one was open for 16% of the time, Pallas kernels for 0%

profile of v9, /device:TPU:1, one launch (start us, length us, event | category | flops | bytes accessed | tf_op | source)
XLA Modules:
  0.0 281.9 jit_solution(14416735692433959844)
XLA Ops:
  0.0 17.0 %collective-permute-start.6 = (bf16[1,16,4096]{2,1,0:T(8,128)(2,1)}, bf16[1,16,4096]{2,1,0:T(8,128)(2,1)S(1)}, u32[]{:S(2)}, u32[]{:S(2)}) collective-permute-start(bf16[1,16,4096]{2,1,0:T(8,128)(2,1)} %param.6), channel_id=1, source_target_pairs={{0,257},{1,256},{256,1},{257,0},{2,259},{3,258},{258,3},{259,2},{4... | collective-permute-start | bytes 393224 | tf_op jit(solution)/shard_map/ppermute | solution.py:105
  18.9 3.9 %collective-permute-start.5 = (s32[16,2]{0,1:T(2,128)}, s32[16,2]{0,1:T(2,128)S(1)}, u32[]{:S(2)}, u32[]{:S(2)}) collective-permute-start(s32[16,2]{0,1:T(2,128)} %bitcast.204), channel_id=1, source_target_pairs={{0,1},{1,0},{2,3},{3,2},{4,5},{5,4},{6,7},{7,6},{8,9},{9,8},{10,11... | collective-permute-start | bytes 392 | tf_op jit(solution)/shard_map/ppermute | solution.py:11
  23.6 8.7 %collective-permute-done.5 = s32[16,2]{0,1:T(2,128)S(1)} collective-permute-done((s32[16,2]{0,1:T(2,128)}, s32[16,2]{0,1:T(2,128)S(1)}, u32[]{:S(2)}, u32[]{:S(2)}) %collective-permute-start.5) | collective-permute-done | bytes 160 | tf_op jit(solution)/shard_map/ppermute | solution.py:11
  36.9 7.6 %all-to-all-start.2 = ((bf16[2,32,4096]{2,0,1:T(2,128)(2,1)}), bf16[2,32,4096]{2,0,1:T(2,128)(2,1)S(1)}, u32[]{:S(2)}, u32[]{:S(2)}) async-start(bf16[2,32,4096]{2,0,1:T(2,128)(2,1)} %copy.47), calls=%async_computation.2 | async-start | bytes 1048576 | tf_op jit(solution)/shard_map/all_to_all | solution.py:64
  45.8 25.4 %all-to-all-done.2 = bf16[2,32,4096]{2,0,1:T(2,128)(2,1)S(1)} async-done(((bf16[2,32,4096]{2,0,1:T(2,128)(2,1)}), bf16[2,32,4096]{2,0,1:T(2,128)(2,1)S(1)}, u32[]{:S(2)}, u32[]{:S(2)}) %all-to-all-start.2) | async-done | bytes 524320 | tf_op jit(solution)/shard_map/all_to_all | solution.py:64
  76.4 8.8 %all-to-all-start = ((bf16[2,32,4096]{2,0,1:T(2,128)(2,1)}), bf16[2,32,4096]{2,0,1:T(2,128)(2,1)}, u32[]{:S(2)}, u32[]{:S(2)}) async-start(bf16[2,32,4096]{2,0,1:T(2,128)(2,1)} %copy.41), calls=%async_computation | async-start | bytes 1048576 | tf_op jit(solution)/shard_map/all_to_all | solution.py:64
  86.4 4.5 %collective-permute-start.8 = (bf16[2,2,32,4096]{3,2,1,0:T(8,128)(2,1)}, bf16[2,2,32,4096]{3,2,1,0:T(8,128)(2,1)}, u32[]{:S(2)}, u32[]{:S(2)}) collective-permute-start(bf16[2,2,32,4096]{3,2,1,0:T(8,128)(2,1)} %pad_maximum_fusion.1), channel_id=1, source_target_pairs={{0,4},{2,6},{4,0},{6,2},{1,5},{3,7},{5,1},{7,3},{8,12},{10,14},{12... | collective-permute-start | bytes 3145736 | tf_op jit(solution)/shard_map/ppermute | solution.py:16
  91.0 21.0 %all-to-all-done = bf16[2,32,4096]{2,0,1:T(2,128)(2,1)} async-done(((bf16[2,32,4096]{2,0,1:T(2,128)(2,1)}), bf16[2,32,4096]{2,0,1:T(2,128)(2,1)}, u32[]{:S(2)}, u32[]{:S(2)}) %all-to-all-start) | async-done | bytes 524320 | tf_op jit(solution)/shard_map/all_to_all | solution.py:64
  115.4 4.2 %convolution_convert_fusion = bf16[128,4096]{1,0:T(8,128)(2,1)} fusion(bf16[1,1,256,4096]{3,2,1,0:T(8,128)(2,1)S(1)} %copy-done, bf16[128,4096]{1,0:T(8,128)(2,1)} %bitcast.35, bf16[1,1,4096,256]{3,2,1,0:T(8,128)(2,1)} %param.9), kind=kOutput, calls=%fused_computation | convolution fusion | flops 537690112 | bytes 6291456 | tf_op jit(solution)/shard_map/dot_general | solution.py:69
  119.6 4.8 %collective-permute-start.9 = (bf16[2,64,4096]{2,1,0:T(8,128)(2,1)}, bf16[2,64,4096]{2,1,0:T(8,128)(2,1)}, u32[]{:S(2)}, u32[]{:S(2)}) collective-permute-start(bf16[2,64,4096]{2,1,0:T(8,128)(2,1)} %bitcast.199), channel_id=1, source_target_pairs={{0,4},{2,6},{4,0},{6,2},{1,5},{3,7},{5,1},{7,3},{8,12},{10,14},{12... | collective-permute-start | bytes 3145736 | tf_op jit(solution)/shard_map/ppermute | solution.py:16
  127.1 4.5 %collective-permute-start.2 = (bf16[2,2,32,4096]{3,2,1,0:T(8,128)(2,1)}, bf16[2,2,32,4096]{3,2,1,0:T(8,128)(2,1)}, u32[]{:S(2)}, u32[]{:S(2)}) collective-permute-start(bf16[2,2,32,4096]{3,2,1,0:T(8,128)(2,1)} %pad_maximum_fusion), channel_id=1, source_target_pairs={{0,4},{2,6},{4,0},{6,2},{1,5},{3,7},{5,1},{7,3},{8,12},{10,14},{12... | collective-permute-start | bytes 3145736 | tf_op jit(solution)/shard_map/ppermute | solution.py:16
  131.6 17.4 %collective-permute-done.9 = bf16[2,64,4096]{2,1,0:T(8,128)(2,1)} collective-permute-done((bf16[2,64,4096]{2,1,0:T(8,128)(2,1)}, bf16[2,64,4096]{2,1,0:T(8,128)(2,1)}, u32[]{:S(2)}, u32[]{:S(2)}) %collective-permute-start.9) | collective-permute-done | bytes 1048608 | tf_op jit(solution)/shard_map/ppermute | solution.py:16
  149.0 4.0 %fusion.25 = bf16[64,4096]{1,0:T(8,128)(2,1)} fusion(bf16[2,64,4096]{2,1,0:T(8,128)(2,1)} %collective-permute-done.9, bf16[1,1,256,4096]{3,2,1,0:T(8,128)(2,1)S(1)} %copy-done, bf16[64,4096]{1,0:T(8,128)(2,1)} %bitcast.197, bf16[1,1,4096,256]{3,2,1,0:T(8,128)(2,1)} %param.9), kind=kOutput, calls=%fused_computation.38 | convolution fusion | flops 269893632 | bytes 5767168 | tf_op jit(solution)/shard_map/dot_general | solution.py:69
  155.8 4.0 %fusion.1 = f32[64,4096]{1,0:T(8,128)} fusion(bf16[1,1,256,4096]{3,2,1,0:T(8,128)(2,1)S(1)} %copy-done, bf16[64,4096]{1,0:T(8,128)(2,1)S(1)} %bitcast.189, bf16[1,1,4096,256]{3,2,1,0:T(8,128)(2,1)} %param.9), kind=kOutput, calls=%fused_computation.5 | convolution fusion | flops 269107200 | bytes 5767168 | tf_op jit(solution)/shard_map/dot_general | solution.py:69
  159.8 11.7 %collective-permute-done.2 = bf16[2,2,32,4096]{3,2,1,0:T(8,128)(2,1)} collective-permute-done((bf16[2,2,32,4096]{3,2,1,0:T(8,128)(2,1)}, bf16[2,2,32,4096]{3,2,1,0:T(8,128)(2,1)}, u32[]{:S(2)}, u32[]{:S(2)}) %collective-permute-start.2) | collective-permute-done | bytes 1048608 | tf_op jit(solution)/shard_map/ppermute | solution.py:16
  171.5 4.2 %convolution_convert_fusion.1 = bf16[128,4096]{1,0:T(8,128)(2,1)} fusion(bf16[1,1,256,4096]{3,2,1,0:T(8,128)(2,1)S(1)} %copy-done, bf16[128,4096]{1,0:T(8,128)(2,1)} %bitcast.16, bf16[1,1,4096,256]{3,2,1,0:T(8,128)(2,1)} %param.9), kind=kOutput, calls=%fused_computation.1 | convolution fusion | flops 537690112 | bytes 6291456 | tf_op jit(solution)/shard_map/dot_general | solution.py:69
  185.6 10.2 %all-to-all-start.3 = ((bf16[2,32,4096]{2,0,1:T(2,128)(2,1)}), bf16[2,32,4096]{2,0,1:T(2,128)(2,1)S(1)}, u32[]{:S(2)}, u32[]{:S(2)}) async-start(bf16[2,32,4096]{2,0,1:T(2,128)(2,1)} %copy.51), calls=%async_computation.3 | async-start | bytes 1048576 | tf_op jit(solution)/shard_map/all_to_all | solution.py:81
  195.8 9.1 %collective-permute-done.3 = bf16[2,64,4096]{2,1,0:T(8,128)(2,1)} collective-permute-done((bf16[2,64,4096]{2,1,0:T(8,128)(2,1)}, bf16[2,64,4096]{2,1,0:T(8,128)(2,1)}, u32[]{:S(2)}, u32[]{:S(2)}) %collective-permute-start.3) | collective-permute-done | bytes 1048608 | tf_op jit(solution)/shard_map/ppermute | solution.py:16
  204.9 4.1 %fusion.28 = bf16[64,4096]{1,0:T(8,128)(2,1)} fusion(bf16[2,64,4096]{2,1,0:T(8,128)(2,1)} %collective-permute-done.3, bf16[1,1,256,4096]{3,2,1,0:T(8,128)(2,1)S(1)} %copy-done, bf16[64,4096]{1,0:T(8,128)(2,1)} %bitcast.19, bf16[1,1,4096,256]{3,2,1,0:T(8,128)(2,1)} %param.9), kind=kOutput, calls=%fused_computation.43 | convolution fusion | flops 269893632 | bytes 5767168 | tf_op jit(solution)/shard_map/dot_general | solution.py:69
  211.9 4.0 %fusion.3 = f32[64,4096]{1,0:T(8,128)} fusion(bf16[1,1,256,4096]{3,2,1,0:T(8,128)(2,1)S(1)} %copy-done, bf16[64,4096]{1,0:T(8,128)(2,1)S(1)} %bitcast.187, bf16[1,1,4096,256]{3,2,1,0:T(8,128)(2,1)} %param.9), kind=kOutput, calls=%fused_computation.10 | convolution fusion | flops 269107200 | bytes 5767168 | tf_op jit(solution)/shard_map/dot_general | solution.py:69
  222.7 14.4 %all-to-all-start.1 = ((bf16[2,32,4096]{2,0,1:T(2,128)(2,1)}), bf16[2,32,4096]{2,0,1:T(2,128)(2,1)S(1)}, u32[]{:S(2)}, u32[]{:S(2)}) async-start(bf16[2,32,4096]{2,0,1:T(2,128)(2,1)} %copy.45), calls=%async_computation.1 | async-start | bytes 1048576 | tf_op jit(solution)/shard_map/all_to_all | solution.py:81
  237.8 9.1 %collective-permute-start.11 = (bf16[16,4096]{1,0:T(8,128)(2,1)S(1)}, bf16[16,4096]{1,0:T(8,128)(2,1)S(1)}, u32[]{:S(2)}, u32[]{:S(2)}) collective-permute-start(bf16[16,4096]{1,0:T(8,128)(2,1)S(1)} %convolution_convert_fusion.8), channel_id=1, source_target_pairs={{0,1},{1,0},{2,3},{3,2},{4,5},{5,4},{6,7},{7,6},{8,9},{9,8},{10,11... | collective-permute-start | bytes 393224 | tf_op jit(solution)/shard_map/ppermute | solution.py:11
  246.9 22.0 %all-to-all-done.1 = bf16[2,32,4096]{2,0,1:T(2,128)(2,1)S(1)} async-done(((bf16[2,32,4096]{2,0,1:T(2,128)(2,1)}), bf16[2,32,4096]{2,0,1:T(2,128)(2,1)S(1)}, u32[]{:S(2)}, u32[]{:S(2)}) %all-to-all-start.1) | async-done | bytes 524320 | tf_op jit(solution)/shard_map/all_to_all | solution.py:81
  269.5 10.7 %collective-permute-start.12 = (bf16[1,16,4096]{2,1,0:T(8,128)(2,1)S(1)}, bf16[1,16,4096]{2,1,0:T(8,128)(2,1)S(1)}, u32[]{:S(2)}, u32[]{:S(2)}) collective-permute-start(bf16[1,16,4096]{2,1,0:T(8,128)(2,1)S(1)} %fusion.6), channel_id=1, source_target_pairs={{0,256},{256,0},{1,257},{257,1},{2,258},{258,2},{3,259},{259,3},{4... | collective-permute-start | bytes 393224 | tf_op jit(solution)/shard_map/ppermute | solution.py:11
  (75 shorter events, 46.0 us)
Async XLA Ops:
  0.0 115.4 %copy-start = (bf16[1,1,256,4096]{3,2,1,0:T(8,128)(2,1)S(1)}, bf16[1,1,256,4096]{3,2,1,0:T(8,128)(2,1)}, u32[]{:S(2)}) copy-start(bf16[1,1,256,4096]{3,2,1,0:T(8,128)(2,1)} %param.10) | copy-start | bytes 6291460
  0.0 45.0 %copy-start.4 = (s32[1,16,2]{1,2,0:T(2,128)S(1)}, s32[1,16,2]{1,2,0:T(2,128)}, u32[]{:S(2)}) copy-start(s32[1,16,2]{1,2,0:T(2,128)} %param.11) | copy-start | bytes 388
  0.0 45.2 %copy-start.3 = (f32[1,4096]{1,0:T(1,128)S(1)}, f32[1,4096]{1,0:T(1,128)}, u32[]{:S(2)}) copy-start(f32[1,4096]{1,0:T(1,128)} %param.7) | copy-start | bytes 49156
  0.0 45.2 %copy-start.2 = (bf16[1,4096,32]{1,2,0:T(8,128)(2,1)S(1)}, bf16[1,4096,32]{1,2,0:T(8,128)(2,1)}, u32[]{:S(2)}) copy-start(bf16[1,4096,32]{1,2,0:T(8,128)(2,1)} %param.8) | copy-start | bytes 786436
  0.0 32.8 %collective-permute-start.6 = (bf16[1,16,4096]{2,1,0:T(8,128)(2,1)}, bf16[1,16,4096]{2,1,0:T(8,128)(2,1)S(1)}, u32[]{:S(2)}, u32[]{:S(2)}) collective-permute-start(bf16[1,16,4096]{2,1,0:T(8,128)(2,1)} %param.6), channel_id=1, source_target_pairs={{0,257},{1,256},{256,1},{257,0},{2,259},{3,258},{258,3},{259,2},{4... | collective-permute-start | bytes 393224 | tf_op jit(solution)/shard_map/ppermute | solution.py:105
  17.0 28.1 %collective-permute-start = (bf16[1,16,4096]{2,1,0:T(8,128)(2,1)}, bf16[1,16,4096]{2,1,0:T(8,128)(2,1)S(1)}, u32[]{:S(2)}, u32[]{:S(2)}) collective-permute-start(bf16[1,16,4096]{2,1,0:T(8,128)(2,1)} %param.6), channel_id=1, source_target_pairs={{0,256},{256,0},{1,257},{257,1},{2,258},{258,2},{3,259},{259,3},{4... | collective-permute-start | bytes 393224 | tf_op jit(solution)/shard_map/ppermute | solution.py:11
  18.9 13.3 %collective-permute-start.5 = (s32[16,2]{0,1:T(2,128)}, s32[16,2]{0,1:T(2,128)S(1)}, u32[]{:S(2)}, u32[]{:S(2)}) collective-permute-start(s32[16,2]{0,1:T(2,128)} %bitcast.204), channel_id=1, source_target_pairs={{0,1},{1,0},{2,3},{3,2},{4,5},{5,4},{6,7},{7,6},{8,9},{9,8},{10,11... | collective-permute-start | bytes 392 | tf_op jit(solution)/shard_map/ppermute | solution.py:11
  36.9 34.3 %all-to-all-start.2 = ((bf16[2,32,4096]{2,0,1:T(2,128)(2,1)}), bf16[2,32,4096]{2,0,1:T(2,128)(2,1)S(1)}, u32[]{:S(2)}, u32[]{:S(2)}) async-start(bf16[2,32,4096]{2,0,1:T(2,128)(2,1)} %copy.47), calls=%async_computation.2 | async-start | bytes 1048576 | tf_op jit(solution)/shard_map/all_to_all | solution.py:64
  71.5 13.7 %collective-permute-start.7 = (bf16[2,32,4096]{2,1,0:T(8,128)(2,1)S(1)}, bf16[2,32,4096]{2,1,0:T(8,128)(2,1)S(1)}, u32[]{:S(2)}, u32[]{:S(2)}) collective-permute-start(bf16[2,32,4096]{2,1,0:T(8,128)(2,1)S(1)} %copy.57), channel_id=1, source_target_pairs={{0,2},{2,0},{4,6},{6,4},{1,3},{3,1},{5,7},{7,5},{8,10},{10,8},{12,... | collective-permute-start | bytes 1572872 | tf_op jit(solution)/shard_map/ppermute | solution.py:16
  76.4 35.5 %all-to-all-start = ((bf16[2,32,4096]{2,0,1:T(2,128)(2,1)}), bf16[2,32,4096]{2,0,1:T(2,128)(2,1)}, u32[]{:S(2)}, u32[]{:S(2)}) async-start(bf16[2,32,4096]{2,0,1:T(2,128)(2,1)} %copy.41), calls=%async_computation | async-start | bytes 1048576 | tf_op jit(solution)/shard_map/all_to_all | solution.py:64
  85.2 5.7 %copy-start.1 = (bf16[2,32,4096]{2,1,0:T(8,128)(2,1)}, bf16[2,32,4096]{2,1,0:T(8,128)(2,1)S(1)}, u32[]{:S(2)}) copy-start(bf16[2,32,4096]{2,1,0:T(8,128)(2,1)S(1)} %collective-permute-done.7) | copy-start | bytes 1572868
  86.4 28.9 %collective-permute-start.8 = (bf16[2,2,32,4096]{3,2,1,0:T(8,128)(2,1)}, bf16[2,2,32,4096]{3,2,1,0:T(8,128)(2,1)}, u32[]{:S(2)}, u32[]{:S(2)}) collective-permute-start(bf16[2,2,32,4096]{3,2,1,0:T(8,128)(2,1)} %pad_maximum_fusion.1), channel_id=1, source_target_pairs={{0,4},{2,6},{4,0},{6,2},{1,5},{3,7},{5,1},{7,3},{8,12},{10,14},{12... | collective-permute-start | bytes 3145736 | tf_op jit(solution)/shard_map/ppermute | solution.py:16
  113.3 11.6 %collective-permute-start.1 = (bf16[2,32,4096]{2,1,0:T(8,128)(2,1)S(1)}, bf16[2,32,4096]{2,1,0:T(8,128)(2,1)}, u32[]{:S(2)}, u32[]{:S(2)}) collective-permute-start(bf16[2,32,4096]{2,1,0:T(8,128)(2,1)S(1)} %copy.58), channel_id=1, source_target_pairs={{0,2},{2,0},{4,6},{6,4},{1,3},{3,1},{5,7},{7,5},{8,10},{10,8},{12,... | collective-permute-start | bytes 1572872 | tf_op jit(solution)/shard_map/ppermute | solution.py:16
  119.6 29.4 %collective-permute-start.9 = (bf16[2,64,4096]{2,1,0:T(8,128)(2,1)}, bf16[2,64,4096]{2,1,0:T(8,128)(2,1)}, u32[]{:S(2)}, u32[]{:S(2)}) collective-permute-start(bf16[2,64,4096]{2,1,0:T(8,128)(2,1)} %bitcast.199), channel_id=1, source_target_pairs={{0,4},{2,6},{4,0},{6,2},{1,5},{3,7},{5,1},{7,3},{8,12},{10,14},{12... | collective-permute-start | bytes 3145736 | tf_op jit(solution)/shard_map/ppermute | solution.py:16
  127.1 44.4 %collective-permute-start.2 = (bf16[2,2,32,4096]{3,2,1,0:T(8,128)(2,1)}, bf16[2,2,32,4096]{3,2,1,0:T(8,128)(2,1)}, u32[]{:S(2)}, u32[]{:S(2)}) collective-permute-start(bf16[2,2,32,4096]{3,2,1,0:T(8,128)(2,1)} %pad_maximum_fusion), channel_id=1, source_target_pairs={{0,4},{2,6},{4,0},{6,2},{1,5},{3,7},{5,1},{7,3},{8,12},{10,14},{12... | collective-permute-start | bytes 3145736 | tf_op jit(solution)/shard_map/ppermute | solution.py:16
  153.1 29.5 %collective-permute-start.10 = (bf16[64,4096]{1,0:T(8,128)(2,1)}, bf16[64,4096]{1,0:T(8,128)(2,1)}, u32[]{:S(2)}, u32[]{:S(2)}) collective-permute-start(bf16[64,4096]{1,0:T(8,128)(2,1)} %fusion.25), channel_id=1, source_target_pairs={{0,2},{2,0},{4,6},{6,4},{1,3},{3,1},{5,7},{7,5},{8,10},{10,8},{12,... | collective-permute-start | bytes 1572872 | tf_op jit(solution)/shard_map/ppermute | solution.py:16
  175.7 29.2 %collective-permute-start.3 = (bf16[2,64,4096]{2,1,0:T(8,128)(2,1)}, bf16[2,64,4096]{2,1,0:T(8,128)(2,1)}, u32[]{:S(2)}, u32[]{:S(2)}) collective-permute-start(bf16[2,64,4096]{2,1,0:T(8,128)(2,1)} %bitcast.198), channel_id=1, source_target_pairs={{0,4},{2,6},{4,0},{6,2},{1,5},{3,7},{5,1},{7,3},{8,12},{10,14},{12... | collective-permute-start | bytes 3145736 | tf_op jit(solution)/shard_map/ppermute | solution.py:16
  185.6 37.1 %all-to-all-start.3 = ((bf16[2,32,4096]{2,0,1:T(2,128)(2,1)}), bf16[2,32,4096]{2,0,1:T(2,128)(2,1)S(1)}, u32[]{:S(2)}, u32[]{:S(2)}) async-start(bf16[2,32,4096]{2,0,1:T(2,128)(2,1)} %copy.51), calls=%async_computation.3 | async-start | bytes 1048576 | tf_op jit(solution)/shard_map/all_to_all | solution.py:81
  209.0 10.7 %collective-permute-start.4 = (bf16[64,4096]{1,0:T(8,128)(2,1)}, bf16[64,4096]{1,0:T(8,128)(2,1)}, u32[]{:S(2)}, u32[]{:S(2)}) collective-permute-start(bf16[64,4096]{1,0:T(8,128)(2,1)} %fusion.28), channel_id=1, source_target_pairs={{0,2},{2,0},{4,6},{6,4},{1,3},{3,1},{5,7},{7,5},{8,10},{10,8},{12,... | collective-permute-start | bytes 1572872 | tf_op jit(solution)/shard_map/ppermute | solution.py:16
  222.7 46.2 %all-to-all-start.1 = ((bf16[2,32,4096]{2,0,1:T(2,128)(2,1)}), bf16[2,32,4096]{2,0,1:T(2,128)(2,1)S(1)}, u32[]{:S(2)}, u32[]{:S(2)}) async-start(bf16[2,32,4096]{2,0,1:T(2,128)(2,1)} %copy.45), calls=%async_computation.1 | async-start | bytes 1048576 | tf_op jit(solution)/shard_map/all_to_all | solution.py:81
  237.8 31.4 %collective-permute-start.11 = (bf16[16,4096]{1,0:T(8,128)(2,1)S(1)}, bf16[16,4096]{1,0:T(8,128)(2,1)S(1)}, u32[]{:S(2)}, u32[]{:S(2)}) collective-permute-start(bf16[16,4096]{1,0:T(8,128)(2,1)S(1)} %convolution_convert_fusion.8), channel_id=1, source_target_pairs={{0,1},{1,0},{2,3},{3,2},{4,5},{5,4},{6,7},{7,6},{8,9},{9,8},{10,11... | collective-permute-start | bytes 393224 | tf_op jit(solution)/shard_map/ppermute | solution.py:11
  269.5 11.7 %collective-permute-start.12 = (bf16[1,16,4096]{2,1,0:T(8,128)(2,1)S(1)}, bf16[1,16,4096]{2,1,0:T(8,128)(2,1)S(1)}, u32[]{:S(2)}, u32[]{:S(2)}) collective-permute-start(bf16[1,16,4096]{2,1,0:T(8,128)(2,1)S(1)} %fusion.6), channel_id=1, source_target_pairs={{0,256},{256,0},{1,257},{257,1},{2,258},{258,2},{3,259},{259,3},{4... | collective-permute-start | bytes 393224 | tf_op jit(solution)/shard_map/ppermute | solution.py:11

commit v10 on v8

--- a/solution.py
+++ b/solution.py
@@ -116,12 +116,18 @@
         ((a, c) for a in range(n_q) for c in range(n_zh) if (a, c) != (0, 0)),
         key=lambda step: (step[1], -step[0]),
     )
-    rows = [normalize(arrived, norm_gain[0])]
-    picks = [expert_ids[0]]
+    normed = normalize(arrived, norm_gain[0])
+    own_pick = expert_ids[0]
+    model_width = normed.shape[1]
+    lanes = 128
+    tag = jnp.pad(own_pick.astype(jnp.bfloat16), ((0, 0), (0, lanes - top_count)))
+    packed = jnp.concatenate([normed, tag], axis=1)
+    rows = [normed]
+    picks = [own_pick]
     for a, c in offsets:
-        far = lax.ppermute(sent, ("section", "q2", "zh"), shifted_pairs((n_sec, n_q, n_zh), (1, a, c)))
-        rows.append(normalize(far[0], norm_gain[0]))
-        picks.append(lax.ppermute(expert_ids[0], ("q2", "zh"), shifted_pairs((n_q, n_zh), (a, c))))
+        far = lax.ppermute(packed, ("q2", "zh"), shifted_pairs((n_q, n_zh), (a, c)))
+        rows.append(far[:, :model_width])
+        picks.append(far[:, model_width:model_width + top_count].astype(jnp.int32))
     w_first = w_in[0, 0]
     w_second = w_out[0, 0]
     chunk = len(rows) // 2

time: 261 us -> 252 us (0.966); the launches traced: 256 us -> 251 us
  waiting for transfers between devices: 66.1 us -> 62.2 us
  blocking collectives: 19.6 us -> 16.6 us
    ppermute x6 -> x3, starting transfers between devices: 38.7 us -> 16.2 us  [on_device(): far = lax.ppermute(packed, ('q2', 'zh'), shifted_pairs((n_q, n_zh), (a, c)))]
    ppermute x14, starting transfers between devices: 51 us -> 63 us  [passed_along(): return lax.ppermute(value, axis, pairs)]
    ppermute x3, starting transfers between devices: 16.5 us -> 27.5 us  [on_device(): lax.ppermute(sums[j].astype(jnp.bfloat16), ('q2', 'zh'), home)]
    ppermute x3, waiting for transfers between devices: 15.5 us -> 9.11 us  [on_device(): lax.ppermute(sums[j].astype(jnp.bfloat16), ('q2', 'zh'), home)]
    ppermute x6 -> x3, waiting for transfers between devices: 18.5 us -> 21.7 us  [on_device(): far = lax.ppermute(packed, ('q2', 'zh'), shifted_pairs((n_q, n_zh), (a, c)))]
    all_to_all x1, blocking collectives: 19.6 us -> 16.6 us  [expert_pass(): lax.all_to_all(slot_grid, QUARTER, split_axis=1, concat_axis=1, tiled=True)]
  transfers between devices with their start and end apart: 26 -> 23, of which waited for: 12 -> 12; matrix products, arithmetic and copies ran while one was open for 15% -> 15% of each run, Pallas kernels for 0% -> 0%
where the time goes in v10:
time: 252 us; the launch traced here: 251 us
  starting transfers between devices  126 us (50%)
  waiting for transfers between devices  62.2 us (25%)
  matrix products  32.8 us (13%)
  blocking collectives  16.6 us (7%)
  local copies, waits for them, and re-layouts  8.62 us (3%)
  other arithmetic  3.97 us (2%)
    ppermute x14, starting transfers between devices, passed_along(): return lax.ppermute(value, axis, pairs)  63 us
    ppermute x14, waiting for transfers between devices, passed_along(): return lax.ppermute(value, axis, pairs)  31.4 us
    dot_general x8, matrix products, expert_pass(): jnp.dot(hidden, w_second, preferred_element_type=jnp.float32)  30.1 us
    ppermute x3, starting transfers between devices, on_device(): lax.ppermute(sums[j].astype(jnp.bfloat16), ('q2', 'zh'), home)  27.5 us
    ppermute x3, waiting for transfers between devices, on_device(): far = lax.ppermute(packed, ('q2', 'zh'), shifted_pairs((n_q, n_zh), (a, c)))  21.7 us
    all_to_all x1, blocking collectives, expert_pass(): lax.all_to_all(slot_grid, QUARTER, split_axis=1, concat_axis=1, tiled=True)  16.6 us
    ppermute x3, starting transfers between devices, on_device(): far = lax.ppermute(packed, ('q2', 'zh'), shifted_pairs((n_q, n_zh), (a, c)))  16.2 us
    all_to_all x2, starting transfers between devices, expert_pass(): lax.all_to_all(summed.astype(jnp.bfloat16).reshape(lead, n_local, model_w...  13.9 us
  transfers between devices with their start and end apart: 23, of which 12 were waited for; matrix products, arithmetic and copies ran while one was open for 15% of the time, Pallas kernels for 0%

profile of v10, /device:TPU:1, one launch (start us, length us, event | category | flops | bytes accessed | tf_op | source)
XLA Modules:
  0.0 250.6 jit_solution(15013345539872863171)
XLA Ops:
  0.0 8.9 %collective-permute-start = (bf16[1,16,4096]{2,1,0:T(8,128)(2,1)}, bf16[1,16,4096]{2,1,0:T(8,128)(2,1)S(1)}, u32[]{:S(2)}, u32[]{:S(2)}) collective-permute-start(bf16[1,16,4096]{2,1,0:T(8,128)(2,1)} %param.6), channel_id=1, source_target_pairs={{0,256},{256,0},{1,257},{257,1},{2,258},{258,2},{3,259},{259,3},{4... | collective-permute-start | bytes 393224 | tf_op jit(solution)/shard_map/ppermute | solution.py:14
  14.5 10.6 %collective-permute-start.10 = (bf16[16,4224]{1,0:T(8,128)(2,1)S(1)}, bf16[16,4224]{1,0:T(8,128)(2,1)S(1)}, u32[]{:S(2)}, u32[]{:S(2)}) collective-permute-start(bf16[16,4224]{1,0:T(8,128)(2,1)S(1)} %fusion.38), channel_id=1, source_target_pairs={{0,1},{1,0},{128,129},{129,128},{2,3},{3,2},{130,131},{131,130},{4... | collective-permute-start | bytes 405512 | tf_op jit(solution)/shard_map/ppermute | solution.py:128
  30.3 20.3 %collective-permute-done.9 = bf16[16,4224]{1,0:T(8,128)(2,1)S(1)} collective-permute-done((bf16[16,4224]{1,0:T(8,128)(2,1)S(1)}, bf16[16,4224]{1,0:T(8,128)(2,1)S(1)}, u32[]{:S(2)}, u32[]{:S(2)}) %collective-permute-start.9) | collective-permute-done | bytes 135200 | tf_op jit(solution)/shard_map/ppermute | solution.py:128
  54.4 16.6 %all_to_all.20 = bf16[4,16,4096]{2,0,1:T(4,128)(2,1)S(1)} all-to-all(bf16[4,16,4096]{2,0,1:T(4,128)(2,1)S(1)} %copy.170), channel_id=1, replica_groups=mesh['section'=2,'q2'=2,'r'=4,'x'=4,'y'=4,'zh'=2] {'r','x'}, dimensions={1} | all-to-all | bytes 1048576 | tf_op jit(solution)/shard_map/all_to_all | solution.py:65
  71.3 4.7 %collective-permute-start.15 = (bf16[4,16,4096]{2,1,0:T(8,128)(2,1)S(1)}, bf16[4,16,4096]{2,1,0:T(8,128)(2,1)}, u32[]{:S(2)}, u32[]{:S(2)}) collective-permute-start(bf16[4,16,4096]{2,1,0:T(8,128)(2,1)S(1)} %copy.171), channel_id=1, source_target_pairs={{0,6},{2,0},{4,2},{6,4},{1,7},{3,1},{5,3},{7,5},{8,14},{10,8},{12,... | collective-permute-start | bytes 1572872 | tf_op jit(solution)/shard_map/ppermute | solution.py:14
  77.5 5.5 %all-to-all-start = ((bf16[4,16,4096]{2,0,1:T(4,128)(2,1)}), bf16[4,16,4096]{2,0,1:T(4,128)(2,1)S(1)}, u32[]{:S(2)}, u32[]{:S(2)}) async-start(bf16[4,16,4096]{2,0,1:T(4,128)(2,1)} %copy.159), calls=%async_computation | async-start | bytes 1048576 | tf_op jit(solution)/shard_map/all_to_all | solution.py:65
  87.9 4.0 %convolution_convert_fusion.2 = bf16[64,4096]{1,0:T(8,128)(2,1)} fusion(bf16[1,1,256,4096]{3,2,1,0:T(8,128)(2,1)S(1)} %copy-done, bf16[64,4096]{1,0:T(8,128)(2,1)} %bitcast.22, bf16[1,1,4096,256]{3,2,1,0:T(8,128)(2,1)} %param.9), kind=kOutput, calls=%fused_computation.2 | convolution fusion | flops 268845056 | bytes 5242880 | tf_op jit(solution)/shard_map/dot_general | solution.py:72
  97.8 4.0 %convolution_convert_fusion.3 = bf16[64,4096]{1,0:T(8,128)(2,1)} fusion(bf16[1,1,256,4096]{3,2,1,0:T(8,128)(2,1)S(1)} %copy-done, bf16[64,4096]{1,0:T(8,128)(2,1)} %bitcast.21, bf16[1,1,4096,256]{3,2,1,0:T(8,128)(2,1)} %param.9), kind=kOutput, calls=%fused_computation.3 | convolution fusion | flops 268845056 | bytes 5242880 | tf_op jit(solution)/shard_map/dot_general | solution.py:72
  104.0 7.6 %collective-permute-done.11 = bf16[4,16,4096]{2,1,0:T(8,128)(2,1)} collective-permute-done((bf16[4,16,4096]{2,1,0:T(8,128)(2,1)S(1)}, bf16[4,16,4096]{2,1,0:T(8,128)(2,1)}, u32[]{:S(2)}, u32[]{:S(2)}) %collective-permute-start.11) | collective-permute-done | bytes 524320 | tf_op jit(solution)/shard_map/ppermute | solution.py:14
  111.6 4.0 %convolution_convert_fusion.4 = bf16[64,4096]{1,0:T(8,128)(2,1)} fusion(bf16[1,1,256,4096]{3,2,1,0:T(8,128)(2,1)S(1)} %copy-done, bf16[64,4096]{1,0:T(8,128)(2,1)} %bitcast.20, bf16[1,1,4096,256]{3,2,1,0:T(8,128)(2,1)} %param.9), kind=kOutput, calls=%fused_computation.4 | convolution fusion | flops 268845056 | bytes 5242880 | tf_op jit(solution)/shard_map/dot_general | solution.py:72
  121.1 4.5 %collective-permute-start.4 = (bf16[4,16,4096]{2,1,0:T(8,128)(2,1)}, bf16[4,16,4096]{2,1,0:T(8,128)(2,1)}, u32[]{:S(2)}, u32[]{:S(2)}) collective-permute-start(bf16[4,16,4096]{2,1,0:T(8,128)(2,1)} %copy.160), channel_id=1, source_target_pairs={{0,4},{2,6},{4,0},{6,2},{1,5},{3,7},{5,1},{7,3},{8,12},{10,14},{12... | collective-permute-start | bytes 1572872 | tf_op jit(solution)/shard_map/ppermute | solution.py:14
  136.1 6.7 %all-to-all-start.3 = ((bf16[4,16,4096]{2,0,1:T(4,128)(2,1)}), bf16[4,16,4096]{2,0,1:T(4,128)(2,1)S(1)}, u32[]{:S(2)}, u32[]{:S(2)}) async-start(bf16[4,16,4096]{2,0,1:T(4,128)(2,1)} %copy.175), calls=%async_computation.3 | async-start | bytes 1048576 | tf_op jit(solution)/shard_map/all_to_all | solution.py:77
  152.0 7.2 %collective-permute-start.5 = (bf16[64,4096]{1,0:T(8,128)(2,1)}, bf16[64,4096]{1,0:T(8,128)(2,1)}, u32[]{:S(2)}, u32[]{:S(2)}) collective-permute-start(bf16[64,4096]{1,0:T(8,128)(2,1)} %convolution_convert_fusion.7), channel_id=1, source_target_pairs={{0,4},{2,6},{4,0},{6,2},{1,5},{3,7},{5,1},{7,3},{8,12},{10,14},{12... | collective-permute-start | bytes 1572872 | tf_op jit(solution)/shard_map/ppermute | solution.py:14
  159.2 4.0 %convolution_convert_fusion.8 = bf16[64,4096]{1,0:T(8,128)(2,1)} fusion(bf16[1,1,256,4096]{3,2,1,0:T(8,128)(2,1)S(1)} %copy-done, bf16[64,4096]{1,0:T(8,128)(2,1)} %bitcast.11, bf16[1,1,4096,256]{3,2,1,0:T(8,128)(2,1)} %param.9), kind=kOutput, calls=%fused_computation.9 | convolution fusion | flops 268845056 | bytes 5242880 | tf_op jit(solution)/shard_map/dot_general | solution.py:72
  163.1 5.1 %collective-permute-start.3 = (bf16[64,4096]{1,0:T(8,128)(2,1)}, bf16[64,4096]{1,0:T(8,128)(2,1)S(1)}, u32[]{:S(2)}, u32[]{:S(2)}) collective-permute-start(bf16[64,4096]{1,0:T(8,128)(2,1)} %convolution_convert_fusion.8), channel_id=1, source_target_pairs={{0,6},{2,0},{4,2},{6,4},{1,7},{3,1},{5,3},{7,5},{8,14},{10,8},{12,... | collective-permute-start | bytes 1572872 | tf_op jit(solution)/shard_map/ppermute | solution.py:14
  168.3 8.5 %collective-permute-done.5 = bf16[64,4096]{1,0:T(8,128)(2,1)} collective-permute-done((bf16[64,4096]{1,0:T(8,128)(2,1)}, bf16[64,4096]{1,0:T(8,128)(2,1)}, u32[]{:S(2)}, u32[]{:S(2)}) %collective-permute-start.5) | collective-permute-done | bytes 524320 | tf_op jit(solution)/shard_map/ppermute | solution.py:14
  176.8 7.5 %collective-permute-done.3 = bf16[64,4096]{1,0:T(8,128)(2,1)S(1)} collective-permute-done((bf16[64,4096]{1,0:T(8,128)(2,1)}, bf16[64,4096]{1,0:T(8,128)(2,1)S(1)}, u32[]{:S(2)}, u32[]{:S(2)}) %collective-permute-start.3) | collective-permute-done | bytes 524320 | tf_op jit(solution)/shard_map/ppermute | solution.py:14
  190.0 7.2 %all-to-all-start.1 = ((bf16[4,16,4096]{2,0,1:T(4,128)(2,1)}), bf16[4,16,4096]{2,0,1:T(4,128)(2,1)S(1)}, u32[]{:S(2)}, u32[]{:S(2)}) async-start(bf16[4,16,4096]{2,0,1:T(4,128)(2,1)} %copy.164), calls=%async_computation.1 | async-start | bytes 1048576 | tf_op jit(solution)/shard_map/all_to_all | solution.py:77
  197.9 9.2 %collective-permute-start.18 = (bf16[16,4096]{1,0:T(8,128)(2,1)S(1)}, bf16[16,4096]{1,0:T(8,128)(2,1)S(1)}, u32[]{:S(2)}, u32[]{:S(2)}) collective-permute-start(bf16[16,4096]{1,0:T(8,128)(2,1)S(1)} %get-tuple-element.10), channel_id=1, source_target_pairs={{0,1},{1,0},{128,129},{129,128},{2,3},{3,2},{130,131},{131,130},{4... | collective-permute-start | bytes 393224 | tf_op jit(solution)/shard_map/ppermute | solution.py:145
  207.1 6.6 %collective-permute-start.17 = (bf16[16,4096]{1,0:T(8,128)(2,1)S(1)}, bf16[16,4096]{1,0:T(8,128)(2,1)S(1)}, u32[]{:S(2)}, u32[]{:S(2)}) collective-permute-start(bf16[16,4096]{1,0:T(8,128)(2,1)S(1)} %get-tuple-element.9), channel_id=1, source_target_pairs={{0,129},{1,128},{128,1},{129,0},{2,131},{3,130},{130,3},{131,2},{4... | collective-permute-start | bytes 393224 | tf_op jit(solution)/shard_map/ppermute | solution.py:145
  214.4 11.7 %collective-permute-start.8 = (bf16[16,4096]{1,0:T(8,128)(2,1)S(1)}, bf16[16,4096]{1,0:T(8,128)(2,1)S(1)}, u32[]{:S(2)}, u32[]{:S(2)}) collective-permute-start(bf16[16,4096]{1,0:T(8,128)(2,1)S(1)} %slice.65), channel_id=1, source_target_pairs={{0,128},{1,129},{128,0},{129,1},{2,130},{3,131},{130,2},{131,3},{4... | collective-permute-start | bytes 393224 | tf_op jit(solution)/shard_map/ppermute | solution.py:145
  226.1 4.1 %collective-permute-done.17 = bf16[16,4096]{1,0:T(8,128)(2,1)S(1)} collective-permute-done((bf16[16,4096]{1,0:T(8,128)(2,1)S(1)}, bf16[16,4096]{1,0:T(8,128)(2,1)S(1)}, u32[]{:S(2)}, u32[]{:S(2)}) %collective-permute-start.17) | collective-permute-done | bytes 131104 | tf_op jit(solution)/shard_map/ppermute | solution.py:145
  230.2 5.0 %collective-permute-done.8 = bf16[16,4096]{1,0:T(8,128)(2,1)S(1)} collective-permute-done((bf16[16,4096]{1,0:T(8,128)(2,1)S(1)}, bf16[16,4096]{1,0:T(8,128)(2,1)S(1)}, u32[]{:S(2)}, u32[]{:S(2)}) %collective-permute-start.8) | collective-permute-done | bytes 131104 | tf_op jit(solution)/shard_map/ppermute | solution.py:145
  235.3 13.7 %collective-permute-start.19 = (bf16[1,16,4096]{2,1,0:T(8,128)(2,1)S(1)}, bf16[1,16,4096]{2,1,0:T(8,128)(2,1)S(1)}, u32[]{:S(2)}, u32[]{:S(2)}) collective-permute-start(bf16[1,16,4096]{2,1,0:T(8,128)(2,1)S(1)} %fusion.39), channel_id=1, source_target_pairs={{0,256},{256,0},{1,257},{257,1},{2,258},{258,2},{3,259},{259,3},{4... | collective-permute-start | bytes 393224 | tf_op jit(solution)/shard_map/ppermute | solution.py:14
  (102 shorter events, 62.9 us)
Async XLA Ops:
  0.0 87.9 %copy-start = (bf16[1,1,256,4096]{3,2,1,0:T(8,128)(2,1)S(1)}, bf16[1,1,256,4096]{3,2,1,0:T(8,128)(2,1)}, u32[]{:S(2)}) copy-start(bf16[1,1,256,4096]{3,2,1,0:T(8,128)(2,1)} %param.10) | copy-start | bytes 6291460
  0.0 10.0 %collective-permute-start = (bf16[1,16,4096]{2,1,0:T(8,128)(2,1)}, bf16[1,16,4096]{2,1,0:T(8,128)(2,1)S(1)}, u32[]{:S(2)}, u32[]{:S(2)}) collective-permute-start(bf16[1,16,4096]{2,1,0:T(8,128)(2,1)} %param.6), channel_id=1, source_target_pairs={{0,256},{256,0},{1,257},{257,1},{2,258},{258,2},{3,259},{259,3},{4... | collective-permute-start | bytes 393224 | tf_op jit(solution)/shard_map/ppermute | solution.py:14
  11.1 17.6 %collective-permute-start.1 = (bf16[16,4224]{1,0:T(8,128)(2,1)S(1)}, bf16[16,4224]{1,0:T(8,128)(2,1)S(1)}, u32[]{:S(2)}, u32[]{:S(2)}) collective-permute-start(bf16[16,4224]{1,0:T(8,128)(2,1)S(1)} %fusion.38), channel_id=1, source_target_pairs={{0,128},{1,129},{128,0},{129,1},{2,130},{3,131},{130,2},{131,3},{4... | collective-permute-start | bytes 405512 | tf_op jit(solution)/shard_map/ppermute | solution.py:128
  14.5 15.6 %collective-permute-start.10 = (bf16[16,4224]{1,0:T(8,128)(2,1)S(1)}, bf16[16,4224]{1,0:T(8,128)(2,1)S(1)}, u32[]{:S(2)}, u32[]{:S(2)}) collective-permute-start(bf16[16,4224]{1,0:T(8,128)(2,1)S(1)} %fusion.38), channel_id=1, source_target_pairs={{0,1},{1,0},{128,129},{129,128},{2,3},{3,2},{130,131},{131,130},{4... | collective-permute-start | bytes 405512 | tf_op jit(solution)/shard_map/ppermute | solution.py:128
  25.2 25.4 %collective-permute-start.9 = (bf16[16,4224]{1,0:T(8,128)(2,1)S(1)}, bf16[16,4224]{1,0:T(8,128)(2,1)S(1)}, u32[]{:S(2)}, u32[]{:S(2)}) collective-permute-start(bf16[16,4224]{1,0:T(8,128)(2,1)S(1)} %fusion.38), channel_id=1, source_target_pairs={{0,129},{1,128},{128,1},{129,0},{2,131},{3,130},{130,3},{131,2},{4... | collective-permute-start | bytes 405512 | tf_op jit(solution)/shard_map/ppermute | solution.py:128
  71.3 16.6 %collective-permute-start.15 = (bf16[4,16,4096]{2,1,0:T(8,128)(2,1)S(1)}, bf16[4,16,4096]{2,1,0:T(8,128)(2,1)}, u32[]{:S(2)}, u32[]{:S(2)}) collective-permute-start(bf16[4,16,4096]{2,1,0:T(8,128)(2,1)S(1)} %copy.171), channel_id=1, source_target_pairs={{0,6},{2,0},{4,2},{6,4},{1,7},{3,1},{5,3},{7,5},{8,14},{10,8},{12,... | collective-permute-start | bytes 1572872 | tf_op jit(solution)/shard_map/ppermute | solution.py:14
  77.5 40.0 %all-to-all-start = ((bf16[4,16,4096]{2,0,1:T(4,128)(2,1)}), bf16[4,16,4096]{2,0,1:T(4,128)(2,1)S(1)}, u32[]{:S(2)}, u32[]{:S(2)}) async-start(bf16[4,16,4096]{2,0,1:T(4,128)(2,1)} %copy.159), calls=%async_computation | async-start | bytes 1048576 | tf_op jit(solution)/shard_map/all_to_all | solution.py:65
  83.0 14.8 %collective-permute-start.13 = (bf16[4,16,4096]{2,1,0:T(8,128)(2,1)S(1)}, bf16[4,16,4096]{2,1,0:T(8,128)(2,1)}, u32[]{:S(2)}, u32[]{:S(2)}) collective-permute-start(bf16[4,16,4096]{2,1,0:T(8,128)(2,1)S(1)} %copy.171), channel_id=1, source_target_pairs={{0,4},{2,6},{4,0},{6,2},{1,5},{3,7},{5,1},{7,3},{8,12},{10,14},{12... | collective-permute-start | bytes 1572872 | tf_op jit(solution)/shard_map/ppermute | solution.py:14
  85.3 26.3 %collective-permute-start.11 = (bf16[4,16,4096]{2,1,0:T(8,128)(2,1)S(1)}, bf16[4,16,4096]{2,1,0:T(8,128)(2,1)}, u32[]{:S(2)}, u32[]{:S(2)}) collective-permute-start(bf16[4,16,4096]{2,1,0:T(8,128)(2,1)S(1)} %copy.171), channel_id=1, source_target_pairs={{0,2},{2,4},{4,6},{6,0},{1,3},{3,5},{5,7},{7,1},{8,10},{10,12},{12... | collective-permute-start | bytes 1572872 | tf_op jit(solution)/shard_map/ppermute | solution.py:14
  91.9 33.8 %collective-permute-start.16 = (bf16[64,4096]{1,0:T(8,128)(2,1)}, bf16[64,4096]{1,0:T(8,128)(2,1)}, u32[]{:S(2)}, u32[]{:S(2)}) collective-permute-start(bf16[64,4096]{1,0:T(8,128)(2,1)} %convolution_convert_fusion.2), channel_id=1, source_target_pairs={{0,2},{2,4},{4,6},{6,0},{1,3},{3,5},{5,7},{7,1},{8,10},{10,12},{12... | collective-permute-start | bytes 1572872 | tf_op jit(solution)/shard_map/ppermute | solution.py:14
  101.7 29.7 %collective-permute-start.14 = (bf16[64,4096]{1,0:T(8,128)(2,1)}, bf16[64,4096]{1,0:T(8,128)(2,1)}, u32[]{:S(2)}, u32[]{:S(2)}) collective-permute-start(bf16[64,4096]{1,0:T(8,128)(2,1)} %convolution_convert_fusion.3), channel_id=1, source_target_pairs={{0,4},{2,6},{4,0},{6,2},{1,5},{3,7},{5,1},{7,3},{8,12},{10,14},{12... | collective-permute-start | bytes 1572872 | tf_op jit(solution)/shard_map/ppermute | solution.py:14
  115.6 15.9 %collective-permute-start.12 = (bf16[64,4096]{1,0:T(8,128)(2,1)}, bf16[64,4096]{1,0:T(8,128)(2,1)}, u32[]{:S(2)}, u32[]{:S(2)}) collective-permute-start(bf16[64,4096]{1,0:T(8,128)(2,1)} %convolution_convert_fusion.4), channel_id=1, source_target_pairs={{0,6},{2,0},{4,2},{6,4},{1,7},{3,1},{5,3},{7,5},{8,14},{10,8},{12,... | collective-permute-start | bytes 1572872 | tf_op jit(solution)/shard_map/ppermute | solution.py:14
  118.6 24.3 %collective-permute-start.6 = (bf16[4,16,4096]{2,1,0:T(8,128)(2,1)}, bf16[4,16,4096]{2,1,0:T(8,128)(2,1)}, u32[]{:S(2)}, u32[]{:S(2)}) collective-permute-start(bf16[4,16,4096]{2,1,0:T(8,128)(2,1)} %copy.160), channel_id=1, source_target_pairs={{0,6},{2,0},{4,2},{6,4},{1,7},{3,1},{5,3},{7,5},{8,14},{10,8},{12,... | collective-permute-start | bytes 1572872 | tf_op jit(solution)/shard_map/ppermute | solution.py:14
  121.1 26.9 %collective-permute-start.4 = (bf16[4,16,4096]{2,1,0:T(8,128)(2,1)}, bf16[4,16,4096]{2,1,0:T(8,128)(2,1)}, u32[]{:S(2)}, u32[]{:S(2)}) collective-permute-start(bf16[4,16,4096]{2,1,0:T(8,128)(2,1)} %copy.160), channel_id=1, source_target_pairs={{0,4},{2,6},{4,0},{6,2},{1,5},{3,7},{5,1},{7,3},{8,12},{10,14},{12... | collective-permute-start | bytes 1572872 | tf_op jit(solution)/shard_map/ppermute | solution.py:14
  125.7 33.5 %collective-permute-start.2 = (bf16[4,16,4096]{2,1,0:T(8,128)(2,1)}, bf16[4,16,4096]{2,1,0:T(8,128)(2,1)}, u32[]{:S(2)}, u32[]{:S(2)}) collective-permute-start(bf16[4,16,4096]{2,1,0:T(8,128)(2,1)} %copy.160), channel_id=1, source_target_pairs={{0,2},{2,4},{4,6},{6,0},{1,3},{3,5},{5,7},{7,1},{8,10},{10,12},{12... | collective-permute-start | bytes 1572872 | tf_op jit(solution)/shard_map/ppermute | solution.py:14
  136.1 53.9 %all-to-all-start.3 = ((bf16[4,16,4096]{2,0,1:T(4,128)(2,1)}), bf16[4,16,4096]{2,0,1:T(4,128)(2,1)S(1)}, u32[]{:S(2)}, u32[]{:S(2)}) async-start(bf16[4,16,4096]{2,0,1:T(4,128)(2,1)} %copy.175), calls=%async_computation.3 | async-start | bytes 1048576 | tf_op jit(solution)/shard_map/all_to_all | solution.py:77
  146.1 22.2 %collective-permute-start.7 = (bf16[64,4096]{1,0:T(8,128)(2,1)S(1)}, bf16[64,4096]{1,0:T(8,128)(2,1)}, u32[]{:S(2)}, u32[]{:S(2)}) collective-permute-start(bf16[64,4096]{1,0:T(8,128)(2,1)S(1)} %convolution_convert_fusion.6), channel_id=1, source_target_pairs={{0,2},{2,4},{4,6},{6,0},{1,3},{3,5},{5,7},{7,1},{8,10},{10,12},{12... | collective-permute-start | bytes 1572872 | tf_op jit(solution)/shard_map/ppermute | solution.py:14
  152.0 24.9 %collective-permute-start.5 = (bf16[64,4096]{1,0:T(8,128)(2,1)}, bf16[64,4096]{1,0:T(8,128)(2,1)}, u32[]{:S(2)}, u32[]{:S(2)}) collective-permute-start(bf16[64,4096]{1,0:T(8,128)(2,1)} %convolution_convert_fusion.7), channel_id=1, source_target_pairs={{0,4},{2,6},{4,0},{6,2},{1,5},{3,7},{5,1},{7,3},{8,12},{10,14},{12... | collective-permute-start | bytes 1572872 | tf_op jit(solution)/shard_map/ppermute | solution.py:14
  163.1 21.2 %collective-permute-start.3 = (bf16[64,4096]{1,0:T(8,128)(2,1)}, bf16[64,4096]{1,0:T(8,128)(2,1)S(1)}, u32[]{:S(2)}, u32[]{:S(2)}) collective-permute-start(bf16[64,4096]{1,0:T(8,128)(2,1)} %convolution_convert_fusion.8), channel_id=1, source_target_pairs={{0,6},{2,0},{4,2},{6,4},{1,7},{3,1},{5,3},{7,5},{8,14},{10,8},{12,... | collective-permute-start | bytes 1572872 | tf_op jit(solution)/shard_map/ppermute | solution.py:14
  190.0 23.7 %all-to-all-start.1 = ((bf16[4,16,4096]{2,0,1:T(4,128)(2,1)}), bf16[4,16,4096]{2,0,1:T(4,128)(2,1)S(1)}, u32[]{:S(2)}, u32[]{:S(2)}) async-start(bf16[4,16,4096]{2,0,1:T(4,128)(2,1)} %copy.164), calls=%async_computation.1 | async-start | bytes 1048576 | tf_op jit(solution)/shard_map/all_to_all | solution.py:77
  197.9 28.2 %collective-permute-start.18 = (bf16[16,4096]{1,0:T(8,128)(2,1)S(1)}, bf16[16,4096]{1,0:T(8,128)(2,1)S(1)}, u32[]{:S(2)}, u32[]{:S(2)}) collective-permute-start(bf16[16,4096]{1,0:T(8,128)(2,1)S(1)} %get-tuple-element.10), channel_id=1, source_target_pairs={{0,1},{1,0},{128,129},{129,128},{2,3},{3,2},{130,131},{131,130},{4... | collective-permute-start | bytes 393224 | tf_op jit(solution)/shard_map/ppermute | solution.py:145
  207.1 23.1 %collective-permute-start.17 = (bf16[16,4096]{1,0:T(8,128)(2,1)S(1)}, bf16[16,4096]{1,0:T(8,128)(2,1)S(1)}, u32[]{:S(2)}, u32[]{:S(2)}) collective-permute-start(bf16[16,4096]{1,0:T(8,128)(2,1)S(1)} %get-tuple-element.9), channel_id=1, source_target_pairs={{0,129},{1,128},{128,1},{129,0},{2,131},{3,130},{130,3},{131,2},{4... | collective-permute-start | bytes 393224 | tf_op jit(solution)/shard_map/ppermute | solution.py:145
  214.4 20.8 %collective-permute-start.8 = (bf16[16,4096]{1,0:T(8,128)(2,1)S(1)}, bf16[16,4096]{1,0:T(8,128)(2,1)S(1)}, u32[]{:S(2)}, u32[]{:S(2)}) collective-permute-start(bf16[16,4096]{1,0:T(8,128)(2,1)S(1)} %slice.65), channel_id=1, source_target_pairs={{0,128},{1,129},{128,0},{129,1},{2,130},{3,131},{130,2},{131,3},{4... | collective-permute-start | bytes 393224 | tf_op jit(solution)/shard_map/ppermute | solution.py:145
  235.3 14.7 %collective-permute-start.19 = (bf16[1,16,4096]{2,1,0:T(8,128)(2,1)S(1)}, bf16[1,16,4096]{2,1,0:T(8,128)(2,1)S(1)}, u32[]{:S(2)}, u32[]{:S(2)}) collective-permute-start(bf16[1,16,4096]{2,1,0:T(8,128)(2,1)S(1)} %fusion.39), channel_id=1, source_target_pairs={{0,256},{256,0},{1,257},{257,1},{2,258},{258,2},{3,259},{259,3},{4... | collective-permute-start | bytes 393224 | tf_op jit(solution)/shard_map/ppermute | solution.py:14
  (2 other events, 53.9 us)

commit v11 on v10

--- a/solution.py
+++ b/solution.py
@@ -139,12 +139,17 @@
         )
         halves.append(expert_pass(slots, combine, w_first, w_second))
     sums = jnp.concatenate(halves, axis=0).reshape(len(rows), tok_count, -1)
-    combined = arrived.astype(jnp.float32) + sums[0]
-    for j, (a, c) in enumerate(offsets, start=1):
-        home = shifted_pairs((n_q, n_zh), (-a, -c))
-        combined = combined + lax.ppermute(sums[j].astype(jnp.bfloat16), ("q2", "zh"), home).astype(
-            jnp.float32
-        )
+    steps = [(0, 0)] + offsets
+    row_of = [[0] * n_zh for _ in range(n_q)]
+    for j, (a, c) in enumerate(steps):
+        row_of[a][c] = j
+    row_of = jnp.array(row_of, dtype=jnp.int32)
+    me_q, me_h = lax.axis_index("q2"), lax.axis_index("zh")
+    dest = jnp.arange(n_q * n_zh, dtype=jnp.int32)
+    pick_rows = row_of[(me_q - dest // n_zh) % n_q, (me_h - dest % n_zh) % n_zh]
+    by_home = jnp.take(sums.astype(jnp.bfloat16), pick_rows, axis=0)
+    mine = lax.all_to_all(by_home, ("q2", "zh"), split_axis=0, concat_axis=0, tiled=True)
+    combined = arrived.astype(jnp.float32) + jnp.sum(mine.astype(jnp.float32), axis=0)
     return passed_along(combined.astype(jnp.bfloat16)[None], "section", 1)
 
 

time: 252 us -> 259 us (1.028)
  the two profiles are of different devices: /device:TPU:1 before, /device:TPU:49 now
where the time goes in v11:
time: 259 us; the launch traced here: 258 us
  starting transfers between devices  77.2 us (30%)
  waiting for transfers between devices  70.1 us (27%)
  blocking collectives  63.4 us (24%)
  matrix products  32.7 us (13%)
  local copies, waits for them, and re-layouts  9.82 us (4%)
  other arithmetic  4.19 us (2%)
    ppermute x14, starting transfers between devices, passed_along(): return lax.ppermute(value, axis, pairs)  41.8 us
    all_to_all x1, blocking collectives, on_device(): lax.all_to_all(by_home, ('q2', 'zh'), split_axis=0, concat_axis=0, tiled=...  40.5 us
    ppermute x14, waiting for transfers between devices, passed_along(): return lax.ppermute(value, axis, pairs)  39.1 us
    dot_general x8, matrix products, expert_pass(): jnp.dot(hidden, w_second, preferred_element_type=jnp.float32)  30.1 us
    all_to_all x1, blocking collectives, expert_pass(): lax.all_to_all(slot_grid, QUARTER, split_axis=1, concat_axis=1, tiled=True)  22.9 us
    ppermute x3, starting transfers between devices, on_device(): far = lax.ppermute(packed, ('q2', 'zh'), shifted_pairs((n_q, n_zh), (a, c)))  20.5 us
    ppermute x3, waiting for transfers between devices, on_device(): far = lax.ppermute(packed, ('q2', 'zh'), shifted_pairs((n_q, n_zh), (a, c)))  18.4 us
    all_to_all x2, waiting for transfers between devices, expert_pass(): lax.all_to_all(summed.astype(jnp.bfloat16).reshape(lead, n_local, model_w...  12.6 us
  transfers between devices with their start and end apart: 20, of which 13 were waited for; matrix products, arithmetic and copies ran while one was open for 15% of the time, Pallas kernels for 0%

profile of v11, /device:TPU:49, one launch (start us, length us, event | category | flops | bytes accessed | tf_op | source)
XLA Modules:
  0.0 257.9 jit_solution(12813935944225042800)
XLA Ops:
  4.9 11.6 %collective-permute-start.8 = (bf16[16,4224]{1,0:T(8,128)(2,1)S(1)}, bf16[16,4224]{1,0:T(8,128)(2,1)S(1)}, u32[]{:S(2)}, u32[]{:S(2)}) collective-permute-start(bf16[16,4224]{1,0:T(8,128)(2,1)S(1)} %fusion.37), channel_id=1, source_target_pairs={{0,129},{1,128},{128,1},{129,0},{2,131},{3,130},{130,3},{131,2},{4... | collective-permute-start | bytes 405512 | tf_op jit(solution)/shard_map/ppermute | solution.py:128
  16.5 4.9 %collective-permute-start.9 = (bf16[16,4224]{1,0:T(8,128)(2,1)S(1)}, bf16[16,4224]{1,0:T(8,128)(2,1)S(1)}, u32[]{:S(2)}, u32[]{:S(2)}) collective-permute-start(bf16[16,4224]{1,0:T(8,128)(2,1)S(1)} %fusion.37), channel_id=1, source_target_pairs={{0,1},{1,0},{128,129},{129,128},{2,3},{3,2},{130,131},{131,130},{4... | collective-permute-start | bytes 405512 | tf_op jit(solution)/shard_map/ppermute | solution.py:128
  21.4 4.0 %collective-permute-start.1 = (bf16[16,4224]{1,0:T(8,128)(2,1)S(1)}, bf16[16,4224]{1,0:T(8,128)(2,1)S(1)}, u32[]{:S(2)}, u32[]{:S(2)}) collective-permute-start(bf16[16,4224]{1,0:T(8,128)(2,1)S(1)} %fusion.37), channel_id=1, source_target_pairs={{0,128},{1,129},{128,0},{129,1},{2,130},{3,131},{130,2},{131,3},{4... | collective-permute-start | bytes 405512 | tf_op jit(solution)/shard_map/ppermute | solution.py:128
  25.4 5.0 %collective-permute-done.8 = bf16[16,4224]{1,0:T(8,128)(2,1)S(1)} collective-permute-done((bf16[16,4224]{1,0:T(8,128)(2,1)S(1)}, bf16[16,4224]{1,0:T(8,128)(2,1)S(1)}, u32[]{:S(2)}, u32[]{:S(2)}) %collective-permute-start.8) | collective-permute-done | bytes 135200 | tf_op jit(solution)/shard_map/ppermute | solution.py:128
  30.5 7.4 %collective-permute-done.9 = bf16[16,4224]{1,0:T(8,128)(2,1)S(1)} collective-permute-done((bf16[16,4224]{1,0:T(8,128)(2,1)S(1)}, bf16[16,4224]{1,0:T(8,128)(2,1)S(1)}, u32[]{:S(2)}, u32[]{:S(2)}) %collective-permute-start.9) | collective-permute-done | bytes 135200 | tf_op jit(solution)/shard_map/ppermute | solution.py:128
  38.7 6.0 %collective-permute-done.1 = bf16[16,4224]{1,0:T(8,128)(2,1)S(1)} collective-permute-done((bf16[16,4224]{1,0:T(8,128)(2,1)S(1)}, bf16[16,4224]{1,0:T(8,128)(2,1)S(1)}, u32[]{:S(2)}, u32[]{:S(2)}) %collective-permute-start.1) | collective-permute-done | bytes 135200 | tf_op jit(solution)/shard_map/ppermute | solution.py:128
  49.2 22.9 %all_to_all.25 = bf16[4,16,4096]{2,0,1:T(4,128)(2,1)S(1)} all-to-all(bf16[4,16,4096]{2,0,1:T(4,128)(2,1)S(1)} %copy.82), channel_id=1, replica_groups=mesh['section'=2,'q2'=2,'r'=4,'x'=4,'y'=4,'zh'=2] {'r','x'}, dimensions={1} | all-to-all | bytes 1048576 | tf_op jit(solution)/shard_map/all_to_all | solution.py:65
  76.8 5.1 %all-to-all-start.2 = ((bf16[4,16,4096]{2,0,1:T(4,128)(2,1)}), bf16[4,16,4096]{2,0,1:T(4,128)(2,1)S(1)}, u32[]{:S(2)}, u32[]{:S(2)}) async-start(bf16[4,16,4096]{2,0,1:T(4,128)(2,1)} %copy.93), calls=%async_computation.2 | async-start | bytes 1048576 | tf_op jit(solution)/shard_map/all_to_all | solution.py:65
  87.0 4.0 %convolution_convert_fusion.8 = bf16[64,4096]{1,0:T(8,128)(2,1)} fusion(bf16[1,1,256,4096]{3,2,1,0:T(8,128)(2,1)S(1)} %copy-done, bf16[64,4096]{1,0:T(8,128)(2,1)} %bitcast.11, bf16[1,1,4096,256]{3,2,1,0:T(8,128)(2,1)} %param.10), kind=kOutput, calls=%fused_computation.11 | convolution fusion | flops 268845056 | bytes 5242880 | tf_op jit(solution)/shard_map/dot_general | solution.py:72
  91.0 4.0 %collective-permute-start.3 = (bf16[64,4096]{1,0:T(8,128)(2,1)}, bf16[64,4096]{1,0:T(8,128)(2,1)}, u32[]{:S(2)}, u32[]{:S(2)}) collective-permute-start(bf16[64,4096]{1,0:T(8,128)(2,1)} %convolution_convert_fusion.8), channel_id=1, source_target_pairs={{0,6},{2,0},{4,2},{6,4},{1,7},{3,1},{5,3},{7,5},{8,14},{10,8},{12,... | collective-permute-start | bytes 1572872 | tf_op jit(solution)/shard_map/ppermute | solution.py:14
  96.9 4.0 %convolution_convert_fusion.7 = bf16[64,4096]{1,0:T(8,128)(2,1)} fusion(bf16[1,1,256,4096]{3,2,1,0:T(8,128)(2,1)S(1)} %copy-done, bf16[64,4096]{1,0:T(8,128)(2,1)} %bitcast.12, bf16[1,1,4096,256]{3,2,1,0:T(8,128)(2,1)} %param.10), kind=kOutput, calls=%fused_computation.10 | convolution fusion | flops 268845056 | bytes 5242880 | tf_op jit(solution)/shard_map/dot_general | solution.py:72
  100.9 4.8 %collective-permute-start.5 = (bf16[64,4096]{1,0:T(8,128)(2,1)}, bf16[64,4096]{1,0:T(8,128)(2,1)}, u32[]{:S(2)}, u32[]{:S(2)}) collective-permute-start(bf16[64,4096]{1,0:T(8,128)(2,1)} %convolution_convert_fusion.7), channel_id=1, source_target_pairs={{0,4},{2,6},{4,0},{6,2},{1,5},{3,7},{5,1},{7,3},{8,12},{10,14},{12... | collective-permute-start | bytes 1572872 | tf_op jit(solution)/shard_map/ppermute | solution.py:14
  108.7 4.0 %convolution_convert_fusion.6 = bf16[64,4096]{1,0:T(8,128)(2,1)} fusion(bf16[1,1,256,4096]{3,2,1,0:T(8,128)(2,1)S(1)} %copy-done, bf16[64,4096]{1,0:T(8,128)(2,1)} %bitcast.13, bf16[1,1,4096,256]{3,2,1,0:T(8,128)(2,1)} %param.10), kind=kOutput, calls=%fused_computation.9 | convolution fusion | flops 268845056 | bytes 5242880 | tf_op jit(solution)/shard_map/dot_general | solution.py:72
  123.0 4.0 %collective-permute-start.14 = (bf16[4,16,4096]{2,1,0:T(8,128)(2,1)}, bf16[4,16,4096]{2,1,0:T(8,128)(2,1)}, u32[]{:S(2)}, u32[]{:S(2)}) collective-permute-start(bf16[4,16,4096]{2,1,0:T(8,128)(2,1)} %copy.94), channel_id=1, source_target_pairs={{0,6},{2,0},{4,2},{6,4},{1,7},{3,1},{5,3},{7,5},{8,14},{10,8},{12,... | collective-permute-start | bytes 1572872 | tf_op jit(solution)/shard_map/ppermute | solution.py:14
  127.0 5.1 %collective-permute-done.7 = bf16[64,4096]{1,0:T(8,128)(2,1)} collective-permute-done((bf16[64,4096]{1,0:T(8,128)(2,1)}, bf16[64,4096]{1,0:T(8,128)(2,1)}, u32[]{:S(2)}, u32[]{:S(2)}) %collective-permute-start.7) | collective-permute-done | bytes 524320 | tf_op jit(solution)/shard_map/ppermute | solution.py:14
  136.7 4.0 %all-to-all-start.1 = ((bf16[4,16,4096]{2,0,1:T(4,128)(2,1)}), bf16[4,16,4096]{2,0,1:T(4,128)(2,1)S(1)}, u32[]{:S(2)}, u32[]{:S(2)}) async-start(bf16[4,16,4096]{2,0,1:T(4,128)(2,1)} %copy.87), calls=%async_computation.1 | async-start | bytes 1048576 | tf_op jit(solution)/shard_map/all_to_all | solution.py:77
  140.7 3.9 %collective-permute-done.10 = bf16[4,16,4096]{2,1,0:T(8,128)(2,1)} collective-permute-done((bf16[4,16,4096]{2,1,0:T(8,128)(2,1)}, bf16[4,16,4096]{2,1,0:T(8,128)(2,1)}, u32[]{:S(2)}, u32[]{:S(2)}) %collective-permute-start.10) | collective-permute-done | bytes 524320 | tf_op jit(solution)/shard_map/ppermute | solution.py:14
  153.3 4.0 %convolution_convert_fusion.3 = bf16[64,4096]{1,0:T(8,128)(2,1)} fusion(bf16[1,1,256,4096]{3,2,1,0:T(8,128)(2,1)S(1)} %copy-done, bf16[64,4096]{1,0:T(8,128)(2,1)} %bitcast.21, bf16[1,1,4096,256]{3,2,1,0:T(8,128)(2,1)} %param.10), kind=kOutput, calls=%fused_computation.5 | convolution fusion | flops 268845056 | bytes 5242880 | tf_op jit(solution)/shard_map/dot_general | solution.py:72
  159.6 4.0 %convolution_convert_fusion.2 = bf16[64,4096]{1,0:T(8,128)(2,1)} fusion(bf16[1,1,256,4096]{3,2,1,0:T(8,128)(2,1)S(1)} %copy-done, bf16[64,4096]{1,0:T(8,128)(2,1)} %bitcast.22, bf16[1,1,4096,256]{3,2,1,0:T(8,128)(2,1)} %param.10), kind=kOutput, calls=%fused_computation.4 | convolution fusion | flops 268845056 | bytes 5242880 | tf_op jit(solution)/shard_map/dot_general | solution.py:72
  165.5 5.8 %collective-permute-done.13 = bf16[64,4096]{1,0:T(8,128)(2,1)} collective-permute-done((bf16[64,4096]{1,0:T(8,128)(2,1)}, bf16[64,4096]{1,0:T(8,128)(2,1)}, u32[]{:S(2)}, u32[]{:S(2)}) %collective-permute-start.13) | collective-permute-done | bytes 524320 | tf_op jit(solution)/shard_map/ppermute | solution.py:14
  171.3 14.4 %collective-permute-done.15 = bf16[64,4096]{1,0:T(8,128)(2,1)S(1)} collective-permute-done((bf16[64,4096]{1,0:T(8,128)(2,1)}, bf16[64,4096]{1,0:T(8,128)(2,1)S(1)}, u32[]{:S(2)}, u32[]{:S(2)}) %collective-permute-start.15) | collective-permute-done | bytes 524320 | tf_op jit(solution)/shard_map/ppermute | solution.py:14
  191.3 5.9 %all-to-all-start.3 = ((bf16[4,16,4096]{2,0,1:T(4,128)(2,1)}), bf16[4,16,4096]{2,0,1:T(4,128)(2,1)S(1)}, u32[]{:S(2)}, u32[]{:S(2)}) async-start(bf16[4,16,4096]{2,0,1:T(4,128)(2,1)} %copy.98), calls=%async_computation.3 | async-start | bytes 1048576 | tf_op jit(solution)/shard_map/all_to_all | solution.py:77
  198.6 12.6 %all-to-all-done.3 = bf16[4,16,4096]{2,0,1:T(4,128)(2,1)S(1)} async-done(((bf16[4,16,4096]{2,0,1:T(4,128)(2,1)}), bf16[4,16,4096]{2,0,1:T(4,128)(2,1)S(1)}, u32[]{:S(2)}, u32[]{:S(2)}) %all-to-all-start.3) | async-done | bytes 524320 | tf_op jit(solution)/shard_map/all_to_all | solution.py:77
  212.6 40.5 %all_to_all.26 = bf16[4,16,4096]{2,1,0:T(8,128)(2,1)S(1)} all-to-all(bf16[4,16,4096]{2,1,0:T(8,128)(2,1)S(1)} %broadcast_select_fusion), channel_id=1, replica_groups=mesh['section'=2,'q2'=2,'r'=4,'x'=4,'y'=4,'zh'=2] {'q2','zh'}, dimensions={0} | all-to-all | bytes 1048576 | tf_op jit(solution)/shard_map/all_to_all | solution.py:151
  (106 shorter events, 65.8 us)
Async XLA Ops:
  0.0 87.0 %copy-start = (bf16[1,1,256,4096]{3,2,1,0:T(8,128)(2,1)S(1)}, bf16[1,1,256,4096]{3,2,1,0:T(8,128)(2,1)}, u32[]{:S(2)}) copy-start(bf16[1,1,256,4096]{3,2,1,0:T(8,128)(2,1)} %param.11) | copy-start | bytes 6291460
  0.0 47.9 %copy-start.3 = (bf16[1,4096,32]{1,2,0:T(8,128)(2,1)S(1)}, bf16[1,4096,32]{1,2,0:T(8,128)(2,1)}, u32[]{:S(2)}) copy-start(bf16[1,4096,32]{1,2,0:T(8,128)(2,1)} %param.9) | copy-start | bytes 786436
  0.0 3.9 %collective-permute-start = (bf16[1,16,4096]{2,1,0:T(8,128)(2,1)}, bf16[1,16,4096]{2,1,0:T(8,128)(2,1)S(1)}, u32[]{:S(2)}, u32[]{:S(2)}) collective-permute-start(bf16[1,16,4096]{2,1,0:T(8,128)(2,1)} %param.7), channel_id=1, source_target_pairs={{0,256},{256,0},{1,257},{257,1},{2,258},{258,2},{3,259},{259,3},{4... | collective-permute-start | bytes 393224 | tf_op jit(solution)/shard_map/ppermute | solution.py:14
  4.9 25.5 %collective-permute-start.8 = (bf16[16,4224]{1,0:T(8,128)(2,1)S(1)}, bf16[16,4224]{1,0:T(8,128)(2,1)S(1)}, u32[]{:S(2)}, u32[]{:S(2)}) collective-permute-start(bf16[16,4224]{1,0:T(8,128)(2,1)S(1)} %fusion.37), channel_id=1, source_target_pairs={{0,129},{1,128},{128,1},{129,0},{2,131},{3,130},{130,3},{131,2},{4... | collective-permute-start | bytes 405512 | tf_op jit(solution)/shard_map/ppermute | solution.py:128
  16.5 21.4 %collective-permute-start.9 = (bf16[16,4224]{1,0:T(8,128)(2,1)S(1)}, bf16[16,4224]{1,0:T(8,128)(2,1)S(1)}, u32[]{:S(2)}, u32[]{:S(2)}) collective-permute-start(bf16[16,4224]{1,0:T(8,128)(2,1)S(1)} %fusion.37), channel_id=1, source_target_pairs={{0,1},{1,0},{128,129},{129,128},{2,3},{3,2},{130,131},{131,130},{4... | collective-permute-start | bytes 405512 | tf_op jit(solution)/shard_map/ppermute | solution.py:128
  21.4 23.3 %collective-permute-start.1 = (bf16[16,4224]{1,0:T(8,128)(2,1)S(1)}, bf16[16,4224]{1,0:T(8,128)(2,1)S(1)}, u32[]{:S(2)}, u32[]{:S(2)}) collective-permute-start(bf16[16,4224]{1,0:T(8,128)(2,1)S(1)} %fusion.37), channel_id=1, source_target_pairs={{0,128},{1,129},{128,0},{129,1},{2,130},{3,131},{130,2},{131,3},{4... | collective-permute-start | bytes 405512 | tf_op jit(solution)/shard_map/ppermute | solution.py:128
  72.4 14.6 %collective-permute-start.2 = (bf16[4,16,4096]{2,1,0:T(8,128)(2,1)S(1)}, bf16[4,16,4096]{2,1,0:T(8,128)(2,1)}, u32[]{:S(2)}, u32[]{:S(2)}) collective-permute-start(bf16[4,16,4096]{2,1,0:T(8,128)(2,1)S(1)} %copy.83), channel_id=1, source_target_pairs={{0,2},{2,4},{4,6},{6,0},{1,3},{3,5},{5,7},{7,1},{8,10},{10,12},{12... | collective-permute-start | bytes 1572872 | tf_op jit(solution)/shard_map/ppermute | solution.py:14
  76.8 39.6 %all-to-all-start.2 = ((bf16[4,16,4096]{2,0,1:T(4,128)(2,1)}), bf16[4,16,4096]{2,0,1:T(4,128)(2,1)S(1)}, u32[]{:S(2)}, u32[]{:S(2)}) async-start(bf16[4,16,4096]{2,0,1:T(4,128)(2,1)} %copy.93), calls=%async_computation.2 | async-start | bytes 1048576 | tf_op jit(solution)/shard_map/all_to_all | solution.py:65
  82.0 14.9 %collective-permute-start.4 = (bf16[4,16,4096]{2,1,0:T(8,128)(2,1)S(1)}, bf16[4,16,4096]{2,1,0:T(8,128)(2,1)}, u32[]{:S(2)}, u32[]{:S(2)}) collective-permute-start(bf16[4,16,4096]{2,1,0:T(8,128)(2,1)S(1)} %copy.83), channel_id=1, source_target_pairs={{0,4},{2,6},{4,0},{6,2},{1,5},{3,7},{5,1},{7,3},{8,12},{10,14},{12... | collective-permute-start | bytes 1572872 | tf_op jit(solution)/shard_map/ppermute | solution.py:14
  84.2 24.5 %collective-permute-start.6 = (bf16[4,16,4096]{2,1,0:T(8,128)(2,1)S(1)}, bf16[4,16,4096]{2,1,0:T(8,128)(2,1)}, u32[]{:S(2)}, u32[]{:S(2)}) collective-permute-start(bf16[4,16,4096]{2,1,0:T(8,128)(2,1)S(1)} %copy.83), channel_id=1, source_target_pairs={{0,6},{2,0},{4,2},{6,4},{1,7},{3,1},{5,3},{7,5},{8,14},{10,8},{12,... | collective-permute-start | bytes 1572872 | tf_op jit(solution)/shard_map/ppermute | solution.py:14
  91.0 32.0 %collective-permute-start.3 = (bf16[64,4096]{1,0:T(8,128)(2,1)}, bf16[64,4096]{1,0:T(8,128)(2,1)}, u32[]{:S(2)}, u32[]{:S(2)}) collective-permute-start(bf16[64,4096]{1,0:T(8,128)(2,1)} %convolution_convert_fusion.8), channel_id=1, source_target_pairs={{0,6},{2,0},{4,2},{6,4},{1,7},{3,1},{5,3},{7,5},{8,14},{10,8},{12,... | collective-permute-start | bytes 1572872 | tf_op jit(solution)/shard_map/ppermute | solution.py:14
  100.9 26.1 %collective-permute-start.5 = (bf16[64,4096]{1,0:T(8,128)(2,1)}, bf16[64,4096]{1,0:T(8,128)(2,1)}, u32[]{:S(2)}, u32[]{:S(2)}) collective-permute-start(bf16[64,4096]{1,0:T(8,128)(2,1)} %convolution_convert_fusion.7), channel_id=1, source_target_pairs={{0,4},{2,6},{4,0},{6,2},{1,5},{3,7},{5,1},{7,3},{8,12},{10,14},{12... | collective-permute-start | bytes 1572872 | tf_op jit(solution)/shard_map/ppermute | solution.py:14
  112.7 19.5 %collective-permute-start.7 = (bf16[64,4096]{1,0:T(8,128)(2,1)}, bf16[64,4096]{1,0:T(8,128)(2,1)}, u32[]{:S(2)}, u32[]{:S(2)}) collective-permute-start(bf16[64,4096]{1,0:T(8,128)(2,1)} %convolution_convert_fusion.6), channel_id=1, source_target_pairs={{0,2},{2,4},{4,6},{6,0},{1,3},{3,5},{5,7},{7,1},{8,10},{10,12},{12... | collective-permute-start | bytes 1572872 | tf_op jit(solution)/shard_map/ppermute | solution.py:14
  117.5 27.1 %collective-permute-start.10 = (bf16[4,16,4096]{2,1,0:T(8,128)(2,1)}, bf16[4,16,4096]{2,1,0:T(8,128)(2,1)}, u32[]{:S(2)}, u32[]{:S(2)}) collective-permute-start(bf16[4,16,4096]{2,1,0:T(8,128)(2,1)} %copy.94), channel_id=1, source_target_pairs={{0,2},{2,4},{4,6},{6,0},{1,3},{3,5},{5,7},{7,1},{8,10},{10,12},{12... | collective-permute-start | bytes 1572872 | tf_op jit(solution)/shard_map/ppermute | solution.py:14
  119.4 33.9 %collective-permute-start.12 = (bf16[4,16,4096]{2,1,0:T(8,128)(2,1)}, bf16[4,16,4096]{2,1,0:T(8,128)(2,1)}, u32[]{:S(2)}, u32[]{:S(2)}) collective-permute-start(bf16[4,16,4096]{2,1,0:T(8,128)(2,1)} %copy.94), channel_id=1, source_target_pairs={{0,4},{2,6},{4,0},{6,2},{1,5},{3,7},{5,1},{7,3},{8,12},{10,14},{12... | collective-permute-start | bytes 1572872 | tf_op jit(solution)/shard_map/ppermute | solution.py:14
  123.0 36.6 %collective-permute-start.14 = (bf16[4,16,4096]{2,1,0:T(8,128)(2,1)}, bf16[4,16,4096]{2,1,0:T(8,128)(2,1)}, u32[]{:S(2)}, u32[]{:S(2)}) collective-permute-start(bf16[4,16,4096]{2,1,0:T(8,128)(2,1)} %copy.94), channel_id=1, source_target_pairs={{0,6},{2,0},{4,2},{6,4},{1,7},{3,1},{5,3},{7,5},{8,14},{10,8},{12,... | collective-permute-start | bytes 1572872 | tf_op jit(solution)/shard_map/ppermute | solution.py:14
  136.7 54.6 %all-to-all-start.1 = ((bf16[4,16,4096]{2,0,1:T(4,128)(2,1)}), bf16[4,16,4096]{2,0,1:T(4,128)(2,1)S(1)}, u32[]{:S(2)}, u32[]{:S(2)}) async-start(bf16[4,16,4096]{2,0,1:T(4,128)(2,1)} %copy.87), calls=%async_computation.1 | async-start | bytes 1048576 | tf_op jit(solution)/shard_map/all_to_all | solution.py:77
  147.8 17.7 %collective-permute-start.11 = (bf16[64,4096]{1,0:T(8,128)(2,1)S(1)}, bf16[64,4096]{1,0:T(8,128)(2,1)}, u32[]{:S(2)}, u32[]{:S(2)}) collective-permute-start(bf16[64,4096]{1,0:T(8,128)(2,1)S(1)} %convolution_convert_fusion.4), channel_id=1, source_target_pairs={{0,6},{2,0},{4,2},{6,4},{1,7},{3,1},{5,3},{7,5},{8,14},{10,8},{12,... | collective-permute-start | bytes 1572872 | tf_op jit(solution)/shard_map/ppermute | solution.py:14
  157.3 14.0 %collective-permute-start.13 = (bf16[64,4096]{1,0:T(8,128)(2,1)}, bf16[64,4096]{1,0:T(8,128)(2,1)}, u32[]{:S(2)}, u32[]{:S(2)}) collective-permute-start(bf16[64,4096]{1,0:T(8,128)(2,1)} %convolution_convert_fusion.3), channel_id=1, source_target_pairs={{0,4},{2,6},{4,0},{6,2},{1,5},{3,7},{5,1},{7,3},{8,12},{10,14},{12... | collective-permute-start | bytes 1572872 | tf_op jit(solution)/shard_map/ppermute | solution.py:14
  163.6 22.1 %collective-permute-start.15 = (bf16[64,4096]{1,0:T(8,128)(2,1)}, bf16[64,4096]{1,0:T(8,128)(2,1)S(1)}, u32[]{:S(2)}, u32[]{:S(2)}) collective-permute-start(bf16[64,4096]{1,0:T(8,128)(2,1)} %convolution_convert_fusion.2), channel_id=1, source_target_pairs={{0,2},{2,4},{4,6},{6,0},{1,3},{3,5},{5,7},{7,1},{8,10},{10,12},{12... | collective-permute-start | bytes 1572872 | tf_op jit(solution)/shard_map/ppermute | solution.py:14
  185.7 0.8 copy-start.2
  190.1 7.1 %copy-start.1 = (s32[2,2]{1,0:T(2,128)S(1)}, s32[2,2]{1,0:T(2,128)}, u32[]{:S(2)}) copy-start(s32[2,2]{1,0:T(2,128)} %constant.147.clone) | copy-start | bytes 52
  191.3 19.9 %all-to-all-start.3 = ((bf16[4,16,4096]{2,0,1:T(4,128)(2,1)}), bf16[4,16,4096]{2,0,1:T(4,128)(2,1)S(1)}, u32[]{:S(2)}, u32[]{:S(2)}) async-start(bf16[4,16,4096]{2,0,1:T(4,128)(2,1)} %copy.98), calls=%async_computation.3 | async-start | bytes 1048576 | tf_op jit(solution)/shard_map/all_to_all | solution.py:77
  253.2 4.1 %collective-permute-start.16 = (bf16[1,16,4096]{2,1,0:T(8,128)(2,1)S(1)}, bf16[1,16,4096]{2,1,0:T(8,128)(2,1)S(1)}, u32[]{:S(2)}, u32[]{:S(2)}) collective-permute-start(bf16[1,16,4096]{2,1,0:T(8,128)(2,1)S(1)} %fusion.32), channel_id=1, source_target_pairs={{0,256},{256,0},{1,257},{257,1},{2,258},{258,2},{3,259},{259,3},{4... | collective-permute-start | bytes 393224 | tf_op jit(solution)/shard_map/ppermute | solution.py:14

commit v12 on v10

--- a/solution.py
+++ b/solution.py
@@ -130,7 +130,7 @@
         picks.append(far[:, model_width:model_width + top_count].astype(jnp.int32))
     w_first = w_in[0, 0]
     w_second = w_out[0, 0]
-    chunk = len(rows) // 2
+    chunk = 1
     halves = []
     for part in (slice(0, chunk), slice(chunk, len(rows))):
         slots, combine = dispatch(

time: 252 us -> 277 us (1.099)
  waiting for transfers between devices: 62.2 us -> 104 us
  blocking collectives: 16.6 us -> 0 us
  starting transfers between devices: 126 us -> 123 us
  local copies, waits for them, and re-layouts: 8.62 us -> 11.6 us
    all_to_all x1 -> x2, waiting for transfers between devices: 0.01 us -> 21.6 us  [expert_pass(): lax.all_to_all(slot_grid, QUARTER, split_axis=1, concat_axis=1, tiled=True)]
    all_to_all x1 -> x0, blocking collectives: 16.6 us -> none  [expert_pass(): lax.all_to_all(slot_grid, QUARTER, split_axis=1, concat_axis=1, tiled=True)]
    ppermute x14, waiting for transfers between devices: 31.4 us -> 43.8 us  [passed_along(): return lax.ppermute(value, axis, pairs)]
    ppermute x3, starting transfers between devices: 27.5 us -> 16.7 us  [on_device(): lax.ppermute(sums[j].astype(jnp.bfloat16), ('q2', 'zh'), home)]
    all_to_all x1 -> x2, starting transfers between devices: 5.54 us -> 13.5 us  [expert_pass(): lax.all_to_all(slot_grid, QUARTER, split_axis=1, concat_axis=1, tiled=True)]
    ppermute x3, waiting for transfers between devices: 9.11 us -> 17 us  [on_device(): lax.ppermute(sums[j].astype(jnp.bfloat16), ('q2', 'zh'), home)]
    ppermute x14, starting transfers between devices: 63 us -> 57.6 us  [passed_along(): return lax.ppermute(value, axis, pairs)]
    all_to_all x2, starting transfers between devices: 13.9 us -> 18.7 us  [expert_pass(): lax.all_to_all(summed.astype(jnp.bfloat16).reshape(lead, n_local, model_w...]
  transfers between devices with their start and end apart: 23 -> 24, of which waited for: 12 -> 12; matrix products, arithmetic and copies ran while one was open for 15% -> 14% of each run, Pallas kernels for 0% -> 0%
where the time goes in v12:
time: 277 us; the launch traced here: 276 us
  starting transfers between devices  123 us (44%)
  waiting for transfers between devices  104 us (38%)
  matrix products  33.1 us (12%)
  local copies, waits for them, and re-layouts  11.6 us (4%)
  other arithmetic  3.56 us (1%)
    ppermute x14, starting transfers between devices, passed_along(): return lax.ppermute(value, axis, pairs)  57.6 us
    ppermute x14, waiting for transfers between devices, passed_along(): return lax.ppermute(value, axis, pairs)  43.8 us
    dot_general x8, matrix products, expert_pass(): jnp.dot(hidden, w_second, preferred_element_type=jnp.float32)  28.6 us
    ppermute x3, waiting for transfers between devices, on_device(): far = lax.ppermute(packed, ('q2', 'zh'), shifted_pairs((n_q, n_zh), (a, c)))  21.9 us
    all_to_all x2, waiting for transfers between devices, expert_pass(): lax.all_to_all(slot_grid, QUARTER, split_axis=1, concat_axis=1, tiled=True)  21.6 us
    all_to_all x2, starting transfers between devices, expert_pass(): lax.all_to_all(summed.astype(jnp.bfloat16).reshape(lead, n_local, model_w...  18.7 us
    ppermute x3, waiting for transfers between devices, on_device(): lax.ppermute(sums[j].astype(jnp.bfloat16), ('q2', 'zh'), home)  17 us
    ppermute x3, starting transfers between devices, on_device(): lax.ppermute(sums[j].astype(jnp.bfloat16), ('q2', 'zh'), home)  16.7 us
  transfers between devices with their start and end apart: 24, of which 12 were waited for; matrix products, arithmetic and copies ran while one was open for 14% of the time, Pallas kernels for 0%

profile of v12, /device:TPU:1, one launch (start us, length us, event | category | flops | bytes accessed | tf_op | source)
XLA Modules:
  0.0 275.7 jit_solution(16030741796455075038)
XLA Ops:
  0.0 8.9 %collective-permute-start = (bf16[1,16,4096]{2,1,0:T(8,128)(2,1)}, bf16[1,16,4096]{2,1,0:T(8,128)(2,1)S(1)}, u32[]{:S(2)}, u32[]{:S(2)}) collective-permute-start(bf16[1,16,4096]{2,1,0:T(8,128)(2,1)} %param.6), channel_id=1, source_target_pairs={{0,256},{256,0},{1,257},{257,1},{2,258},{258,2},{3,259},{259,3},{4... | collective-permute-start | bytes 393224 | tf_op jit(solution)/shard_map/ppermute | solution.py:14
  11.1 7.1 %collective-permute-start.8 = (bf16[16,4224]{1,0:T(8,128)(2,1)S(1)}, bf16[16,4224]{1,0:T(8,128)(2,1)S(1)}, u32[]{:S(2)}, u32[]{:S(2)}) collective-permute-start(bf16[16,4224]{1,0:T(8,128)(2,1)S(1)} %fusion.43), channel_id=1, source_target_pairs={{0,129},{1,128},{128,1},{129,0},{2,131},{3,130},{130,3},{131,2},{4... | collective-permute-start | bytes 405512 | tf_op jit(solution)/shard_map/ppermute | solution.py:128
  18.2 4.9 %collective-permute-start.9 = (bf16[16,4224]{1,0:T(8,128)(2,1)S(1)}, bf16[16,4224]{1,0:T(8,128)(2,1)S(1)}, u32[]{:S(2)}, u32[]{:S(2)}) collective-permute-start(bf16[16,4224]{1,0:T(8,128)(2,1)S(1)} %fusion.43), channel_id=1, source_target_pairs={{0,1},{1,0},{128,129},{129,128},{2,3},{3,2},{130,131},{131,130},{4... | collective-permute-start | bytes 405512 | tf_op jit(solution)/shard_map/ppermute | solution.py:128
  23.1 4.2 %collective-permute-start.7 = (bf16[16,4224]{1,0:T(8,128)(2,1)S(1)}, bf16[16,4224]{1,0:T(8,128)(2,1)S(1)}, u32[]{:S(2)}, u32[]{:S(2)}) collective-permute-start(bf16[16,4224]{1,0:T(8,128)(2,1)S(1)} %fusion.43), channel_id=1, source_target_pairs={{0,128},{1,129},{128,0},{129,1},{2,130},{3,131},{130,2},{131,3},{4... | collective-permute-start | bytes 405512 | tf_op jit(solution)/shard_map/ppermute | solution.py:128
  27.3 11.9 %collective-permute-done.8 = bf16[16,4224]{1,0:T(8,128)(2,1)S(1)} collective-permute-done((bf16[16,4224]{1,0:T(8,128)(2,1)S(1)}, bf16[16,4224]{1,0:T(8,128)(2,1)S(1)}, u32[]{:S(2)}, u32[]{:S(2)}) %collective-permute-start.8) | collective-permute-done | bytes 135200 | tf_op jit(solution)/shard_map/ppermute | solution.py:128
  39.3 10.0 %collective-permute-done.9 = bf16[16,4224]{1,0:T(8,128)(2,1)S(1)} collective-permute-done((bf16[16,4224]{1,0:T(8,128)(2,1)S(1)}, bf16[16,4224]{1,0:T(8,128)(2,1)S(1)}, u32[]{:S(2)}, u32[]{:S(2)}) %collective-permute-start.9) | collective-permute-done | bytes 135200 | tf_op jit(solution)/shard_map/ppermute | solution.py:128
  54.2 5.7 %all-to-all-start.2 = ((bf16[6,16,4096]{2,0,1:T(8,128)(2,1)}), bf16[6,16,4096]{2,0,1:T(8,128)(2,1)S(1)}, u32[]{:S(2)}, u32[]{:S(2)}) async-start(bf16[6,16,4096]{2,0,1:T(8,128)(2,1)} %copy.104), calls=%async_computation.2 | async-start | bytes 2097152 | tf_op jit(solution)/shard_map/all_to_all | solution.py:65
  60.4 21.6 %all-to-all-done.2 = bf16[6,16,4096]{2,0,1:T(8,128)(2,1)S(1)} async-done(((bf16[6,16,4096]{2,0,1:T(8,128)(2,1)}), bf16[6,16,4096]{2,0,1:T(8,128)(2,1)S(1)}, u32[]{:S(2)}, u32[]{:S(2)}) %all-to-all-start.2) | async-done | bytes 786464 | tf_op jit(solution)/shard_map/all_to_all | solution.py:65
  87.8 4.5 %collective-permute-start.12 = (bf16[6,16,4096]{2,1,0:T(8,128)(2,1)}, bf16[6,16,4096]{2,1,0:T(8,128)(2,1)}, u32[]{:S(2)}, u32[]{:S(2)}) collective-permute-start(bf16[6,16,4096]{2,1,0:T(8,128)(2,1)} %copy.105), channel_id=1, source_target_pairs={{0,4},{2,6},{4,0},{6,2},{1,5},{3,7},{5,1},{7,3},{8,12},{10,14},{12... | collective-permute-start | bytes 2359304 | tf_op jit(solution)/shard_map/ppermute | solution.py:14
  95.5 7.0 %collective-permute-done.10 = bf16[6,16,4096]{2,1,0:T(8,128)(2,1)S(1)} collective-permute-done((bf16[6,16,4096]{2,1,0:T(8,128)(2,1)}, bf16[6,16,4096]{2,1,0:T(8,128)(2,1)S(1)}, u32[]{:S(2)}, u32[]{:S(2)}) %collective-permute-start.10) | collective-permute-done | bytes 786464 | tf_op jit(solution)/shard_map/ppermute | solution.py:14
  110.0 10.6 %collective-permute-done.12 = bf16[6,16,4096]{2,1,0:T(8,128)(2,1)} collective-permute-done((bf16[6,16,4096]{2,1,0:T(8,128)(2,1)}, bf16[6,16,4096]{2,1,0:T(8,128)(2,1)}, u32[]{:S(2)}, u32[]{:S(2)}) %collective-permute-start.12) | collective-permute-done | bytes 786464 | tf_op jit(solution)/shard_map/ppermute | solution.py:14
  120.6 4.0 %convolution_convert_fusion.1 = bf16[96,4096]{1,0:T(8,128)(2,1)} fusion(bf16[1,1,256,4096]{3,2,1,0:T(8,128)(2,1)S(1)} %copy-done, bf16[96,4096]{1,0:T(8,128)(2,1)} %bitcast.23, bf16[1,1,4096,256]{3,2,1,0:T(8,128)(2,1)} %param.9), kind=kOutput, calls=%fused_computation.1 | convolution fusion | flops 403267584 | bytes 5767168 | tf_op jit(solution)/shard_map/dot_general | solution.py:72
  126.9 4.1 %convolution_convert_fusion = bf16[96,4096]{1,0:T(8,128)(2,1)} fusion(bf16[1,1,256,4096]{3,2,1,0:T(8,128)(2,1)S(1)} %copy-done, bf16[96,4096]{1,0:T(8,128)(2,1)} %bitcast.24, bf16[1,1,4096,256]{3,2,1,0:T(8,128)(2,1)} %param.9), kind=kOutput, calls=%fused_computation | convolution fusion | flops 403267584 | bytes 5767168 | tf_op jit(solution)/shard_map/dot_general | solution.py:72
  131.0 4.1 %collective-permute-start.15 = (bf16[96,4096]{1,0:T(8,128)(2,1)}, bf16[96,4096]{1,0:T(8,128)(2,1)}, u32[]{:S(2)}, u32[]{:S(2)}) collective-permute-start(bf16[96,4096]{1,0:T(8,128)(2,1)} %convolution_convert_fusion), channel_id=1, source_target_pairs={{0,2},{2,4},{4,6},{6,0},{1,3},{3,5},{5,7},{7,1},{8,10},{10,12},{12... | collective-permute-start | bytes 2359304 | tf_op jit(solution)/shard_map/ppermute | solution.py:14
  136.4 7.8 %all-to-all-start = ((bf16[2,16,4096]{2,0,1:T(2,128)(2,1)}), bf16[2,16,4096]{2,0,1:T(2,128)(2,1)S(1)}, u32[]{:S(2)}, u32[]{:S(2)}) async-start(bf16[2,16,4096]{2,0,1:T(2,128)(2,1)} %copy.91), calls=%async_computation | async-start | bytes 524288 | tf_op jit(solution)/shard_map/all_to_all | solution.py:65
  146.0 14.7 %collective-permute-done.15 = bf16[96,4096]{1,0:T(8,128)(2,1)} collective-permute-done((bf16[96,4096]{1,0:T(8,128)(2,1)}, bf16[96,4096]{1,0:T(8,128)(2,1)}, u32[]{:S(2)}, u32[]{:S(2)}) %collective-permute-start.15) | collective-permute-done | bytes 786464 | tf_op jit(solution)/shard_map/ppermute | solution.py:14
  166.0 11.8 %all-to-all-start.3 = ((bf16[6,16,4096]{2,0,1:T(8,128)(2,1)}), bf16[6,16,4096]{2,0,1:T(8,128)(2,1)S(1)}, u32[]{:S(2)}, u32[]{:S(2)}) async-start(bf16[6,16,4096]{2,0,1:T(8,128)(2,1)} %copy.109), calls=%async_computation.3 | async-start | bytes 2097152 | tf_op jit(solution)/shard_map/all_to_all | solution.py:77
  182.9 4.2 %collective-permute-start.5 = (bf16[2,16,4096]{2,1,0:T(8,128)(2,1)}, bf16[2,16,4096]{2,1,0:T(8,128)(2,1)}, u32[]{:S(2)}, u32[]{:S(2)}) collective-permute-start(bf16[2,16,4096]{2,1,0:T(8,128)(2,1)} %copy.92), channel_id=1, source_target_pairs={{0,6},{2,0},{4,2},{6,4},{1,7},{3,1},{5,3},{7,5},{8,14},{10,8},{12,... | collective-permute-start | bytes 786440 | tf_op jit(solution)/shard_map/ppermute | solution.py:14
  207.3 7.1 %collective-permute-done.6 = bf16[32,4096]{1,0:T(8,128)(2,1)S(1)} collective-permute-done((bf16[32,4096]{1,0:T(8,128)(2,1)}, bf16[32,4096]{1,0:T(8,128)(2,1)S(1)}, u32[]{:S(2)}, u32[]{:S(2)}) %collective-permute-start.6) | collective-permute-done | bytes 262176 | tf_op jit(solution)/shard_map/ppermute | solution.py:14
  219.3 7.0 %all-to-all-start.1 = ((bf16[2,16,4096]{2,0,1:T(2,128)(2,1)}), bf16[2,16,4096]{2,0,1:T(2,128)(2,1)S(1)}, u32[]{:S(2)}, u32[]{:S(2)}) async-start(bf16[2,16,4096]{2,0,1:T(2,128)(2,1)} %copy.96), calls=%async_computation.1 | async-start | bytes 524288 | tf_op jit(solution)/shard_map/all_to_all | solution.py:77
  231.3 8.3 %collective-permute-start.17 = (bf16[16,4096]{1,0:T(8,128)(2,1)S(1)}, bf16[16,4096]{1,0:T(8,128)(2,1)S(1)}, u32[]{:S(2)}, u32[]{:S(2)}) collective-permute-start(bf16[16,4096]{1,0:T(8,128)(2,1)S(1)} %get-tuple-element.13), channel_id=1, source_target_pairs={{0,129},{1,128},{128,1},{129,0},{2,131},{3,130},{130,3},{131,2},{4... | collective-permute-start | bytes 393224 | tf_op jit(solution)/shard_map/ppermute | solution.py:145
  239.6 5.0 %collective-permute-start.18 = (bf16[16,4096]{1,0:T(8,128)(2,1)S(1)}, bf16[16,4096]{1,0:T(8,128)(2,1)S(1)}, u32[]{:S(2)}, u32[]{:S(2)}) collective-permute-start(bf16[16,4096]{1,0:T(8,128)(2,1)S(1)} %get-tuple-element.12), channel_id=1, source_target_pairs={{0,1},{1,0},{128,129},{129,128},{2,3},{3,2},{130,131},{131,130},{4... | collective-permute-start | bytes 393224 | tf_op jit(solution)/shard_map/ppermute | solution.py:145
  244.8 17.0 %collective-permute-done.18 = bf16[16,4096]{1,0:T(8,128)(2,1)S(1)} collective-permute-done((bf16[16,4096]{1,0:T(8,128)(2,1)S(1)}, bf16[16,4096]{1,0:T(8,128)(2,1)S(1)}, u32[]{:S(2)}, u32[]{:S(2)}) %collective-permute-start.18) | collective-permute-done | bytes 131104 | tf_op jit(solution)/shard_map/ppermute | solution.py:145
  262.1 11.9 %collective-permute-start.19 = (bf16[1,16,4096]{2,1,0:T(8,128)(2,1)S(1)}, bf16[1,16,4096]{2,1,0:T(8,128)(2,1)S(1)}, u32[]{:S(2)}, u32[]{:S(2)}) collective-permute-start(bf16[1,16,4096]{2,1,0:T(8,128)(2,1)S(1)} %fusion.6), channel_id=1, source_target_pairs={{0,256},{256,0},{1,257},{257,1},{2,258},{258,2},{3,259},{259,3},{4... | collective-permute-start | bytes 393224 | tf_op jit(solution)/shard_map/ppermute | solution.py:14
  (104 shorter events, 72.0 us)
Async XLA Ops:
  0.0 10.0 %collective-permute-start = (bf16[1,16,4096]{2,1,0:T(8,128)(2,1)}, bf16[1,16,4096]{2,1,0:T(8,128)(2,1)S(1)}, u32[]{:S(2)}, u32[]{:S(2)}) collective-permute-start(bf16[1,16,4096]{2,1,0:T(8,128)(2,1)} %param.6), channel_id=1, source_target_pairs={{0,256},{256,0},{1,257},{257,1},{2,258},{258,2},{3,259},{259,3},{4... | collective-permute-start | bytes 393224 | tf_op jit(solution)/shard_map/ppermute | solution.py:14
  11.1 28.1 %collective-permute-start.8 = (bf16[16,4224]{1,0:T(8,128)(2,1)S(1)}, bf16[16,4224]{1,0:T(8,128)(2,1)S(1)}, u32[]{:S(2)}, u32[]{:S(2)}) collective-permute-start(bf16[16,4224]{1,0:T(8,128)(2,1)S(1)} %fusion.43), channel_id=1, source_target_pairs={{0,129},{1,128},{128,1},{129,0},{2,131},{3,130},{130,3},{131,2},{4... | collective-permute-start | bytes 405512 | tf_op jit(solution)/shard_map/ppermute | solution.py:128
  18.2 31.1 %collective-permute-start.9 = (bf16[16,4224]{1,0:T(8,128)(2,1)S(1)}, bf16[16,4224]{1,0:T(8,128)(2,1)S(1)}, u32[]{:S(2)}, u32[]{:S(2)}) collective-permute-start(bf16[16,4224]{1,0:T(8,128)(2,1)S(1)} %fusion.43), channel_id=1, source_target_pairs={{0,1},{1,0},{128,129},{129,128},{2,3},{3,2},{130,131},{131,130},{4... | collective-permute-start | bytes 405512 | tf_op jit(solution)/shard_map/ppermute | solution.py:128
  23.1 26.3 %collective-permute-start.7 = (bf16[16,4224]{1,0:T(8,128)(2,1)S(1)}, bf16[16,4224]{1,0:T(8,128)(2,1)S(1)}, u32[]{:S(2)}, u32[]{:S(2)}) collective-permute-start(bf16[16,4224]{1,0:T(8,128)(2,1)S(1)} %fusion.43), channel_id=1, source_target_pairs={{0,128},{1,129},{128,0},{129,1},{2,130},{3,131},{130,2},{131,3},{4... | collective-permute-start | bytes 405512 | tf_op jit(solution)/shard_map/ppermute | solution.py:128
  54.2 27.9 %all-to-all-start.2 = ((bf16[6,16,4096]{2,0,1:T(8,128)(2,1)}), bf16[6,16,4096]{2,0,1:T(8,128)(2,1)S(1)}, u32[]{:S(2)}, u32[]{:S(2)}) async-start(bf16[6,16,4096]{2,0,1:T(8,128)(2,1)} %copy.104), calls=%async_computation.2 | async-start | bytes 2097152 | tf_op jit(solution)/shard_map/all_to_all | solution.py:65
  83.4 19.1 %collective-permute-start.10 = (bf16[6,16,4096]{2,1,0:T(8,128)(2,1)}, bf16[6,16,4096]{2,1,0:T(8,128)(2,1)S(1)}, u32[]{:S(2)}, u32[]{:S(2)}) collective-permute-start(bf16[6,16,4096]{2,1,0:T(8,128)(2,1)} %copy.105), channel_id=1, source_target_pairs={{0,2},{2,4},{4,6},{6,0},{1,3},{3,5},{5,7},{7,1},{8,10},{10,12},{12... | collective-permute-start | bytes 2359304 | tf_op jit(solution)/shard_map/ppermute | solution.py:14
  87.8 32.8 %collective-permute-start.12 = (bf16[6,16,4096]{2,1,0:T(8,128)(2,1)}, bf16[6,16,4096]{2,1,0:T(8,128)(2,1)}, u32[]{:S(2)}, u32[]{:S(2)}) collective-permute-start(bf16[6,16,4096]{2,1,0:T(8,128)(2,1)} %copy.105), channel_id=1, source_target_pairs={{0,4},{2,6},{4,0},{6,2},{1,5},{3,7},{5,1},{7,3},{8,12},{10,14},{12... | collective-permute-start | bytes 2359304 | tf_op jit(solution)/shard_map/ppermute | solution.py:14
  92.5 34.4 %collective-permute-start.14 = (bf16[6,16,4096]{2,1,0:T(8,128)(2,1)}, bf16[6,16,4096]{2,1,0:T(8,128)(2,1)}, u32[]{:S(2)}, u32[]{:S(2)}) collective-permute-start(bf16[6,16,4096]{2,1,0:T(8,128)(2,1)} %copy.105), channel_id=1, source_target_pairs={{0,6},{2,0},{4,2},{6,4},{1,7},{3,1},{5,3},{7,5},{8,14},{10,8},{12,... | collective-permute-start | bytes 2359304 | tf_op jit(solution)/shard_map/ppermute | solution.py:14
  106.6 39.4 %collective-permute-start.11 = (bf16[96,4096]{1,0:T(8,128)(2,1)S(1)}, bf16[96,4096]{1,0:T(8,128)(2,1)}, u32[]{:S(2)}, u32[]{:S(2)}) collective-permute-start(bf16[96,4096]{1,0:T(8,128)(2,1)S(1)} %convolution_convert_fusion.2), channel_id=1, source_target_pairs={{0,6},{2,0},{4,2},{6,4},{1,7},{3,1},{5,3},{7,5},{8,14},{10,8},{12,... | collective-permute-start | bytes 2359304 | tf_op jit(solution)/shard_map/ppermute | solution.py:14
  124.6 21.4 %collective-permute-start.13 = (bf16[96,4096]{1,0:T(8,128)(2,1)}, bf16[96,4096]{1,0:T(8,128)(2,1)}, u32[]{:S(2)}, u32[]{:S(2)}) collective-permute-start(bf16[96,4096]{1,0:T(8,128)(2,1)} %convolution_convert_fusion.1), channel_id=1, source_target_pairs={{0,4},{2,6},{4,0},{6,2},{1,5},{3,7},{5,1},{7,3},{8,12},{10,14},{12... | collective-permute-start | bytes 2359304 | tf_op jit(solution)/shard_map/ppermute | solution.py:14
  131.0 29.7 %collective-permute-start.15 = (bf16[96,4096]{1,0:T(8,128)(2,1)}, bf16[96,4096]{1,0:T(8,128)(2,1)}, u32[]{:S(2)}, u32[]{:S(2)}) collective-permute-start(bf16[96,4096]{1,0:T(8,128)(2,1)} %convolution_convert_fusion), channel_id=1, source_target_pairs={{0,2},{2,4},{4,6},{6,0},{1,3},{3,5},{5,7},{7,1},{8,10},{10,12},{12... | collective-permute-start | bytes 2359304 | tf_op jit(solution)/shard_map/ppermute | solution.py:14
  136.4 29.5 %all-to-all-start = ((bf16[2,16,4096]{2,0,1:T(2,128)(2,1)}), bf16[2,16,4096]{2,0,1:T(2,128)(2,1)S(1)}, u32[]{:S(2)}, u32[]{:S(2)}) async-start(bf16[2,16,4096]{2,0,1:T(2,128)(2,1)} %copy.91), calls=%async_computation | async-start | bytes 524288 | tf_op jit(solution)/shard_map/all_to_all | solution.py:65
  166.0 53.3 %all-to-all-start.3 = ((bf16[6,16,4096]{2,0,1:T(8,128)(2,1)}), bf16[6,16,4096]{2,0,1:T(8,128)(2,1)S(1)}, u32[]{:S(2)}, u32[]{:S(2)}) async-start(bf16[6,16,4096]{2,0,1:T(8,128)(2,1)} %copy.109), calls=%async_computation.3 | async-start | bytes 2097152 | tf_op jit(solution)/shard_map/all_to_all | solution.py:77
  178.6 9.6 %collective-permute-start.1 = (bf16[2,16,4096]{2,1,0:T(8,128)(2,1)}, bf16[2,16,4096]{2,1,0:T(8,128)(2,1)S(1)}, u32[]{:S(2)}, u32[]{:S(2)}) collective-permute-start(bf16[2,16,4096]{2,1,0:T(8,128)(2,1)} %copy.92), channel_id=1, source_target_pairs={{0,2},{2,4},{4,6},{6,0},{1,3},{3,5},{5,7},{7,1},{8,10},{10,12},{12... | collective-permute-start | bytes 786440 | tf_op jit(solution)/shard_map/ppermute | solution.py:14
  180.5 13.3 %collective-permute-start.3 = (bf16[2,16,4096]{2,1,0:T(8,128)(2,1)}, bf16[2,16,4096]{2,1,0:T(8,128)(2,1)}, u32[]{:S(2)}, u32[]{:S(2)}) collective-permute-start(bf16[2,16,4096]{2,1,0:T(8,128)(2,1)} %copy.92), channel_id=1, source_target_pairs={{0,4},{2,6},{4,0},{6,2},{1,5},{3,7},{5,1},{7,3},{8,12},{10,14},{12... | collective-permute-start | bytes 786440 | tf_op jit(solution)/shard_map/ppermute | solution.py:14
  182.9 18.0 %collective-permute-start.5 = (bf16[2,16,4096]{2,1,0:T(8,128)(2,1)}, bf16[2,16,4096]{2,1,0:T(8,128)(2,1)}, u32[]{:S(2)}, u32[]{:S(2)}) collective-permute-start(bf16[2,16,4096]{2,1,0:T(8,128)(2,1)} %copy.92), channel_id=1, source_target_pairs={{0,6},{2,0},{4,2},{6,4},{1,7},{3,1},{5,3},{7,5},{8,14},{10,8},{12,... | collective-permute-start | bytes 786440 | tf_op jit(solution)/shard_map/ppermute | solution.py:14
  191.9 15.4 %collective-permute-start.2 = (bf16[32,4096]{1,0:T(8,128)(2,1)S(1)}, bf16[32,4096]{1,0:T(8,128)(2,1)}, u32[]{:S(2)}, u32[]{:S(2)}) collective-permute-start(bf16[32,4096]{1,0:T(8,128)(2,1)S(1)} %convolution_convert_fusion.8), channel_id=1, source_target_pairs={{0,6},{2,0},{4,2},{6,4},{1,7},{3,1},{5,3},{7,5},{8,14},{10,8},{12,... | collective-permute-start | bytes 786440 | tf_op jit(solution)/shard_map/ppermute | solution.py:14
  197.5 9.7 %collective-permute-start.4 = (bf16[32,4096]{1,0:T(8,128)(2,1)}, bf16[32,4096]{1,0:T(8,128)(2,1)}, u32[]{:S(2)}, u32[]{:S(2)}) collective-permute-start(bf16[32,4096]{1,0:T(8,128)(2,1)} %convolution_convert_fusion.7), channel_id=1, source_target_pairs={{0,4},{2,6},{4,0},{6,2},{1,5},{3,7},{5,1},{7,3},{8,12},{10,14},{12... | collective-permute-start | bytes 786440 | tf_op jit(solution)/shard_map/ppermute | solution.py:14
  204.5 9.9 %collective-permute-start.6 = (bf16[32,4096]{1,0:T(8,128)(2,1)}, bf16[32,4096]{1,0:T(8,128)(2,1)S(1)}, u32[]{:S(2)}, u32[]{:S(2)}) collective-permute-start(bf16[32,4096]{1,0:T(8,128)(2,1)} %convolution_convert_fusion.6), channel_id=1, source_target_pairs={{0,2},{2,4},{4,6},{6,0},{1,3},{3,5},{5,7},{7,1},{8,10},{10,12},{12... | collective-permute-start | bytes 786440 | tf_op jit(solution)/shard_map/ppermute | solution.py:14
  219.3 25.4 %all-to-all-start.1 = ((bf16[2,16,4096]{2,0,1:T(2,128)(2,1)}), bf16[2,16,4096]{2,0,1:T(2,128)(2,1)S(1)}, u32[]{:S(2)}, u32[]{:S(2)}) async-start(bf16[2,16,4096]{2,0,1:T(2,128)(2,1)} %copy.96), calls=%async_computation.1 | async-start | bytes 524288 | tf_op jit(solution)/shard_map/all_to_all | solution.py:77
  227.9 16.9 %collective-permute-start.16 = (bf16[16,4096]{1,0:T(8,128)(2,1)S(1)}, bf16[16,4096]{1,0:T(8,128)(2,1)S(1)}, u32[]{:S(2)}, u32[]{:S(2)}) collective-permute-start(bf16[16,4096]{1,0:T(8,128)(2,1)S(1)} %get-tuple-element.11), channel_id=1, source_target_pairs={{0,128},{1,129},{128,0},{129,1},{2,130},{3,131},{130,2},{131,3},{4... | collective-permute-start | bytes 393224 | tf_op jit(solution)/shard_map/ppermute | solution.py:145
  231.3 13.4 %collective-permute-start.17 = (bf16[16,4096]{1,0:T(8,128)(2,1)S(1)}, bf16[16,4096]{1,0:T(8,128)(2,1)S(1)}, u32[]{:S(2)}, u32[]{:S(2)}) collective-permute-start(bf16[16,4096]{1,0:T(8,128)(2,1)S(1)} %get-tuple-element.13), channel_id=1, source_target_pairs={{0,129},{1,128},{128,1},{129,0},{2,131},{3,130},{130,3},{131,2},{4... | collective-permute-start | bytes 393224 | tf_op jit(solution)/shard_map/ppermute | solution.py:145
  239.6 22.2 %collective-permute-start.18 = (bf16[16,4096]{1,0:T(8,128)(2,1)S(1)}, bf16[16,4096]{1,0:T(8,128)(2,1)S(1)}, u32[]{:S(2)}, u32[]{:S(2)}) collective-permute-start(bf16[16,4096]{1,0:T(8,128)(2,1)S(1)} %get-tuple-element.12), channel_id=1, source_target_pairs={{0,1},{1,0},{128,129},{129,128},{2,3},{3,2},{130,131},{131,130},{4... | collective-permute-start | bytes 393224 | tf_op jit(solution)/shard_map/ppermute | solution.py:145
  262.1 12.9 %collective-permute-start.19 = (bf16[1,16,4096]{2,1,0:T(8,128)(2,1)S(1)}, bf16[1,16,4096]{2,1,0:T(8,128)(2,1)S(1)}, u32[]{:S(2)}, u32[]{:S(2)}) collective-permute-start(bf16[1,16,4096]{2,1,0:T(8,128)(2,1)S(1)} %fusion.6), channel_id=1, source_target_pairs={{0,256},{256,0},{1,257},{257,1},{2,258},{258,2},{3,259},{259,3},{4... | collective-permute-start | bytes 393224 | tf_op jit(solution)/shard_map/ppermute | solution.py:14
  (6 other events, 145.4 us)

commit v13 on v10

--- a/solution.py
+++ b/solution.py
@@ -103,13 +103,13 @@
     return pairs
 
 
-def on_device(sent, norm_gain, router, w_in, w_out, expert_ids):
+def layer_body(sent, norm_gain, router, w_in, w_out, expert_ids):
     arrived = passed_along(sent, "section", 1)[0]
     tok_count = arrived.shape[0]
     experts = router.shape[2]
     top_count = expert_ids.shape[2]
     capacity = max(2, (5 * top_count * tok_count + 4 * experts - 1) // (4 * experts))
-    n_sec, n_q, n_zh = (lax.axis_size(a) for a in ("section", "q2", "zh"))
+    _, n_q, n_zh = (lax.axis_size(a) for a in ("section", "q2", "zh"))
     n_local = experts // n_q
     home_q = lax.axis_index("q2")
     offsets = sorted(
@@ -142,9 +142,8 @@
     combined = arrived.astype(jnp.float32) + sums[0]
     for j, (a, c) in enumerate(offsets, start=1):
         home = shifted_pairs((n_q, n_zh), (-a, -c))
-        combined = combined + lax.ppermute(sums[j].astype(jnp.bfloat16), ("q2", "zh"), home).astype(
-            jnp.float32
-        )
+        returned = lax.ppermute(sums[j].astype(jnp.bfloat16), ("q2", "zh"), home)
+        combined = combined + returned.astype(jnp.float32)
     return passed_along(combined.astype(jnp.bfloat16)[None], "section", 1)
 
 
@@ -160,7 +159,7 @@
     hidden_units = ("y", "zh")
     tokens = experts_at + hidden_units
     return jax.shard_map(
-        on_device,
+        layer_body,
         mesh=fine,
         in_specs=(
             P("section", tokens, None),

time: 252 us -> 252 us (level)
  no operation moved by 1% of the time
where the time goes in v13:
time: 252 us; the launch traced here: 251 us
  starting transfers between devices  126 us (50%)
  waiting for transfers between devices  62.2 us (25%)
  matrix products  32.8 us (13%)
  blocking collectives  16.6 us (7%)
  local copies, waits for them, and re-layouts  8.62 us (3%)
  other arithmetic  3.97 us (2%)
    ppermute x14, starting transfers between devices, passed_along(): return lax.ppermute(value, axis, pairs)  63 us
    ppermute x14, waiting for transfers between devices, passed_along(): return lax.ppermute(value, axis, pairs)  31.4 us
    dot_general x8, matrix products, expert_pass(): jnp.dot(hidden, w_second, preferred_element_type=jnp.float32)  30.1 us
    ppermute x3, starting transfers between devices, layer_body(): returned = lax.ppermute(sums[j].astype(jnp.bfloat16), ('q2', 'zh'), home)  27.5 us
    ppermute x3, waiting for transfers between devices, layer_body(): far = lax.ppermute(packed, ('q2', 'zh'), shifted_pairs((n_q, n_zh), (a, c)))  21.7 us
    all_to_all x1, blocking collectives, expert_pass(): lax.all_to_all(slot_grid, QUARTER, split_axis=1, concat_axis=1, tiled=True)  16.6 us
    ppermute x3, starting transfers between devices, layer_body(): far = lax.ppermute(packed, ('q2', 'zh'), shifted_pairs((n_q, n_zh), (a, c)))  16.2 us
    all_to_all x2, starting transfers between devices, expert_pass(): lax.all_to_all(summed.astype(jnp.bfloat16).reshape(lead, n_local, model_w...  13.9 us
  transfers between devices with their start and end apart: 23, of which 12 were waited for; matrix products, arithmetic and copies ran while one was open for 15% of the time, Pallas kernels for 0%

profile of v13, /device:TPU:1, one launch (start us, length us, event | category | flops | bytes accessed | tf_op | source)
XLA Modules:
  0.0 250.6 jit_solution(15013345539872863171)
XLA Ops:
  0.0 8.9 %collective-permute-start = (bf16[1,16,4096]{2,1,0:T(8,128)(2,1)}, bf16[1,16,4096]{2,1,0:T(8,128)(2,1)S(1)}, u32[]{:S(2)}, u32[]{:S(2)}) collective-permute-start(bf16[1,16,4096]{2,1,0:T(8,128)(2,1)} %param.6), channel_id=1, source_target_pairs={{0,256},{256,0},{1,257},{257,1},{2,258},{258,2},{3,259},{259,3},{4... | collective-permute-start | bytes 393224 | tf_op jit(solution)/shard_map/ppermute | solution.py:14
  14.5 10.6 %collective-permute-start.10 = (bf16[16,4224]{1,0:T(8,128)(2,1)S(1)}, bf16[16,4224]{1,0:T(8,128)(2,1)S(1)}, u32[]{:S(2)}, u32[]{:S(2)}) collective-permute-start(bf16[16,4224]{1,0:T(8,128)(2,1)S(1)} %fusion.38), channel_id=1, source_target_pairs={{0,1},{1,0},{128,129},{129,128},{2,3},{3,2},{130,131},{131,130},{4... | collective-permute-start | bytes 405512 | tf_op jit(solution)/shard_map/ppermute | solution.py:128
  30.3 20.3 %collective-permute-done.9 = bf16[16,4224]{1,0:T(8,128)(2,1)S(1)} collective-permute-done((bf16[16,4224]{1,0:T(8,128)(2,1)S(1)}, bf16[16,4224]{1,0:T(8,128)(2,1)S(1)}, u32[]{:S(2)}, u32[]{:S(2)}) %collective-permute-start.9) | collective-permute-done | bytes 135200 | tf_op jit(solution)/shard_map/ppermute | solution.py:128
  54.4 16.6 %all_to_all.20 = bf16[4,16,4096]{2,0,1:T(4,128)(2,1)S(1)} all-to-all(bf16[4,16,4096]{2,0,1:T(4,128)(2,1)S(1)} %copy.170), channel_id=1, replica_groups=mesh['section'=2,'q2'=2,'r'=4,'x'=4,'y'=4,'zh'=2] {'r','x'}, dimensions={1} | all-to-all | bytes 1048576 | tf_op jit(solution)/shard_map/all_to_all | solution.py:65
  71.3 4.7 %collective-permute-start.15 = (bf16[4,16,4096]{2,1,0:T(8,128)(2,1)S(1)}, bf16[4,16,4096]{2,1,0:T(8,128)(2,1)}, u32[]{:S(2)}, u32[]{:S(2)}) collective-permute-start(bf16[4,16,4096]{2,1,0:T(8,128)(2,1)S(1)} %copy.171), channel_id=1, source_target_pairs={{0,6},{2,0},{4,2},{6,4},{1,7},{3,1},{5,3},{7,5},{8,14},{10,8},{12,... | collective-permute-start | bytes 1572872 | tf_op jit(solution)/shard_map/ppermute | solution.py:14
  77.5 5.5 %all-to-all-start = ((bf16[4,16,4096]{2,0,1:T(4,128)(2,1)}), bf16[4,16,4096]{2,0,1:T(4,128)(2,1)S(1)}, u32[]{:S(2)}, u32[]{:S(2)}) async-start(bf16[4,16,4096]{2,0,1:T(4,128)(2,1)} %copy.159), calls=%async_computation | async-start | bytes 1048576 | tf_op jit(solution)/shard_map/all_to_all | solution.py:65
  87.9 4.0 %convolution_convert_fusion.2 = bf16[64,4096]{1,0:T(8,128)(2,1)} fusion(bf16[1,1,256,4096]{3,2,1,0:T(8,128)(2,1)S(1)} %copy-done, bf16[64,4096]{1,0:T(8,128)(2,1)} %bitcast.22, bf16[1,1,4096,256]{3,2,1,0:T(8,128)(2,1)} %param.9), kind=kOutput, calls=%fused_computation.2 | convolution fusion | flops 268845056 | bytes 5242880 | tf_op jit(solution)/shard_map/dot_general | solution.py:72
  97.8 4.0 %convolution_convert_fusion.3 = bf16[64,4096]{1,0:T(8,128)(2,1)} fusion(bf16[1,1,256,4096]{3,2,1,0:T(8,128)(2,1)S(1)} %copy-done, bf16[64,4096]{1,0:T(8,128)(2,1)} %bitcast.21, bf16[1,1,4096,256]{3,2,1,0:T(8,128)(2,1)} %param.9), kind=kOutput, calls=%fused_computation.3 | convolution fusion | flops 268845056 | bytes 5242880 | tf_op jit(solution)/shard_map/dot_general | solution.py:72
  104.0 7.6 %collective-permute-done.11 = bf16[4,16,4096]{2,1,0:T(8,128)(2,1)} collective-permute-done((bf16[4,16,4096]{2,1,0:T(8,128)(2,1)S(1)}, bf16[4,16,4096]{2,1,0:T(8,128)(2,1)}, u32[]{:S(2)}, u32[]{:S(2)}) %collective-permute-start.11) | collective-permute-done | bytes 524320 | tf_op jit(solution)/shard_map/ppermute | solution.py:14
  111.6 4.0 %convolution_convert_fusion.4 = bf16[64,4096]{1,0:T(8,128)(2,1)} fusion(bf16[1,1,256,4096]{3,2,1,0:T(8,128)(2,1)S(1)} %copy-done, bf16[64,4096]{1,0:T(8,128)(2,1)} %bitcast.20, bf16[1,1,4096,256]{3,2,1,0:T(8,128)(2,1)} %param.9), kind=kOutput, calls=%fused_computation.4 | convolution fusion | flops 268845056 | bytes 5242880 | tf_op jit(solution)/shard_map/dot_general | solution.py:72
  121.1 4.5 %collective-permute-start.4 = (bf16[4,16,4096]{2,1,0:T(8,128)(2,1)}, bf16[4,16,4096]{2,1,0:T(8,128)(2,1)}, u32[]{:S(2)}, u32[]{:S(2)}) collective-permute-start(bf16[4,16,4096]{2,1,0:T(8,128)(2,1)} %copy.160), channel_id=1, source_target_pairs={{0,4},{2,6},{4,0},{6,2},{1,5},{3,7},{5,1},{7,3},{8,12},{10,14},{12... | collective-permute-start | bytes 1572872 | tf_op jit(solution)/shard_map/ppermute | solution.py:14
  136.1 6.7 %all-to-all-start.3 = ((bf16[4,16,4096]{2,0,1:T(4,128)(2,1)}), bf16[4,16,4096]{2,0,1:T(4,128)(2,1)S(1)}, u32[]{:S(2)}, u32[]{:S(2)}) async-start(bf16[4,16,4096]{2,0,1:T(4,128)(2,1)} %copy.175), calls=%async_computation.3 | async-start | bytes 1048576 | tf_op jit(solution)/shard_map/all_to_all | solution.py:77
  152.0 7.2 %collective-permute-start.5 = (bf16[64,4096]{1,0:T(8,128)(2,1)}, bf16[64,4096]{1,0:T(8,128)(2,1)}, u32[]{:S(2)}, u32[]{:S(2)}) collective-permute-start(bf16[64,4096]{1,0:T(8,128)(2,1)} %convolution_convert_fusion.7), channel_id=1, source_target_pairs={{0,4},{2,6},{4,0},{6,2},{1,5},{3,7},{5,1},{7,3},{8,12},{10,14},{12... | collective-permute-start | bytes 1572872 | tf_op jit(solution)/shard_map/ppermute | solution.py:14
  159.2 4.0 %convolution_convert_fusion.8 = bf16[64,4096]{1,0:T(8,128)(2,1)} fusion(bf16[1,1,256,4096]{3,2,1,0:T(8,128)(2,1)S(1)} %copy-done, bf16[64,4096]{1,0:T(8,128)(2,1)} %bitcast.11, bf16[1,1,4096,256]{3,2,1,0:T(8,128)(2,1)} %param.9), kind=kOutput, calls=%fused_computation.9 | convolution fusion | flops 268845056 | bytes 5242880 | tf_op jit(solution)/shard_map/dot_general | solution.py:72
  163.1 5.1 %collective-permute-start.3 = (bf16[64,4096]{1,0:T(8,128)(2,1)}, bf16[64,4096]{1,0:T(8,128)(2,1)S(1)}, u32[]{:S(2)}, u32[]{:S(2)}) collective-permute-start(bf16[64,4096]{1,0:T(8,128)(2,1)} %convolution_convert_fusion.8), channel_id=1, source_target_pairs={{0,6},{2,0},{4,2},{6,4},{1,7},{3,1},{5,3},{7,5},{8,14},{10,8},{12,... | collective-permute-start | bytes 1572872 | tf_op jit(solution)/shard_map/ppermute | solution.py:14
  168.3 8.5 %collective-permute-done.5 = bf16[64,4096]{1,0:T(8,128)(2,1)} collective-permute-done((bf16[64,4096]{1,0:T(8,128)(2,1)}, bf16[64,4096]{1,0:T(8,128)(2,1)}, u32[]{:S(2)}, u32[]{:S(2)}) %collective-permute-start.5) | collective-permute-done | bytes 524320 | tf_op jit(solution)/shard_map/ppermute | solution.py:14
  176.8 7.5 %collective-permute-done.3 = bf16[64,4096]{1,0:T(8,128)(2,1)S(1)} collective-permute-done((bf16[64,4096]{1,0:T(8,128)(2,1)}, bf16[64,4096]{1,0:T(8,128)(2,1)S(1)}, u32[]{:S(2)}, u32[]{:S(2)}) %collective-permute-start.3) | collective-permute-done | bytes 524320 | tf_op jit(solution)/shard_map/ppermute | solution.py:14
  190.0 7.2 %all-to-all-start.1 = ((bf16[4,16,4096]{2,0,1:T(4,128)(2,1)}), bf16[4,16,4096]{2,0,1:T(4,128)(2,1)S(1)}, u32[]{:S(2)}, u32[]{:S(2)}) async-start(bf16[4,16,4096]{2,0,1:T(4,128)(2,1)} %copy.164), calls=%async_computation.1 | async-start | bytes 1048576 | tf_op jit(solution)/shard_map/all_to_all | solution.py:77
  197.9 9.2 %collective-permute-start.18 = (bf16[16,4096]{1,0:T(8,128)(2,1)S(1)}, bf16[16,4096]{1,0:T(8,128)(2,1)S(1)}, u32[]{:S(2)}, u32[]{:S(2)}) collective-permute-start(bf16[16,4096]{1,0:T(8,128)(2,1)S(1)} %get-tuple-element.10), channel_id=1, source_target_pairs={{0,1},{1,0},{128,129},{129,128},{2,3},{3,2},{130,131},{131,130},{4... | collective-permute-start | bytes 393224 | tf_op jit(solution)/shard_map/ppermute | solution.py:145
  207.1 6.6 %collective-permute-start.17 = (bf16[16,4096]{1,0:T(8,128)(2,1)S(1)}, bf16[16,4096]{1,0:T(8,128)(2,1)S(1)}, u32[]{:S(2)}, u32[]{:S(2)}) collective-permute-start(bf16[16,4096]{1,0:T(8,128)(2,1)S(1)} %get-tuple-element.9), channel_id=1, source_target_pairs={{0,129},{1,128},{128,1},{129,0},{2,131},{3,130},{130,3},{131,2},{4... | collective-permute-start | bytes 393224 | tf_op jit(solution)/shard_map/ppermute | solution.py:145
  214.4 11.7 %collective-permute-start.8 = (bf16[16,4096]{1,0:T(8,128)(2,1)S(1)}, bf16[16,4096]{1,0:T(8,128)(2,1)S(1)}, u32[]{:S(2)}, u32[]{:S(2)}) collective-permute-start(bf16[16,4096]{1,0:T(8,128)(2,1)S(1)} %slice.65), channel_id=1, source_target_pairs={{0,128},{1,129},{128,0},{129,1},{2,130},{3,131},{130,2},{131,3},{4... | collective-permute-start | bytes 393224 | tf_op jit(solution)/shard_map/ppermute | solution.py:145
  226.1 4.1 %collective-permute-done.17 = bf16[16,4096]{1,0:T(8,128)(2,1)S(1)} collective-permute-done((bf16[16,4096]{1,0:T(8,128)(2,1)S(1)}, bf16[16,4096]{1,0:T(8,128)(2,1)S(1)}, u32[]{:S(2)}, u32[]{:S(2)}) %collective-permute-start.17) | collective-permute-done | bytes 131104 | tf_op jit(solution)/shard_map/ppermute | solution.py:145
  230.2 5.0 %collective-permute-done.8 = bf16[16,4096]{1,0:T(8,128)(2,1)S(1)} collective-permute-done((bf16[16,4096]{1,0:T(8,128)(2,1)S(1)}, bf16[16,4096]{1,0:T(8,128)(2,1)S(1)}, u32[]{:S(2)}, u32[]{:S(2)}) %collective-permute-start.8) | collective-permute-done | bytes 131104 | tf_op jit(solution)/shard_map/ppermute | solution.py:145
  235.3 13.7 %collective-permute-start.19 = (bf16[1,16,4096]{2,1,0:T(8,128)(2,1)S(1)}, bf16[1,16,4096]{2,1,0:T(8,128)(2,1)S(1)}, u32[]{:S(2)}, u32[]{:S(2)}) collective-permute-start(bf16[1,16,4096]{2,1,0:T(8,128)(2,1)S(1)} %fusion.39), channel_id=1, source_target_pairs={{0,256},{256,0},{1,257},{257,1},{2,258},{258,2},{3,259},{259,3},{4... | collective-permute-start | bytes 393224 | tf_op jit(solution)/shard_map/ppermute | solution.py:14
  (102 shorter events, 62.9 us)
Async XLA Ops:
  0.0 87.9 %copy-start = (bf16[1,1,256,4096]{3,2,1,0:T(8,128)(2,1)S(1)}, bf16[1,1,256,4096]{3,2,1,0:T(8,128)(2,1)}, u32[]{:S(2)}) copy-start(bf16[1,1,256,4096]{3,2,1,0:T(8,128)(2,1)} %param.10) | copy-start | bytes 6291460
  0.0 10.0 %collective-permute-start = (bf16[1,16,4096]{2,1,0:T(8,128)(2,1)}, bf16[1,16,4096]{2,1,0:T(8,128)(2,1)S(1)}, u32[]{:S(2)}, u32[]{:S(2)}) collective-permute-start(bf16[1,16,4096]{2,1,0:T(8,128)(2,1)} %param.6), channel_id=1, source_target_pairs={{0,256},{256,0},{1,257},{257,1},{2,258},{258,2},{3,259},{259,3},{4... | collective-permute-start | bytes 393224 | tf_op jit(solution)/shard_map/ppermute | solution.py:14
  11.1 17.6 %collective-permute-start.1 = (bf16[16,4224]{1,0:T(8,128)(2,1)S(1)}, bf16[16,4224]{1,0:T(8,128)(2,1)S(1)}, u32[]{:S(2)}, u32[]{:S(2)}) collective-permute-start(bf16[16,4224]{1,0:T(8,128)(2,1)S(1)} %fusion.38), channel_id=1, source_target_pairs={{0,128},{1,129},{128,0},{129,1},{2,130},{3,131},{130,2},{131,3},{4... | collective-permute-start | bytes 405512 | tf_op jit(solution)/shard_map/ppermute | solution.py:128
  14.5 15.6 %collective-permute-start.10 = (bf16[16,4224]{1,0:T(8,128)(2,1)S(1)}, bf16[16,4224]{1,0:T(8,128)(2,1)S(1)}, u32[]{:S(2)}, u32[]{:S(2)}) collective-permute-start(bf16[16,4224]{1,0:T(8,128)(2,1)S(1)} %fusion.38), channel_id=1, source_target_pairs={{0,1},{1,0},{128,129},{129,128},{2,3},{3,2},{130,131},{131,130},{4... | collective-permute-start | bytes 405512 | tf_op jit(solution)/shard_map/ppermute | solution.py:128
  25.2 25.4 %collective-permute-start.9 = (bf16[16,4224]{1,0:T(8,128)(2,1)S(1)}, bf16[16,4224]{1,0:T(8,128)(2,1)S(1)}, u32[]{:S(2)}, u32[]{:S(2)}) collective-permute-start(bf16[16,4224]{1,0:T(8,128)(2,1)S(1)} %fusion.38), channel_id=1, source_target_pairs={{0,129},{1,128},{128,1},{129,0},{2,131},{3,130},{130,3},{131,2},{4... | collective-permute-start | bytes 405512 | tf_op jit(solution)/shard_map/ppermute | solution.py:128
  71.3 16.6 %collective-permute-start.15 = (bf16[4,16,4096]{2,1,0:T(8,128)(2,1)S(1)}, bf16[4,16,4096]{2,1,0:T(8,128)(2,1)}, u32[]{:S(2)}, u32[]{:S(2)}) collective-permute-start(bf16[4,16,4096]{2,1,0:T(8,128)(2,1)S(1)} %copy.171), channel_id=1, source_target_pairs={{0,6},{2,0},{4,2},{6,4},{1,7},{3,1},{5,3},{7,5},{8,14},{10,8},{12,... | collective-permute-start | bytes 1572872 | tf_op jit(solution)/shard_map/ppermute | solution.py:14
  77.5 40.0 %all-to-all-start = ((bf16[4,16,4096]{2,0,1:T(4,128)(2,1)}), bf16[4,16,4096]{2,0,1:T(4,128)(2,1)S(1)}, u32[]{:S(2)}, u32[]{:S(2)}) async-start(bf16[4,16,4096]{2,0,1:T(4,128)(2,1)} %copy.159), calls=%async_computation | async-start | bytes 1048576 | tf_op jit(solution)/shard_map/all_to_all | solution.py:65
  83.0 14.8 %collective-permute-start.13 = (bf16[4,16,4096]{2,1,0:T(8,128)(2,1)S(1)}, bf16[4,16,4096]{2,1,0:T(8,128)(2,1)}, u32[]{:S(2)}, u32[]{:S(2)}) collective-permute-start(bf16[4,16,4096]{2,1,0:T(8,128)(2,1)S(1)} %copy.171), channel_id=1, source_target_pairs={{0,4},{2,6},{4,0},{6,2},{1,5},{3,7},{5,1},{7,3},{8,12},{10,14},{12... | collective-permute-start | bytes 1572872 | tf_op jit(solution)/shard_map/ppermute | solution.py:14
  85.3 26.3 %collective-permute-start.11 = (bf16[4,16,4096]{2,1,0:T(8,128)(2,1)S(1)}, bf16[4,16,4096]{2,1,0:T(8,128)(2,1)}, u32[]{:S(2)}, u32[]{:S(2)}) collective-permute-start(bf16[4,16,4096]{2,1,0:T(8,128)(2,1)S(1)} %copy.171), channel_id=1, source_target_pairs={{0,2},{2,4},{4,6},{6,0},{1,3},{3,5},{5,7},{7,1},{8,10},{10,12},{12... | collective-permute-start | bytes 1572872 | tf_op jit(solution)/shard_map/ppermute | solution.py:14
  91.9 33.8 %collective-permute-start.16 = (bf16[64,4096]{1,0:T(8,128)(2,1)}, bf16[64,4096]{1,0:T(8,128)(2,1)}, u32[]{:S(2)}, u32[]{:S(2)}) collective-permute-start(bf16[64,4096]{1,0:T(8,128)(2,1)} %convolution_convert_fusion.2), channel_id=1, source_target_pairs={{0,2},{2,4},{4,6},{6,0},{1,3},{3,5},{5,7},{7,1},{8,10},{10,12},{12... | collective-permute-start | bytes 1572872 | tf_op jit(solution)/shard_map/ppermute | solution.py:14
  101.7 29.7 %collective-permute-start.14 = (bf16[64,4096]{1,0:T(8,128)(2,1)}, bf16[64,4096]{1,0:T(8,128)(2,1)}, u32[]{:S(2)}, u32[]{:S(2)}) collective-permute-start(bf16[64,4096]{1,0:T(8,128)(2,1)} %convolution_convert_fusion.3), channel_id=1, source_target_pairs={{0,4},{2,6},{4,0},{6,2},{1,5},{3,7},{5,1},{7,3},{8,12},{10,14},{12... | collective-permute-start | bytes 1572872 | tf_op jit(solution)/shard_map/ppermute | solution.py:14
  115.6 15.9 %collective-permute-start.12 = (bf16[64,4096]{1,0:T(8,128)(2,1)}, bf16[64,4096]{1,0:T(8,128)(2,1)}, u32[]{:S(2)}, u32[]{:S(2)}) collective-permute-start(bf16[64,4096]{1,0:T(8,128)(2,1)} %convolution_convert_fusion.4), channel_id=1, source_target_pairs={{0,6},{2,0},{4,2},{6,4},{1,7},{3,1},{5,3},{7,5},{8,14},{10,8},{12,... | collective-permute-start | bytes 1572872 | tf_op jit(solution)/shard_map/ppermute | solution.py:14
  118.6 24.3 %collective-permute-start.6 = (bf16[4,16,4096]{2,1,0:T(8,128)(2,1)}, bf16[4,16,4096]{2,1,0:T(8,128)(2,1)}, u32[]{:S(2)}, u32[]{:S(2)}) collective-permute-start(bf16[4,16,4096]{2,1,0:T(8,128)(2,1)} %copy.160), channel_id=1, source_target_pairs={{0,6},{2,0},{4,2},{6,4},{1,7},{3,1},{5,3},{7,5},{8,14},{10,8},{12,... | collective-permute-start | bytes 1572872 | tf_op jit(solution)/shard_map/ppermute | solution.py:14
  121.1 26.9 %collective-permute-start.4 = (bf16[4,16,4096]{2,1,0:T(8,128)(2,1)}, bf16[4,16,4096]{2,1,0:T(8,128)(2,1)}, u32[]{:S(2)}, u32[]{:S(2)}) collective-permute-start(bf16[4,16,4096]{2,1,0:T(8,128)(2,1)} %copy.160), channel_id=1, source_target_pairs={{0,4},{2,6},{4,0},{6,2},{1,5},{3,7},{5,1},{7,3},{8,12},{10,14},{12... | collective-permute-start | bytes 1572872 | tf_op jit(solution)/shard_map/ppermute | solution.py:14
  125.7 33.5 %collective-permute-start.2 = (bf16[4,16,4096]{2,1,0:T(8,128)(2,1)}, bf16[4,16,4096]{2,1,0:T(8,128)(2,1)}, u32[]{:S(2)}, u32[]{:S(2)}) collective-permute-start(bf16[4,16,4096]{2,1,0:T(8,128)(2,1)} %copy.160), channel_id=1, source_target_pairs={{0,2},{2,4},{4,6},{6,0},{1,3},{3,5},{5,7},{7,1},{8,10},{10,12},{12... | collective-permute-start | bytes 1572872 | tf_op jit(solution)/shard_map/ppermute | solution.py:14
  136.1 53.9 %all-to-all-start.3 = ((bf16[4,16,4096]{2,0,1:T(4,128)(2,1)}), bf16[4,16,4096]{2,0,1:T(4,128)(2,1)S(1)}, u32[]{:S(2)}, u32[]{:S(2)}) async-start(bf16[4,16,4096]{2,0,1:T(4,128)(2,1)} %copy.175), calls=%async_computation.3 | async-start | bytes 1048576 | tf_op jit(solution)/shard_map/all_to_all | solution.py:77
  146.1 22.2 %collective-permute-start.7 = (bf16[64,4096]{1,0:T(8,128)(2,1)S(1)}, bf16[64,4096]{1,0:T(8,128)(2,1)}, u32[]{:S(2)}, u32[]{:S(2)}) collective-permute-start(bf16[64,4096]{1,0:T(8,128)(2,1)S(1)} %convolution_convert_fusion.6), channel_id=1, source_target_pairs={{0,2},{2,4},{4,6},{6,0},{1,3},{3,5},{5,7},{7,1},{8,10},{10,12},{12... | collective-permute-start | bytes 1572872 | tf_op jit(solution)/shard_map/ppermute | solution.py:14
  152.0 24.9 %collective-permute-start.5 = (bf16[64,4096]{1,0:T(8,128)(2,1)}, bf16[64,4096]{1,0:T(8,128)(2,1)}, u32[]{:S(2)}, u32[]{:S(2)}) collective-permute-start(bf16[64,4096]{1,0:T(8,128)(2,1)} %convolution_convert_fusion.7), channel_id=1, source_target_pairs={{0,4},{2,6},{4,0},{6,2},{1,5},{3,7},{5,1},{7,3},{8,12},{10,14},{12... | collective-permute-start | bytes 1572872 | tf_op jit(solution)/shard_map/ppermute | solution.py:14
  163.1 21.2 %collective-permute-start.3 = (bf16[64,4096]{1,0:T(8,128)(2,1)}, bf16[64,4096]{1,0:T(8,128)(2,1)S(1)}, u32[]{:S(2)}, u32[]{:S(2)}) collective-permute-start(bf16[64,4096]{1,0:T(8,128)(2,1)} %convolution_convert_fusion.8), channel_id=1, source_target_pairs={{0,6},{2,0},{4,2},{6,4},{1,7},{3,1},{5,3},{7,5},{8,14},{10,8},{12,... | collective-permute-start | bytes 1572872 | tf_op jit(solution)/shard_map/ppermute | solution.py:14
  190.0 23.7 %all-to-all-start.1 = ((bf16[4,16,4096]{2,0,1:T(4,128)(2,1)}), bf16[4,16,4096]{2,0,1:T(4,128)(2,1)S(1)}, u32[]{:S(2)}, u32[]{:S(2)}) async-start(bf16[4,16,4096]{2,0,1:T(4,128)(2,1)} %copy.164), calls=%async_computation.1 | async-start | bytes 1048576 | tf_op jit(solution)/shard_map/all_to_all | solution.py:77
  197.9 28.2 %collective-permute-start.18 = (bf16[16,4096]{1,0:T(8,128)(2,1)S(1)}, bf16[16,4096]{1,0:T(8,128)(2,1)S(1)}, u32[]{:S(2)}, u32[]{:S(2)}) collective-permute-start(bf16[16,4096]{1,0:T(8,128)(2,1)S(1)} %get-tuple-element.10), channel_id=1, source_target_pairs={{0,1},{1,0},{128,129},{129,128},{2,3},{3,2},{130,131},{131,130},{4... | collective-permute-start | bytes 393224 | tf_op jit(solution)/shard_map/ppermute | solution.py:145
  207.1 23.1 %collective-permute-start.17 = (bf16[16,4096]{1,0:T(8,128)(2,1)S(1)}, bf16[16,4096]{1,0:T(8,128)(2,1)S(1)}, u32[]{:S(2)}, u32[]{:S(2)}) collective-permute-start(bf16[16,4096]{1,0:T(8,128)(2,1)S(1)} %get-tuple-element.9), channel_id=1, source_target_pairs={{0,129},{1,128},{128,1},{129,0},{2,131},{3,130},{130,3},{131,2},{4... | collective-permute-start | bytes 393224 | tf_op jit(solution)/shard_map/ppermute | solution.py:145
  214.4 20.8 %collective-permute-start.8 = (bf16[16,4096]{1,0:T(8,128)(2,1)S(1)}, bf16[16,4096]{1,0:T(8,128)(2,1)S(1)}, u32[]{:S(2)}, u32[]{:S(2)}) collective-permute-start(bf16[16,4096]{1,0:T(8,128)(2,1)S(1)} %slice.65), channel_id=1, source_target_pairs={{0,128},{1,129},{128,0},{129,1},{2,130},{3,131},{130,2},{131,3},{4... | collective-permute-start | bytes 393224 | tf_op jit(solution)/shard_map/ppermute | solution.py:145
  235.3 14.7 %collective-permute-start.19 = (bf16[1,16,4096]{2,1,0:T(8,128)(2,1)S(1)}, bf16[1,16,4096]{2,1,0:T(8,128)(2,1)S(1)}, u32[]{:S(2)}, u32[]{:S(2)}) collective-permute-start(bf16[1,16,4096]{2,1,0:T(8,128)(2,1)S(1)} %fusion.39), channel_id=1, source_target_pairs={{0,256},{256,0},{1,257},{257,1},{2,258},{258,2},{3,259},{259,3},{4... | collective-permute-start | bytes 393224 | tf_op jit(solution)/shard_map/ppermute | solution.py:14
  (2 other events, 53.9 us)
